TPU v7x, 32 devices: a whole 2x2x4 slice. The times are simulated.
32 devices in a mesh: sep: 2 (over x), row: 16 (over z, y, core).
Axes of the slice: x: 2, y: 2, z: 4, core: 2. Of those that a mesh axis runs over, the one named last changes fastest.
Arguments:
- right_sides: bfloat16 [256, 256, 128], P(('sep', 'row')), parts along dimension 0, may hold values from -6 to 6
- diagonal_blocks: bfloat16 [256, 256, 256], P(('sep', 'row')), parts along dimension 0, may hold values from -0.375 to 0.375
- lower_rows: bfloat16 [256, 256, 256], P(('sep', 'row')), parts along dimension 0, may hold values from -0.375 to 0.375
- lower_cols: bfloat16 [256, 256, 256], P(('sep', 'row')), parts along dimension 0, may hold values from -0.09375 to 0.09375
- lower_trans: bfloat16 [256, 256, 256], P(('sep', 'row')), parts along dimension 0, may hold values from -2 to 2
- upper_rows: bfloat16 [256, 256, 256], P(('sep', 'row')), parts along dimension 0, may hold values from -0.375 to 0.375
- upper_cols: bfloat16 [256, 256, 256], P(('sep', 'row')), parts along dimension 0, may hold values from -0.09375 to 0.09375
- upper_trans: bfloat16 [256, 256, 256], P(('sep', 'row')), parts along dimension 0, may hold values from -2 to 2
Outputs:
- product: bfloat16 [256, 256, 128], P(('sep', 'row')), parts along dimension 0
There are 2 independent parts, one for each index of `sep`. A program takes and returns all parts, laid end to end along the dimension named above; each array names one. Nothing has to cross between parts.
All inputs are finite; a program needn't handle non-finite values.
Results may differ from a plain program's by a relative error of at most 0.0045.
Values sent between devices are 32-bit elements; how exact they have to be, the bound alone decides.
No kernel may reach another device: no remote copies, remote signals or barrier semaphores. Data moves between devices by JAX's collectives and lax.ppermute only.
A program may use at most 192 MiB of HBM per device.

v0:
```python
import jax
import jax.numpy as jnp
from jax import lax
from jax.sharding import PartitionSpec as P


def prefix(part, axis, combine, identity, reverse):
    count = lax.axis_size(axis)
    place = lax.axis_index(axis)
    ahead = count - 1 - place if reverse else place
    gathered = jax.tree.map(lambda a: lax.all_gather(a, axis), part)
    state = jax.tree.map(lambda a, e: jnp.zeros_like(a) + jnp.asarray(e, a.dtype), part, identity)

    def one(lap, state):
        source = count - 1 - lap if reverse else lap
        return combine(
            state, jax.tree.map(lambda a: lax.dynamic_index_in_dim(a, source, 0, False), gathered)
        )

    return lax.fori_loop(0, ahead, one, state)


def compose(earlier, later):
    early_map, early_state = earlier
    late_map, late_state = later
    joined_map = jnp.dot(late_map, early_map, precision=lax.Precision.HIGHEST)
    joined_state = jnp.dot(late_map, early_state, precision=lax.Precision.HIGHEST) + late_state
    return (joined_map, joined_state)


def local_sweep(transfer, sources, backward):
    order_rank = transfer.shape[1]

    def advance(carry, pair):
        product_now, state_now = carry
        matrix, source = pair
        state_next = jnp.dot(matrix, state_now, precision=lax.Precision.HIGHEST) + source
        product_next = jnp.dot(matrix, product_now, precision=lax.Precision.HIGHEST)
        return ((product_next, state_next), (product_now, state_now))

    start = (
        jnp.eye(order_rank, dtype=jnp.float32),
        jnp.zeros((order_rank, sources.shape[2]), jnp.float32),
    )
    summary, entering = lax.scan(advance, start, (transfer, sources), reverse=backward)
    return (summary, entering[0], entering[1])


def shards(
    right_sides,
    diagonal_blocks,
    lower_rows,
    lower_cols,
    lower_trans,
    upper_rows,
    upper_cols,
    upper_trans,
):
    lower_source = jnp.einsum(
        "kbr,kbc->krc", lower_cols, right_sides, preferred_element_type=jnp.float32
    )
    upper_source = jnp.einsum(
        "kbr,kbc->krc", upper_cols, right_sides, preferred_element_type=jnp.float32
    )
    lower_summary, lower_prefix, lower_local = local_sweep(
        lower_trans.astype(jnp.float32), lower_source, False
    )
    upper_summary, upper_prefix, upper_local = local_sweep(
        upper_trans.astype(jnp.float32), upper_source, True
    )
    neutral = (
        jnp.eye(lower_summary[0].shape[0], dtype=jnp.float32),
        jnp.zeros_like(lower_summary[1]),
    )
    lower_enter = prefix(lower_summary, "row", compose, neutral, False)[1]
    upper_enter = prefix(upper_summary, "row", compose, neutral, True)[1]
    lower_state = lower_local + jnp.einsum(
        "kij,jc->kic", lower_prefix, lower_enter, precision=lax.Precision.HIGHEST
    )
    upper_state = upper_local + jnp.einsum(
        "kij,jc->kic", upper_prefix, upper_enter, precision=lax.Precision.HIGHEST
    )
    total = jnp.einsum(
        "kab,kbc->kac", diagonal_blocks, right_sides, preferred_element_type=jnp.float32
    )
    total = total + jnp.einsum(
        "kbr,krc->kbc",
        lower_rows,
        lower_state.astype(jnp.bfloat16),
        preferred_element_type=jnp.float32,
    )
    total = total + jnp.einsum(
        "kbr,krc->kbc",
        upper_rows,
        upper_state.astype(jnp.bfloat16),
        preferred_element_type=jnp.float32,
    )
    return total.astype(jnp.bfloat16)


def solution(mesh):
    in_specs = (
        P(("sep", "row"), None, None),
        P(("sep", "row"), None, None),
        P(("sep", "row"), None, None),
        P(("sep", "row"), None, None),
        P(("sep", "row"), None, None),
        P(("sep", "row"), None, None),
        P(("sep", "row"), None, None),
        P(("sep", "row"), None, None),
    )
    out_specs = P(("sep", "row"), None, None)
    return jax.shard_map(shards, mesh=mesh, in_specs=in_specs, out_specs=out_specs, check_vma=False)
```

profile of v0, /device:TPU:1, one launch (start us, length us, event | category | flops | bytes accessed | tf_op | source)
XLA Modules:
  0.0 265.8 jit_solution(2359927775009474995)
XLA Ops:
  6.6 2.9 %convert_element_type.23 = f32[8,256,256]{2,1,0:T(8,128)} convert(bf16[8,256,256]{2,1,0:T(8,128)(2,1)} %param.20) | non-fusion elementwise | flops 524288 | bytes 3145728 | tf_op jit(solution)/shard_map/convert_element_type | solution.py:66
  9.5 1.5 fusion.35
  11.0 1.5 broadcast.10.clone.1
  12.5 28.2 %while.66 = (s32[]{:T(128)}, f32[256,256]{1,0:T(8,128)S(1)}, f32[256,128]{1,0:T(8,128)S(1)}, f32[8,256,256]{2,1,0:T(8,128)}, f32[8,256,128]{2,1,0:T(8,128)S(1)},...) while((s32[]{:T(128)}, f32[256,256]{1,0:T(8,128)S(1)}, ...), condition=%wide.region_1.2_spmd.clone, body=%wide.region_0.1_spmd.clone.sunk | while | flops 302088192 | bytes 3016812 | solution.py:45
  12.6 1.4 convolution_add_fusion.13
  14.7 1.3 fusion.75
  16.1 1.4 convolution_add_fusion.13
  18.3 1.3 fusion.75
  19.7 1.4 convolution_add_fusion.13
  21.8 1.3 fusion.75
  23.2 1.4 convolution_add_fusion.13
  25.3 1.3 fusion.75
  26.7 1.4 convolution_add_fusion.13
  28.9 1.3 fusion.75
  30.2 1.4 convolution_add_fusion.13
  32.4 1.3 fusion.75
  33.8 1.4 convolution_add_fusion.13
  35.9 1.3 fusion.75
  37.3 1.4 convolution_add_fusion.13
  39.4 1.3 fusion.75
  42.3 1.5 convert_element_type.25
  43.8 2.5 fusion.36
  46.3 1.5 broadcast.10.clone
  48.9 25.1 %while.67 = (s32[]{:T(128)}, f32[256,256]{1,0:T(8,128)S(1)}, f32[256,128]{1,0:T(8,128)S(1)}, f32[8,256,256]{2,1,0:T(8,128)}, f32[8,256,128]{2,1,0:T(8,128)}, /*i...) while((s32[]{:T(128)}, f32[256,256]{1,0:T(8,128)S(1)}, ...), condition=%wide.region_5.6_spmd.clone, body=%wide.region_4.5_spmd.clone.sunk | while | flops 302088192 | bytes 3016327 | solution.py:45
  68.4 1.3 convolution_add_fusion.14
  75.3 10.3 %all-gather.11.cloned.1.call-done = f32[4096,128]{1,0:T(8,128)} async-done(((f32[256,128]{1,0:T(8,128)}), f32[4096,128]{1,0:T(8,128)}) %all-gather.11.cloned.1.call-update) | async-done | bytes 2097168 | tf_op jit(solution)/shard_map/all_gather | solution.py:11
  85.5 51.3 %all-gather.9.cloned.1.call-done = f32[4096,256]{1,0:T(8,128)} async-done(((f32[256,256]{1,0:T(8,128)}), f32[4096,256]{1,0:T(8,128)}) %all-gather.9.cloned.1.call-update) | async-done | bytes 4194320 | tf_op jit(solution)/shard_map/all_gather | solution.py:11
  136.8 1.6 while.64
  136.9 1.5 convolution_add_fusion.11
  138.4 40.6 %all-gather.15.cloned.1.call-done = f32[4096,128]{1,0:T(8,128)} async-done(((f32[256,128]{1,0:T(8,128)}), f32[4096,128]{1,0:T(8,128)}) %all-gather.15.cloned.1.call-update) | async-done | bytes 2097168 | tf_op jit(solution)/shard_map/all_gather | solution.py:11
  179.0 51.2 %all-gather.13.cloned.1.call-done = f32[4096,256]{1,0:T(8,128)} async-done(((f32[256,256]{1,0:T(8,128)}), f32[4096,256]{1,0:T(8,128)}) %all-gather.13.cloned.1.call-update) | async-done | bytes 4194320 | tf_op jit(solution)/shard_map/all_gather | solution.py:11
  230.2 19.8 %while.65 = (s32[]{:T(128)}, f32[256,128]{1,0:T(8,128)S(1)}, s32[]{:T(128)}, f32[16,256,256]{2,1,0:T(8,128)}, f32[16,256,128]{2,1,0:T(8,128)}, /*index=5*/s32[]{:T(128)}, s32[]{:T(128)}, s32[]{:T(128)}, s32[]{:T(128)}) while((s32[]{:T(128)}, f32[256,128]{1,0:T(8,128)S(1)}, s32[]{:T(128)}, f32[16,256,256]{2,1,0:T(8,128)}, ...), condition=%wide.region_7.8_spmd, body=%wide.region_6.7_spmd.sunk | while | flops 100696072 | bytes 918667 | solution.py:20
  230.2 1.4 convolution_add_fusion.12
  231.6 1.4 convolution_add_fusion.12
  233.1 1.4 convolution_add_fusion.12
  234.5 1.4 convolution_add_fusion.12
  235.9 1.4 convolution_add_fusion.12
  237.3 1.4 convolution_add_fusion.12
  238.7 1.4 convolution_add_fusion.12
  240.1 1.4 convolution_add_fusion.12
  241.5 1.4 convolution_add_fusion.12
  243.0 1.4 convolution_add_fusion.12
  244.4 1.4 convolution_add_fusion.12
  245.8 1.4 convolution_add_fusion.12
  247.2 1.4 convolution_add_fusion.12
  248.6 1.4 convolution_add_fusion.12
  250.0 3.2 %fusion.29 = bf16[8,256,128]{2,1,0:T(8,128)(2,1)S(1)} fusion(f32[8,256,128]{2,1,0:T(8,128)} %copy-done.9, f32[8,256,256]{2,1,0:T(8,128)S(1)} %copy-done.3, f32[256,128]{1,0:T(8,128)S(1)} %get-tuple-element.321), kind=kOutput, calls=%fused_computation.42 | convolution fusion | flops 805830656 | bytes 3801088 | tf_op jit(solution)/shard_map/kij,jc->kic/dot_general | solution.py:77
  254.8 1.8 fusion.30
  (143 shorter events, 37.8 us)
Async XLA Ops:
  6.5 2.9 %copy-start = (bf16[8,256,256]{2,1,0:T(8,128)(2,1)S(1)}, bf16[8,256,256]{2,1,0:T(8,128)(2,1)}, u32[]{:S(2)}) copy-start(bf16[8,256,256]{2,1,0:T(8,128)(2,1)} %param.19) | copy-start | bytes 3145732
  6.5 2.9 %copy-start.7 = (bf16[8,256,128]{2,1,0:T(8,128)(2,1)S(1)}, bf16[8,256,128]{2,1,0:T(8,128)(2,1)}, u32[]{:S(2)}) copy-start(bf16[8,256,128]{2,1,0:T(8,128)(2,1)} %param.16) | copy-start | bytes 1572868
  6.5 79.0 %all-gather.11.cloned.1.call-start = ((), (), s32[]{:S(2)}) async-start(), calls=%async_computation.1 | async-start | bytes 2228224 | tf_op jit(solution)/shard_map/all_gather | solution.py:11
  40.8 0.6 copy-start.5
  40.8 0.7 copy-start.2
  40.8 1.5 copy-start.9
  41.4 95.4 %all-gather.9.cloned.1.call-start = ((), (), s32[]{:S(2)}) async-start(), calls=%async_computation | async-start | bytes 4456448 | tf_op jit(solution)/shard_map/all_gather | solution.py:11
  42.2 136.8 %all-gather.15.cloned.1.call-start = ((), (), s32[]{:S(2)}) async-start(), calls=%async_computation.3 | async-start | bytes 2228224 | tf_op jit(solution)/shard_map/all_gather | solution.py:11
  42.3 1.5 copy-start.11
  74.0 0.7 copy-start.6
  74.0 0.7 copy-start.1
  74.7 155.5 %all-gather.13.cloned.1.call-start = ((), (), s32[]{:S(2)}) async-start(), calls=%async_computation.2 | async-start | bytes 4456448 | tf_op jit(solution)/shard_map/all_gather | solution.py:11
  136.8 113.2 %copy-start.3 = (f32[8,256,256]{2,1,0:T(8,128)S(1)}, f32[8,256,256]{2,1,0:T(8,128)}, u32[]{:S(2)}) copy-start(f32[8,256,256]{2,1,0:T(8,128)} %get-tuple-element.318) | copy-start | bytes 6291460
  250.0 3.2 %copy-start.12 = (bf16[8,256,256]{2,1,0:T(8,128)(2,1)S(1)}, bf16[8,256,256]{2,1,0:T(8,128)(2,1)}, u32[]{:S(2)}) copy-start(bf16[8,256,256]{2,1,0:T(8,128)(2,1)} %param.18) | copy-start | bytes 3145732
  250.0 3.6 %copy-start.10 = (f32[8,256,128]{2,1,0:T(8,128)S(1)}, f32[8,256,128]{2,1,0:T(8,128)}, u32[]{:S(2)}) copy-start(f32[8,256,128]{2,1,0:T(8,128)} %get-tuple-element.322) | copy-start | bytes 3145732
  253.2 1.6 copy-start.4
  253.6 3.0 %copy-start.13 = (bf16[8,256,256]{2,1,0:T(8,128)(2,1)S(1)}, bf16[8,256,256]{2,1,0:T(8,128)(2,1)}, u32[]{:S(2)}) copy-start(bf16[8,256,256]{2,1,0:T(8,128)(2,1)} %param.21) | copy-start | bytes 3145732
  256.7 1.0 copy-start.8
  256.7 1.4 copy-start.14
Sparse Core Ops, SparseCore 0:
  41.6 43.9 all-gather.10
  87.7 49.1 all-gather.8
  139.0 39.9 all-gather.14
  181.0 49.1 all-gather.12
where the time goes:
time: 269 us; the launch traced here: 266 us
  waiting for transfers between devices  155 us (58%)
  matrix products  66.6 us (25%)
  local copies, waits for them, and re-layouts  19.9 us (7%)
  between operations  13.4 us (5%)
  other arithmetic  9.87 us (4%)
    all_gather x4, waiting for transfers between devices, prefix(): gathered = jax.tree.map(lambda a: lax.all_gather(a, axis), part)  153 us
    dot_general x16, matrix products, advance(): jnp.dot(matrix, state_now, precision=lax.Precision.HIGHEST) + source  21.2 us
    dot_general x15, matrix products, compose(): jnp.dot(late_map, early_state, precision=lax.Precision.HIGHEST) + late_state  20.6 us
    dot_general x16, matrix products, advance(): product_next = jnp.dot(matrix, product_now, precision=lax.Precision.HIGHEST)  13.6 us
    dynamic_update_slice x16, local copies, waits for them, and re-layouts, local_sweep(): lax.scan(advance, start, (transfer, sources), reverse=backward)  11.7 us
    dynamic_update_slice x16, other arithmetic, local_sweep(): lax.scan(advance, start, (transfer, sources), reverse=backward)  5.48 us
  transfers between devices with their start and end apart: 4, of which 4 were waited for; matrix products, arithmetic and copies ran while one was open for 12% of the time, Pallas kernels for 0%

commit v1 on v0

--- a/solution.py
+++ b/solution.py
@@ -2,22 +2,6 @@
 import jax.numpy as jnp
 from jax import lax
 from jax.sharding import PartitionSpec as P
-
-
-def prefix(part, axis, combine, identity, reverse):
-    count = lax.axis_size(axis)
-    place = lax.axis_index(axis)
-    ahead = count - 1 - place if reverse else place
-    gathered = jax.tree.map(lambda a: lax.all_gather(a, axis), part)
-    state = jax.tree.map(lambda a, e: jnp.zeros_like(a) + jnp.asarray(e, a.dtype), part, identity)
-
-    def one(lap, state):
-        source = count - 1 - lap if reverse else lap
-        return combine(
-            state, jax.tree.map(lambda a: lax.dynamic_index_in_dim(a, source, 0, False), gathered)
-        )
-
-    return lax.fori_loop(0, ahead, one, state)
 
 
 def compose(earlier, later):
@@ -26,6 +10,30 @@
     joined_map = jnp.dot(late_map, early_map, precision=lax.Precision.HIGHEST)
     joined_state = jnp.dot(late_map, early_state, precision=lax.Precision.HIGHEST) + late_state
     return (joined_map, joined_state)
+
+
+def scan_enter(summary, axis, reverse):
+    count = lax.axis_size(axis)
+    early_map, early_state = summary
+    shift = 1
+    while shift < count:
+        if reverse:
+            pairs = [(i + shift, i) for i in range(count - shift)]
+        else:
+            pairs = [(i, i + shift) for i in range(count - shift)]
+        last = 2 * shift >= count
+        got_state = lax.ppermute(early_state, axis, pairs)
+        if last:
+            early_state = jnp.dot(early_map, got_state, precision=lax.Precision.HIGHEST) + early_state
+        else:
+            got_map = lax.ppermute(early_map, axis, pairs)
+            early_map, early_state = compose((got_map, got_state), (early_map, early_state))
+        shift *= 2
+    if reverse:
+        pairs = [(i + 1, i) for i in range(count - 1)]
+    else:
+        pairs = [(i, i + 1) for i in range(count - 1)]
+    return lax.ppermute(early_state, axis, pairs)
 
 
 def local_sweep(transfer, sources, backward):
@@ -68,12 +76,8 @@
     upper_summary, upper_prefix, upper_local = local_sweep(
         upper_trans.astype(jnp.float32), upper_source, True
     )
-    neutral = (
-        jnp.eye(lower_summary[0].shape[0], dtype=jnp.float32),
-        jnp.zeros_like(lower_summary[1]),
-    )
-    lower_enter = prefix(lower_summary, "row", compose, neutral, False)[1]
-    upper_enter = prefix(upper_summary, "row", compose, neutral, True)[1]
+    lower_enter = scan_enter(lower_summary, "row", False)
+    upper_enter = scan_enter(upper_summary, "row", True)
     lower_state = lower_local + jnp.einsum(
         "kij,jc->kic", lower_prefix, lower_enter, precision=lax.Precision.HIGHEST
     )

time: 269 us -> 137 us (0.51)
  waiting for transfers between devices: 155 us -> 3.59 us
  starting transfers between devices: 0.12 us -> 49.5 us
  between operations: 13.4 us -> 0.52 us
  matrix products: 66.6 us -> 58.1 us
  other arithmetic: 9.87 us -> 5.96 us
  local copies, waits for them, and re-layouts: 19.9 us -> 17.2 us
    all_gather x4 -> x0, waiting for transfers between devices: 153 us -> none  [prefix(): gathered = jax.tree.map(lambda a: lax.all_gather(a, axis), part)]
    ppermute x0 -> x16, starting transfers between devices: none -> 49.5 us  [the longest x8 21.9 us: scan_enter(): got_state = lax.ppermute(early_state, axis, pairs)]
    dot_general x15 -> x6, matrix products: 20.6 us -> 2.26 us  [compose(): jnp.dot(late_map, early_state, precision=lax.Precision.HIGHEST) + late_state]
    dot_general x16, matrix products: 13.6 us -> 21.2 us  [advance(): product_next = jnp.dot(matrix, product_now, precision=lax.Precision.HIGHEST)]
    dynamic_update_slice x16, other arithmetic: 5.48 us -> 0.25 us  [local_sweep(): lax.scan(advance, start, (transfer, sources), reverse=backward)]
    dot_general x0 -> x8, matrix products: none -> 3.98 us  [the longest x6 3.22 us: compose(): joined_map = jnp.dot(late_map, early_map, precision=lax.Precision.HIGHEST)]
    ppermute x0 -> x16, waiting for transfers between devices: none -> 3.59 us  [the longest x8 3.4 us: scan_enter(): got_state = lax.ppermute(early_state, axis, pairs)]
  transfers between devices with their start and end apart: 4 -> 16, of which waited for: 4 -> 2; matrix products, arithmetic and copies ran while one was open for 12% -> 31% of each run, Pallas kernels for 0% -> 0%
where the time goes in v1:
time: 137 us; the launch traced here: 136 us
  matrix products  58.1 us (42%)
  starting transfers between devices  49.5 us (36%)
  local copies, waits for them, and re-layouts  17.2 us (13%)
  other arithmetic  5.96 us (4%)
  waiting for transfers between devices  3.59 us (3%)
    dot_general x16, matrix products, advance(): jnp.dot(matrix, state_now, precision=lax.Precision.HIGHEST) + source  21.9 us
    ppermute x8, starting transfers between devices, scan_enter(): got_state = lax.ppermute(early_state, axis, pairs)  21.9 us
    dot_general x16, matrix products, advance(): product_next = jnp.dot(matrix, product_now, precision=lax.Precision.HIGHEST)  21.2 us
    ppermute x6, starting transfers between devices, scan_enter(): got_map = lax.ppermute(early_map, axis, pairs)  17.8 us
    dynamic_update_slice x16, local copies, waits for them, and re-layouts, local_sweep(): lax.scan(advance, start, (transfer, sources), reverse=backward)  11.6 us
    ppermute x2, starting transfers between devices, scan_enter(): return lax.ppermute(early_state, axis, pairs)  9.78 us
    ppermute x8, waiting for transfers between devices, scan_enter(): got_state = lax.ppermute(early_state, axis, pairs)  3.4 us
    dot_general x6, matrix products, compose(): joined_map = jnp.dot(late_map, early_map, precision=lax.Precision.HIGHEST)  3.22 us
  transfers between devices with their start and end apart: 16, of which 2 were waited for; matrix products, arithmetic and copies ran while one was open for 31% of the time, Pallas kernels for 0%

profile of v1, /device:TPU:1, one launch (start us, length us, event | category | flops | bytes accessed | tf_op | source)
XLA Modules:
  0.0 135.8 jit_solution(11397035328378960566)
XLA Ops:
  0.1 2.9 %convert_element_type.22 = f32[8,256,256]{2,1,0:T(8,128)} convert(bf16[8,256,256]{2,1,0:T(8,128)(2,1)} %param.16) | non-fusion elementwise | flops 524288 | bytes 3145728 | tf_op jit(solution)/shard_map/convert_element_type | solution.py:74
  2.9 1.5 %fusion.29 = f32[8,256,128]{2,1,0:T(8,128)} fusion(bf16[8,256,256]{2,1,0:T(8,128)(2,1)S(1)} %copy-done, bf16[8,256,128]{2,1,0:T(8,128)(2,1)S(1)} %copy-done.3), kind=kOutput, calls=%fused_computation.49 | convolution fusion | flops 134217728 | bytes 2621440 | tf_op jit(solution)/shard_map/kbr,kbc->krc/dot_general | solution.py:67
  4.4 1.5 %broadcast.10.clone.1 = f32[8,256,256]{2,1,0:T(8,128)} broadcast(f32[]{:T(128)} %constant.55.clone.1), dimensions={} | broadcast | bytes 2097156 | tf_op jit(solution)/shard_map/broadcast.4
  6.0 28.2 %while.38 = (s32[]{:T(128)}, f32[256,256]{1,0:T(8,128)S(1)}, f32[256,128]{1,0:T(8,128)S(1)}, f32[8,256,256]{2,1,0:T(8,128)}, f32[8,256,128]{2,1,0:T(8,128)S(1)},...) while((s32[]{:T(128)}, f32[256,256]{1,0:T(8,128)S(1)}, ...), condition=%wide.region_1.2_spmd.clone, body=%wide.region_0.1_spmd.clone.sunk | while | flops 302088192 | bytes 3016812 | solution.py:53
  6.1 1.4 %convolution_add_fusion.15 = f32[256,128]{1,0:T(8,128)S(1)} fusion(f32[8,256,256]{2,1,0:T(8,128)} %get-tuple-element.412, s32[]{:T(128)} %get-tuple-element.398, f32[8,256,128]{2,1,0:T(8,128)} %get-tuple-element.413, f32[256,128]{1,0:T(8,128)S(1)} %copy.60, pred[]{:T(512)S(6)} %compare.6), kind=kOutput, calls=%fused_computation.clone.1 | convolution fusion | flops 100728832 | bytes 656385 | tf_op jit(solution)/shard_map/while/body/eval_jaxpr/dot_general | solution.py:45
  8.2 1.3 fusion.93
  9.6 1.4 %convolution_add_fusion.15 = f32[256,128]{1,0:T(8,128)S(1)} fusion(f32[8,256,256]{2,1,0:T(8,128)} %get-tuple-element.412, s32[]{:T(128)} %get-tuple-element.398, f32[8,256,128]{2,1,0:T(8,128)} %get-tuple-element.413, f32[256,128]{1,0:T(8,128)S(1)} %copy.60, pred[]{:T(512)S(6)} %compare.6), kind=kOutput, calls=%fused_computation.clone.1 | convolution fusion | flops 100728832 | bytes 656385 | tf_op jit(solution)/shard_map/while/body/eval_jaxpr/dot_general | solution.py:45
  11.7 1.3 fusion.93
  13.1 1.4 %convolution_add_fusion.15 = f32[256,128]{1,0:T(8,128)S(1)} fusion(f32[8,256,256]{2,1,0:T(8,128)} %get-tuple-element.412, s32[]{:T(128)} %get-tuple-element.398, f32[8,256,128]{2,1,0:T(8,128)} %get-tuple-element.413, f32[256,128]{1,0:T(8,128)S(1)} %copy.60, pred[]{:T(512)S(6)} %compare.6), kind=kOutput, calls=%fused_computation.clone.1 | convolution fusion | flops 100728832 | bytes 656385 | tf_op jit(solution)/shard_map/while/body/eval_jaxpr/dot_general | solution.py:45
  15.2 1.3 fusion.93
  16.6 1.4 %convolution_add_fusion.15 = f32[256,128]{1,0:T(8,128)S(1)} fusion(f32[8,256,256]{2,1,0:T(8,128)} %get-tuple-element.412, s32[]{:T(128)} %get-tuple-element.398, f32[8,256,128]{2,1,0:T(8,128)} %get-tuple-element.413, f32[256,128]{1,0:T(8,128)S(1)} %copy.60, pred[]{:T(512)S(6)} %compare.6), kind=kOutput, calls=%fused_computation.clone.1 | convolution fusion | flops 100728832 | bytes 656385 | tf_op jit(solution)/shard_map/while/body/eval_jaxpr/dot_general | solution.py:45
  18.8 1.3 fusion.93
  20.2 1.4 %convolution_add_fusion.15 = f32[256,128]{1,0:T(8,128)S(1)} fusion(f32[8,256,256]{2,1,0:T(8,128)} %get-tuple-element.412, s32[]{:T(128)} %get-tuple-element.398, f32[8,256,128]{2,1,0:T(8,128)} %get-tuple-element.413, f32[256,128]{1,0:T(8,128)S(1)} %copy.60, pred[]{:T(512)S(6)} %compare.6), kind=kOutput, calls=%fused_computation.clone.1 | convolution fusion | flops 100728832 | bytes 656385 | tf_op jit(solution)/shard_map/while/body/eval_jaxpr/dot_general | solution.py:45
  23.7 1.4 %convolution_add_fusion.15 = f32[256,128]{1,0:T(8,128)S(1)} fusion(f32[8,256,256]{2,1,0:T(8,128)} %get-tuple-element.412, s32[]{:T(128)} %get-tuple-element.398, f32[8,256,128]{2,1,0:T(8,128)} %get-tuple-element.413, f32[256,128]{1,0:T(8,128)S(1)} %copy.60, pred[]{:T(512)S(6)} %compare.6), kind=kOutput, calls=%fused_computation.clone.1 | convolution fusion | flops 100728832 | bytes 656385 | tf_op jit(solution)/shard_map/while/body/eval_jaxpr/dot_general | solution.py:45
  25.8 1.3 fusion.93
  27.2 1.4 %convolution_add_fusion.15 = f32[256,128]{1,0:T(8,128)S(1)} fusion(f32[8,256,256]{2,1,0:T(8,128)} %get-tuple-element.412, s32[]{:T(128)} %get-tuple-element.398, f32[8,256,128]{2,1,0:T(8,128)} %get-tuple-element.413, f32[256,128]{1,0:T(8,128)S(1)} %copy.60, pred[]{:T(512)S(6)} %compare.6), kind=kOutput, calls=%fused_computation.clone.1 | convolution fusion | flops 100728832 | bytes 656385 | tf_op jit(solution)/shard_map/while/body/eval_jaxpr/dot_general | solution.py:45
  30.7 1.4 %convolution_add_fusion.15 = f32[256,128]{1,0:T(8,128)S(1)} fusion(f32[8,256,256]{2,1,0:T(8,128)} %get-tuple-element.412, s32[]{:T(128)} %get-tuple-element.398, f32[8,256,128]{2,1,0:T(8,128)} %get-tuple-element.413, f32[256,128]{1,0:T(8,128)S(1)} %copy.60, pred[]{:T(512)S(6)} %compare.6), kind=kOutput, calls=%fused_computation.clone.1 | convolution fusion | flops 100728832 | bytes 656385 | tf_op jit(solution)/shard_map/while/body/eval_jaxpr/dot_general | solution.py:45
  32.9 1.3 fusion.93
  34.2 4.5 %collective-permute-start.3 = (f32[256,128]{1,0:T(8,128)S(1)}, f32[256,128]{1,0:T(8,128)S(1)}, u32[]{:S(2)}, u32[]{:S(2)}) collective-permute-start(f32[256,128]{1,0:T(8,128)S(1)} %get-tuple-element.192), channel_id=1, source_target_pairs={{0,1},{1,2},{2,3},{3,4},{4,5},{5,6},{6,7},{7,8},{8,9},{9,10},{10,1... | collective-permute-start | bytes 393224 | tf_op jit(solution)/shard_map/ppermute | solution.py:25
  38.7 1.9 %collective-permute-start = (f32[256,256]{1,0:T(8,128)S(1)}, f32[256,256]{1,0:T(8,128)}, u32[]{:S(2)}, u32[]{:S(2)}) collective-permute-start(f32[256,256]{1,0:T(8,128)S(1)} %get-tuple-element.191), channel_id=1, source_target_pairs={{0,1},{1,2},{2,3},{3,4},{4,5},{5,6},{6,7},{7,8},{8,9},{9,10},{10,1... | collective-permute-start | bytes 786440 | tf_op jit(solution)/shard_map/ppermute | solution.py:29
  40.7 2.8 %convert_element_type.24 = f32[8,256,256]{2,1,0:T(8,128)} convert(bf16[8,256,256]{2,1,0:T(8,128)(2,1)} %param.19) | non-fusion elementwise | flops 524288 | bytes 3145728 | tf_op jit(solution)/shard_map/convert_element_type | solution.py:77
  43.5 1.6 %fusion.33 = f32[8,256,128]{2,1,0:T(8,128)} fusion(bf16[8,256,256]{2,1,0:T(8,128)(2,1)S(1)} %copy-done.6, bf16[8,256,128]{2,1,0:T(8,128)(2,1)S(1)} %copy-done.3), kind=kOutput, calls=%fused_computation.53 | convolution fusion | flops 134217728 | bytes 2621440 | tf_op jit(solution)/shard_map/kbr,kbc->krc/dot_general | solution.py:70
  45.1 1.5 %broadcast.10.clone = f32[8,256,256]{2,1,0:T(8,128)} broadcast(f32[]{:T(128)} %constant.55.clone.1), dimensions={} | broadcast | bytes 2097156 | tf_op jit(solution)/shard_map/broadcast.4
  46.6 28.2 %while.39 = (s32[]{:T(128)}, f32[256,256]{1,0:T(8,128)S(1)}, f32[256,128]{1,0:T(8,128)S(1)}, f32[8,256,256]{2,1,0:T(8,128)}, f32[8,256,128]{2,1,0:T(8,128)S(1)},...) while((s32[]{:T(128)}, f32[256,256]{1,0:T(8,128)S(1)}, ...), condition=%wide.region_3.4_spmd.clone, body=%wide.region_2.3_spmd.clone.sunk | while | flops 302088192 | bytes 3016327 | solution.py:53
  46.7 1.4 %convolution_add_fusion.16 = f32[256,128]{1,0:T(8,128)S(1)} fusion(f32[8,256,256]{2,1,0:T(8,128)} %get-tuple-element.384, s32[]{:T(128)S(6)} %sub.9, f32[8,256,128]{2,1,0:T(8,128)} %get-tuple-element.385, f32[256,128]{1,0:T(8,128)S(1)} %copy.62, pred[]{:T(512)S(6)} %compare.7), kind=kOutput, calls=%fused_computation.14.clone.1 | convolution fusion | flops 100728832 | bytes 656896 | tf_op jit(solution)/shard_map/while/body/eval_jaxpr/dot_general | solution.py:45
  50.2 1.4 %convolution_add_fusion.16 = f32[256,128]{1,0:T(8,128)S(1)} fusion(f32[8,256,256]{2,1,0:T(8,128)} %get-tuple-element.384, s32[]{:T(128)S(6)} %sub.9, f32[8,256,128]{2,1,0:T(8,128)} %get-tuple-element.385, f32[256,128]{1,0:T(8,128)S(1)} %copy.62, pred[]{:T(512)S(6)} %compare.7), kind=kOutput, calls=%fused_computation.14.clone.1 | convolution fusion | flops 100728832 | bytes 656896 | tf_op jit(solution)/shard_map/while/body/eval_jaxpr/dot_general | solution.py:45
  53.7 1.4 %convolution_add_fusion.16 = f32[256,128]{1,0:T(8,128)S(1)} fusion(f32[8,256,256]{2,1,0:T(8,128)} %get-tuple-element.384, s32[]{:T(128)S(6)} %sub.9, f32[8,256,128]{2,1,0:T(8,128)} %get-tuple-element.385, f32[256,128]{1,0:T(8,128)S(1)} %copy.62, pred[]{:T(512)S(6)} %compare.7), kind=kOutput, calls=%fused_computation.14.clone.1 | convolution fusion | flops 100728832 | bytes 656896 | tf_op jit(solution)/shard_map/while/body/eval_jaxpr/dot_general | solution.py:45
  57.3 1.4 %convolution_add_fusion.16 = f32[256,128]{1,0:T(8,128)S(1)} fusion(f32[8,256,256]{2,1,0:T(8,128)} %get-tuple-element.384, s32[]{:T(128)S(6)} %sub.9, f32[8,256,128]{2,1,0:T(8,128)} %get-tuple-element.385, f32[256,128]{1,0:T(8,128)S(1)} %copy.62, pred[]{:T(512)S(6)} %compare.7), kind=kOutput, calls=%fused_computation.14.clone.1 | convolution fusion | flops 100728832 | bytes 656896 | tf_op jit(solution)/shard_map/while/body/eval_jaxpr/dot_general | solution.py:45
  59.4 1.3 fusion.98
  60.8 1.4 %convolution_add_fusion.16 = f32[256,128]{1,0:T(8,128)S(1)} fusion(f32[8,256,256]{2,1,0:T(8,128)} %get-tuple-element.384, s32[]{:T(128)S(6)} %sub.9, f32[8,256,128]{2,1,0:T(8,128)} %get-tuple-element.385, f32[256,128]{1,0:T(8,128)S(1)} %copy.62, pred[]{:T(512)S(6)} %compare.7), kind=kOutput, calls=%fused_computation.14.clone.1 | convolution fusion | flops 100728832 | bytes 656896 | tf_op jit(solution)/shard_map/while/body/eval_jaxpr/dot_general | solution.py:45
  62.9 1.3 fusion.98
  64.3 1.4 %convolution_add_fusion.16 = f32[256,128]{1,0:T(8,128)S(1)} fusion(f32[8,256,256]{2,1,0:T(8,128)} %get-tuple-element.384, s32[]{:T(128)S(6)} %sub.9, f32[8,256,128]{2,1,0:T(8,128)} %get-tuple-element.385, f32[256,128]{1,0:T(8,128)S(1)} %copy.62, pred[]{:T(512)S(6)} %compare.7), kind=kOutput, calls=%fused_computation.14.clone.1 | convolution fusion | flops 100728832 | bytes 656896 | tf_op jit(solution)/shard_map/while/body/eval_jaxpr/dot_general | solution.py:45
  66.5 1.3 fusion.98
  67.9 1.4 %convolution_add_fusion.16 = f32[256,128]{1,0:T(8,128)S(1)} fusion(f32[8,256,256]{2,1,0:T(8,128)} %get-tuple-element.384, s32[]{:T(128)S(6)} %sub.9, f32[8,256,128]{2,1,0:T(8,128)} %get-tuple-element.385, f32[256,128]{1,0:T(8,128)S(1)} %copy.62, pred[]{:T(512)S(6)} %compare.7), kind=kOutput, calls=%fused_computation.14.clone.1 | convolution fusion | flops 100728832 | bytes 656896 | tf_op jit(solution)/shard_map/while/body/eval_jaxpr/dot_general | solution.py:45
  71.4 1.4 %convolution_add_fusion.16 = f32[256,128]{1,0:T(8,128)S(1)} fusion(f32[8,256,256]{2,1,0:T(8,128)} %get-tuple-element.384, s32[]{:T(128)S(6)} %sub.9, f32[8,256,128]{2,1,0:T(8,128)} %get-tuple-element.385, f32[256,128]{1,0:T(8,128)S(1)} %copy.62, pred[]{:T(512)S(6)} %compare.7), kind=kOutput, calls=%fused_computation.14.clone.1 | convolution fusion | flops 100728832 | bytes 656896 | tf_op jit(solution)/shard_map/while/body/eval_jaxpr/dot_general | solution.py:45
  74.9 3.1 %collective-permute-start.11 = (f32[256,128]{1,0:T(8,128)S(1)}, f32[256,128]{1,0:T(8,128)S(1)}, u32[]{:S(2)}, u32[]{:S(2)}) collective-permute-start(f32[256,128]{1,0:T(8,128)S(1)} %get-tuple-element.196), channel_id=1, source_target_pairs={{1,0},{2,1},{3,2},{4,3},{5,4},{6,5},{7,6},{8,7},{9,8},{10,9},{11,1... | collective-permute-start | bytes 393224 | tf_op jit(solution)/shard_map/ppermute | solution.py:25
  78.0 1.9 %collective-permute-start.8 = (f32[256,256]{1,0:T(8,128)S(1)}, f32[256,256]{1,0:T(8,128)S(1)}, u32[]{:S(2)}, u32[]{:S(2)}) collective-permute-start(f32[256,256]{1,0:T(8,128)S(1)} %get-tuple-element.195), channel_id=1, source_target_pairs={{1,0},{2,1},{3,2},{4,3},{5,4},{6,5},{7,6},{8,7},{9,8},{10,9},{11,1... | collective-permute-start | bytes 786440 | tf_op jit(solution)/shard_map/ppermute | solution.py:29
  80.3 2.6 %collective-permute-start.4 = (f32[256,128]{1,0:T(8,128)S(1)}, f32[256,128]{1,0:T(8,128)S(1)}, u32[]{:S(2)}, u32[]{:S(2)}) collective-permute-start(f32[256,128]{1,0:T(8,128)S(1)} %convolution_add_fusion.12), channel_id=1, source_target_pairs={{0,2},{1,3},{2,4},{3,5},{4,6},{5,7},{6,8},{7,9},{8,10},{9,11},{10,... | collective-permute-start | bytes 393224 | tf_op jit(solution)/shard_map/ppermute | solution.py:25
  84.6 1.3 fusion.30
  85.9 4.7 %collective-permute-start.1 = (f32[256,256]{1,0:T(8,128)S(1)}, f32[256,256]{1,0:T(8,128)S(1)}, u32[]{:S(2)}, u32[]{:S(2)}) collective-permute-start(f32[256,256]{1,0:T(8,128)S(1)} %fusion.30), channel_id=1, source_target_pairs={{0,2},{1,3},{2,4},{3,5},{4,6},{5,7},{6,8},{7,9},{8,10},{9,11},{10,... | collective-permute-start | bytes 786440 | tf_op jit(solution)/shard_map/ppermute | solution.py:29
  91.0 3.2 %collective-permute-start.5 = (f32[256,128]{1,0:T(8,128)S(1)}, f32[256,128]{1,0:T(8,128)S(1)}, u32[]{:S(2)}, u32[]{:S(2)}) collective-permute-start(f32[256,128]{1,0:T(8,128)S(1)} %convolution_add_fusion.11), channel_id=1, source_target_pairs={{0,4},{1,5},{2,6},{3,7},{4,8},{5,9},{6,10},{7,11},{8,12},{9,13},{1... | collective-permute-start | bytes 393224 | tf_op jit(solution)/shard_map/ppermute | solution.py:25
  98.0 6.7 %collective-permute-start.2 = (f32[256,256]{1,0:T(8,128)S(1)}, f32[256,256]{1,0:T(8,128)S(1)}, u32[]{:S(2)}, u32[]{:S(2)}) collective-permute-start(f32[256,256]{1,0:T(8,128)S(1)} %fusion.31), channel_id=1, source_target_pairs={{0,4},{1,5},{2,6},{3,7},{4,8},{5,9},{6,10},{7,11},{8,12},{9,13},{1... | collective-permute-start | bytes 786440 | tf_op jit(solution)/shard_map/ppermute | solution.py:29
  105.1 4.6 %collective-permute-start.6 = (f32[256,128]{1,0:T(8,128)S(1)}, f32[256,128]{1,0:T(8,128)S(1)}, u32[]{:S(2)}, u32[]{:S(2)}) collective-permute-start(f32[256,128]{1,0:T(8,128)S(1)} %convolution_add_fusion.10), channel_id=1, source_target_pairs={{0,8},{1,9},{2,10},{3,11},{4,12},{5,13},{6,14},{7,15},{16,24},{17,... | collective-permute-start | bytes 393224 | tf_op jit(solution)/shard_map/ppermute | solution.py:25
  113.9 3.4 %collective-permute-start.7 = (f32[256,128]{1,0:T(8,128)S(1)}, f32[256,128]{1,0:T(8,128)S(1)}, u32[]{:S(2)}, u32[]{:S(2)}) collective-permute-start(f32[256,128]{1,0:T(8,128)S(1)} %convolution_add_fusion.9), channel_id=1, source_target_pairs={{0,1},{1,2},{2,3},{3,4},{4,5},{5,6},{6,7},{7,8},{8,9},{9,10},{10,1... | collective-permute-start | bytes 393224 | tf_op jit(solution)/shard_map/ppermute | solution.py:36
  117.9 3.4 %collective-permute-done.14 = f32[256,128]{1,0:T(8,128)S(1)} collective-permute-done((f32[256,128]{1,0:T(8,128)S(1)}, f32[256,128]{1,0:T(8,128)S(1)}, u32[]{:S(2)}, u32[]{:S(2)}) %collective-permute-start.14) | collective-permute-done | bytes 131104 | tf_op jit(solution)/shard_map/ppermute | solution.py:25
  121.7 6.4 %collective-permute-start.15 = (f32[256,128]{1,0:T(8,128)S(1)}, f32[256,128]{1,0:T(8,128)S(1)}, u32[]{:S(2)}, u32[]{:S(2)}) collective-permute-start(f32[256,128]{1,0:T(8,128)S(1)} %convolution_add_fusion.5), channel_id=1, source_target_pairs={{1,0},{2,1},{3,2},{4,3},{5,4},{6,5},{7,6},{8,7},{9,8},{10,9},{11,1... | collective-permute-start | bytes 393224 | tf_op jit(solution)/shard_map/ppermute | solution.py:36
  128.1 1.8 %fusion.23 = bf16[8,256,128]{2,1,0:T(8,128)(2,1)S(1)} fusion(f32[8,256,128]{2,1,0:T(8,128)S(1)} %copy-done.5, f32[8,256,256]{2,1,0:T(8,128)S(1)} %copy-done.2, f32[256,128]{1,0:T(8,128)S(1)} %collective-permute-done.7), kind=kOutput, calls=%fused_computation.34 | convolution fusion | flops 805830656 | bytes 3801088 | tf_op jit(solution)/shard_map/kij,jc->kic/dot_general | solution.py:81
  131.6 1.8 %fusion.24 = bf16[8,256,128]{2,1,0:T(8,128)(2,1)S(1)} fusion(f32[8,256,128]{2,1,0:T(8,128)S(1)} %get-tuple-element.193, f32[8,256,256]{2,1,0:T(8,128)S(1)} %copy-done.1, f32[256,128]{1,0:T(8,128)S(1)} %collective-permute-done.15), kind=kOutput, calls=%fused_computation.35 | convolution fusion | flops 805830656 | bytes 3801088 | tf_op jit(solution)/shard_map/kij,jc->kic/dot_general | solution.py:84
  (133 shorter events, 37.4 us)
Async XLA Ops:
  0.0 2.9 %copy-start = (bf16[8,256,256]{2,1,0:T(8,128)(2,1)S(1)}, bf16[8,256,256]{2,1,0:T(8,128)(2,1)}, u32[]{:S(2)}) copy-start(bf16[8,256,256]{2,1,0:T(8,128)(2,1)} %param.15) | copy-start | bytes 3145732
  0.0 2.9 %copy-start.3 = (bf16[8,256,128]{2,1,0:T(8,128)(2,1)S(1)}, bf16[8,256,128]{2,1,0:T(8,128)(2,1)}, u32[]{:S(2)}) copy-start(bf16[8,256,128]{2,1,0:T(8,128)(2,1)} %param.12) | copy-start | bytes 1572868
  34.2 10.9 %copy-start.4 = (f32[8,256,128]{2,1,0:T(8,128)}, f32[8,256,128]{2,1,0:T(8,128)S(1)}, u32[]{:S(2)}) copy-start(f32[8,256,128]{2,1,0:T(8,128)S(1)} %get-tuple-element.189) | copy-start | bytes 3145732
  34.2 45.7 %collective-permute-start.3 = (f32[256,128]{1,0:T(8,128)S(1)}, f32[256,128]{1,0:T(8,128)S(1)}, u32[]{:S(2)}, u32[]{:S(2)}) collective-permute-start(f32[256,128]{1,0:T(8,128)S(1)} %get-tuple-element.192), channel_id=1, source_target_pairs={{0,1},{1,2},{2,3},{3,4},{4,5},{5,6},{6,7},{7,8},{8,9},{9,10},{10,1... | collective-permute-start | bytes 393224 | tf_op jit(solution)/shard_map/ppermute | solution.py:25
  38.7 45.8 %collective-permute-start = (f32[256,256]{1,0:T(8,128)S(1)}, f32[256,256]{1,0:T(8,128)}, u32[]{:S(2)}, u32[]{:S(2)}) collective-permute-start(f32[256,256]{1,0:T(8,128)S(1)} %get-tuple-element.191), channel_id=1, source_target_pairs={{0,1},{1,2},{2,3},{3,4},{4,5},{5,6},{6,7},{7,8},{8,9},{9,10},{10,1... | collective-permute-start | bytes 786440 | tf_op jit(solution)/shard_map/ppermute | solution.py:29
  40.7 2.8 %copy-start.6 = (bf16[8,256,256]{2,1,0:T(8,128)(2,1)S(1)}, bf16[8,256,256]{2,1,0:T(8,128)(2,1)}, u32[]{:S(2)}) copy-start(bf16[8,256,256]{2,1,0:T(8,128)(2,1)} %param.18) | copy-start | bytes 3145732
  74.9 8.0 %collective-permute-start.11 = (f32[256,128]{1,0:T(8,128)S(1)}, f32[256,128]{1,0:T(8,128)S(1)}, u32[]{:S(2)}, u32[]{:S(2)}) collective-permute-start(f32[256,128]{1,0:T(8,128)S(1)} %get-tuple-element.196), channel_id=1, source_target_pairs={{1,0},{2,1},{3,2},{4,3},{5,4},{6,5},{7,6},{8,7},{9,8},{10,9},{11,1... | collective-permute-start | bytes 393224 | tf_op jit(solution)/shard_map/ppermute | solution.py:25
  78.0 16.2 %collective-permute-start.8 = (f32[256,256]{1,0:T(8,128)S(1)}, f32[256,256]{1,0:T(8,128)S(1)}, u32[]{:S(2)}, u32[]{:S(2)}) collective-permute-start(f32[256,256]{1,0:T(8,128)S(1)} %get-tuple-element.195), channel_id=1, source_target_pairs={{1,0},{2,1},{3,2},{4,3},{5,4},{6,5},{7,6},{8,7},{9,8},{10,9},{11,1... | collective-permute-start | bytes 786440 | tf_op jit(solution)/shard_map/ppermute | solution.py:29
  80.3 10.3 %collective-permute-start.4 = (f32[256,128]{1,0:T(8,128)S(1)}, f32[256,128]{1,0:T(8,128)S(1)}, u32[]{:S(2)}, u32[]{:S(2)}) collective-permute-start(f32[256,128]{1,0:T(8,128)S(1)} %convolution_add_fusion.12), channel_id=1, source_target_pairs={{0,2},{1,3},{2,4},{3,5},{4,6},{5,7},{6,8},{7,9},{8,10},{9,11},{10,... | collective-permute-start | bytes 393224 | tf_op jit(solution)/shard_map/ppermute | solution.py:25
  83.3 12.6 %collective-permute-start.12 = (f32[256,128]{1,0:T(8,128)S(1)}, f32[256,128]{1,0:T(8,128)S(1)}, u32[]{:S(2)}, u32[]{:S(2)}) collective-permute-start(f32[256,128]{1,0:T(8,128)S(1)} %convolution_add_fusion.8), channel_id=1, source_target_pairs={{2,0},{3,1},{4,2},{5,3},{6,4},{7,5},{8,6},{9,7},{10,8},{11,9},{12,... | collective-permute-start | bytes 393224 | tf_op jit(solution)/shard_map/ppermute | solution.py:25
  85.9 11.7 %collective-permute-start.1 = (f32[256,256]{1,0:T(8,128)S(1)}, f32[256,256]{1,0:T(8,128)S(1)}, u32[]{:S(2)}, u32[]{:S(2)}) collective-permute-start(f32[256,256]{1,0:T(8,128)S(1)} %fusion.30), channel_id=1, source_target_pairs={{0,2},{1,3},{2,4},{3,5},{4,6},{5,7},{6,8},{7,9},{8,10},{9,11},{10,... | collective-permute-start | bytes 786440 | tf_op jit(solution)/shard_map/ppermute | solution.py:29
  91.0 13.7 %collective-permute-start.5 = (f32[256,128]{1,0:T(8,128)S(1)}, f32[256,128]{1,0:T(8,128)S(1)}, u32[]{:S(2)}, u32[]{:S(2)}) collective-permute-start(f32[256,128]{1,0:T(8,128)S(1)} %convolution_add_fusion.11), channel_id=1, source_target_pairs={{0,4},{1,5},{2,6},{3,7},{4,8},{5,9},{6,10},{7,11},{8,12},{9,13},{1... | collective-permute-start | bytes 393224 | tf_op jit(solution)/shard_map/ppermute | solution.py:25
  94.6 15.2 %collective-permute-start.9 = (f32[256,256]{1,0:T(8,128)S(1)}, f32[256,256]{1,0:T(8,128)S(1)}, u32[]{:S(2)}, u32[]{:S(2)}) collective-permute-start(f32[256,256]{1,0:T(8,128)S(1)} %fusion.34), channel_id=1, source_target_pairs={{2,0},{3,1},{4,2},{5,3},{6,4},{7,5},{8,6},{9,7},{10,8},{11,9},{12,... | collective-permute-start | bytes 786440 | tf_op jit(solution)/shard_map/ppermute | solution.py:29
  96.3 15.2 %collective-permute-start.13 = (f32[256,128]{1,0:T(8,128)S(1)}, f32[256,128]{1,0:T(8,128)S(1)}, u32[]{:S(2)}, u32[]{:S(2)}) collective-permute-start(f32[256,128]{1,0:T(8,128)S(1)} %convolution_add_fusion.7), channel_id=1, source_target_pairs={{4,0},{5,1},{6,2},{7,3},{8,4},{9,5},{10,6},{11,7},{12,8},{13,9},{1... | collective-permute-start | bytes 393224 | tf_op jit(solution)/shard_map/ppermute | solution.py:25
  98.0 15.2 %collective-permute-start.2 = (f32[256,256]{1,0:T(8,128)S(1)}, f32[256,256]{1,0:T(8,128)S(1)}, u32[]{:S(2)}, u32[]{:S(2)}) collective-permute-start(f32[256,256]{1,0:T(8,128)S(1)} %fusion.31), channel_id=1, source_target_pairs={{0,4},{1,5},{2,6},{3,7},{4,8},{5,9},{6,10},{7,11},{8,12},{9,13},{1... | collective-permute-start | bytes 786440 | tf_op jit(solution)/shard_map/ppermute | solution.py:29
  105.1 23.0 %copy-start.2 = (f32[8,256,256]{2,1,0:T(8,128)S(1)}, f32[8,256,256]{2,1,0:T(8,128)}, u32[]{:S(2)}) copy-start(f32[8,256,256]{2,1,0:T(8,128)} %get-tuple-element.190) | copy-start | bytes 6291460
  105.1 23.0 %copy-start.5 = (f32[8,256,128]{2,1,0:T(8,128)S(1)}, f32[8,256,128]{2,1,0:T(8,128)}, u32[]{:S(2)}) copy-start(f32[8,256,128]{2,1,0:T(8,128)} %copy-done.4) | copy-start | bytes 3145732
  105.1 8.4 %collective-permute-start.6 = (f32[256,128]{1,0:T(8,128)S(1)}, f32[256,128]{1,0:T(8,128)S(1)}, u32[]{:S(2)}, u32[]{:S(2)}) collective-permute-start(f32[256,128]{1,0:T(8,128)S(1)} %convolution_add_fusion.10), channel_id=1, source_target_pairs={{0,8},{1,9},{2,10},{3,11},{4,12},{5,13},{6,14},{7,15},{16,24},{17,... | collective-permute-start | bytes 393224 | tf_op jit(solution)/shard_map/ppermute | solution.py:25
  110.2 7.3 %collective-permute-start.10 = (f32[256,256]{1,0:T(8,128)S(1)}, f32[256,256]{1,0:T(8,128)S(1)}, u32[]{:S(2)}, u32[]{:S(2)}) collective-permute-start(f32[256,256]{1,0:T(8,128)S(1)} %fusion.35), channel_id=1, source_target_pairs={{4,0},{5,1},{6,2},{7,3},{8,4},{9,5},{10,6},{11,7},{12,8},{13,9},{1... | collective-permute-start | bytes 786440 | tf_op jit(solution)/shard_map/ppermute | solution.py:29
  111.9 9.4 %collective-permute-start.14 = (f32[256,128]{1,0:T(8,128)S(1)}, f32[256,128]{1,0:T(8,128)S(1)}, u32[]{:S(2)}, u32[]{:S(2)}) collective-permute-start(f32[256,128]{1,0:T(8,128)S(1)} %convolution_add_fusion.6), channel_id=1, source_target_pairs={{8,0},{9,1},{10,2},{11,3},{12,4},{13,5},{14,6},{15,7},{24,16},{25,... | collective-permute-start | bytes 393224 | tf_op jit(solution)/shard_map/ppermute | solution.py:25
  113.9 14.1 %collective-permute-start.7 = (f32[256,128]{1,0:T(8,128)S(1)}, f32[256,128]{1,0:T(8,128)S(1)}, u32[]{:S(2)}, u32[]{:S(2)}) collective-permute-start(f32[256,128]{1,0:T(8,128)S(1)} %convolution_add_fusion.9), channel_id=1, source_target_pairs={{0,1},{1,2},{2,3},{3,4},{4,5},{5,6},{6,7},{7,8},{8,9},{9,10},{10,1... | collective-permute-start | bytes 393224 | tf_op jit(solution)/shard_map/ppermute | solution.py:36
  117.9 12.1 %copy-start.7 = (bf16[8,256,256]{2,1,0:T(8,128)(2,1)S(1)}, bf16[8,256,256]{2,1,0:T(8,128)(2,1)}, u32[]{:S(2)}) copy-start(bf16[8,256,256]{2,1,0:T(8,128)(2,1)} %param.14) | copy-start | bytes 3145732
  121.7 8.8 %collective-permute-start.15 = (f32[256,128]{1,0:T(8,128)S(1)}, f32[256,128]{1,0:T(8,128)S(1)}, u32[]{:S(2)}, u32[]{:S(2)}) collective-permute-start(f32[256,128]{1,0:T(8,128)S(1)} %convolution_add_fusion.5), channel_id=1, source_target_pairs={{1,0},{2,1},{3,2},{4,3},{5,4},{6,5},{7,6},{8,7},{9,8},{10,9},{11,1... | collective-permute-start | bytes 393224 | tf_op jit(solution)/shard_map/ppermute | solution.py:36
  130.0 1.6 %copy-start.1 = (f32[8,256,256]{2,1,0:T(8,128)S(1)}, f32[8,256,256]{2,1,0:T(8,128)}, u32[]{:S(2)}) copy-start(f32[8,256,256]{2,1,0:T(8,128)} %get-tuple-element.194) | copy-start | bytes 6291460
  130.4 2.9 %copy-start.8 = (bf16[8,256,256]{2,1,0:T(8,128)(2,1)S(1)}, bf16[8,256,256]{2,1,0:T(8,128)(2,1)}, u32[]{:S(2)}) copy-start(bf16[8,256,256]{2,1,0:T(8,128)(2,1)} %param.17) | copy-start | bytes 3145732
  133.4 1.2 copy-start.9

commit v2 on v0

v2 whole, which is shorter than its diff:
```python
import jax
import jax.numpy as jnp
from jax import lax
from jax.experimental import pallas as pl
from jax.experimental.pallas import tpu as pltpu
from jax.sharding import PartitionSpec as P

F32 = jnp.float32
BF16 = jnp.bfloat16
HIGHEST = lax.Precision.HIGHEST


def split_dot(matrix, value):
    high = value.astype(BF16)
    low = (value - high.astype(F32)).astype(BF16)
    return jnp.dot(matrix, high, preferred_element_type=F32) + jnp.dot(
        matrix, low, preferred_element_type=F32
    )


def sweep_kernel(
    rhs_ref, lcols_ref, ltrans_ref, ucols_ref, utrans_ref,
    lmap_ref, lstate_ref, lsrc_ref, umap_ref, ustate_ref, usrc_ref,
):
    count = rhs_ref.shape[0]
    lmap = lstate = umap = ustate = None
    for step in range(count):
        lk = step
        uk = count - 1 - step
        lsrc = lax.dot_general(lcols_ref[lk], rhs_ref[lk], (((0,), (0,)), ((), ())), preferred_element_type=F32)
        usrc = lax.dot_general(ucols_ref[uk], rhs_ref[uk], (((0,), (0,)), ((), ())), preferred_element_type=F32)
        lsrc_ref[lk] = lsrc
        usrc_ref[uk] = usrc
        ltrans = ltrans_ref[lk]
        utrans = utrans_ref[uk]
        if step == 0:
            lstate = lsrc
            ustate = usrc
            lmap = ltrans.astype(F32)
            umap = utrans.astype(F32)
        else:
            lstate = split_dot(ltrans, lstate) + lsrc
            ustate = split_dot(utrans, ustate) + usrc
            lmap = split_dot(ltrans, lmap)
            umap = split_dot(utrans, umap)
    lmap_ref[...] = lmap
    lstate_ref[...] = lstate
    umap_ref[...] = umap
    ustate_ref[...] = ustate


def apply_kernel(
    lenter_ref, uenter_ref, ltrans_ref, utrans_ref, lsrc_ref, usrc_ref,
    diag_ref, lrows_ref, urows_ref, out_ref, lround_ref, uround_ref,
):
    count = ltrans_ref.shape[0]
    lstate = lenter_ref[...]
    ustate = uenter_ref[...]
    for step in range(count):
        lk = step
        uk = count - 1 - step
        lround_ref[lk] = lstate.astype(BF16)
        uround_ref[uk] = ustate.astype(BF16)
        if step + 1 < count:
            lstate = split_dot(ltrans_ref[lk], lstate) + lsrc_ref[lk]
            ustate = split_dot(utrans_ref[uk], ustate) + usrc_ref[uk]
    for k in range(count):
        total = diag_ref[k]
        total = total + jnp.dot(lrows_ref[k], lround_ref[k], preferred_element_type=F32)
        total = total + jnp.dot(urows_ref[k], uround_ref[k], preferred_element_type=F32)
        out_ref[k] = total.astype(out_ref.dtype)


def shifted(value, axis, count, shift, reverse):
    if reverse:
        pairs = [(i + shift, i) for i in range(count - shift)]
    else:
        pairs = [(i, i + shift) for i in range(count - shift)]
    return lax.ppermute(value, axis, pairs)


def scan_enter(summary_map, summary_state, axis, reverse):
    count = lax.axis_size(axis)
    rank = summary_map.shape[0]
    both = jnp.concatenate([summary_map, summary_state], axis=1)
    rounds = 0
    while 2 ** (rounds + 1) < count - 1:
        rounds += 1
    shift = 1
    for _ in range(rounds):
        got = shifted(both, axis, count, shift, reverse)
        joined = jnp.dot(both[:, :rank], got, precision=HIGHEST)
        both = joined + jnp.concatenate(
            [jnp.zeros_like(summary_map), both[:, rank:]], axis=1
        )
        shift *= 2
    near = shifted(both, axis, count, 1, reverse)
    far = shifted(both[:, rank:], axis, count, 1 + shift, reverse)
    return jnp.dot(near[:, :rank], far, precision=HIGHEST) + near[:, rank:]


def shards(
    right_sides,
    diagonal_blocks,
    lower_rows,
    lower_cols,
    lower_trans,
    upper_rows,
    upper_cols,
    upper_trans,
):
    count, rows, rhs = right_sides.shape
    rank = lower_trans.shape[1]
    lmap, lstate, lsrc, umap, ustate, usrc = pl.pallas_call(
        sweep_kernel,
        out_shape=(
            jax.ShapeDtypeStruct((rank, rank), F32),
            jax.ShapeDtypeStruct((rank, rhs), F32),
            jax.ShapeDtypeStruct((count, rank, rhs), F32),
            jax.ShapeDtypeStruct((rank, rank), F32),
            jax.ShapeDtypeStruct((rank, rhs), F32),
            jax.ShapeDtypeStruct((count, rank, rhs), F32),
        ),
        name="sweep",
    )(right_sides, lower_cols, lower_trans, upper_cols, upper_trans)
    diag = jnp.einsum(
        "kab,kbc->kac", diagonal_blocks, right_sides, preferred_element_type=F32
    )
    lenter = scan_enter(lmap, lstate, "row", False)
    uenter = scan_enter(umap, ustate, "row", True)
    return pl.pallas_call(
        apply_kernel,
        out_shape=jax.ShapeDtypeStruct((count, rows, rhs), BF16),
        scratch_shapes=[
            pltpu.VMEM((count, rank, rhs), BF16),
            pltpu.VMEM((count, rank, rhs), BF16),
        ],
        name="apply",
    )(lenter, uenter, lower_trans, upper_trans, lsrc, usrc, diag, lower_rows, upper_rows)


def solution(mesh):
    spec = P(("sep", "row"), None, None)
    return jax.shard_map(
        shards, mesh=mesh, in_specs=(spec,) * 8, out_specs=spec, check_vma=False
    )
```

time: 269 us -> 83.1 us (0.31)
  the two profiles are of different devices: /device:TPU:1 before, /device:TPU:25 now
where the time goes in v2:
time: 83.1 us; the launch traced here: 82.7 us
  waiting for transfers between devices  35.4 us (43%)
  starting transfers between devices  26 us (31%)
  Pallas kernels  12.8 us (15%)
  matrix products  7.07 us (9%)
  other arithmetic  1.12 us (1%)
    ppermute x10, waiting for transfers between devices, shifted(): return lax.ppermute(value, axis, pairs)  35.4 us
    ppermute x10, starting transfers between devices, shifted(): return lax.ppermute(value, axis, pairs)  26 us
    pallas_call x1, Pallas kernels, shards(): pl.pallas_call(sweep_kernel, out_shape=(jax.ShapeDtypeStruct((rank, rank)...  6.5 us
    pallas_call x1, Pallas kernels, shards(): pl.pallas_call(apply_kernel, out_shape=jax.ShapeDtypeStruct((count, rows,...  6.26 us
    dot_general x6, matrix products, scan_enter(): joined = jnp.dot(both[:, :rank], got, precision=HIGHEST)  3.6 us
    dot_general x2, matrix products, scan_enter(): return jnp.dot(near[:, :rank], far, precision=HIGHEST) + near[:, rank:]  2.09 us
  transfers between devices with their start and end apart: 10, of which 4 were waited for; matrix products, arithmetic and copies ran while one was open for 7% of the time, Pallas kernels for 0%

profile of v2, /device:TPU:25, one launch (start us, length us, event | category | flops | bytes accessed | tf_op | source)
XLA Modules:
  0.0 82.7 jit_solution(6718397236804361936)
XLA Ops:
  0.0 0.0 copy-start
  0.0 6.5 %sweep.1 = (f32[256,256]{1,0:T(8,128)}, f32[256,128]{1,0:T(8,128)}, f32[8,256,128]{2,1,0:T(8,128)}, f32[256,256]{1,0:T(8,128)}, f32[256,128]{1,0:T(8,128)}, /*index=5*/f32[8,256,128]{2,1,0:T(8,128)}) custom-call(bf16[8,256,128]{2,1,0:T(8,128)(2,1)} %rhs_ref.1, bf16[8,256,256]{2,1,0:T(8,128)(2,1)} %lcols_ref.1, bf16[8,256,256]{2,1,0:T(8,128)(2,1)} %ltrans_ref.3, ...), custom_call_target="tpu_custom_call" | custom-call | tf_op jit(solution)/shard_map/sweep/pallas_call | solution.py:114
  6.5 0.0 copy-start.2
  6.5 0.0 copy-start.4
  6.5 1.1 %pad_maximum_fusion.1 = f32[256,384]{1,0:T(8,128)S(1)} fusion(f32[256,128]{1,0:T(8,128)} %get-tuple-element.14, f32[256,256]{1,0:T(8,128)} %get-tuple-element.13), kind=kLoop, calls=%fused_computation.9 | loop fusion | flops 98304 | bytes 786432 | tf_op jit(solution)/shard_map/concatenate | solution.py:85
  7.6 2.6 %collective-permute-start.5 = (f32[256,384]{1,0:T(8,128)S(1)}, f32[256,384]{1,0:T(8,128)S(1)}, u32[]{:S(2)}, u32[]{:S(2)}) collective-permute-start(f32[256,384]{1,0:T(8,128)S(1)} %pad_maximum_fusion.1), channel_id=1, source_target_pairs={{1,0},{2,1},{3,2},{4,3},{5,4},{6,5},{7,6},{8,7},{9,8},{10,9},{11,1... | collective-permute-start | bytes 1179656 | tf_op jit(solution)/shard_map/ppermute | solution.py:79
  10.2 0.0 copy-done.2
  10.2 0.0 copy-done.4
  10.2 0.0 copy-start.3
  10.2 0.0 copy-start.5
  10.3 3.2 %collective-permute-start = (f32[256,384]{1,0:T(8,128)S(1)}, f32[256,384]{1,0:T(8,128)S(1)}, u32[]{:S(2)}, u32[]{:S(2)}) collective-permute-start(f32[256,384]{1,0:T(8,128)S(1)} %pad_maximum_fusion), channel_id=1, source_target_pairs={{0,1},{1,2},{2,3},{3,4},{4,5},{5,6},{6,7},{7,8},{8,9},{9,10},{10,1... | collective-permute-start | bytes 1179656 | tf_op jit(solution)/shard_map/ppermute | solution.py:79
  13.5 7.5 %collective-permute-done.5 = f32[256,384]{1,0:T(8,128)S(1)} collective-permute-done((f32[256,384]{1,0:T(8,128)S(1)}, f32[256,384]{1,0:T(8,128)S(1)}, u32[]{:S(2)}, u32[]{:S(2)}) %collective-permute-start.5) | collective-permute-done | bytes 393248 | tf_op jit(solution)/shard_map/ppermute | solution.py:79
  21.0 0.0 copy-done.3
  21.0 0.0 copy-done.5
  21.0 0.6 convolution_add_fusion.2
  21.6 1.9 %collective-permute-start.6 = (f32[256,384]{1,0:T(8,128)S(1)}, f32[256,384]{1,0:T(8,128)S(1)}, u32[]{:S(2)}, u32[]{:S(2)}) collective-permute-start(f32[256,384]{1,0:T(8,128)S(1)} %convolution_add_fusion.2), channel_id=1, source_target_pairs={{2,0},{3,1},{4,2},{5,3},{6,4},{7,5},{8,6},{9,7},{10,8},{11,9},{12,... | collective-permute-start | bytes 1179656 | tf_op jit(solution)/shard_map/ppermute | solution.py:79
  23.5 0.0 collective-permute-done
  23.5 0.6 convolution_add_fusion.5
  24.2 3.4 %collective-permute-start.1 = (f32[256,384]{1,0:T(8,128)S(1)}, f32[256,384]{1,0:T(8,128)S(1)}, u32[]{:S(2)}, u32[]{:S(2)}) collective-permute-start(f32[256,384]{1,0:T(8,128)S(1)} %convolution_add_fusion.5), channel_id=1, source_target_pairs={{0,2},{1,3},{2,4},{3,5},{4,6},{5,7},{6,8},{7,9},{8,10},{9,11},{10,... | collective-permute-start | bytes 1179656 | tf_op jit(solution)/shard_map/ppermute | solution.py:79
  27.6 13.3 %collective-permute-done.6 = f32[256,384]{1,0:T(8,128)S(1)} collective-permute-done((f32[256,384]{1,0:T(8,128)S(1)}, f32[256,384]{1,0:T(8,128)S(1)}, u32[]{:S(2)}, u32[]{:S(2)}) %collective-permute-start.6) | collective-permute-done | bytes 393248 | tf_op jit(solution)/shard_map/ppermute | solution.py:79
  40.9 0.6 convolution_add_fusion.1
  41.5 2.7 %collective-permute-start.7 = (f32[256,384]{1,0:T(8,128)S(1)}, f32[256,384]{1,0:T(8,128)S(1)}, u32[]{:S(2)}, u32[]{:S(2)}) collective-permute-start(f32[256,384]{1,0:T(8,128)S(1)} %convolution_add_fusion.1), channel_id=1, source_target_pairs={{4,0},{5,1},{6,2},{7,3},{8,4},{9,5},{10,6},{11,7},{12,8},{13,9},{1... | collective-permute-start | bytes 1179656 | tf_op jit(solution)/shard_map/ppermute | solution.py:79
  44.2 0.0 collective-permute-done.1
  44.2 0.6 convolution_add_fusion.4
  44.8 1.3 %collective-permute-start.2 = (f32[256,384]{1,0:T(8,128)S(1)}, f32[256,384]{1,0:T(8,128)S(1)}, u32[]{:S(2)}, u32[]{:S(2)}) collective-permute-start(f32[256,384]{1,0:T(8,128)S(1)} %convolution_add_fusion.4), channel_id=1, source_target_pairs={{0,4},{1,5},{2,6},{3,7},{4,8},{5,9},{6,10},{7,11},{8,12},{9,13},{1... | collective-permute-start | bytes 1179656 | tf_op jit(solution)/shard_map/ppermute | solution.py:79
  46.2 6.8 %collective-permute-done.7 = f32[256,384]{1,0:T(8,128)S(1)} collective-permute-done((f32[256,384]{1,0:T(8,128)S(1)}, f32[256,384]{1,0:T(8,128)S(1)}, u32[]{:S(2)}, u32[]{:S(2)}) %collective-permute-start.7) | collective-permute-done | bytes 393248 | tf_op jit(solution)/shard_map/ppermute | solution.py:79
  53.0 0.6 convolution_add_fusion
  53.6 2.1 %collective-permute-start.8 = (f32[256,384]{1,0:T(8,128)S(1)}, f32[256,384]{1,0:T(8,128)S(1)}, u32[]{:S(2)}, u32[]{:S(2)}) collective-permute-start(f32[256,384]{1,0:T(8,128)S(1)} %convolution_add_fusion), channel_id=1, source_target_pairs={{1,0},{2,1},{3,2},{4,3},{5,4},{6,5},{7,6},{8,7},{9,8},{10,9},{11,1... | collective-permute-start | bytes 1179656 | tf_op jit(solution)/shard_map/ppermute | solution.py:79
  55.7 0.0 copy-start.1
  55.7 4.0 %collective-permute-start.9 = (f32[256,128]{1,0:T(8,128)S(1)}, f32[256,128]{1,0:T(8,128)S(1)}, u32[]{:S(2)}, u32[]{:S(2)}) collective-permute-start(f32[256,128]{1,0:T(8,128)S(1)} %slice.68), channel_id=1, source_target_pairs={{9,0},{10,1},{11,2},{12,3},{13,4},{14,5},{15,6},{25,16},{26,17},{2... | collective-permute-start | bytes 393224 | tf_op jit(solution)/shard_map/ppermute | solution.py:79
  59.8 0.0 collective-permute-done.2
  59.8 0.6 convolution_add_fusion.3
  60.4 3.5 %collective-permute-start.3 = (f32[256,384]{1,0:T(8,128)S(1)}, f32[256,384]{1,0:T(8,128)S(1)}, u32[]{:S(2)}, u32[]{:S(2)}) collective-permute-start(f32[256,384]{1,0:T(8,128)S(1)} %convolution_add_fusion.3), channel_id=1, source_target_pairs={{0,1},{1,2},{2,3},{3,4},{4,5},{5,6},{6,7},{7,8},{8,9},{9,10},{10,1... | collective-permute-start | bytes 1179656 | tf_op jit(solution)/shard_map/ppermute | solution.py:79
  63.9 0.0 copy-done
  63.9 0.0 copy-done.1
  63.9 1.4 %fusion.6.diag_ref = f32[8,256,128]{2,1,0:T(8,128)} fusion(bf16[8,256,256]{2,1,0:T(8,128)(2,1)S(1)} %copy-done, bf16[8,256,128]{2,1,0:T(8,128)(2,1)S(1)} %copy-done.1), kind=kOutput, calls=%fused_computation.16 | convolution fusion | flops 134217728 | bytes 2621440 | tf_op jit(solution)/shard_map/kab,kbc->kac/dot_general | solution.py:126
  65.3 1.3 %collective-permute-start.4 = (f32[256,128]{1,0:T(8,128)S(1)}, f32[256,128]{1,0:T(8,128)S(1)}, u32[]{:S(2)}, u32[]{:S(2)}) collective-permute-start(f32[256,128]{1,0:T(8,128)S(1)} %slice.61), channel_id=1, source_target_pairs={{0,9},{1,10},{2,11},{3,12},{4,13},{5,14},{6,15},{16,25},{17,26},{1... | collective-permute-start | bytes 393224 | tf_op jit(solution)/shard_map/ppermute | solution.py:79
  66.6 0.0 collective-permute-done.9
  66.6 0.0 collective-permute-done.8
  66.6 1.0 %convolution_add_fusion.6.uenter_ref = f32[256,128]{1,0:T(8,128)} fusion(f32[256,128]{1,0:T(8,128)S(1)} %collective-permute-done.9, f32[256,384]{1,0:T(8,128)S(1)} %collective-permute-done.8), kind=kOutput, calls=%fused_computation.6 | convolution fusion | flops 100696064 | bytes 655360 | tf_op jit(solution)/shard_map/dot_general | solution.py:99
  67.7 7.8 %collective-permute-done.4 = f32[256,128]{1,0:T(8,128)S(1)} collective-permute-done((f32[256,128]{1,0:T(8,128)S(1)}, f32[256,128]{1,0:T(8,128)S(1)}, u32[]{:S(2)}, u32[]{:S(2)}) %collective-permute-start.4) | collective-permute-done | bytes 131104 | tf_op jit(solution)/shard_map/ppermute | solution.py:79
  75.4 0.0 collective-permute-done.3
  75.4 1.1 %convolution_add_fusion.7.lenter_ref = f32[256,128]{1,0:T(8,128)} fusion(f32[256,128]{1,0:T(8,128)S(1)} %collective-permute-done.4, f32[256,384]{1,0:T(8,128)S(1)} %collective-permute-done.3), kind=kOutput, calls=%fused_computation.7 | convolution fusion | flops 100696064 | bytes 655360 | tf_op jit(solution)/shard_map/dot_general | solution.py:99
  76.5 6.3 %apply.1 = bf16[8,256,128]{2,1,0:T(8,128)(2,1)} custom-call(f32[256,128]{1,0:T(8,128)} %convolution_add_fusion.7.lenter_ref, f32[256,128]{1,0:T(8,128)} %convolution_add_fusion.6.uenter_ref, bf16[8,256,256]{2,1,0:T(8,128)(2,1)} %ltrans_ref.3, bf16[8,256,256]{2,1,0:T(8,128)(2,1)} %utrans_ref.3, f32[8,256,128]{2,1,0:T(8,128)} %get-tuple-element.15.lsrc_ref, ...), custom_call_target="tpu_custom_call" | custom-call | tf_op jit(solution)/shard_map/apply/pallas_call | solution.py:131
  (7 shorter events, 0.1 us)
Async XLA Ops:
  0.0 63.9 %copy-start = (bf16[8,256,256]{2,1,0:T(8,128)(2,1)S(1)}, bf16[8,256,256]{2,1,0:T(8,128)(2,1)}, u32[]{:S(2)}) copy-start(bf16[8,256,256]{2,1,0:T(8,128)(2,1)} %param.9) | copy-start | bytes 3145732
  6.5 3.7 %copy-start.2 = (f32[256,256]{1,0:T(8,128)S(1)}, f32[256,256]{1,0:T(8,128)}, u32[]{:S(2)}) copy-start(f32[256,256]{1,0:T(8,128)} %get-tuple-element.11) | copy-start | bytes 786436
  6.5 3.7 %copy-start.4 = (f32[256,128]{1,0:T(8,128)S(1)}, f32[256,128]{1,0:T(8,128)}, u32[]{:S(2)}) copy-start(f32[256,128]{1,0:T(8,128)} %get-tuple-element.12) | copy-start | bytes 393220
  7.6 13.4 %collective-permute-start.5 = (f32[256,384]{1,0:T(8,128)S(1)}, f32[256,384]{1,0:T(8,128)S(1)}, u32[]{:S(2)}, u32[]{:S(2)}) collective-permute-start(f32[256,384]{1,0:T(8,128)S(1)} %pad_maximum_fusion.1), channel_id=1, source_target_pairs={{1,0},{2,1},{3,2},{4,3},{5,4},{6,5},{7,6},{8,7},{9,8},{10,9},{11,1... | collective-permute-start | bytes 1179656 | tf_op jit(solution)/shard_map/ppermute | solution.py:79
  10.2 10.8 %copy-start.3 = (f32[256,256]{1,0:T(8,128)S(1)}, f32[256,256]{1,0:T(8,128)}, u32[]{:S(2)}) copy-start(f32[256,256]{1,0:T(8,128)} %get-tuple-element.13) | copy-start | bytes 786436
  10.2 10.8 %copy-start.5 = (f32[256,128]{1,0:T(8,128)S(1)}, f32[256,128]{1,0:T(8,128)}, u32[]{:S(2)}) copy-start(f32[256,128]{1,0:T(8,128)} %get-tuple-element.14) | copy-start | bytes 393220
  10.3 13.3 %collective-permute-start = (f32[256,384]{1,0:T(8,128)S(1)}, f32[256,384]{1,0:T(8,128)S(1)}, u32[]{:S(2)}, u32[]{:S(2)}) collective-permute-start(f32[256,384]{1,0:T(8,128)S(1)} %pad_maximum_fusion), channel_id=1, source_target_pairs={{0,1},{1,2},{2,3},{3,4},{4,5},{5,6},{6,7},{7,8},{8,9},{9,10},{10,1... | collective-permute-start | bytes 1179656 | tf_op jit(solution)/shard_map/ppermute | solution.py:79
  21.6 19.2 %collective-permute-start.6 = (f32[256,384]{1,0:T(8,128)S(1)}, f32[256,384]{1,0:T(8,128)S(1)}, u32[]{:S(2)}, u32[]{:S(2)}) collective-permute-start(f32[256,384]{1,0:T(8,128)S(1)} %convolution_add_fusion.2), channel_id=1, source_target_pairs={{2,0},{3,1},{4,2},{5,3},{6,4},{7,5},{8,6},{9,7},{10,8},{11,9},{12,... | collective-permute-start | bytes 1179656 | tf_op jit(solution)/shard_map/ppermute | solution.py:79
  24.2 20.1 %collective-permute-start.1 = (f32[256,384]{1,0:T(8,128)S(1)}, f32[256,384]{1,0:T(8,128)S(1)}, u32[]{:S(2)}, u32[]{:S(2)}) collective-permute-start(f32[256,384]{1,0:T(8,128)S(1)} %convolution_add_fusion.5), channel_id=1, source_target_pairs={{0,2},{1,3},{2,4},{3,5},{4,6},{5,7},{6,8},{7,9},{8,10},{9,11},{10,... | collective-permute-start | bytes 1179656 | tf_op jit(solution)/shard_map/ppermute | solution.py:79
  41.5 11.5 %collective-permute-start.7 = (f32[256,384]{1,0:T(8,128)S(1)}, f32[256,384]{1,0:T(8,128)S(1)}, u32[]{:S(2)}, u32[]{:S(2)}) collective-permute-start(f32[256,384]{1,0:T(8,128)S(1)} %convolution_add_fusion.1), channel_id=1, source_target_pairs={{4,0},{5,1},{6,2},{7,3},{8,4},{9,5},{10,6},{11,7},{12,8},{13,9},{1... | collective-permute-start | bytes 1179656 | tf_op jit(solution)/shard_map/ppermute | solution.py:79
  44.8 15.0 %collective-permute-start.2 = (f32[256,384]{1,0:T(8,128)S(1)}, f32[256,384]{1,0:T(8,128)S(1)}, u32[]{:S(2)}, u32[]{:S(2)}) collective-permute-start(f32[256,384]{1,0:T(8,128)S(1)} %convolution_add_fusion.4), channel_id=1, source_target_pairs={{0,4},{1,5},{2,6},{3,7},{4,8},{5,9},{6,10},{7,11},{8,12},{9,13},{1... | collective-permute-start | bytes 1179656 | tf_op jit(solution)/shard_map/ppermute | solution.py:79
  53.6 13.0 %collective-permute-start.8 = (f32[256,384]{1,0:T(8,128)S(1)}, f32[256,384]{1,0:T(8,128)S(1)}, u32[]{:S(2)}, u32[]{:S(2)}) collective-permute-start(f32[256,384]{1,0:T(8,128)S(1)} %convolution_add_fusion), channel_id=1, source_target_pairs={{1,0},{2,1},{3,2},{4,3},{5,4},{6,5},{7,6},{8,7},{9,8},{10,9},{11,1... | collective-permute-start | bytes 1179656 | tf_op jit(solution)/shard_map/ppermute | solution.py:79
  55.7 8.2 %copy-start.1 = (bf16[8,256,128]{2,1,0:T(8,128)(2,1)S(1)}, bf16[8,256,128]{2,1,0:T(8,128)(2,1)}, u32[]{:S(2)}) copy-start(bf16[8,256,128]{2,1,0:T(8,128)(2,1)} %rhs_ref.1) | copy-start | bytes 1572868
  55.7 10.9 %collective-permute-start.9 = (f32[256,128]{1,0:T(8,128)S(1)}, f32[256,128]{1,0:T(8,128)S(1)}, u32[]{:S(2)}, u32[]{:S(2)}) collective-permute-start(f32[256,128]{1,0:T(8,128)S(1)} %slice.68), channel_id=1, source_target_pairs={{9,0},{10,1},{11,2},{12,3},{13,4},{14,5},{15,6},{25,16},{26,17},{2... | collective-permute-start | bytes 393224 | tf_op jit(solution)/shard_map/ppermute | solution.py:79
  60.4 15.0 %collective-permute-start.3 = (f32[256,384]{1,0:T(8,128)S(1)}, f32[256,384]{1,0:T(8,128)S(1)}, u32[]{:S(2)}, u32[]{:S(2)}) collective-permute-start(f32[256,384]{1,0:T(8,128)S(1)} %convolution_add_fusion.3), channel_id=1, source_target_pairs={{0,1},{1,2},{2,3},{3,4},{4,5},{5,6},{6,7},{7,8},{8,9},{9,10},{10,1... | collective-permute-start | bytes 1179656 | tf_op jit(solution)/shard_map/ppermute | solution.py:79
  65.3 10.1 %collective-permute-start.4 = (f32[256,128]{1,0:T(8,128)S(1)}, f32[256,128]{1,0:T(8,128)S(1)}, u32[]{:S(2)}, u32[]{:S(2)}) collective-permute-start(f32[256,128]{1,0:T(8,128)S(1)} %slice.61), channel_id=1, source_target_pairs={{0,9},{1,10},{2,11},{3,12},{4,13},{5,14},{6,15},{16,25},{17,26},{1... | collective-permute-start | bytes 393224 | tf_op jit(solution)/shard_map/ppermute | solution.py:79

commit v3 on v2

--- a/solution.py
+++ b/solution.py
@@ -99,6 +99,42 @@
     return jnp.dot(near[:, :rank], far, precision=HIGHEST) + near[:, rank:]
 
 
+def chip_shift(value, axis, chips, shift):
+    pairs = [(2 * c, 2 * (c + shift)) for c in range(chips - shift)]
+    pairs += [(2 * c + 1, 2 * (c - shift) + 1) for c in range(shift, chips)]
+    return lax.ppermute(value, axis, pairs)
+
+
+def scan_chips(lmap, lstate, umap, ustate, axis):
+    count = lax.axis_size(axis)
+    chips = count // 2
+    rank = lmap.shape[0]
+    first = lax.axis_index(axis) % 2 == 0
+    lower = jnp.concatenate([lmap, lstate], axis=1)
+    upper = jnp.concatenate([umap, ustate], axis=1)
+    own = jnp.where(first, lower, upper)
+    partner = [(2 * c, 2 * c + 1) for c in range(chips)]
+    partner += [(2 * c + 1, 2 * c) for c in range(chips)]
+    got = lax.ppermute(jnp.where(first, upper, lower), axis, partner)
+    tail = jnp.concatenate([jnp.zeros_like(lmap), got[:, rank:]], axis=1)
+    both = jnp.dot(got[:, :rank], own, precision=HIGHEST) + tail
+    rounds = 0
+    while 2 ** (rounds + 1) < chips - 1:
+        rounds += 1
+    shift = 1
+    for _ in range(rounds):
+        got = chip_shift(both, axis, chips, shift)
+        tail = jnp.concatenate([jnp.zeros_like(lmap), both[:, rank:]], axis=1)
+        both = jnp.dot(both[:, :rank], got, precision=HIGHEST) + tail
+        shift *= 2
+    near = chip_shift(both, axis, chips, 1)
+    far = chip_shift(both[:, rank:], axis, chips, 1 + shift)
+    enter = jnp.dot(near[:, :rank], far, precision=HIGHEST) + near[:, rank:]
+    send = jnp.dot(own[:, :rank], enter, precision=HIGHEST) + own[:, rank:]
+    other = lax.ppermute(send, axis, partner)
+    return jnp.where(first, enter, other), jnp.where(first, other, enter)
+
+
 def shards(
     right_sides,
     diagonal_blocks,
@@ -126,8 +162,12 @@
     diag = jnp.einsum(
         "kab,kbc->kac", diagonal_blocks, right_sides, preferred_element_type=F32
     )
-    lenter = scan_enter(lmap, lstate, "row", False)
-    uenter = scan_enter(umap, ustate, "row", True)
+    count_row = lax.axis_size("row")
+    if count_row % 2 == 0 and count_row >= 4:
+        lenter, uenter = scan_chips(lmap, lstate, umap, ustate, "row")
+    else:
+        lenter = scan_enter(lmap, lstate, "row", False)
+        uenter = scan_enter(umap, ustate, "row", True)
     return pl.pallas_call(
         apply_kernel,
         out_shape=jax.ShapeDtypeStruct((count, rows, rhs), BF16),

time: 83.1 us -> 58.1 us (0.70)
  the two profiles are of different devices: /device:TPU:25 before, /device:TPU:1 now
where the time goes in v3:
time: 58.1 us; the launch traced here: 57.8 us
  waiting for transfers between devices  28.5 us (49%)
  Pallas kernels  12.8 us (22%)
  starting transfers between devices  9.62 us (17%)
  matrix products  3.94 us (7%)
  local copies, waits for them, and re-layouts  2.03 us (3%)
  other arithmetic  0.77 us (1%)
    ppermute x4, waiting for transfers between devices, chip_shift(): return lax.ppermute(value, axis, pairs)  26.7 us
    pallas_call x1, Pallas kernels, shards(): pl.pallas_call(sweep_kernel, out_shape=(jax.ShapeDtypeStruct((rank, rank)...  6.5 us
    pallas_call x1, Pallas kernels, shards(): pl.pallas_call(apply_kernel, out_shape=jax.ShapeDtypeStruct((count, rows,...  6.27 us
    ppermute x4, starting transfers between devices, chip_shift(): return lax.ppermute(value, axis, pairs)  5.3 us
    ppermute x1, starting transfers between devices, scan_chips(): other = lax.ppermute(send, axis, partner)  4.24 us
    unnamed x12, local copies, waits for them, and re-layouts  1.97 us
    ppermute x1, waiting for transfers between devices, scan_chips(): got = lax.ppermute(jnp.where(first, upper, lower), axis, partner)  1.71 us
    dot_general x1, matrix products, shards(): jnp.einsum('kab,kbc->kac', diagonal_blocks, right_sides, preferred_elemen...  1.39 us
  transfers between devices with their start and end apart: 6, of which 5 were waited for; matrix products, arithmetic and copies ran while one was open for 2% of the time, Pallas kernels for 0%

profile of v3, /device:TPU:1, one launch (start us, length us, event | category | flops | bytes accessed | tf_op | source)
XLA Modules:
  0.0 57.8 jit_solution(5427984429044095014)
XLA Ops:
  0.0 0.0 copy-start
  0.0 6.5 %sweep.1 = (f32[256,256]{1,0:T(8,128)}, f32[256,128]{1,0:T(8,128)}, f32[8,256,128]{2,1,0:T(8,128)}, f32[256,256]{1,0:T(8,128)}, f32[256,128]{1,0:T(8,128)}, /*index=5*/f32[8,256,128]{2,1,0:T(8,128)}) custom-call(bf16[8,256,128]{2,1,0:T(8,128)(2,1)} %rhs_ref.1, bf16[8,256,256]{2,1,0:T(8,128)(2,1)} %lcols_ref.1, bf16[8,256,256]{2,1,0:T(8,128)(2,1)} %ltrans_ref.3, ...), custom_call_target="tpu_custom_call" | custom-call | tf_op jit(solution)/shard_map/sweep/pallas_call | solution.py:150
  6.5 0.0 copy-start.2
  6.5 1.0 %constant_dynamic-update-slice_fusion.1 = f32[256,384]{1,0:T(8,128)S(1)} fusion(f32[256,256]{1,0:T(8,128)} %get-tuple-element.11), kind=kLoop, calls=%fused_computation.15 | loop fusion | bytes 524288
  7.5 0.0 copy-done.2
  7.5 0.0 copy-start.3
  7.5 0.0 copy-start.4
  7.6 0.8 %copy-done.3 = f32[256,128]{1,0:T(8,128)S(1)} copy-done((f32[256,128]{1,0:T(8,128)S(1)}, f32[256,128]{1,0:T(8,128)}, u32[]{:S(2)}) %copy-start.3) | copy-done | bytes 131096
  8.4 0.1 copy-done.4
  8.5 0.1 broadcast_select_fusion.1
  8.6 0.1 collective-permute-start
  8.7 1.7 %collective-permute-done = f32[256,384]{1,0:T(8,128)S(1)} collective-permute-done((f32[256,384]{1,0:T(8,128)S(1)}, f32[256,384]{1,0:T(8,128)S(1)}, u32[]{:S(2)}, u32[]{:S(2)}) %collective-permute-start) | collective-permute-done | bytes 393248 | tf_op jit(solution)/shard_map/ppermute | solution.py:118
  10.4 0.6 %convolution_add_fusion.2 = f32[256,384]{1,0:T(8,128)S(1)} fusion(f32[256,384]{1,0:T(8,128)S(1)} %get-tuple-element.18, f32[256,128]{1,0:T(8,128)S(1)} %slice.45, f32[256,384]{1,0:T(8,128)S(1)} %collective-permute-done), kind=kOutput, calls=%fused_computation.2 | convolution fusion | flops 302088192 | bytes 1179648 | tf_op jit(solution)/shard_map/dot_general | solution.py:120
  11.0 1.3 %collective-permute-start.1 = (f32[256,384]{1,0:T(8,128)S(1)}, f32[256,384]{1,0:T(8,128)S(1)}, u32[]{:S(2)}, u32[]{:S(2)}) collective-permute-start(f32[256,384]{1,0:T(8,128)S(1)} %convolution_add_fusion.2), channel_id=1, source_target_pairs={{0,2},{2,4},{4,6},{6,8},{8,10},{10,12},{12,14},{3,1},{5,3},{7,5},{... | collective-permute-start | bytes 1179656 | tf_op jit(solution)/shard_map/ppermute | solution.py:105
  12.3 8.1 %collective-permute-done.1 = f32[256,384]{1,0:T(8,128)S(1)} collective-permute-done((f32[256,384]{1,0:T(8,128)S(1)}, f32[256,384]{1,0:T(8,128)S(1)}, u32[]{:S(2)}, u32[]{:S(2)}) %collective-permute-start.1) | collective-permute-done | bytes 393248 | tf_op jit(solution)/shard_map/ppermute | solution.py:105
  20.4 0.6 %convolution_add_fusion.1 = f32[256,384]{1,0:T(8,128)S(1)} fusion(f32[256,384]{1,0:T(8,128)S(1)} %collective-permute-done.1, f32[256,128]{1,0:T(8,128)S(1)} %slice.47, f32[256,384]{1,0:T(8,128)S(1)} %convolution_add_fusion.2), kind=kOutput, calls=%fused_computation.1 | convolution fusion | flops 302088192 | bytes 1179648 | tf_op jit(solution)/shard_map/dot_general | solution.py:128
  21.0 1.3 %collective-permute-start.2 = (f32[256,384]{1,0:T(8,128)S(1)}, f32[256,384]{1,0:T(8,128)S(1)}, u32[]{:S(2)}, u32[]{:S(2)}) collective-permute-start(f32[256,384]{1,0:T(8,128)S(1)} %convolution_add_fusion.1), channel_id=1, source_target_pairs={{0,4},{2,6},{4,8},{6,10},{8,12},{10,14},{5,1},{7,3},{9,5},{11,7},{... | collective-permute-start | bytes 1179656 | tf_op jit(solution)/shard_map/ppermute | solution.py:105
  22.4 11.5 %collective-permute-done.2 = f32[256,384]{1,0:T(8,128)S(1)} collective-permute-done((f32[256,384]{1,0:T(8,128)S(1)}, f32[256,384]{1,0:T(8,128)S(1)}, u32[]{:S(2)}, u32[]{:S(2)}) %collective-permute-start.2) | collective-permute-done | bytes 393248 | tf_op jit(solution)/shard_map/ppermute | solution.py:105
  33.8 0.6 %convolution_add_fusion = f32[256,384]{1,0:T(8,128)S(1)} fusion(f32[256,384]{1,0:T(8,128)S(1)} %collective-permute-done.2, f32[256,128]{1,0:T(8,128)S(1)} %slice.49, f32[256,384]{1,0:T(8,128)S(1)} %convolution_add_fusion.1), kind=kOutput, calls=%fused_computation | convolution fusion | flops 302088192 | bytes 1179648 | tf_op jit(solution)/shard_map/dot_general | solution.py:128
  34.4 1.3 %collective-permute-start.3 = (f32[256,384]{1,0:T(8,128)S(1)}, f32[256,384]{1,0:T(8,128)S(1)}, u32[]{:S(2)}, u32[]{:S(2)}) collective-permute-start(f32[256,384]{1,0:T(8,128)S(1)} %convolution_add_fusion), channel_id=1, source_target_pairs={{0,2},{2,4},{4,6},{6,8},{8,10},{10,12},{12,14},{3,1},{5,3},{7,5},{... | collective-permute-start | bytes 1179656 | tf_op jit(solution)/shard_map/ppermute | solution.py:105
  35.8 0.0 copy-start.1
  35.8 1.4 %collective-permute-start.4 = (f32[256,128]{1,0:T(8,128)S(1)}, f32[256,128]{1,0:T(8,128)S(1)}, u32[]{:S(2)}, u32[]{:S(2)}) collective-permute-start(f32[256,128]{1,0:T(8,128)S(1)} %slice.51), channel_id=1, source_target_pairs={{0,10},{2,12},{4,14},{11,1},{13,3},{15,5},{16,26},{18,28},{20,30},... | collective-permute-start | bytes 393224 | tf_op jit(solution)/shard_map/ppermute | solution.py:105
  37.2 7.0 %collective-permute-done.4 = f32[256,128]{1,0:T(8,128)S(1)} collective-permute-done((f32[256,128]{1,0:T(8,128)S(1)}, f32[256,128]{1,0:T(8,128)S(1)}, u32[]{:S(2)}, u32[]{:S(2)}) %collective-permute-start.4) | collective-permute-done | bytes 131104 | tf_op jit(solution)/shard_map/ppermute | solution.py:105
  44.2 0.2 collective-permute-done.3
  44.4 0.4 convolution_add_fusion.4
  44.7 0.4 convolution_add_fusion.3
  45.1 4.2 %collective-permute-start.5 = (f32[256,128]{1,0:T(8,128)S(1)}, f32[256,128]{1,0:T(8,128)S(1)}, u32[]{:S(2)}, u32[]{:S(2)}) collective-permute-start(f32[256,128]{1,0:T(8,128)S(1)} %convolution_add_fusion.3), channel_id=1, source_target_pairs={{0,1},{2,3},{4,5},{6,7},{8,9},{10,11},{12,13},{14,15},{1,0},{3,2},... | collective-permute-start | bytes 393224 | tf_op jit(solution)/shard_map/ppermute | solution.py:134
  49.4 0.0 copy-done
  49.4 0.0 copy-done.1
  49.4 1.4 %fusion.5.diag_ref = f32[8,256,128]{2,1,0:T(8,128)} fusion(bf16[8,256,256]{2,1,0:T(8,128)(2,1)S(1)} %copy-done, bf16[8,256,128]{2,1,0:T(8,128)(2,1)S(1)} %copy-done.1), kind=kOutput, calls=%fused_computation.18 | convolution fusion | flops 134217728 | bytes 2621440 | tf_op jit(solution)/shard_map/kab,kbc->kac/dot_general | solution.py:162
  50.8 0.0 collective-permute-done.5
  50.8 0.7 %broadcast_select_fusion.2 = (f32[256,128]{1,0:T(8,128)}, f32[256,128]{1,0:T(8,128)}) fusion(f32[256,128]{1,0:T(8,128)S(1)} %collective-permute-done.5, f32[256,128]{1,0:T(8,128)S(1)} %convolution_add_fusion.4, pred[]{:T(512)S(6)} %eq.5), kind=kLoop, calls=%fused_computation.12 | loop fusion | flops 65536 | bytes 524289 | tf_op jit(solution)/shard_map/jit(_where)/select_n | solution.py:135
  51.5 6.3 %apply.1 = bf16[8,256,128]{2,1,0:T(8,128)(2,1)} custom-call(f32[256,128]{1,0:T(8,128)} %get-tuple-element.20.lenter_ref, f32[256,128]{1,0:T(8,128)} %get-tuple-element.19.uenter_ref, bf16[8,256,256]{2,1,0:T(8,128)(2,1)} %ltrans_ref.3, bf16[8,256,256]{2,1,0:T(8,128)(2,1)} %utrans_ref.3, f32[8,256,128]{2,1,0:T(8,128)} %get-tuple-element.15.lsrc_ref, ...), custom_call_target="tpu_custom_call" | custom-call | tf_op jit(solution)/shard_map/apply/pallas_call | solution.py:171
  (6 shorter events, 0.1 us)
Async XLA Ops:
  0.0 49.4 %copy-start = (bf16[8,256,256]{2,1,0:T(8,128)(2,1)S(1)}, bf16[8,256,256]{2,1,0:T(8,128)(2,1)}, u32[]{:S(2)}) copy-start(bf16[8,256,256]{2,1,0:T(8,128)(2,1)} %param.9) | copy-start | bytes 3145732
  6.5 1.0 %copy-start.2 = (f32[256,256]{1,0:T(8,128)S(1)}, f32[256,256]{1,0:T(8,128)}, u32[]{:S(2)}) copy-start(f32[256,256]{1,0:T(8,128)} %get-tuple-element.13) | copy-start | bytes 786436
  7.5 0.9 %copy-start.3 = (f32[256,128]{1,0:T(8,128)S(1)}, f32[256,128]{1,0:T(8,128)}, u32[]{:S(2)}) copy-start(f32[256,128]{1,0:T(8,128)} %get-tuple-element.14) | copy-start | bytes 393220
  7.5 1.0 %copy-start.4 = (f32[256,128]{1,0:T(8,128)S(1)}, f32[256,128]{1,0:T(8,128)}, u32[]{:S(2)}) copy-start(f32[256,128]{1,0:T(8,128)} %get-tuple-element.12) | copy-start | bytes 393220
  8.6 1.8 %collective-permute-start = (f32[256,384]{1,0:T(8,128)S(1)}, f32[256,384]{1,0:T(8,128)S(1)}, u32[]{:S(2)}, u32[]{:S(2)}) collective-permute-start(f32[256,384]{1,0:T(8,128)S(1)} %get-tuple-element.17), channel_id=1, source_target_pairs={{0,1},{2,3},{4,5},{6,7},{8,9},{10,11},{12,13},{14,15},{1,0},{3,2},... | collective-permute-start | bytes 1179656 | tf_op jit(solution)/shard_map/ppermute | solution.py:118
  11.0 9.4 %collective-permute-start.1 = (f32[256,384]{1,0:T(8,128)S(1)}, f32[256,384]{1,0:T(8,128)S(1)}, u32[]{:S(2)}, u32[]{:S(2)}) collective-permute-start(f32[256,384]{1,0:T(8,128)S(1)} %convolution_add_fusion.2), channel_id=1, source_target_pairs={{0,2},{2,4},{4,6},{6,8},{8,10},{10,12},{12,14},{3,1},{5,3},{7,5},{... | collective-permute-start | bytes 1179656 | tf_op jit(solution)/shard_map/ppermute | solution.py:105
  21.0 12.8 %collective-permute-start.2 = (f32[256,384]{1,0:T(8,128)S(1)}, f32[256,384]{1,0:T(8,128)S(1)}, u32[]{:S(2)}, u32[]{:S(2)}) collective-permute-start(f32[256,384]{1,0:T(8,128)S(1)} %convolution_add_fusion.1), channel_id=1, source_target_pairs={{0,4},{2,6},{4,8},{6,10},{8,12},{10,14},{5,1},{7,3},{9,5},{11,7},{... | collective-permute-start | bytes 1179656 | tf_op jit(solution)/shard_map/ppermute | solution.py:105
  34.4 9.9 %collective-permute-start.3 = (f32[256,384]{1,0:T(8,128)S(1)}, f32[256,384]{1,0:T(8,128)S(1)}, u32[]{:S(2)}, u32[]{:S(2)}) collective-permute-start(f32[256,384]{1,0:T(8,128)S(1)} %convolution_add_fusion), channel_id=1, source_target_pairs={{0,2},{2,4},{4,6},{6,8},{8,10},{10,12},{12,14},{3,1},{5,3},{7,5},{... | collective-permute-start | bytes 1179656 | tf_op jit(solution)/shard_map/ppermute | solution.py:105
  35.8 13.6 %copy-start.1 = (bf16[8,256,128]{2,1,0:T(8,128)(2,1)S(1)}, bf16[8,256,128]{2,1,0:T(8,128)(2,1)}, u32[]{:S(2)}) copy-start(bf16[8,256,128]{2,1,0:T(8,128)(2,1)} %rhs_ref.1) | copy-start | bytes 1572868
  35.8 8.4 %collective-permute-start.4 = (f32[256,128]{1,0:T(8,128)S(1)}, f32[256,128]{1,0:T(8,128)S(1)}, u32[]{:S(2)}, u32[]{:S(2)}) collective-permute-start(f32[256,128]{1,0:T(8,128)S(1)} %slice.51), channel_id=1, source_target_pairs={{0,10},{2,12},{4,14},{11,1},{13,3},{15,5},{16,26},{18,28},{20,30},... | collective-permute-start | bytes 393224 | tf_op jit(solution)/shard_map/ppermute | solution.py:105
  45.1 5.6 %collective-permute-start.5 = (f32[256,128]{1,0:T(8,128)S(1)}, f32[256,128]{1,0:T(8,128)S(1)}, u32[]{:S(2)}, u32[]{:S(2)}) collective-permute-start(f32[256,128]{1,0:T(8,128)S(1)} %convolution_add_fusion.3), channel_id=1, source_target_pairs={{0,1},{2,3},{4,5},{6,7},{8,9},{10,11},{12,13},{14,15},{1,0},{3,2},... | collective-permute-start | bytes 393224 | tf_op jit(solution)/shard_map/ppermute | solution.py:134

commit v4 on v3

--- a/solution.py
+++ b/solution.py
@@ -102,7 +102,13 @@
 def chip_shift(value, axis, chips, shift):
     pairs = [(2 * c, 2 * (c + shift)) for c in range(chips - shift)]
     pairs += [(2 * c + 1, 2 * (c - shift) + 1) for c in range(shift, chips)]
-    return lax.ppermute(value, axis, pairs)
+    width = value.shape[1]
+    piece = 128 if width % 128 == 0 else width
+    parts = [
+        lax.ppermute(value[:, i : i + piece], axis, pairs)
+        for i in range(0, width, piece)
+    ]
+    return parts[0] if len(parts) == 1 else jnp.concatenate(parts, axis=1)
 
 
 def scan_chips(lmap, lstate, umap, ustate, axis):

time: 58.1 us -> 63.9 us (1.100)
  starting transfers between devices: 9.62 us -> 20.7 us
  waiting for transfers between devices: 28.5 us -> 22.9 us
    ppermute x4 -> x10, starting transfers between devices: 5.3 us -> 13.1 us  [chip_shift(): lax.ppermute(value[:, i:i + piece], axis, pairs)]
    ppermute x4 -> x10, waiting for transfers between devices: 26.7 us -> 21.2 us  [chip_shift(): lax.ppermute(value[:, i:i + piece], axis, pairs)]
    ppermute x1, starting transfers between devices: 4.24 us -> 7.61 us  [scan_chips(): other = lax.ppermute(send, axis, partner)]
  transfers between devices with their start and end apart: 6 -> 12, of which waited for: 5 -> 11; matrix products, arithmetic and copies ran while one was open for 2% -> 2% of each run, Pallas kernels for 0% -> 0%
where the time goes in v4:
time: 63.9 us; the launch traced here: 63.5 us
  waiting for transfers between devices  22.9 us (36%)
  starting transfers between devices  20.7 us (32%)
  Pallas kernels  12.8 us (20%)
  matrix products  3.96 us (6%)
  local copies, waits for them, and re-layouts  2.08 us (3%)
  other arithmetic  0.76 us (1%)
    ppermute x10, waiting for transfers between devices, chip_shift(): lax.ppermute(value[:, i:i + piece], axis, pairs)  21.2 us
    ppermute x10, starting transfers between devices, chip_shift(): lax.ppermute(value[:, i:i + piece], axis, pairs)  13.1 us
    ppermute x1, starting transfers between devices, scan_chips(): other = lax.ppermute(send, axis, partner)  7.61 us
    pallas_call x1, Pallas kernels, shards(): pl.pallas_call(sweep_kernel, out_shape=(jax.ShapeDtypeStruct((rank, rank)...  6.5 us
    pallas_call x1, Pallas kernels, shards(): pl.pallas_call(apply_kernel, out_shape=jax.ShapeDtypeStruct((count, rows,...  6.28 us
    unnamed x12, local copies, waits for them, and re-layouts  1.97 us
    ppermute x1, waiting for transfers between devices, scan_chips(): got = lax.ppermute(jnp.where(first, upper, lower), axis, partner)  1.71 us
    dot_general x1, matrix products, shards(): jnp.einsum('kab,kbc->kac', diagonal_blocks, right_sides, preferred_elemen...  1.4 us
  transfers between devices with their start and end apart: 12, of which 11 were waited for; matrix products, arithmetic and copies ran while one was open for 2% of the time, Pallas kernels for 0%

profile of v4, /device:TPU:1, one launch (start us, length us, event | category | flops | bytes accessed | tf_op | source)
XLA Modules:
  0.0 63.5 jit_solution(15431530111959414392)
XLA Ops:
  0.0 0.0 copy-start
  0.0 6.5 %sweep.1 = (f32[256,256]{1,0:T(8,128)}, f32[256,128]{1,0:T(8,128)}, f32[8,256,128]{2,1,0:T(8,128)}, f32[256,256]{1,0:T(8,128)}, f32[256,128]{1,0:T(8,128)}, /*index=5*/f32[8,256,128]{2,1,0:T(8,128)}) custom-call(bf16[8,256,128]{2,1,0:T(8,128)(2,1)} %rhs_ref.1, bf16[8,256,256]{2,1,0:T(8,128)(2,1)} %lcols_ref.1, bf16[8,256,256]{2,1,0:T(8,128)(2,1)} %ltrans_ref.3, ...), custom_call_target="tpu_custom_call" | custom-call | tf_op jit(solution)/shard_map/sweep/pallas_call | solution.py:156
  6.5 0.0 copy-start.2
  6.5 1.0 %constant_dynamic-update-slice_fusion.1 = f32[256,384]{1,0:T(8,128)S(1)} fusion(f32[256,256]{1,0:T(8,128)} %get-tuple-element.11), kind=kLoop, calls=%fused_computation.27 | loop fusion | bytes 524288
  7.5 0.0 copy-done.2
  7.5 0.0 copy-start.3
  7.5 0.0 copy-start.4
  7.6 0.8 %copy-done.3 = f32[256,128]{1,0:T(8,128)S(1)} copy-done((f32[256,128]{1,0:T(8,128)S(1)}, f32[256,128]{1,0:T(8,128)}, u32[]{:S(2)}) %copy-start.3) | copy-done | bytes 131096
  8.4 0.1 copy-done.4
  8.5 0.1 broadcast_select_fusion.1
  8.6 0.1 collective-permute-start
  8.7 1.7 %collective-permute-done = f32[256,384]{1,0:T(8,128)S(1)} collective-permute-done((f32[256,384]{1,0:T(8,128)S(1)}, f32[256,384]{1,0:T(8,128)S(1)}, u32[]{:S(2)}, u32[]{:S(2)}) %collective-permute-start) | collective-permute-done | bytes 393248 | tf_op jit(solution)/shard_map/ppermute | solution.py:124
  10.4 0.6 convolution_add_fusion.2
  11.0 1.3 %collective-permute-start.3 = (f32[256,128]{1,0:T(8,128)S(1)}, f32[256,128]{1,0:T(8,128)S(1)}, u32[]{:S(2)}, u32[]{:S(2)}) collective-permute-start(f32[256,128]{1,0:T(8,128)S(1)} %get-tuple-element.26), channel_id=1, source_target_pairs={{0,2},{2,4},{4,6},{6,8},{8,10},{10,12},{12,14},{3,1},{5,3},{7,5},{... | collective-permute-start | bytes 393224 | tf_op jit(solution)/shard_map/ppermute | solution.py:108
  12.3 1.3 %collective-permute-start.2 = (f32[256,128]{1,0:T(8,128)S(1)}, f32[256,128]{1,0:T(8,128)S(1)}, u32[]{:S(2)}, u32[]{:S(2)}) collective-permute-start(f32[256,128]{1,0:T(8,128)S(1)} %get-tuple-element.27), channel_id=1, source_target_pairs={{0,2},{2,4},{4,6},{6,8},{8,10},{10,12},{12,14},{3,1},{5,3},{7,5},{... | collective-permute-start | bytes 393224 | tf_op jit(solution)/shard_map/ppermute | solution.py:108
  13.6 1.3 %collective-permute-start.1 = (f32[256,128]{1,0:T(8,128)S(1)}, f32[256,128]{1,0:T(8,128)S(1)}, u32[]{:S(2)}, u32[]{:S(2)}) collective-permute-start(f32[256,128]{1,0:T(8,128)S(1)} %get-tuple-element.25), channel_id=1, source_target_pairs={{0,2},{2,4},{4,6},{6,8},{8,10},{10,12},{12,14},{3,1},{5,3},{7,5},{... | collective-permute-start | bytes 393224 | tf_op jit(solution)/shard_map/ppermute | solution.py:108
  14.9 2.7 %collective-permute-done.3 = f32[256,128]{1,0:T(8,128)S(1)} collective-permute-done((f32[256,128]{1,0:T(8,128)S(1)}, f32[256,128]{1,0:T(8,128)S(1)}, u32[]{:S(2)}, u32[]{:S(2)}) %collective-permute-start.3) | collective-permute-done | bytes 131104 | tf_op jit(solution)/shard_map/ppermute | solution.py:108
  17.7 1.9 %collective-permute-done.2 = f32[256,128]{1,0:T(8,128)S(1)} collective-permute-done((f32[256,128]{1,0:T(8,128)S(1)}, f32[256,128]{1,0:T(8,128)S(1)}, u32[]{:S(2)}, u32[]{:S(2)}) %collective-permute-start.2) | collective-permute-done | bytes 131104 | tf_op jit(solution)/shard_map/ppermute | solution.py:108
  19.6 1.9 %collective-permute-done.1 = f32[256,128]{1,0:T(8,128)S(1)} collective-permute-done((f32[256,128]{1,0:T(8,128)S(1)}, f32[256,128]{1,0:T(8,128)S(1)}, u32[]{:S(2)}, u32[]{:S(2)}) %collective-permute-start.1) | collective-permute-done | bytes 131104 | tf_op jit(solution)/shard_map/ppermute | solution.py:108
  21.5 0.6 convolution_add_fusion.1
  22.2 1.3 %collective-permute-start.6 = (f32[256,128]{1,0:T(8,128)S(1)}, f32[256,128]{1,0:T(8,128)S(1)}, u32[]{:S(2)}, u32[]{:S(2)}) collective-permute-start(f32[256,128]{1,0:T(8,128)S(1)} %get-tuple-element.23), channel_id=1, source_target_pairs={{0,4},{2,6},{4,8},{6,10},{8,12},{10,14},{5,1},{7,3},{9,5},{11,7},{... | collective-permute-start | bytes 393224 | tf_op jit(solution)/shard_map/ppermute | solution.py:108
  23.5 1.3 %collective-permute-start.5 = (f32[256,128]{1,0:T(8,128)S(1)}, f32[256,128]{1,0:T(8,128)S(1)}, u32[]{:S(2)}, u32[]{:S(2)}) collective-permute-start(f32[256,128]{1,0:T(8,128)S(1)} %get-tuple-element.24), channel_id=1, source_target_pairs={{0,4},{2,6},{4,8},{6,10},{8,12},{10,14},{5,1},{7,3},{9,5},{11,7},{... | collective-permute-start | bytes 393224 | tf_op jit(solution)/shard_map/ppermute | solution.py:108
  24.8 1.3 %collective-permute-start.4 = (f32[256,128]{1,0:T(8,128)S(1)}, f32[256,128]{1,0:T(8,128)S(1)}, u32[]{:S(2)}, u32[]{:S(2)}) collective-permute-start(f32[256,128]{1,0:T(8,128)S(1)} %get-tuple-element.22), channel_id=1, source_target_pairs={{0,4},{2,6},{4,8},{6,10},{8,12},{10,14},{5,1},{7,3},{9,5},{11,7},{... | collective-permute-start | bytes 393224 | tf_op jit(solution)/shard_map/ppermute | solution.py:108
  26.1 4.4 %collective-permute-done.6 = f32[256,128]{1,0:T(8,128)S(1)} collective-permute-done((f32[256,128]{1,0:T(8,128)S(1)}, f32[256,128]{1,0:T(8,128)S(1)}, u32[]{:S(2)}, u32[]{:S(2)}) %collective-permute-start.6) | collective-permute-done | bytes 131104 | tf_op jit(solution)/shard_map/ppermute | solution.py:108
  30.4 1.9 %collective-permute-done.5 = f32[256,128]{1,0:T(8,128)S(1)} collective-permute-done((f32[256,128]{1,0:T(8,128)S(1)}, f32[256,128]{1,0:T(8,128)S(1)}, u32[]{:S(2)}, u32[]{:S(2)}) %collective-permute-start.5) | collective-permute-done | bytes 131104 | tf_op jit(solution)/shard_map/ppermute | solution.py:108
  32.4 1.9 %collective-permute-done.4 = f32[256,128]{1,0:T(8,128)S(1)} collective-permute-done((f32[256,128]{1,0:T(8,128)S(1)}, f32[256,128]{1,0:T(8,128)S(1)}, u32[]{:S(2)}, u32[]{:S(2)}) %collective-permute-start.4) | collective-permute-done | bytes 131104 | tf_op jit(solution)/shard_map/ppermute | solution.py:108
  34.3 0.6 convolution_add_fusion
  34.9 1.3 %collective-permute-start.10 = (f32[256,128]{1,0:T(8,128)S(1)}, f32[256,128]{1,0:T(8,128)S(1)}, u32[]{:S(2)}, u32[]{:S(2)}) collective-permute-start(f32[256,128]{1,0:T(8,128)S(1)} %get-tuple-element.20), channel_id=1, source_target_pairs={{0,2},{2,4},{4,6},{6,8},{8,10},{10,12},{12,14},{3,1},{5,3},{7,5},{... | collective-permute-start | bytes 393224 | tf_op jit(solution)/shard_map/ppermute | solution.py:108
  36.2 1.3 %collective-permute-start.9 = (f32[256,128]{1,0:T(8,128)S(1)}, f32[256,128]{1,0:T(8,128)S(1)}, u32[]{:S(2)}, u32[]{:S(2)}) collective-permute-start(f32[256,128]{1,0:T(8,128)S(1)} %get-tuple-element.20), channel_id=1, source_target_pairs={{0,10},{2,12},{4,14},{11,1},{13,3},{15,5},{16,26},{18,28},{20,30},... | collective-permute-start | bytes 393224 | tf_op jit(solution)/shard_map/ppermute | solution.py:108
  37.5 1.3 %collective-permute-start.8 = (f32[256,128]{1,0:T(8,128)S(1)}, f32[256,128]{1,0:T(8,128)S(1)}, u32[]{:S(2)}, u32[]{:S(2)}) collective-permute-start(f32[256,128]{1,0:T(8,128)S(1)} %get-tuple-element.21), channel_id=1, source_target_pairs={{0,2},{2,4},{4,6},{6,8},{8,10},{10,12},{12,14},{3,1},{5,3},{7,5},{... | collective-permute-start | bytes 393224 | tf_op jit(solution)/shard_map/ppermute | solution.py:108
  38.8 0.0 copy-start.1
  38.9 1.4 %collective-permute-start.7 = (f32[256,128]{1,0:T(8,128)S(1)}, f32[256,128]{1,0:T(8,128)S(1)}, u32[]{:S(2)}, u32[]{:S(2)}) collective-permute-start(f32[256,128]{1,0:T(8,128)S(1)} %get-tuple-element.19), channel_id=1, source_target_pairs={{0,2},{2,4},{4,6},{6,8},{8,10},{10,12},{12,14},{3,1},{5,3},{7,5},{... | collective-permute-start | bytes 393224 | tf_op jit(solution)/shard_map/ppermute | solution.py:108
  40.3 0.4 collective-permute-done.10
  40.7 4.1 %collective-permute-done.9 = f32[256,128]{1,0:T(8,128)S(1)} collective-permute-done((f32[256,128]{1,0:T(8,128)S(1)}, f32[256,128]{1,0:T(8,128)S(1)}, u32[]{:S(2)}, u32[]{:S(2)}) %collective-permute-start.9) | collective-permute-done | bytes 131104 | tf_op jit(solution)/shard_map/ppermute | solution.py:108
  44.7 0.5 collective-permute-done.8
  45.3 1.4 %collective-permute-done.7 = f32[256,128]{1,0:T(8,128)S(1)} collective-permute-done((f32[256,128]{1,0:T(8,128)S(1)}, f32[256,128]{1,0:T(8,128)S(1)}, u32[]{:S(2)}, u32[]{:S(2)}) %collective-permute-start.7) | collective-permute-done | bytes 131104 | tf_op jit(solution)/shard_map/ppermute | solution.py:108
  46.7 0.4 convolution_add_fusion.4
  47.1 0.4 convolution_add_fusion.3
  47.5 7.6 %collective-permute-start.11 = (f32[256,128]{1,0:T(8,128)S(1)}, f32[256,128]{1,0:T(8,128)S(1)}, u32[]{:S(2)}, u32[]{:S(2)}) collective-permute-start(f32[256,128]{1,0:T(8,128)S(1)} %convolution_add_fusion.3), channel_id=1, source_target_pairs={{0,1},{2,3},{4,5},{6,7},{8,9},{10,11},{12,13},{14,15},{1,0},{3,2},... | collective-permute-start | bytes 393224 | tf_op jit(solution)/shard_map/ppermute | solution.py:140
  55.1 0.0 copy-done
  55.1 0.0 copy-done.1
  55.1 1.4 %fusion.23.diag_ref = f32[8,256,128]{2,1,0:T(8,128)} fusion(bf16[8,256,256]{2,1,0:T(8,128)(2,1)S(1)} %copy-done, bf16[8,256,128]{2,1,0:T(8,128)(2,1)S(1)} %copy-done.1), kind=kOutput, calls=%fused_computation.36 | convolution fusion | flops 134217728 | bytes 2621440 | tf_op jit(solution)/shard_map/kab,kbc->kac/dot_general | solution.py:168
  56.5 0.0 collective-permute-done.11
  56.5 0.7 %broadcast_select_fusion.2 = (f32[256,128]{1,0:T(8,128)}, f32[256,128]{1,0:T(8,128)}) fusion(f32[256,128]{1,0:T(8,128)S(1)} %collective-permute-done.11, f32[256,128]{1,0:T(8,128)S(1)} %convolution_add_fusion.4, pred[]{:T(512)S(6)} %eq.5), kind=kLoop, calls=%fused_computation.24 | loop fusion | flops 65536 | bytes 524289 | tf_op jit(solution)/shard_map/jit(_where)/select_n | solution.py:141
  57.2 6.3 %apply.1 = bf16[8,256,128]{2,1,0:T(8,128)(2,1)} custom-call(f32[256,128]{1,0:T(8,128)} %get-tuple-element.29.lenter_ref, f32[256,128]{1,0:T(8,128)} %get-tuple-element.28.uenter_ref, bf16[8,256,256]{2,1,0:T(8,128)(2,1)} %ltrans_ref.3, bf16[8,256,256]{2,1,0:T(8,128)(2,1)} %utrans_ref.3, f32[8,256,128]{2,1,0:T(8,128)} %get-tuple-element.15.lsrc_ref, ...), custom_call_target="tpu_custom_call" | custom-call | tf_op jit(solution)/shard_map/apply/pallas_call | solution.py:177
  (6 shorter events, 0.1 us)
Async XLA Ops:
  0.0 55.1 %copy-start = (bf16[8,256,256]{2,1,0:T(8,128)(2,1)S(1)}, bf16[8,256,256]{2,1,0:T(8,128)(2,1)}, u32[]{:S(2)}) copy-start(bf16[8,256,256]{2,1,0:T(8,128)(2,1)} %param.9) | copy-start | bytes 3145732
  6.5 1.0 %copy-start.2 = (f32[256,256]{1,0:T(8,128)S(1)}, f32[256,256]{1,0:T(8,128)}, u32[]{:S(2)}) copy-start(f32[256,256]{1,0:T(8,128)} %get-tuple-element.13) | copy-start | bytes 786436
  7.5 0.9 %copy-start.3 = (f32[256,128]{1,0:T(8,128)S(1)}, f32[256,128]{1,0:T(8,128)}, u32[]{:S(2)}) copy-start(f32[256,128]{1,0:T(8,128)} %get-tuple-element.14) | copy-start | bytes 393220
  7.5 1.0 %copy-start.4 = (f32[256,128]{1,0:T(8,128)S(1)}, f32[256,128]{1,0:T(8,128)}, u32[]{:S(2)}) copy-start(f32[256,128]{1,0:T(8,128)} %get-tuple-element.12) | copy-start | bytes 393220
  8.6 1.8 %collective-permute-start = (f32[256,384]{1,0:T(8,128)S(1)}, f32[256,384]{1,0:T(8,128)S(1)}, u32[]{:S(2)}, u32[]{:S(2)}) collective-permute-start(f32[256,384]{1,0:T(8,128)S(1)} %get-tuple-element.17), channel_id=1, source_target_pairs={{0,1},{2,3},{4,5},{6,7},{8,9},{10,11},{12,13},{14,15},{1,0},{3,2},... | collective-permute-start | bytes 1179656 | tf_op jit(solution)/shard_map/ppermute | solution.py:124
  11.0 6.6 %collective-permute-start.3 = (f32[256,128]{1,0:T(8,128)S(1)}, f32[256,128]{1,0:T(8,128)S(1)}, u32[]{:S(2)}, u32[]{:S(2)}) collective-permute-start(f32[256,128]{1,0:T(8,128)S(1)} %get-tuple-element.26), channel_id=1, source_target_pairs={{0,2},{2,4},{4,6},{6,8},{8,10},{10,12},{12,14},{3,1},{5,3},{7,5},{... | collective-permute-start | bytes 393224 | tf_op jit(solution)/shard_map/ppermute | solution.py:108
  12.3 7.2 %collective-permute-start.2 = (f32[256,128]{1,0:T(8,128)S(1)}, f32[256,128]{1,0:T(8,128)S(1)}, u32[]{:S(2)}, u32[]{:S(2)}) collective-permute-start(f32[256,128]{1,0:T(8,128)S(1)} %get-tuple-element.27), channel_id=1, source_target_pairs={{0,2},{2,4},{4,6},{6,8},{8,10},{10,12},{12,14},{3,1},{5,3},{7,5},{... | collective-permute-start | bytes 393224 | tf_op jit(solution)/shard_map/ppermute | solution.py:108
  13.6 7.9 %collective-permute-start.1 = (f32[256,128]{1,0:T(8,128)S(1)}, f32[256,128]{1,0:T(8,128)S(1)}, u32[]{:S(2)}, u32[]{:S(2)}) collective-permute-start(f32[256,128]{1,0:T(8,128)S(1)} %get-tuple-element.25), channel_id=1, source_target_pairs={{0,2},{2,4},{4,6},{6,8},{8,10},{10,12},{12,14},{3,1},{5,3},{7,5},{... | collective-permute-start | bytes 393224 | tf_op jit(solution)/shard_map/ppermute | solution.py:108
  22.2 8.3 %collective-permute-start.6 = (f32[256,128]{1,0:T(8,128)S(1)}, f32[256,128]{1,0:T(8,128)S(1)}, u32[]{:S(2)}, u32[]{:S(2)}) collective-permute-start(f32[256,128]{1,0:T(8,128)S(1)} %get-tuple-element.23), channel_id=1, source_target_pairs={{0,4},{2,6},{4,8},{6,10},{8,12},{10,14},{5,1},{7,3},{9,5},{11,7},{... | collective-permute-start | bytes 393224 | tf_op jit(solution)/shard_map/ppermute | solution.py:108
  23.5 8.9 %collective-permute-start.5 = (f32[256,128]{1,0:T(8,128)S(1)}, f32[256,128]{1,0:T(8,128)S(1)}, u32[]{:S(2)}, u32[]{:S(2)}) collective-permute-start(f32[256,128]{1,0:T(8,128)S(1)} %get-tuple-element.24), channel_id=1, source_target_pairs={{0,4},{2,6},{4,8},{6,10},{8,12},{10,14},{5,1},{7,3},{9,5},{11,7},{... | collective-permute-start | bytes 393224 | tf_op jit(solution)/shard_map/ppermute | solution.py:108
  24.8 9.5 %collective-permute-start.4 = (f32[256,128]{1,0:T(8,128)S(1)}, f32[256,128]{1,0:T(8,128)S(1)}, u32[]{:S(2)}, u32[]{:S(2)}) collective-permute-start(f32[256,128]{1,0:T(8,128)S(1)} %get-tuple-element.22), channel_id=1, source_target_pairs={{0,4},{2,6},{4,8},{6,10},{8,12},{10,14},{5,1},{7,3},{9,5},{11,7},{... | collective-permute-start | bytes 393224 | tf_op jit(solution)/shard_map/ppermute | solution.py:108
  34.9 5.7 %collective-permute-start.10 = (f32[256,128]{1,0:T(8,128)S(1)}, f32[256,128]{1,0:T(8,128)S(1)}, u32[]{:S(2)}, u32[]{:S(2)}) collective-permute-start(f32[256,128]{1,0:T(8,128)S(1)} %get-tuple-element.20), channel_id=1, source_target_pairs={{0,2},{2,4},{4,6},{6,8},{8,10},{10,12},{12,14},{3,1},{5,3},{7,5},{... | collective-permute-start | bytes 393224 | tf_op jit(solution)/shard_map/ppermute | solution.py:108
  36.2 8.5 %collective-permute-start.9 = (f32[256,128]{1,0:T(8,128)S(1)}, f32[256,128]{1,0:T(8,128)S(1)}, u32[]{:S(2)}, u32[]{:S(2)}) collective-permute-start(f32[256,128]{1,0:T(8,128)S(1)} %get-tuple-element.20), channel_id=1, source_target_pairs={{0,10},{2,12},{4,14},{11,1},{13,3},{15,5},{16,26},{18,28},{20,30},... | collective-permute-start | bytes 393224 | tf_op jit(solution)/shard_map/ppermute | solution.py:108
  37.5 7.7 %collective-permute-start.8 = (f32[256,128]{1,0:T(8,128)S(1)}, f32[256,128]{1,0:T(8,128)S(1)}, u32[]{:S(2)}, u32[]{:S(2)}) collective-permute-start(f32[256,128]{1,0:T(8,128)S(1)} %get-tuple-element.21), channel_id=1, source_target_pairs={{0,2},{2,4},{4,6},{6,8},{8,10},{10,12},{12,14},{3,1},{5,3},{7,5},{... | collective-permute-start | bytes 393224 | tf_op jit(solution)/shard_map/ppermute | solution.py:108
  38.8 16.2 %copy-start.1 = (bf16[8,256,128]{2,1,0:T(8,128)(2,1)S(1)}, bf16[8,256,128]{2,1,0:T(8,128)(2,1)}, u32[]{:S(2)}) copy-start(bf16[8,256,128]{2,1,0:T(8,128)(2,1)} %rhs_ref.1) | copy-start | bytes 1572868
  38.9 7.8 %collective-permute-start.7 = (f32[256,128]{1,0:T(8,128)S(1)}, f32[256,128]{1,0:T(8,128)S(1)}, u32[]{:S(2)}, u32[]{:S(2)}) collective-permute-start(f32[256,128]{1,0:T(8,128)S(1)} %get-tuple-element.19), channel_id=1, source_target_pairs={{0,2},{2,4},{4,6},{6,8},{8,10},{10,12},{12,14},{3,1},{5,3},{7,5},{... | collective-permute-start | bytes 393224 | tf_op jit(solution)/shard_map/ppermute | solution.py:108
  47.5 9.0 %collective-permute-start.11 = (f32[256,128]{1,0:T(8,128)S(1)}, f32[256,128]{1,0:T(8,128)S(1)}, u32[]{:S(2)}, u32[]{:S(2)}) collective-permute-start(f32[256,128]{1,0:T(8,128)S(1)} %convolution_add_fusion.3), channel_id=1, source_target_pairs={{0,1},{2,3},{4,5},{6,7},{8,9},{10,11},{12,13},{14,15},{1,0},{3,2},... | collective-permute-start | bytes 393224 | tf_op jit(solution)/shard_map/ppermute | solution.py:140

commit v5 on v3

--- a/solution.py
+++ b/solution.py
@@ -118,18 +118,25 @@
     got = lax.ppermute(jnp.where(first, upper, lower), axis, partner)
     tail = jnp.concatenate([jnp.zeros_like(lmap), got[:, rank:]], axis=1)
     both = jnp.dot(got[:, :rank], own, precision=HIGHEST) + tail
-    rounds = 0
-    while 2 ** (rounds + 1) < chips - 1:
-        rounds += 1
-    shift = 1
-    for _ in range(rounds):
-        got = chip_shift(both, axis, chips, shift)
-        tail = jnp.concatenate([jnp.zeros_like(lmap), both[:, rank:]], axis=1)
-        both = jnp.dot(both[:, :rank], got, precision=HIGHEST) + tail
-        shift *= 2
-    near = chip_shift(both, axis, chips, 1)
-    far = chip_shift(both[:, rank:], axis, chips, 1 + shift)
-    enter = jnp.dot(near[:, :rank], far, precision=HIGHEST) + near[:, rank:]
+    if chips <= 8:
+        out = both[:, rank:]
+        for step in range(chips - 1):
+            enter = chip_shift(out, axis, chips, 1)
+            if step + 2 < chips:
+                out = jnp.dot(both[:, :rank], enter, precision=HIGHEST) + both[:, rank:]
+    else:
+        rounds = 0
+        while 2 ** (rounds + 1) < chips - 1:
+            rounds += 1
+        shift = 1
+        for _ in range(rounds):
+            got = chip_shift(both, axis, chips, shift)
+            tail = jnp.concatenate([jnp.zeros_like(lmap), both[:, rank:]], axis=1)
+            both = jnp.dot(both[:, :rank], got, precision=HIGHEST) + tail
+            shift *= 2
+        near = chip_shift(both, axis, chips, 1)
+        far = chip_shift(both[:, rank:], axis, chips, 1 + shift)
+        enter = jnp.dot(near[:, :rank], far, precision=HIGHEST) + near[:, rank:]
     send = jnp.dot(own[:, :rank], enter, precision=HIGHEST) + own[:, rank:]
     other = lax.ppermute(send, axis, partner)
     return jnp.where(first, enter, other), jnp.where(first, other, enter)

time: 58.1 us -> 77.8 us (1.34)
  the two profiles are of different devices: /device:TPU:1 before, /device:TPU:25 now
where the time goes in v5:
time: 77.8 us; the launch traced here: 77.5 us
  starting transfers between devices  40.6 us (52%)
  waiting for transfers between devices  16.6 us (21%)
  Pallas kernels  12.8 us (16%)
  matrix products  4.62 us (6%)
  local copies, waits for them, and re-layouts  2.01 us (3%)
  other arithmetic  0.78 us (1%)
    ppermute x7, starting transfers between devices, chip_shift(): return lax.ppermute(value, axis, pairs)  29.6 us
    ppermute x7, waiting for transfers between devices, chip_shift(): return lax.ppermute(value, axis, pairs)  15.2 us
    ppermute x1, starting transfers between devices, scan_chips(): other = lax.ppermute(send, axis, partner)  10.2 us
    pallas_call x1, Pallas kernels, shards(): pl.pallas_call(sweep_kernel, out_shape=(jax.ShapeDtypeStruct((rank, rank)...  6.5 us
    pallas_call x1, Pallas kernels, shards(): pl.pallas_call(apply_kernel, out_shape=jax.ShapeDtypeStruct((count, rows,...  6.27 us
    dot_general x6, matrix products, scan_chips(): out = jnp.dot(both[:, :rank], enter, precision=HIGHEST) + both[:, rank:]  2.26 us
    unnamed x12, local copies, waits for them, and re-layouts  1.97 us
  transfers between devices with their start and end apart: 9, of which 8 were waited for; matrix products, arithmetic and copies ran while one was open for 2% of the time, Pallas kernels for 0%

profile of v5, /device:TPU:25, one launch (start us, length us, event | category | flops | bytes accessed | tf_op | source)
XLA Modules:
  0.0 77.5 jit_solution(7336398112006589770)
XLA Ops:
  0.0 0.0 copy-start
  0.0 6.5 %sweep.1 = (f32[256,256]{1,0:T(8,128)}, f32[256,128]{1,0:T(8,128)}, f32[8,256,128]{2,1,0:T(8,128)}, f32[256,256]{1,0:T(8,128)}, f32[256,128]{1,0:T(8,128)}, /*index=5*/f32[8,256,128]{2,1,0:T(8,128)}) custom-call(bf16[8,256,128]{2,1,0:T(8,128)(2,1)} %rhs_ref.1, bf16[8,256,256]{2,1,0:T(8,128)(2,1)} %lcols_ref.1, bf16[8,256,256]{2,1,0:T(8,128)(2,1)} %ltrans_ref.3, ...), custom_call_target="tpu_custom_call" | custom-call | tf_op jit(solution)/shard_map/sweep/pallas_call | solution.py:157
  6.5 0.0 copy-start.2
  6.5 1.0 %constant_dynamic-update-slice_fusion.1 = f32[256,384]{1,0:T(8,128)S(1)} fusion(f32[256,256]{1,0:T(8,128)} %get-tuple-element.11), kind=kLoop, calls=%fused_computation.21 | loop fusion | bytes 524288
  7.5 0.0 copy-done.2
  7.5 0.0 copy-start.3
  7.5 0.0 copy-start.4
  7.6 0.8 %copy-done.3 = f32[256,128]{1,0:T(8,128)S(1)} copy-done((f32[256,128]{1,0:T(8,128)S(1)}, f32[256,128]{1,0:T(8,128)}, u32[]{:S(2)}) %copy-start.3) | copy-done | bytes 131096
  8.4 0.1 copy-done.4
  8.5 0.1 broadcast_select_fusion.1
  8.6 0.7 collective-permute-start
  9.3 1.3 %collective-permute-done = f32[256,384]{1,0:T(8,128)S(1)} collective-permute-done((f32[256,384]{1,0:T(8,128)S(1)}, f32[256,384]{1,0:T(8,128)S(1)}, u32[]{:S(2)}, u32[]{:S(2)}) %collective-permute-start) | collective-permute-done | bytes 393248 | tf_op jit(solution)/shard_map/ppermute | solution.py:118
  10.7 0.6 convolution_add_fusion
  11.3 3.0 %collective-permute-start.1 = (f32[256,128]{1,0:T(8,128)S(1)}, f32[256,128]{1,0:T(8,128)S(1)}, u32[]{:S(2)}, u32[]{:S(2)}) collective-permute-start(f32[256,128]{1,0:T(8,128)S(1)} %slice.38), channel_id=1, source_target_pairs={{0,2},{2,4},{4,6},{6,8},{8,10},{10,12},{12,14},{3,1},{5,3},{7,5},{... | collective-permute-start | bytes 393224 | tf_op jit(solution)/shard_map/ppermute | solution.py:105
  14.4 2.7 %collective-permute-done.1 = f32[256,128]{1,0:T(8,128)S(1)} collective-permute-done((f32[256,128]{1,0:T(8,128)S(1)}, f32[256,128]{1,0:T(8,128)S(1)}, u32[]{:S(2)}, u32[]{:S(2)}) %collective-permute-start.1) | collective-permute-done | bytes 131104 | tf_op jit(solution)/shard_map/ppermute | solution.py:105
  17.0 0.4 convolution_add_fusion.7
  17.4 4.0 %collective-permute-start.2 = (f32[256,128]{1,0:T(8,128)S(1)}, f32[256,128]{1,0:T(8,128)S(1)}, u32[]{:S(2)}, u32[]{:S(2)}) collective-permute-start(f32[256,128]{1,0:T(8,128)S(1)} %convolution_add_fusion.7), channel_id=1, source_target_pairs={{0,2},{2,4},{4,6},{6,8},{8,10},{10,12},{12,14},{3,1},{5,3},{7,5},{... | collective-permute-start | bytes 393224 | tf_op jit(solution)/shard_map/ppermute | solution.py:105
  21.5 1.9 %collective-permute-done.2 = f32[256,128]{1,0:T(8,128)S(1)} collective-permute-done((f32[256,128]{1,0:T(8,128)S(1)}, f32[256,128]{1,0:T(8,128)S(1)}, u32[]{:S(2)}, u32[]{:S(2)}) %collective-permute-start.2) | collective-permute-done | bytes 131104 | tf_op jit(solution)/shard_map/ppermute | solution.py:105
  23.4 0.4 convolution_add_fusion.6
  23.8 4.7 %collective-permute-start.3 = (f32[256,128]{1,0:T(8,128)S(1)}, f32[256,128]{1,0:T(8,128)S(1)}, u32[]{:S(2)}, u32[]{:S(2)}) collective-permute-start(f32[256,128]{1,0:T(8,128)S(1)} %convolution_add_fusion.6), channel_id=1, source_target_pairs={{0,2},{2,4},{4,6},{6,8},{8,10},{10,12},{12,14},{3,1},{5,3},{7,5},{... | collective-permute-start | bytes 393224 | tf_op jit(solution)/shard_map/ppermute | solution.py:105
  28.4 1.9 %collective-permute-done.3 = f32[256,128]{1,0:T(8,128)S(1)} collective-permute-done((f32[256,128]{1,0:T(8,128)S(1)}, f32[256,128]{1,0:T(8,128)S(1)}, u32[]{:S(2)}, u32[]{:S(2)}) %collective-permute-start.3) | collective-permute-done | bytes 131104 | tf_op jit(solution)/shard_map/ppermute | solution.py:105
  30.4 0.4 convolution_add_fusion.5
  30.8 4.7 %collective-permute-start.4 = (f32[256,128]{1,0:T(8,128)S(1)}, f32[256,128]{1,0:T(8,128)S(1)}, u32[]{:S(2)}, u32[]{:S(2)}) collective-permute-start(f32[256,128]{1,0:T(8,128)S(1)} %convolution_add_fusion.5), channel_id=1, source_target_pairs={{0,2},{2,4},{4,6},{6,8},{8,10},{10,12},{12,14},{3,1},{5,3},{7,5},{... | collective-permute-start | bytes 393224 | tf_op jit(solution)/shard_map/ppermute | solution.py:105
  35.4 1.9 %collective-permute-done.4 = f32[256,128]{1,0:T(8,128)S(1)} collective-permute-done((f32[256,128]{1,0:T(8,128)S(1)}, f32[256,128]{1,0:T(8,128)S(1)}, u32[]{:S(2)}, u32[]{:S(2)}) %collective-permute-start.4) | collective-permute-done | bytes 131104 | tf_op jit(solution)/shard_map/ppermute | solution.py:105
  37.4 0.4 convolution_add_fusion.4
  37.7 4.7 %collective-permute-start.5 = (f32[256,128]{1,0:T(8,128)S(1)}, f32[256,128]{1,0:T(8,128)S(1)}, u32[]{:S(2)}, u32[]{:S(2)}) collective-permute-start(f32[256,128]{1,0:T(8,128)S(1)} %convolution_add_fusion.4), channel_id=1, source_target_pairs={{0,2},{2,4},{4,6},{6,8},{8,10},{10,12},{12,14},{3,1},{5,3},{7,5},{... | collective-permute-start | bytes 393224 | tf_op jit(solution)/shard_map/ppermute | solution.py:105
  42.4 2.2 %collective-permute-done.5 = f32[256,128]{1,0:T(8,128)S(1)} collective-permute-done((f32[256,128]{1,0:T(8,128)S(1)}, f32[256,128]{1,0:T(8,128)S(1)}, u32[]{:S(2)}, u32[]{:S(2)}) %collective-permute-start.5) | collective-permute-done | bytes 131104 | tf_op jit(solution)/shard_map/ppermute | solution.py:105
  44.6 0.4 convolution_add_fusion.3
  45.0 0.0 copy-start.1
  45.0 4.6 %collective-permute-start.6 = (f32[256,128]{1,0:T(8,128)S(1)}, f32[256,128]{1,0:T(8,128)S(1)}, u32[]{:S(2)}, u32[]{:S(2)}) collective-permute-start(f32[256,128]{1,0:T(8,128)S(1)} %convolution_add_fusion.3), channel_id=1, source_target_pairs={{0,2},{2,4},{4,6},{6,8},{8,10},{10,12},{12,14},{3,1},{5,3},{7,5},{... | collective-permute-start | bytes 393224 | tf_op jit(solution)/shard_map/ppermute | solution.py:105
  49.6 2.7 %collective-permute-done.6 = f32[256,128]{1,0:T(8,128)S(1)} collective-permute-done((f32[256,128]{1,0:T(8,128)S(1)}, f32[256,128]{1,0:T(8,128)S(1)}, u32[]{:S(2)}, u32[]{:S(2)}) %collective-permute-start.6) | collective-permute-done | bytes 131104 | tf_op jit(solution)/shard_map/ppermute | solution.py:105
  52.2 0.4 convolution_add_fusion.2
  52.6 3.9 %collective-permute-start.7 = (f32[256,128]{1,0:T(8,128)S(1)}, f32[256,128]{1,0:T(8,128)S(1)}, u32[]{:S(2)}, u32[]{:S(2)}) collective-permute-start(f32[256,128]{1,0:T(8,128)S(1)} %convolution_add_fusion.2), channel_id=1, source_target_pairs={{0,2},{2,4},{4,6},{6,8},{8,10},{10,12},{12,14},{3,1},{5,3},{7,5},{... | collective-permute-start | bytes 393224 | tf_op jit(solution)/shard_map/ppermute | solution.py:105
  56.6 1.9 %collective-permute-done.7 = f32[256,128]{1,0:T(8,128)S(1)} collective-permute-done((f32[256,128]{1,0:T(8,128)S(1)}, f32[256,128]{1,0:T(8,128)S(1)}, u32[]{:S(2)}, u32[]{:S(2)}) %collective-permute-start.7) | collective-permute-done | bytes 131104 | tf_op jit(solution)/shard_map/ppermute | solution.py:105
  58.5 0.4 convolution_add_fusion.1
  58.9 10.2 %collective-permute-start.8 = (f32[256,128]{1,0:T(8,128)S(1)}, f32[256,128]{1,0:T(8,128)S(1)}, u32[]{:S(2)}, u32[]{:S(2)}) collective-permute-start(f32[256,128]{1,0:T(8,128)S(1)} %convolution_add_fusion.1), channel_id=1, source_target_pairs={{0,1},{2,3},{4,5},{6,7},{8,9},{10,11},{12,13},{14,15},{1,0},{3,2},... | collective-permute-start | bytes 393224 | tf_op jit(solution)/shard_map/ppermute | solution.py:141
  69.1 0.0 copy-done
  69.1 0.0 copy-done.1
  69.1 1.4 %fusion.8.diag_ref = f32[8,256,128]{2,1,0:T(8,128)} fusion(bf16[8,256,256]{2,1,0:T(8,128)(2,1)S(1)} %copy-done, bf16[8,256,128]{2,1,0:T(8,128)(2,1)S(1)} %copy-done.1), kind=kOutput, calls=%fused_computation.24 | convolution fusion | flops 134217728 | bytes 2621440 | tf_op jit(solution)/shard_map/kab,kbc->kac/dot_general | solution.py:169
  70.5 0.0 collective-permute-done.8
  70.5 0.7 broadcast_select_fusion.2
  71.2 6.3 %apply.1 = bf16[8,256,128]{2,1,0:T(8,128)(2,1)} custom-call(f32[256,128]{1,0:T(8,128)} %get-tuple-element.20.lenter_ref, f32[256,128]{1,0:T(8,128)} %get-tuple-element.19.uenter_ref, bf16[8,256,256]{2,1,0:T(8,128)(2,1)} %ltrans_ref.3, bf16[8,256,256]{2,1,0:T(8,128)(2,1)} %utrans_ref.3, f32[8,256,128]{2,1,0:T(8,128)} %get-tuple-element.15.lsrc_ref, ...), custom_call_target="tpu_custom_call" | custom-call | tf_op jit(solution)/shard_map/apply/pallas_call | solution.py:178
  (4 shorter events, 0.1 us)
Async XLA Ops:
  0.0 69.1 %copy-start = (bf16[8,256,256]{2,1,0:T(8,128)(2,1)S(1)}, bf16[8,256,256]{2,1,0:T(8,128)(2,1)}, u32[]{:S(2)}) copy-start(bf16[8,256,256]{2,1,0:T(8,128)(2,1)} %param.9) | copy-start | bytes 3145732
  6.5 1.0 %copy-start.2 = (f32[256,256]{1,0:T(8,128)S(1)}, f32[256,256]{1,0:T(8,128)}, u32[]{:S(2)}) copy-start(f32[256,256]{1,0:T(8,128)} %get-tuple-element.13) | copy-start | bytes 786436
  7.5 0.9 %copy-start.3 = (f32[256,128]{1,0:T(8,128)S(1)}, f32[256,128]{1,0:T(8,128)}, u32[]{:S(2)}) copy-start(f32[256,128]{1,0:T(8,128)} %get-tuple-element.14) | copy-start | bytes 393220
  7.5 1.0 %copy-start.4 = (f32[256,128]{1,0:T(8,128)S(1)}, f32[256,128]{1,0:T(8,128)}, u32[]{:S(2)}) copy-start(f32[256,128]{1,0:T(8,128)} %get-tuple-element.12) | copy-start | bytes 393220
  8.6 2.1 %collective-permute-start = (f32[256,384]{1,0:T(8,128)S(1)}, f32[256,384]{1,0:T(8,128)S(1)}, u32[]{:S(2)}, u32[]{:S(2)}) collective-permute-start(f32[256,384]{1,0:T(8,128)S(1)} %get-tuple-element.17), channel_id=1, source_target_pairs={{0,1},{2,3},{4,5},{6,7},{8,9},{10,11},{12,13},{14,15},{1,0},{3,2},... | collective-permute-start | bytes 1179656 | tf_op jit(solution)/shard_map/ppermute | solution.py:118
  11.3 5.7 %collective-permute-start.1 = (f32[256,128]{1,0:T(8,128)S(1)}, f32[256,128]{1,0:T(8,128)S(1)}, u32[]{:S(2)}, u32[]{:S(2)}) collective-permute-start(f32[256,128]{1,0:T(8,128)S(1)} %slice.38), channel_id=1, source_target_pairs={{0,2},{2,4},{4,6},{6,8},{8,10},{10,12},{12,14},{3,1},{5,3},{7,5},{... | collective-permute-start | bytes 393224 | tf_op jit(solution)/shard_map/ppermute | solution.py:105
  17.4 6.0 %collective-permute-start.2 = (f32[256,128]{1,0:T(8,128)S(1)}, f32[256,128]{1,0:T(8,128)S(1)}, u32[]{:S(2)}, u32[]{:S(2)}) collective-permute-start(f32[256,128]{1,0:T(8,128)S(1)} %convolution_add_fusion.7), channel_id=1, source_target_pairs={{0,2},{2,4},{4,6},{6,8},{8,10},{10,12},{12,14},{3,1},{5,3},{7,5},{... | collective-permute-start | bytes 393224 | tf_op jit(solution)/shard_map/ppermute | solution.py:105
  23.8 6.6 %collective-permute-start.3 = (f32[256,128]{1,0:T(8,128)S(1)}, f32[256,128]{1,0:T(8,128)S(1)}, u32[]{:S(2)}, u32[]{:S(2)}) collective-permute-start(f32[256,128]{1,0:T(8,128)S(1)} %convolution_add_fusion.6), channel_id=1, source_target_pairs={{0,2},{2,4},{4,6},{6,8},{8,10},{10,12},{12,14},{3,1},{5,3},{7,5},{... | collective-permute-start | bytes 393224 | tf_op jit(solution)/shard_map/ppermute | solution.py:105
  30.8 6.6 %collective-permute-start.4 = (f32[256,128]{1,0:T(8,128)S(1)}, f32[256,128]{1,0:T(8,128)S(1)}, u32[]{:S(2)}, u32[]{:S(2)}) collective-permute-start(f32[256,128]{1,0:T(8,128)S(1)} %convolution_add_fusion.5), channel_id=1, source_target_pairs={{0,2},{2,4},{4,6},{6,8},{8,10},{10,12},{12,14},{3,1},{5,3},{7,5},{... | collective-permute-start | bytes 393224 | tf_op jit(solution)/shard_map/ppermute | solution.py:105
  37.7 6.9 %collective-permute-start.5 = (f32[256,128]{1,0:T(8,128)S(1)}, f32[256,128]{1,0:T(8,128)S(1)}, u32[]{:S(2)}, u32[]{:S(2)}) collective-permute-start(f32[256,128]{1,0:T(8,128)S(1)} %convolution_add_fusion.4), channel_id=1, source_target_pairs={{0,2},{2,4},{4,6},{6,8},{8,10},{10,12},{12,14},{3,1},{5,3},{7,5},{... | collective-permute-start | bytes 393224 | tf_op jit(solution)/shard_map/ppermute | solution.py:105
  45.0 24.1 %copy-start.1 = (bf16[8,256,128]{2,1,0:T(8,128)(2,1)S(1)}, bf16[8,256,128]{2,1,0:T(8,128)(2,1)}, u32[]{:S(2)}) copy-start(bf16[8,256,128]{2,1,0:T(8,128)(2,1)} %rhs_ref.1) | copy-start | bytes 1572868
  45.0 7.2 %collective-permute-start.6 = (f32[256,128]{1,0:T(8,128)S(1)}, f32[256,128]{1,0:T(8,128)S(1)}, u32[]{:S(2)}, u32[]{:S(2)}) collective-permute-start(f32[256,128]{1,0:T(8,128)S(1)} %convolution_add_fusion.3), channel_id=1, source_target_pairs={{0,2},{2,4},{4,6},{6,8},{8,10},{10,12},{12,14},{3,1},{5,3},{7,5},{... | collective-permute-start | bytes 393224 | tf_op jit(solution)/shard_map/ppermute | solution.py:105
  52.6 5.9 %collective-permute-start.7 = (f32[256,128]{1,0:T(8,128)S(1)}, f32[256,128]{1,0:T(8,128)S(1)}, u32[]{:S(2)}, u32[]{:S(2)}) collective-permute-start(f32[256,128]{1,0:T(8,128)S(1)} %convolution_add_fusion.2), channel_id=1, source_target_pairs={{0,2},{2,4},{4,6},{6,8},{8,10},{10,12},{12,14},{3,1},{5,3},{7,5},{... | collective-permute-start | bytes 393224 | tf_op jit(solution)/shard_map/ppermute | solution.py:105
  58.9 11.6 %collective-permute-start.8 = (f32[256,128]{1,0:T(8,128)S(1)}, f32[256,128]{1,0:T(8,128)S(1)}, u32[]{:S(2)}, u32[]{:S(2)}) collective-permute-start(f32[256,128]{1,0:T(8,128)S(1)} %convolution_add_fusion.1), channel_id=1, source_target_pairs={{0,1},{2,3},{4,5},{6,7},{8,9},{10,11},{12,13},{14,15},{1,0},{3,2},... | collective-permute-start | bytes 393224 | tf_op jit(solution)/shard_map/ppermute | solution.py:141

commit v6 on v3

--- a/solution.py
+++ b/solution.py
@@ -20,7 +20,7 @@
 
 def sweep_kernel(
     rhs_ref, lcols_ref, ltrans_ref, ucols_ref, utrans_ref,
-    lmap_ref, lstate_ref, lsrc_ref, umap_ref, ustate_ref, usrc_ref,
+    lmap_ref, lsrc_ref, umap_ref, usrc_ref,
 ):
     count = rhs_ref.shape[0]
     lmap = lstate = umap = ustate = None
@@ -43,19 +43,21 @@
             ustate = split_dot(utrans, ustate) + usrc
             lmap = split_dot(ltrans, lmap)
             umap = split_dot(utrans, umap)
-    lmap_ref[...] = lmap
-    lstate_ref[...] = lstate
-    umap_ref[...] = umap
-    ustate_ref[...] = ustate
+    rank = lmap.shape[0]
+    lmap_ref[:, :rank] = lmap
+    lmap_ref[:, rank:] = lstate
+    umap_ref[:, :rank] = umap
+    umap_ref[:, rank:] = ustate
 
 
 def apply_kernel(
-    lenter_ref, uenter_ref, ltrans_ref, utrans_ref, lsrc_ref, usrc_ref,
+    flag_ref, enter_ref, other_ref, ltrans_ref, utrans_ref, lsrc_ref, usrc_ref,
     diag_ref, lrows_ref, urows_ref, out_ref, lround_ref, uround_ref,
 ):
     count = ltrans_ref.shape[0]
-    lstate = lenter_ref[...]
-    ustate = uenter_ref[...]
+    first = flag_ref[0] == 0
+    lstate = jnp.where(first, enter_ref[...], other_ref[...])
+    ustate = jnp.where(first, other_ref[...], enter_ref[...])
     for step in range(count):
         lk = step
         uk = count - 1 - step
@@ -105,18 +107,16 @@
     return lax.ppermute(value, axis, pairs)
 
 
-def scan_chips(lmap, lstate, umap, ustate, axis):
+def scan_chips(lower, upper, axis):
     count = lax.axis_size(axis)
     chips = count // 2
-    rank = lmap.shape[0]
+    rank = lower.shape[0]
     first = lax.axis_index(axis) % 2 == 0
-    lower = jnp.concatenate([lmap, lstate], axis=1)
-    upper = jnp.concatenate([umap, ustate], axis=1)
     own = jnp.where(first, lower, upper)
     partner = [(2 * c, 2 * c + 1) for c in range(chips)]
     partner += [(2 * c + 1, 2 * c) for c in range(chips)]
     got = lax.ppermute(jnp.where(first, upper, lower), axis, partner)
-    tail = jnp.concatenate([jnp.zeros_like(lmap), got[:, rank:]], axis=1)
+    tail = jnp.concatenate([jnp.zeros((rank, rank), F32), got[:, rank:]], axis=1)
     both = jnp.dot(got[:, :rank], own, precision=HIGHEST) + tail
     rounds = 0
     while 2 ** (rounds + 1) < chips - 1:
@@ -124,7 +124,7 @@
     shift = 1
     for _ in range(rounds):
         got = chip_shift(both, axis, chips, shift)
-        tail = jnp.concatenate([jnp.zeros_like(lmap), both[:, rank:]], axis=1)
+        tail = jnp.concatenate([jnp.zeros((rank, rank), F32), both[:, rank:]], axis=1)
         both = jnp.dot(both[:, :rank], got, precision=HIGHEST) + tail
         shift *= 2
     near = chip_shift(both, axis, chips, 1)
@@ -132,7 +132,7 @@
     enter = jnp.dot(near[:, :rank], far, precision=HIGHEST) + near[:, rank:]
     send = jnp.dot(own[:, :rank], enter, precision=HIGHEST) + own[:, rank:]
     other = lax.ppermute(send, axis, partner)
-    return jnp.where(first, enter, other), jnp.where(first, other, enter)
+    return enter, other
 
 
 def shards(
@@ -147,14 +147,12 @@
 ):
     count, rows, rhs = right_sides.shape
     rank = lower_trans.shape[1]
-    lmap, lstate, lsrc, umap, ustate, usrc = pl.pallas_call(
+    lboth, lsrc, uboth, usrc = pl.pallas_call(
         sweep_kernel,
         out_shape=(
-            jax.ShapeDtypeStruct((rank, rank), F32),
-            jax.ShapeDtypeStruct((rank, rhs), F32),
+            jax.ShapeDtypeStruct((rank, rank + rhs), F32),
             jax.ShapeDtypeStruct((count, rank, rhs), F32),
-            jax.ShapeDtypeStruct((rank, rank), F32),
-            jax.ShapeDtypeStruct((rank, rhs), F32),
+            jax.ShapeDtypeStruct((rank, rank + rhs), F32),
             jax.ShapeDtypeStruct((count, rank, rhs), F32),
         ),
         name="sweep",
@@ -164,10 +162,13 @@
     )
     count_row = lax.axis_size("row")
     if count_row % 2 == 0 and count_row >= 4:
-        lenter, uenter = scan_chips(lmap, lstate, umap, ustate, "row")
+        enter, other = scan_chips(lboth, uboth, "row")
+        flag = jnp.full((1,), lax.axis_index("row") % 2, jnp.int32)
     else:
-        lenter = scan_enter(lmap, lstate, "row", False)
-        uenter = scan_enter(umap, ustate, "row", True)
+        enter = scan_enter(lboth[:, :rank], lboth[:, rank:], "row", False)
+        other = scan_enter(uboth[:, :rank], uboth[:, rank:], "row", True)
+        flag = jnp.zeros((1,), jnp.int32)
+    vmem = pl.BlockSpec(memory_space=pltpu.VMEM)
     return pl.pallas_call(
         apply_kernel,
         out_shape=jax.ShapeDtypeStruct((count, rows, rhs), BF16),
@@ -175,8 +176,9 @@
             pltpu.VMEM((count, rank, rhs), BF16),
             pltpu.VMEM((count, rank, rhs), BF16),
         ],
+        in_specs=[pl.BlockSpec(memory_space=pltpu.SMEM)] + [vmem] * 9,
         name="apply",
-    )(lenter, uenter, lower_trans, upper_trans, lsrc, usrc, diag, lower_rows, upper_rows)
+    )(flag, enter, other, lower_trans, upper_trans, lsrc, usrc, diag, lower_rows, upper_rows)
 
 
 def solution(mesh):

time: 58.1 us -> 57.3 us (0.986)
  local copies, waits for them, and re-layouts: 2.03 us -> 0.95 us
    select_n x1, other arithmetic: 0.06 us -> 1.17 us  [scan_chips(): got = lax.ppermute(jnp.where(first, upper, lower), axis, partner)]
    unnamed x12 -> x8, local copies, waits for them, and re-layouts: 1.97 us -> 0.91 us
    select_n x1 -> x0, other arithmetic: 0.72 us -> none  [scan_chips(): return (jnp.where(first, enter, other), jnp.where(first, other, enter))]
  transfers between devices with their start and end apart: 6 -> 6, of which waited for: 5 -> 5; matrix products, arithmetic and copies ran while one was open for 2% -> 3% of each run, Pallas kernels for 0% -> 0%
where the time goes in v6:
time: 57.3 us; the launch traced here: 56.9 us
  waiting for transfers between devices  28.5 us (50%)
  Pallas kernels  12.7 us (22%)
  starting transfers between devices  9.56 us (17%)
  matrix products  3.96 us (7%)
  other arithmetic  1.17 us (2%)
  local copies, waits for them, and re-layouts  0.95 us (2%)
    ppermute x4, waiting for transfers between devices, chip_shift(): return lax.ppermute(value, axis, pairs)  26.7 us
    pallas_call x1, Pallas kernels, shards(): pl.pallas_call(sweep_kernel, out_shape=(jax.ShapeDtypeStruct((rank, rank...  6.43 us
    pallas_call x1, Pallas kernels, shards(): pl.pallas_call(apply_kernel, out_shape=jax.ShapeDtypeStruct((count, rows,...  6.27 us
    ppermute x4, starting transfers between devices, chip_shift(): return lax.ppermute(value, axis, pairs)  5.3 us
    ppermute x1, starting transfers between devices, scan_chips(): other = lax.ppermute(send, axis, partner)  4.18 us
    ppermute x1, waiting for transfers between devices, scan_chips(): got = lax.ppermute(jnp.where(first, upper, lower), axis, partner)  1.71 us
    dot_general x1, matrix products, shards(): jnp.einsum('kab,kbc->kac', diagonal_blocks, right_sides, preferred_elemen...  1.41 us
    dot_general x2, matrix products, scan_chips(): both = jnp.dot(both[:, :rank], got, precision=HIGHEST) + tail  1.2 us
  transfers between devices with their start and end apart: 6, of which 5 were waited for; matrix products, arithmetic and copies ran while one was open for 3% of the time, Pallas kernels for 0%

profile of v6, /device:TPU:1, one launch (start us, length us, event | category | flops | bytes accessed | tf_op | source)
XLA Modules:
  0.0 56.9 jit_solution(6628615620453832639)
XLA Ops:
  0.0 0.0 copy-start
  0.0 6.4 %sweep.1 = (f32[256,384]{1,0:T(8,128)}, f32[8,256,128]{2,1,0:T(8,128)}, f32[256,384]{1,0:T(8,128)}, f32[8,256,128]{2,1,0:T(8,128)}) custom-call(bf16[8,256,128]{2,1,0:T(8,128)(2,1)} %rhs_ref.1, bf16[8,256,256]{2,1,0:T(8,128)(2,1)} %lcols_ref.1, bf16[8,256,256]{2,1,0:T(8,128)(2,1)} %ltrans_ref.3, bf16[8,256,256]{2,1,0:T(8,128)(2,1)} %ucols_ref.1, ...), custom_call_target="tpu_custom_call" | custom-call | tf_op jit(solution)/shard_map/sweep/pallas_call | solution.py:150
  6.4 1.2 %broadcast_select_fusion.1 = (f32[256,384]{1,0:T(8,128)S(1)}, f32[256,384]{1,0:T(8,128)S(1)}) fusion(f32[256,384]{1,0:T(8,128)} %get-tuple-element.9, f32[256,384]{1,0:T(8,128)} %get-tuple-element.10, pred[]{:T(512)S(6)} %eq.6), kind=kLoop, calls=%fused_computation.11 | loop fusion | flops 196608 | bytes 1572865 | tf_op jit(solution)/shard_map/jit(_where)/select_n | solution.py:118
  7.6 0.1 collective-permute-start
  7.7 1.7 %collective-permute-done = f32[256,384]{1,0:T(8,128)S(1)} collective-permute-done((f32[256,384]{1,0:T(8,128)S(1)}, f32[256,384]{1,0:T(8,128)S(1)}, u32[]{:S(2)}, u32[]{:S(2)}) %collective-permute-start) | collective-permute-done | bytes 393248 | tf_op jit(solution)/shard_map/ppermute | solution.py:118
  9.4 0.6 %convolution_add_fusion.2 = f32[256,384]{1,0:T(8,128)S(1)} fusion(f32[256,384]{1,0:T(8,128)S(1)} %get-tuple-element.14, f32[256,128]{1,0:T(8,128)S(1)} %slice.45, f32[256,384]{1,0:T(8,128)S(1)} %collective-permute-done), kind=kOutput, calls=%fused_computation.2 | convolution fusion | flops 302088192 | bytes 1179648 | tf_op jit(solution)/shard_map/dot_general | solution.py:120
  10.0 1.3 %collective-permute-start.1 = (f32[256,384]{1,0:T(8,128)S(1)}, f32[256,384]{1,0:T(8,128)S(1)}, u32[]{:S(2)}, u32[]{:S(2)}) collective-permute-start(f32[256,384]{1,0:T(8,128)S(1)} %convolution_add_fusion.2), channel_id=1, source_target_pairs={{0,2},{2,4},{4,6},{6,8},{8,10},{10,12},{12,14},{3,1},{5,3},{7,5},{... | collective-permute-start | bytes 1179656 | tf_op jit(solution)/shard_map/ppermute | solution.py:107
  11.3 8.1 %collective-permute-done.1 = f32[256,384]{1,0:T(8,128)S(1)} collective-permute-done((f32[256,384]{1,0:T(8,128)S(1)}, f32[256,384]{1,0:T(8,128)S(1)}, u32[]{:S(2)}, u32[]{:S(2)}) %collective-permute-start.1) | collective-permute-done | bytes 393248 | tf_op jit(solution)/shard_map/ppermute | solution.py:107
  19.4 0.6 %convolution_add_fusion.1 = f32[256,384]{1,0:T(8,128)S(1)} fusion(f32[256,384]{1,0:T(8,128)S(1)} %collective-permute-done.1, f32[256,128]{1,0:T(8,128)S(1)} %slice.47, f32[256,384]{1,0:T(8,128)S(1)} %convolution_add_fusion.2), kind=kOutput, calls=%fused_computation.1 | convolution fusion | flops 302088192 | bytes 1179648 | tf_op jit(solution)/shard_map/dot_general | solution.py:128
  20.0 1.3 %collective-permute-start.2 = (f32[256,384]{1,0:T(8,128)S(1)}, f32[256,384]{1,0:T(8,128)S(1)}, u32[]{:S(2)}, u32[]{:S(2)}) collective-permute-start(f32[256,384]{1,0:T(8,128)S(1)} %convolution_add_fusion.1), channel_id=1, source_target_pairs={{0,4},{2,6},{4,8},{6,10},{8,12},{10,14},{5,1},{7,3},{9,5},{11,7},{... | collective-permute-start | bytes 1179656 | tf_op jit(solution)/shard_map/ppermute | solution.py:107
  21.4 11.5 %collective-permute-done.2 = f32[256,384]{1,0:T(8,128)S(1)} collective-permute-done((f32[256,384]{1,0:T(8,128)S(1)}, f32[256,384]{1,0:T(8,128)S(1)}, u32[]{:S(2)}, u32[]{:S(2)}) %collective-permute-start.2) | collective-permute-done | bytes 393248 | tf_op jit(solution)/shard_map/ppermute | solution.py:107
  32.8 0.6 %convolution_add_fusion = f32[256,384]{1,0:T(8,128)S(1)} fusion(f32[256,384]{1,0:T(8,128)S(1)} %collective-permute-done.2, f32[256,128]{1,0:T(8,128)S(1)} %slice.49, f32[256,384]{1,0:T(8,128)S(1)} %convolution_add_fusion.1), kind=kOutput, calls=%fused_computation | convolution fusion | flops 302088192 | bytes 1179648 | tf_op jit(solution)/shard_map/dot_general | solution.py:128
  33.4 1.3 %collective-permute-start.3 = (f32[256,384]{1,0:T(8,128)S(1)}, f32[256,384]{1,0:T(8,128)S(1)}, u32[]{:S(2)}, u32[]{:S(2)}) collective-permute-start(f32[256,384]{1,0:T(8,128)S(1)} %convolution_add_fusion), channel_id=1, source_target_pairs={{0,2},{2,4},{4,6},{6,8},{8,10},{10,12},{12,14},{3,1},{5,3},{7,5},{... | collective-permute-start | bytes 1179656 | tf_op jit(solution)/shard_map/ppermute | solution.py:107
  34.8 0.0 copy-start.1
  34.8 1.4 %collective-permute-start.4 = (f32[256,128]{1,0:T(8,128)S(1)}, f32[256,128]{1,0:T(8,128)S(1)}, u32[]{:S(2)}, u32[]{:S(2)}) collective-permute-start(f32[256,128]{1,0:T(8,128)S(1)} %slice.51), channel_id=1, source_target_pairs={{0,10},{2,12},{4,14},{11,1},{13,3},{15,5},{16,26},{18,28},{20,30},... | collective-permute-start | bytes 393224 | tf_op jit(solution)/shard_map/ppermute | solution.py:107
  36.2 7.0 %collective-permute-done.4 = f32[256,128]{1,0:T(8,128)S(1)} collective-permute-done((f32[256,128]{1,0:T(8,128)S(1)}, f32[256,128]{1,0:T(8,128)S(1)}, u32[]{:S(2)}, u32[]{:S(2)}) %collective-permute-start.4) | collective-permute-done | bytes 131104 | tf_op jit(solution)/shard_map/ppermute | solution.py:107
  43.2 0.2 collective-permute-done.3
  43.4 0.4 convolution_add_fusion.4.enter_ref
  43.7 0.0 copy-start.2
  43.8 0.4 convolution_add_fusion.3
  44.1 0.2 copy-done.2
  44.4 4.2 %collective-permute-start.5 = (f32[256,128]{1,0:T(8,128)S(1)}, f32[256,128]{1,0:T(8,128)S(1)}, u32[]{:S(2)}, u32[]{:S(2)}) collective-permute-start(f32[256,128]{1,0:T(8,128)S(1)} %convolution_add_fusion.3), channel_id=1, source_target_pairs={{0,1},{2,3},{4,5},{6,7},{8,9},{10,11},{12,13},{14,15},{1,0},{3,2},... | collective-permute-start | bytes 393224 | tf_op jit(solution)/shard_map/ppermute | solution.py:134
  48.6 0.0 copy-done
  48.6 0.0 copy-done.1
  48.6 1.4 %fusion.5.diag_ref = f32[8,256,128]{2,1,0:T(8,128)} fusion(bf16[8,256,256]{2,1,0:T(8,128)(2,1)S(1)} %copy-done, bf16[8,256,128]{2,1,0:T(8,128)(2,1)S(1)} %copy-done.1), kind=kOutput, calls=%fused_computation.12 | convolution fusion | flops 134217728 | bytes 2621440 | tf_op jit(solution)/shard_map/kab,kbc->kac/dot_general | solution.py:160
  50.0 0.0 collective-permute-done.5.other_ref
  50.0 0.0 copy-start.3
  50.0 0.7 %copy-done.3 = f32[256,128]{1,0:T(8,128)} copy-done((f32[256,128]{1,0:T(8,128)}, f32[256,128]{1,0:T(8,128)S(1)}, u32[]{:S(2)}) %copy-start.3) | copy-done | bytes 131096
  50.6 6.3 %apply.1 = bf16[8,256,128]{2,1,0:T(8,128)(2,1)} custom-call(s32[1]{0:T(128)} %bitcast.flag_ref, f32[256,128]{1,0:T(8,128)} %copy-done.2, f32[256,128]{1,0:T(8,128)} %copy-done.3, bf16[8,256,256]{2,1,0:T(8,128)(2,1)} %ltrans_ref.3, bf16[8,256,256]{2,1,0:T(8,128)(2,1)} %utrans_ref.3, f32[8,256,128]{2,1,0:T(8,128)} %get-tuple-element.11.lsrc_ref, ...), custom_call_target="tpu_custom_call" | custom-call | tf_op jit(solution)/shard_map/apply/pallas_call | solution.py:172
  (4 shorter events, 0.0 us)
Async XLA Ops:
  0.0 48.6 %copy-start = (bf16[8,256,256]{2,1,0:T(8,128)(2,1)S(1)}, bf16[8,256,256]{2,1,0:T(8,128)(2,1)}, u32[]{:S(2)}) copy-start(bf16[8,256,256]{2,1,0:T(8,128)(2,1)} %param.9) | copy-start | bytes 3145732
  7.6 1.8 %collective-permute-start = (f32[256,384]{1,0:T(8,128)S(1)}, f32[256,384]{1,0:T(8,128)S(1)}, u32[]{:S(2)}, u32[]{:S(2)}) collective-permute-start(f32[256,384]{1,0:T(8,128)S(1)} %get-tuple-element.13), channel_id=1, source_target_pairs={{0,1},{2,3},{4,5},{6,7},{8,9},{10,11},{12,13},{14,15},{1,0},{3,2},... | collective-permute-start | bytes 1179656 | tf_op jit(solution)/shard_map/ppermute | solution.py:118
  10.0 9.4 %collective-permute-start.1 = (f32[256,384]{1,0:T(8,128)S(1)}, f32[256,384]{1,0:T(8,128)S(1)}, u32[]{:S(2)}, u32[]{:S(2)}) collective-permute-start(f32[256,384]{1,0:T(8,128)S(1)} %convolution_add_fusion.2), channel_id=1, source_target_pairs={{0,2},{2,4},{4,6},{6,8},{8,10},{10,12},{12,14},{3,1},{5,3},{7,5},{... | collective-permute-start | bytes 1179656 | tf_op jit(solution)/shard_map/ppermute | solution.py:107
  20.0 12.8 %collective-permute-start.2 = (f32[256,384]{1,0:T(8,128)S(1)}, f32[256,384]{1,0:T(8,128)S(1)}, u32[]{:S(2)}, u32[]{:S(2)}) collective-permute-start(f32[256,384]{1,0:T(8,128)S(1)} %convolution_add_fusion.1), channel_id=1, source_target_pairs={{0,4},{2,6},{4,8},{6,10},{8,12},{10,14},{5,1},{7,3},{9,5},{11,7},{... | collective-permute-start | bytes 1179656 | tf_op jit(solution)/shard_map/ppermute | solution.py:107
  33.4 9.9 %collective-permute-start.3 = (f32[256,384]{1,0:T(8,128)S(1)}, f32[256,384]{1,0:T(8,128)S(1)}, u32[]{:S(2)}, u32[]{:S(2)}) collective-permute-start(f32[256,384]{1,0:T(8,128)S(1)} %convolution_add_fusion), channel_id=1, source_target_pairs={{0,2},{2,4},{4,6},{6,8},{8,10},{10,12},{12,14},{3,1},{5,3},{7,5},{... | collective-permute-start | bytes 1179656 | tf_op jit(solution)/shard_map/ppermute | solution.py:107
  34.8 13.8 %copy-start.1 = (bf16[8,256,128]{2,1,0:T(8,128)(2,1)S(1)}, bf16[8,256,128]{2,1,0:T(8,128)(2,1)}, u32[]{:S(2)}) copy-start(bf16[8,256,128]{2,1,0:T(8,128)(2,1)} %rhs_ref.1) | copy-start | bytes 1572868
  34.8 8.4 %collective-permute-start.4 = (f32[256,128]{1,0:T(8,128)S(1)}, f32[256,128]{1,0:T(8,128)S(1)}, u32[]{:S(2)}, u32[]{:S(2)}) collective-permute-start(f32[256,128]{1,0:T(8,128)S(1)} %slice.51), channel_id=1, source_target_pairs={{0,10},{2,12},{4,14},{11,1},{13,3},{15,5},{16,26},{18,28},{20,30},... | collective-permute-start | bytes 393224 | tf_op jit(solution)/shard_map/ppermute | solution.py:107
  43.7 0.6 %copy-start.2 = (f32[256,128]{1,0:T(8,128)}, f32[256,128]{1,0:T(8,128)S(1)}, u32[]{:S(2)}) copy-start(f32[256,128]{1,0:T(8,128)S(1)} %convolution_add_fusion.4.enter_ref) | copy-start | bytes 393220
  44.4 5.6 %collective-permute-start.5 = (f32[256,128]{1,0:T(8,128)S(1)}, f32[256,128]{1,0:T(8,128)S(1)}, u32[]{:S(2)}, u32[]{:S(2)}) collective-permute-start(f32[256,128]{1,0:T(8,128)S(1)} %convolution_add_fusion.3), channel_id=1, source_target_pairs={{0,1},{2,3},{4,5},{6,7},{8,9},{10,11},{12,13},{14,15},{1,0},{3,2},... | collective-permute-start | bytes 393224 | tf_op jit(solution)/shard_map/ppermute | solution.py:134
  50.0 0.7 %copy-start.3 = (f32[256,128]{1,0:T(8,128)}, f32[256,128]{1,0:T(8,128)S(1)}, u32[]{:S(2)}) copy-start(f32[256,128]{1,0:T(8,128)S(1)} %collective-permute-done.5.other_ref) | copy-start | bytes 393220

commit v7 on v6

v7 whole, which is shorter than its diff:
```python
import jax
import jax.numpy as jnp
from jax import lax
from jax.experimental import pallas as pl
from jax.experimental.pallas import tpu as pltpu
from jax.sharding import PartitionSpec as P

F32 = jnp.float32
BF16 = jnp.bfloat16
HIGHEST = lax.Precision.HIGHEST


def split_dot(matrix, value):
    high = value.astype(BF16)
    low = (value - high.astype(F32)).astype(BF16)
    return jnp.dot(matrix, high, preferred_element_type=F32) + jnp.dot(
        matrix, low, preferred_element_type=F32
    )


def split(value):
    high = value.astype(BF16)
    return high, (value - high.astype(F32)).astype(BF16)


def wide_dot(left, right):
    left_high, left_low = split(left)
    right_high, right_low = split(right)
    total = jnp.dot(left_high, right_high, preferred_element_type=F32)
    total = total + jnp.dot(left_high, right_low, preferred_element_type=F32)
    return total + jnp.dot(left_low, right_high, preferred_element_type=F32)


def tree_product(factors):
    level = [
        jnp.dot(factors[i], factors[i + 1], preferred_element_type=F32)
        if i + 1 < len(factors)
        else factors[i].astype(F32)
        for i in range(0, len(factors), 2)
    ]
    while len(level) > 1:
        level = [
            wide_dot(level[i], level[i + 1]) if i + 1 < len(level) else level[i]
            for i in range(0, len(level), 2)
        ]
    return level[0]


def sweep_kernel(
    flag_ref, rhs_ref, lcols_ref, ltrans_ref, ucols_ref, utrans_ref, diag_ref,
    own_ref, give_ref, lsrc_ref, usrc_ref, dprod_ref,
):
    count = rhs_ref.shape[0]
    lstate = ustate = None
    for step in range(count):
        lk = step
        uk = count - 1 - step
        lsrc = lax.dot_general(lcols_ref[lk], rhs_ref[lk], (((0,), (0,)), ((), ())), preferred_element_type=F32)
        usrc = lax.dot_general(ucols_ref[uk], rhs_ref[uk], (((0,), (0,)), ((), ())), preferred_element_type=F32)
        lsrc_ref[lk] = lsrc
        usrc_ref[uk] = usrc
        if step == 0:
            lstate = lsrc
            ustate = usrc
        else:
            lstate = split_dot(ltrans_ref[lk], lstate) + lsrc
            ustate = split_dot(utrans_ref[uk], ustate) + usrc
    lmap = tree_product([ltrans_ref[k] for k in reversed(range(count))])
    umap = tree_product([utrans_ref[k] for k in range(count)])
    for k in range(count):
        dprod_ref[k] = jnp.dot(diag_ref[k], rhs_ref[k], preferred_element_type=F32)
    rank = lmap.shape[0]
    first = flag_ref[0] == 0

    @pl.when(first)
    def _():
        own_ref[:, :rank] = lmap
        own_ref[:, rank:] = lstate
        give_ref[:, :rank] = umap
        give_ref[:, rank:] = ustate

    @pl.when(jnp.logical_not(first))
    def _():
        own_ref[:, :rank] = umap
        own_ref[:, rank:] = ustate
        give_ref[:, :rank] = lmap
        give_ref[:, rank:] = lstate


def apply_kernel(
    flag_ref, enter_ref, other_ref, ltrans_ref, utrans_ref, lsrc_ref, usrc_ref,
    diag_ref, lrows_ref, urows_ref, out_ref,
):
    count = ltrans_ref.shape[0]
    first = flag_ref[0] == 0
    lstate = jnp.where(first, enter_ref[...], other_ref[...])
    ustate = jnp.where(first, other_ref[...], enter_ref[...])
    lround = [None] * count
    uround = [None] * count

    def finish(k):
        total = diag_ref[k]
        total = total + jnp.dot(lrows_ref[k], lround[k], preferred_element_type=F32)
        total = total + jnp.dot(urows_ref[k], uround[k], preferred_element_type=F32)
        out_ref[k] = total.astype(out_ref.dtype)

    for step in range(count):
        lk = step
        uk = count - 1 - step
        lround[lk] = lstate.astype(BF16)
        uround[uk] = ustate.astype(BF16)
        if uround[lk] is not None:
            finish(lk)
        if uk != lk and lround[uk] is not None:
            finish(uk)
        if step + 1 < count:
            lstate = split_dot(ltrans_ref[lk], lstate) + lsrc_ref[lk]
            ustate = split_dot(utrans_ref[uk], ustate) + usrc_ref[uk]


def chip_shift(value, axis, chips, shift):
    pairs = [(2 * c, 2 * (c + shift)) for c in range(chips - shift)]
    pairs += [(2 * c + 1, 2 * (c - shift) + 1) for c in range(shift, chips)]
    return lax.ppermute(value, axis, pairs)


def scan_chips(own, give, axis):
    count = lax.axis_size(axis)
    chips = count // 2
    rank = own.shape[0]
    partner = [(2 * c, 2 * c + 1) for c in range(chips)]
    partner += [(2 * c + 1, 2 * c) for c in range(chips)]
    got = lax.ppermute(give, axis, partner)
    tail = jnp.concatenate([jnp.zeros((rank, rank), F32), got[:, rank:]], axis=1)
    both = jnp.dot(got[:, :rank], own, precision=HIGHEST) + tail
    rounds = 0
    while 2 ** (rounds + 1) < chips - 1:
        rounds += 1
    shift = 1
    for _ in range(rounds):
        got = chip_shift(both, axis, chips, shift)
        tail = jnp.concatenate([jnp.zeros((rank, rank), F32), both[:, rank:]], axis=1)
        both = jnp.dot(both[:, :rank], got, precision=HIGHEST) + tail
        shift *= 2
    near = chip_shift(both, axis, chips, 1)
    far = chip_shift(both[:, rank:], axis, chips, 1 + shift)
    enter = jnp.dot(near[:, :rank], far, precision=HIGHEST) + near[:, rank:]
    send = jnp.dot(own[:, :rank], enter, precision=HIGHEST) + own[:, rank:]
    other = lax.ppermute(send, axis, partner)
    return enter, other


def shards(
    right_sides,
    diagonal_blocks,
    lower_rows,
    lower_cols,
    lower_trans,
    upper_rows,
    upper_cols,
    upper_trans,
):
    count, rows, rhs = right_sides.shape
    rank = lower_trans.shape[1]
    count_row = lax.axis_size("row")
    chip_scan = count_row % 2 == 0 and count_row >= 4
    if chip_scan:
        flag = jnp.full((1,), lax.axis_index("row") % 2, jnp.int32)
    else:
        flag = jnp.zeros((1,), jnp.int32)
    vmem = pl.BlockSpec(memory_space=pltpu.VMEM)
    smem = pl.BlockSpec(memory_space=pltpu.SMEM)
    own, give, lsrc, usrc, diag = pl.pallas_call(
        sweep_kernel,
        out_shape=(
            jax.ShapeDtypeStruct((rank, rank + rhs), F32),
            jax.ShapeDtypeStruct((rank, rank + rhs), F32),
            jax.ShapeDtypeStruct((count, rank, rhs), F32),
            jax.ShapeDtypeStruct((count, rank, rhs), F32),
            jax.ShapeDtypeStruct((count, rows, rhs), F32),
        ),
        in_specs=[smem] + [vmem] * 6,
        name="sweep",
    )(flag, right_sides, lower_cols, lower_trans, upper_cols, upper_trans, diagonal_blocks)
    if chip_scan:
        enter, other = scan_chips(own, give, "row")
    else:
        enter = scan_enter(own[:, :rank], own[:, rank:], "row", False)
        other = scan_enter(give[:, :rank], give[:, rank:], "row", True)
    return pl.pallas_call(
        apply_kernel,
        out_shape=jax.ShapeDtypeStruct((count, rows, rhs), BF16),
        in_specs=[smem] + [vmem] * 9,
        name="apply",
    )(flag, enter, other, lower_trans, upper_trans, lsrc, usrc, diag, lower_rows, upper_rows)


def solution(mesh):
    spec = P(("sep", "row"), None, None)
    return jax.shard_map(
        shards, mesh=mesh, in_specs=(spec,) * 8, out_specs=spec, check_vma=False
    )
```

time: 57.3 us -> 58.7 us (1.024)
  Pallas kernels: 12.7 us -> 14.2 us
  waiting for transfers between devices: 28.5 us -> 29.8 us
  other arithmetic: 1.17 us -> 0 us
    pallas_call x1, Pallas kernels: 6.43 us -> 8.11 us  [shards(): pl.pallas_call(sweep_kernel, out_shape=(jax.ShapeDtypeStruct((rank, rank...]
    dot_general x1 -> x0, matrix products: 1.41 us -> none  [shards(): jnp.einsum('kab,kbc->kac', diagonal_blocks, right_sides, preferred_elemen...]
    select_n x1 -> x0, other arithmetic: 1.17 us -> none  [scan_chips(): got = lax.ppermute(jnp.where(first, upper, lower), axis, partner)]
    dot_general x1, matrix products: 0.6 us -> 1.59 us  [scan_chips(): both = jnp.dot(got[:, :rank], own, precision=HIGHEST) + tail]
    ppermute x1, waiting for transfers between devices: 0.01 us -> 0.99 us  [scan_chips(): other = lax.ppermute(send, axis, partner)]
  transfers between devices with their start and end apart: 6 -> 6, of which waited for: 5 -> 6; matrix products, arithmetic and copies ran while one was open for 3% -> 0% of each run, Pallas kernels for 0% -> 0%
where the time goes in v7:
time: 58.7 us; the launch traced here: 58.1 us
  waiting for transfers between devices  29.8 us (51%)
  Pallas kernels  14.2 us (24%)
  starting transfers between devices  9.48 us (16%)
  matrix products  3.54 us (6%)
  local copies, waits for them, and re-layouts  0.97 us (2%)
    ppermute x4, waiting for transfers between devices, chip_shift(): return lax.ppermute(value, axis, pairs)  26.9 us
    pallas_call x1, Pallas kernels, shards(): pl.pallas_call(sweep_kernel, out_shape=(jax.ShapeDtypeStruct((rank, rank...  8.11 us
    pallas_call x1, Pallas kernels, shards(): pl.pallas_call(apply_kernel, out_shape=jax.ShapeDtypeStruct((count, rows,...  6.12 us
    ppermute x4, starting transfers between devices, chip_shift(): return lax.ppermute(value, axis, pairs)  5.3 us
    ppermute x1, starting transfers between devices, scan_chips(): other = lax.ppermute(send, axis, partner)  4.18 us
    ppermute x1, waiting for transfers between devices, scan_chips(): got = lax.ppermute(give, axis, partner)  1.93 us
    dot_general x1, matrix products, scan_chips(): both = jnp.dot(got[:, :rank], own, precision=HIGHEST) + tail  1.59 us
    dot_general x2, matrix products, scan_chips(): both = jnp.dot(both[:, :rank], got, precision=HIGHEST) + tail  1.2 us
  transfers between devices with their start and end apart: 6, of which 6 were waited for; matrix products, arithmetic and copies ran while one was open for 0% of the time, Pallas kernels for 0%

profile of v7, /device:TPU:1, one launch (start us, length us, event | category | flops | bytes accessed | tf_op | source)
XLA Modules:
  0.0 58.1 jit_solution(17205819473749289653)
XLA Ops:
  0.0 8.1 %sweep.1 = (f32[256,384]{1,0:T(8,128)}, f32[256,384]{1,0:T(8,128)}, f32[8,256,128]{2,1,0:T(8,128)}, f32[8,256,128]{2,1,0:T(8,128)}, f32[8,256,128]{2,1,0:T(8,128)}) custom-call(s32[1]{0:T(128)} %bitcast.flag_ref, bf16[8,256,128]{2,1,0:T(8,128)(2,1)} %rhs_ref.1, bf16[8,256,256]{2,1,0:T(8,128)(2,1)} %lcols_ref.1, bf16[8,256,256]{2,1,0:T(8,128)(2,1)} %ltrans_ref.3, ...), custom_call_target="tpu_custom_call" | custom-call | tf_op jit(solution)/shard_map/sweep/pallas_call | solution.py:173
  8.1 0.0 collective-permute-start
  8.1 1.9 %collective-permute-done = f32[256,384]{1,0:T(8,128)S(1)} collective-permute-done((f32[256,384]{1,0:T(8,128)}, f32[256,384]{1,0:T(8,128)S(1)}, u32[]{:S(2)}, u32[]{:S(2)}) %collective-permute-start) | collective-permute-done | bytes 393248 | tf_op jit(solution)/shard_map/ppermute | solution.py:133
  10.1 1.6 %convolution_add_fusion.2 = f32[256,384]{1,0:T(8,128)S(1)} fusion(f32[256,384]{1,0:T(8,128)} %get-tuple-element.11, f32[256,128]{1,0:T(8,128)S(1)} %slice.45, f32[256,384]{1,0:T(8,128)S(1)} %collective-permute-done), kind=kOutput, calls=%fused_computation.2 | convolution fusion | flops 302088192 | bytes 1179648 | tf_op jit(solution)/shard_map/dot_general | solution.py:135
  11.7 1.3 %collective-permute-start.1 = (f32[256,384]{1,0:T(8,128)S(1)}, f32[256,384]{1,0:T(8,128)S(1)}, u32[]{:S(2)}, u32[]{:S(2)}) collective-permute-start(f32[256,384]{1,0:T(8,128)S(1)} %convolution_add_fusion.2), channel_id=1, source_target_pairs={{0,2},{2,4},{4,6},{6,8},{8,10},{10,12},{12,14},{3,1},{5,3},{7,5},{... | collective-permute-start | bytes 1179656 | tf_op jit(solution)/shard_map/ppermute | solution.py:124
  13.0 8.1 %collective-permute-done.1 = f32[256,384]{1,0:T(8,128)S(1)} collective-permute-done((f32[256,384]{1,0:T(8,128)S(1)}, f32[256,384]{1,0:T(8,128)S(1)}, u32[]{:S(2)}, u32[]{:S(2)}) %collective-permute-start.1) | collective-permute-done | bytes 393248 | tf_op jit(solution)/shard_map/ppermute | solution.py:124
  21.1 0.6 %convolution_add_fusion.1 = f32[256,384]{1,0:T(8,128)S(1)} fusion(f32[256,384]{1,0:T(8,128)S(1)} %collective-permute-done.1, f32[256,128]{1,0:T(8,128)S(1)} %slice.47, f32[256,384]{1,0:T(8,128)S(1)} %convolution_add_fusion.2), kind=kOutput, calls=%fused_computation.1 | convolution fusion | flops 302088192 | bytes 1179648 | tf_op jit(solution)/shard_map/dot_general | solution.py:143
  21.7 1.3 %collective-permute-start.2 = (f32[256,384]{1,0:T(8,128)S(1)}, f32[256,384]{1,0:T(8,128)S(1)}, u32[]{:S(2)}, u32[]{:S(2)}) collective-permute-start(f32[256,384]{1,0:T(8,128)S(1)} %convolution_add_fusion.1), channel_id=1, source_target_pairs={{0,4},{2,6},{4,8},{6,10},{8,12},{10,14},{5,1},{7,3},{9,5},{11,7},{... | collective-permute-start | bytes 1179656 | tf_op jit(solution)/shard_map/ppermute | solution.py:124
  23.0 11.5 %collective-permute-done.2 = f32[256,384]{1,0:T(8,128)S(1)} collective-permute-done((f32[256,384]{1,0:T(8,128)S(1)}, f32[256,384]{1,0:T(8,128)S(1)}, u32[]{:S(2)}, u32[]{:S(2)}) %collective-permute-start.2) | collective-permute-done | bytes 393248 | tf_op jit(solution)/shard_map/ppermute | solution.py:124
  34.5 0.6 %convolution_add_fusion = f32[256,384]{1,0:T(8,128)S(1)} fusion(f32[256,384]{1,0:T(8,128)S(1)} %collective-permute-done.2, f32[256,128]{1,0:T(8,128)S(1)} %slice.49, f32[256,384]{1,0:T(8,128)S(1)} %convolution_add_fusion.1), kind=kOutput, calls=%fused_computation | convolution fusion | flops 302088192 | bytes 1179648 | tf_op jit(solution)/shard_map/dot_general | solution.py:143
  35.1 0.0 copy-start.1
  35.1 1.4 %collective-permute-start.3 = (f32[256,384]{1,0:T(8,128)S(1)}, f32[256,384]{1,0:T(8,128)S(1)}, u32[]{:S(2)}, u32[]{:S(2)}) collective-permute-start(f32[256,384]{1,0:T(8,128)S(1)} %convolution_add_fusion), channel_id=1, source_target_pairs={{0,2},{2,4},{4,6},{6,8},{8,10},{10,12},{12,14},{3,1},{5,3},{7,5},{... | collective-permute-start | bytes 1179656 | tf_op jit(solution)/shard_map/ppermute | solution.py:124
  36.5 1.3 %collective-permute-start.4 = (f32[256,128]{1,0:T(8,128)S(1)}, f32[256,128]{1,0:T(8,128)S(1)}, u32[]{:S(2)}, u32[]{:S(2)}) collective-permute-start(f32[256,128]{1,0:T(8,128)S(1)} %slice.51), channel_id=1, source_target_pairs={{0,10},{2,12},{4,14},{11,1},{13,3},{15,5},{16,26},{18,28},{20,30},... | collective-permute-start | bytes 393224 | tf_op jit(solution)/shard_map/ppermute | solution.py:124
  37.8 7.0 %collective-permute-done.4 = f32[256,128]{1,0:T(8,128)S(1)} collective-permute-done((f32[256,128]{1,0:T(8,128)S(1)}, f32[256,128]{1,0:T(8,128)S(1)}, u32[]{:S(2)}, u32[]{:S(2)}) %collective-permute-start.4) | collective-permute-done | bytes 131104 | tf_op jit(solution)/shard_map/ppermute | solution.py:124
  44.8 0.3 collective-permute-done.3
  45.1 0.4 convolution_add_fusion.4.enter_ref
  45.5 0.0 copy-done.1
  45.5 0.0 copy-start
  45.5 0.4 convolution_add_fusion.3
  45.9 0.3 copy-done
  46.2 4.2 %collective-permute-start.5 = (f32[256,128]{1,0:T(8,128)S(1)}, f32[256,128]{1,0:T(8,128)S(1)}, u32[]{:S(2)}, u32[]{:S(2)}) collective-permute-start(f32[256,128]{1,0:T(8,128)S(1)} %convolution_add_fusion.3), channel_id=1, source_target_pairs={{0,1},{2,3},{4,5},{6,7},{8,9},{10,11},{12,13},{14,15},{1,0},{3,2},... | collective-permute-start | bytes 393224 | tf_op jit(solution)/shard_map/ppermute | solution.py:149
  50.4 1.0 %collective-permute-done.5.other_ref = f32[256,128]{1,0:T(8,128)S(1)} collective-permute-done((f32[256,128]{1,0:T(8,128)S(1)}, f32[256,128]{1,0:T(8,128)S(1)}, u32[]{:S(2)}, u32[]{:S(2)}) %collective-permute-start.5) | collective-permute-done | bytes 131104 | tf_op jit(solution)/shard_map/ppermute | solution.py:149
  51.3 0.0 copy-start.2
  51.3 0.7 %copy-done.2 = f32[256,128]{1,0:T(8,128)} copy-done((f32[256,128]{1,0:T(8,128)}, f32[256,128]{1,0:T(8,128)S(1)}, u32[]{:S(2)}) %copy-start.2) | copy-done | bytes 131096
  52.0 6.1 %apply.1 = bf16[8,256,128]{2,1,0:T(8,128)(2,1)} custom-call(s32[1]{0:T(128)} %bitcast.flag_ref, f32[256,128]{1,0:T(8,128)} %copy-done, f32[256,128]{1,0:T(8,128)} %copy-done.2, bf16[8,256,256]{2,1,0:T(8,128)(2,1)} %ltrans_ref.3, bf16[8,256,256]{2,1,0:T(8,128)(2,1)} %utrans_ref.3, f32[8,256,128]{2,1,0:T(8,128)} %get-tuple-element.12.lsrc_ref, ...), custom_call_target="tpu_custom_call" | custom-call | tf_op jit(solution)/shard_map/apply/pallas_call | solution.py:190
  (4 shorter events, 0.0 us)
Async XLA Ops:
  8.1 1.9 %collective-permute-start = (f32[256,384]{1,0:T(8,128)}, f32[256,384]{1,0:T(8,128)S(1)}, u32[]{:S(2)}, u32[]{:S(2)}) collective-permute-start(f32[256,384]{1,0:T(8,128)} %get-tuple-element.10), channel_id=1, source_target_pairs={{0,1},{2,3},{4,5},{6,7},{8,9},{10,11},{12,13},{14,15},{1,0},{3,2},... | collective-permute-start | bytes 1179656 | tf_op jit(solution)/shard_map/ppermute | solution.py:133
  11.7 9.4 %collective-permute-start.1 = (f32[256,384]{1,0:T(8,128)S(1)}, f32[256,384]{1,0:T(8,128)S(1)}, u32[]{:S(2)}, u32[]{:S(2)}) collective-permute-start(f32[256,384]{1,0:T(8,128)S(1)} %convolution_add_fusion.2), channel_id=1, source_target_pairs={{0,2},{2,4},{4,6},{6,8},{8,10},{10,12},{12,14},{3,1},{5,3},{7,5},{... | collective-permute-start | bytes 1179656 | tf_op jit(solution)/shard_map/ppermute | solution.py:124
  21.7 12.8 %collective-permute-start.2 = (f32[256,384]{1,0:T(8,128)S(1)}, f32[256,384]{1,0:T(8,128)S(1)}, u32[]{:S(2)}, u32[]{:S(2)}) collective-permute-start(f32[256,384]{1,0:T(8,128)S(1)} %convolution_add_fusion.1), channel_id=1, source_target_pairs={{0,4},{2,6},{4,8},{6,10},{8,12},{10,14},{5,1},{7,3},{9,5},{11,7},{... | collective-permute-start | bytes 1179656 | tf_op jit(solution)/shard_map/ppermute | solution.py:124
  35.1 10.5 %copy-start.1 = (f32[256,384]{1,0:T(8,128)S(1)}, f32[256,384]{1,0:T(8,128)}, u32[]{:S(2)}) copy-start(f32[256,384]{1,0:T(8,128)} %get-tuple-element.11) | copy-start | bytes 1179652
  35.1 10.1 %collective-permute-start.3 = (f32[256,384]{1,0:T(8,128)S(1)}, f32[256,384]{1,0:T(8,128)S(1)}, u32[]{:S(2)}, u32[]{:S(2)}) collective-permute-start(f32[256,384]{1,0:T(8,128)S(1)} %convolution_add_fusion), channel_id=1, source_target_pairs={{0,2},{2,4},{4,6},{6,8},{8,10},{10,12},{12,14},{3,1},{5,3},{7,5},{... | collective-permute-start | bytes 1179656 | tf_op jit(solution)/shard_map/ppermute | solution.py:124
  36.5 8.3 %collective-permute-start.4 = (f32[256,128]{1,0:T(8,128)S(1)}, f32[256,128]{1,0:T(8,128)S(1)}, u32[]{:S(2)}, u32[]{:S(2)}) collective-permute-start(f32[256,128]{1,0:T(8,128)S(1)} %slice.51), channel_id=1, source_target_pairs={{0,10},{2,12},{4,14},{11,1},{13,3},{15,5},{16,26},{18,28},{20,30},... | collective-permute-start | bytes 393224 | tf_op jit(solution)/shard_map/ppermute | solution.py:124
  45.5 0.7 %copy-start = (f32[256,128]{1,0:T(8,128)}, f32[256,128]{1,0:T(8,128)S(1)}, u32[]{:S(2)}) copy-start(f32[256,128]{1,0:T(8,128)S(1)} %convolution_add_fusion.4.enter_ref) | copy-start | bytes 393220
  46.2 5.2 %collective-permute-start.5 = (f32[256,128]{1,0:T(8,128)S(1)}, f32[256,128]{1,0:T(8,128)S(1)}, u32[]{:S(2)}, u32[]{:S(2)}) collective-permute-start(f32[256,128]{1,0:T(8,128)S(1)} %convolution_add_fusion.3), channel_id=1, source_target_pairs={{0,1},{2,3},{4,5},{6,7},{8,9},{10,11},{12,13},{14,15},{1,0},{3,2},... | collective-permute-start | bytes 393224 | tf_op jit(solution)/shard_map/ppermute | solution.py:149
  51.3 0.7 %copy-start.2 = (f32[256,128]{1,0:T(8,128)}, f32[256,128]{1,0:T(8,128)S(1)}, u32[]{:S(2)}) copy-start(f32[256,128]{1,0:T(8,128)S(1)} %collective-permute-done.5.other_ref) | copy-start | bytes 393220

commit v8 on v6

--- a/solution.py
+++ b/solution.py
@@ -51,26 +51,60 @@
 
 
 def apply_kernel(
-    flag_ref, enter_ref, other_ref, ltrans_ref, utrans_ref, lsrc_ref, usrc_ref,
-    diag_ref, lrows_ref, urows_ref, out_ref, lround_ref, uround_ref,
+    flag_ref, enter_ref, other_ref, ltrans_hbm, utrans_hbm, lsrc_hbm, usrc_hbm,
+    diag_hbm, lrows_hbm, urows_hbm, out_ref,
+    ltrans_ref, utrans_ref, lsrc_ref, usrc_ref, diag_ref, lrows_ref, urows_ref, sems,
 ):
     count = ltrans_ref.shape[0]
+    sources = (ltrans_hbm, utrans_hbm, lsrc_hbm, usrc_hbm, diag_hbm, lrows_hbm, urows_hbm)
+    targets = (ltrans_ref, utrans_ref, lsrc_ref, usrc_ref, diag_ref, lrows_ref, urows_ref)
+    copies = [
+        [pltpu.make_async_copy(sources[a].at[k], targets[a].at[k], sems.at[a, k]) for k in range(count)]
+        for a in range(len(sources))
+    ]
+    order = []
+    for step in range(count):
+        order += [(0, step), (2, step), (1, count - 1 - step), (3, count - 1 - step)]
+    for step in range(count):
+        for k in sorted({step, count - 1 - step}):
+            if max(k, count - 1 - k) == step:
+                order += [(4, k), (5, k), (6, k)]
+    for a, k in order:
+        copies[a][k].start()
+
+    def ready(a, k):
+        copies[a][k].wait()
+        return targets[a][k]
+
     first = flag_ref[0] == 0
     lstate = jnp.where(first, enter_ref[...], other_ref[...])
     ustate = jnp.where(first, other_ref[...], enter_ref[...])
+    lround = [None] * count
+    uround = [None] * count
+
+    def finish(k):
+        total = ready(4, k)
+        total = total + jnp.dot(ready(5, k), lround[k], preferred_element_type=F32)
+        total = total + jnp.dot(ready(6, k), uround[k], preferred_element_type=F32)
+        out_ref[k] = total.astype(out_ref.dtype)
+
     for step in range(count):
         lk = step
         uk = count - 1 - step
-        lround_ref[lk] = lstate.astype(BF16)
-        uround_ref[uk] = ustate.astype(BF16)
+        lround[lk] = lstate.astype(BF16)
+        uround[uk] = ustate.astype(BF16)
+        if uround[lk] is not None:
+            finish(lk)
+        if uk != lk and lround[uk] is not None:
+            finish(uk)
         if step + 1 < count:
-            lstate = split_dot(ltrans_ref[lk], lstate) + lsrc_ref[lk]
-            ustate = split_dot(utrans_ref[uk], ustate) + usrc_ref[uk]
-    for k in range(count):
-        total = diag_ref[k]
-        total = total + jnp.dot(lrows_ref[k], lround_ref[k], preferred_element_type=F32)
-        total = total + jnp.dot(urows_ref[k], uround_ref[k], preferred_element_type=F32)
-        out_ref[k] = total.astype(out_ref.dtype)
+            lstate = split_dot(ready(0, lk), lstate) + ready(2, lk)
+            ustate = split_dot(ready(1, uk), ustate) + ready(3, uk)
+    for step in range(count - 1, count):
+        copies[0][step].wait()
+        copies[2][step].wait()
+        copies[1][count - 1 - step].wait()
+        copies[3][count - 1 - step].wait()
 
 
 def shifted(value, axis, count, shift, reverse):
@@ -169,14 +203,21 @@
         other = scan_enter(uboth[:, :rank], uboth[:, rank:], "row", True)
         flag = jnp.zeros((1,), jnp.int32)
     vmem = pl.BlockSpec(memory_space=pltpu.VMEM)
+    anywhere = pl.BlockSpec(memory_space=pl.ANY)
     return pl.pallas_call(
         apply_kernel,
         out_shape=jax.ShapeDtypeStruct((count, rows, rhs), BF16),
         scratch_shapes=[
-            pltpu.VMEM((count, rank, rhs), BF16),
-            pltpu.VMEM((count, rank, rhs), BF16),
+            pltpu.VMEM((count, rank, rank), BF16),
+            pltpu.VMEM((count, rank, rank), BF16),
+            pltpu.VMEM((count, rank, rhs), F32),
+            pltpu.VMEM((count, rank, rhs), F32),
+            pltpu.VMEM((count, rows, rhs), F32),
+            pltpu.VMEM((count, rows, rank), BF16),
+            pltpu.VMEM((count, rows, rank), BF16),
+            pltpu.SemaphoreType.DMA((7, count)),
         ],
-        in_specs=[pl.BlockSpec(memory_space=pltpu.SMEM)] + [vmem] * 9,
+        in_specs=[pl.BlockSpec(memory_space=pltpu.SMEM), vmem, vmem] + [anywhere] * 7,
         name="apply",
     )(flag, enter, other, lower_trans, upper_trans, lsrc, usrc, diag, lower_rows, upper_rows)
 

time: 57.3 us -> 60.7 us (1.059)
  Pallas kernels: 12.7 us -> 16.1 us
    pallas_call x1, Pallas kernels: 6.27 us -> 9.65 us  [shards(): pl.pallas_call(apply_kernel, out_shape=jax.ShapeDtypeStruct((count, rows,...]
  transfers between devices with their start and end apart: 6 -> 6, of which waited for: 5 -> 5; matrix products, arithmetic and copies ran while one was open for 3% -> 2% of each run, Pallas kernels for 0% -> 0%
where the time goes in v8:
time: 60.7 us; the launch traced here: 60.3 us
  waiting for transfers between devices  28.5 us (47%)
  Pallas kernels  16.1 us (27%)
  starting transfers between devices  9.56 us (16%)
  matrix products  3.96 us (7%)
  other arithmetic  1.17 us (2%)
  local copies, waits for them, and re-layouts  0.95 us (2%)
    ppermute x4, waiting for transfers between devices, chip_shift(): return lax.ppermute(value, axis, pairs)  26.7 us
    pallas_call x1, Pallas kernels, shards(): pl.pallas_call(apply_kernel, out_shape=jax.ShapeDtypeStruct((count, rows,...  9.65 us
    pallas_call x1, Pallas kernels, shards(): pl.pallas_call(sweep_kernel, out_shape=(jax.ShapeDtypeStruct((rank, rank...  6.43 us
    ppermute x4, starting transfers between devices, chip_shift(): return lax.ppermute(value, axis, pairs)  5.3 us
    ppermute x1, starting transfers between devices, scan_chips(): other = lax.ppermute(send, axis, partner)  4.18 us
    ppermute x1, waiting for transfers between devices, scan_chips(): got = lax.ppermute(jnp.where(first, upper, lower), axis, partner)  1.71 us
    dot_general x1, matrix products, shards(): jnp.einsum('kab,kbc->kac', diagonal_blocks, right_sides, preferred_elemen...  1.41 us
  transfers between devices with their start and end apart: 6, of which 5 were waited for; matrix products, arithmetic and copies ran while one was open for 2% of the time, Pallas kernels for 0%

profile of v8, /device:TPU:1, one launch (start us, length us, event | category | flops | bytes accessed | tf_op | source)
XLA Modules:
  0.0 60.3 jit_solution(1742842218563229219)
XLA Ops:
  0.0 0.0 copy-start
  0.0 6.4 %sweep.1 = (f32[256,384]{1,0:T(8,128)}, f32[8,256,128]{2,1,0:T(8,128)}, f32[256,384]{1,0:T(8,128)}, f32[8,256,128]{2,1,0:T(8,128)}) custom-call(bf16[8,256,128]{2,1,0:T(8,128)(2,1)} %rhs_ref.1, bf16[8,256,256]{2,1,0:T(8,128)(2,1)} %lcols_ref.1, bf16[8,256,256]{2,1,0:T(8,128)(2,1)} %ltrans_hbm.1, bf16[8,256,256]{2,1,0:T(8,128)(2,1)} %ucols_ref.1, ...), custom_call_target="tpu_custom_call" | custom-call | tf_op jit(solution)/shard_map/sweep/pallas_call | solution.py:184
  6.4 1.2 %broadcast_select_fusion.1 = (f32[256,384]{1,0:T(8,128)S(1)}, f32[256,384]{1,0:T(8,128)S(1)}) fusion(f32[256,384]{1,0:T(8,128)} %get-tuple-element.9, f32[256,384]{1,0:T(8,128)} %get-tuple-element.10, pred[]{:T(512)S(6)} %eq.6), kind=kLoop, calls=%fused_computation.11 | loop fusion | flops 196608 | bytes 1572865 | tf_op jit(solution)/shard_map/jit(_where)/select_n | solution.py:152
  7.6 0.1 collective-permute-start
  7.7 1.7 %collective-permute-done = f32[256,384]{1,0:T(8,128)S(1)} collective-permute-done((f32[256,384]{1,0:T(8,128)S(1)}, f32[256,384]{1,0:T(8,128)S(1)}, u32[]{:S(2)}, u32[]{:S(2)}) %collective-permute-start) | collective-permute-done | bytes 393248 | tf_op jit(solution)/shard_map/ppermute | solution.py:152
  9.4 0.6 convolution_add_fusion.2
  10.0 1.3 %collective-permute-start.1 = (f32[256,384]{1,0:T(8,128)S(1)}, f32[256,384]{1,0:T(8,128)S(1)}, u32[]{:S(2)}, u32[]{:S(2)}) collective-permute-start(f32[256,384]{1,0:T(8,128)S(1)} %convolution_add_fusion.2), channel_id=1, source_target_pairs={{0,2},{2,4},{4,6},{6,8},{8,10},{10,12},{12,14},{3,1},{5,3},{7,5},{... | collective-permute-start | bytes 1179656 | tf_op jit(solution)/shard_map/ppermute | solution.py:141
  11.3 8.1 %collective-permute-done.1 = f32[256,384]{1,0:T(8,128)S(1)} collective-permute-done((f32[256,384]{1,0:T(8,128)S(1)}, f32[256,384]{1,0:T(8,128)S(1)}, u32[]{:S(2)}, u32[]{:S(2)}) %collective-permute-start.1) | collective-permute-done | bytes 393248 | tf_op jit(solution)/shard_map/ppermute | solution.py:141
  19.4 0.6 convolution_add_fusion.1
  20.0 1.3 %collective-permute-start.2 = (f32[256,384]{1,0:T(8,128)S(1)}, f32[256,384]{1,0:T(8,128)S(1)}, u32[]{:S(2)}, u32[]{:S(2)}) collective-permute-start(f32[256,384]{1,0:T(8,128)S(1)} %convolution_add_fusion.1), channel_id=1, source_target_pairs={{0,4},{2,6},{4,8},{6,10},{8,12},{10,14},{5,1},{7,3},{9,5},{11,7},{... | collective-permute-start | bytes 1179656 | tf_op jit(solution)/shard_map/ppermute | solution.py:141
  21.4 11.5 %collective-permute-done.2 = f32[256,384]{1,0:T(8,128)S(1)} collective-permute-done((f32[256,384]{1,0:T(8,128)S(1)}, f32[256,384]{1,0:T(8,128)S(1)}, u32[]{:S(2)}, u32[]{:S(2)}) %collective-permute-start.2) | collective-permute-done | bytes 393248 | tf_op jit(solution)/shard_map/ppermute | solution.py:141
  32.8 0.6 convolution_add_fusion
  33.4 1.3 %collective-permute-start.3 = (f32[256,384]{1,0:T(8,128)S(1)}, f32[256,384]{1,0:T(8,128)S(1)}, u32[]{:S(2)}, u32[]{:S(2)}) collective-permute-start(f32[256,384]{1,0:T(8,128)S(1)} %convolution_add_fusion), channel_id=1, source_target_pairs={{0,2},{2,4},{4,6},{6,8},{8,10},{10,12},{12,14},{3,1},{5,3},{7,5},{... | collective-permute-start | bytes 1179656 | tf_op jit(solution)/shard_map/ppermute | solution.py:141
  34.8 0.0 copy-start.1
  34.8 1.4 %collective-permute-start.4 = (f32[256,128]{1,0:T(8,128)S(1)}, f32[256,128]{1,0:T(8,128)S(1)}, u32[]{:S(2)}, u32[]{:S(2)}) collective-permute-start(f32[256,128]{1,0:T(8,128)S(1)} %slice.51), channel_id=1, source_target_pairs={{0,10},{2,12},{4,14},{11,1},{13,3},{15,5},{16,26},{18,28},{20,30},... | collective-permute-start | bytes 393224 | tf_op jit(solution)/shard_map/ppermute | solution.py:141
  36.2 7.0 %collective-permute-done.4 = f32[256,128]{1,0:T(8,128)S(1)} collective-permute-done((f32[256,128]{1,0:T(8,128)S(1)}, f32[256,128]{1,0:T(8,128)S(1)}, u32[]{:S(2)}, u32[]{:S(2)}) %collective-permute-start.4) | collective-permute-done | bytes 131104 | tf_op jit(solution)/shard_map/ppermute | solution.py:141
  43.2 0.2 collective-permute-done.3
  43.4 0.4 convolution_add_fusion.4.enter_ref
  43.7 0.0 copy-start.2
  43.8 0.4 convolution_add_fusion.3
  44.1 0.2 copy-done.2
  44.4 4.2 %collective-permute-start.5 = (f32[256,128]{1,0:T(8,128)S(1)}, f32[256,128]{1,0:T(8,128)S(1)}, u32[]{:S(2)}, u32[]{:S(2)}) collective-permute-start(f32[256,128]{1,0:T(8,128)S(1)} %convolution_add_fusion.3), channel_id=1, source_target_pairs={{0,1},{2,3},{4,5},{6,7},{8,9},{10,11},{12,13},{14,15},{1,0},{3,2},... | collective-permute-start | bytes 393224 | tf_op jit(solution)/shard_map/ppermute | solution.py:168
  48.6 0.0 copy-done
  48.6 0.0 copy-done.1
  48.6 1.4 %fusion.5.diag_hbm = f32[8,256,128]{2,1,0:T(8,128)} fusion(bf16[8,256,256]{2,1,0:T(8,128)(2,1)S(1)} %copy-done, bf16[8,256,128]{2,1,0:T(8,128)(2,1)S(1)} %copy-done.1), kind=kOutput, calls=%fused_computation.12 | convolution fusion | flops 134217728 | bytes 2621440 | tf_op jit(solution)/shard_map/kab,kbc->kac/dot_general | solution.py:194
  50.0 0.0 collective-permute-done.5.other_ref
  50.0 0.0 copy-start.3
  50.0 0.7 %copy-done.3 = f32[256,128]{1,0:T(8,128)} copy-done((f32[256,128]{1,0:T(8,128)}, f32[256,128]{1,0:T(8,128)S(1)}, u32[]{:S(2)}) %copy-start.3) | copy-done | bytes 131096
  50.6 9.6 %apply.1 = bf16[8,256,128]{2,1,0:T(8,128)(2,1)} custom-call(s32[1]{0:T(128)} %bitcast.flag_ref, f32[256,128]{1,0:T(8,128)} %copy-done.2, f32[256,128]{1,0:T(8,128)} %copy-done.3, bf16[8,256,256]{2,1,0:T(8,128)(2,1)} %ltrans_hbm.1, bf16[8,256,256]{2,1,0:T(8,128)(2,1)} %utrans_hbm.1, f32[8,256,128]{2,1,0:T(8,128)} %get-tuple-element.11.lsrc_hbm, ...), custom_call_target="tpu_custom_call" | custom-call | tf_op jit(solution)/shard_map/apply/pallas_call | solution.py:207
  (4 shorter events, 0.0 us)
Async XLA Ops:
  0.0 48.6 %copy-start = (bf16[8,256,256]{2,1,0:T(8,128)(2,1)S(1)}, bf16[8,256,256]{2,1,0:T(8,128)(2,1)}, u32[]{:S(2)}) copy-start(bf16[8,256,256]{2,1,0:T(8,128)(2,1)} %param.9) | copy-start | bytes 3145732
  7.6 1.8 %collective-permute-start = (f32[256,384]{1,0:T(8,128)S(1)}, f32[256,384]{1,0:T(8,128)S(1)}, u32[]{:S(2)}, u32[]{:S(2)}) collective-permute-start(f32[256,384]{1,0:T(8,128)S(1)} %get-tuple-element.13), channel_id=1, source_target_pairs={{0,1},{2,3},{4,5},{6,7},{8,9},{10,11},{12,13},{14,15},{1,0},{3,2},... | collective-permute-start | bytes 1179656 | tf_op jit(solution)/shard_map/ppermute | solution.py:152
  10.0 9.4 %collective-permute-start.1 = (f32[256,384]{1,0:T(8,128)S(1)}, f32[256,384]{1,0:T(8,128)S(1)}, u32[]{:S(2)}, u32[]{:S(2)}) collective-permute-start(f32[256,384]{1,0:T(8,128)S(1)} %convolution_add_fusion.2), channel_id=1, source_target_pairs={{0,2},{2,4},{4,6},{6,8},{8,10},{10,12},{12,14},{3,1},{5,3},{7,5},{... | collective-permute-start | bytes 1179656 | tf_op jit(solution)/shard_map/ppermute | solution.py:141
  20.0 12.8 %collective-permute-start.2 = (f32[256,384]{1,0:T(8,128)S(1)}, f32[256,384]{1,0:T(8,128)S(1)}, u32[]{:S(2)}, u32[]{:S(2)}) collective-permute-start(f32[256,384]{1,0:T(8,128)S(1)} %convolution_add_fusion.1), channel_id=1, source_target_pairs={{0,4},{2,6},{4,8},{6,10},{8,12},{10,14},{5,1},{7,3},{9,5},{11,7},{... | collective-permute-start | bytes 1179656 | tf_op jit(solution)/shard_map/ppermute | solution.py:141
  33.4 9.9 %collective-permute-start.3 = (f32[256,384]{1,0:T(8,128)S(1)}, f32[256,384]{1,0:T(8,128)S(1)}, u32[]{:S(2)}, u32[]{:S(2)}) collective-permute-start(f32[256,384]{1,0:T(8,128)S(1)} %convolution_add_fusion), channel_id=1, source_target_pairs={{0,2},{2,4},{4,6},{6,8},{8,10},{10,12},{12,14},{3,1},{5,3},{7,5},{... | collective-permute-start | bytes 1179656 | tf_op jit(solution)/shard_map/ppermute | solution.py:141
  34.8 13.8 %copy-start.1 = (bf16[8,256,128]{2,1,0:T(8,128)(2,1)S(1)}, bf16[8,256,128]{2,1,0:T(8,128)(2,1)}, u32[]{:S(2)}) copy-start(bf16[8,256,128]{2,1,0:T(8,128)(2,1)} %rhs_ref.1) | copy-start | bytes 1572868
  34.8 8.4 %collective-permute-start.4 = (f32[256,128]{1,0:T(8,128)S(1)}, f32[256,128]{1,0:T(8,128)S(1)}, u32[]{:S(2)}, u32[]{:S(2)}) collective-permute-start(f32[256,128]{1,0:T(8,128)S(1)} %slice.51), channel_id=1, source_target_pairs={{0,10},{2,12},{4,14},{11,1},{13,3},{15,5},{16,26},{18,28},{20,30},... | collective-permute-start | bytes 393224 | tf_op jit(solution)/shard_map/ppermute | solution.py:141
  43.7 0.6 %copy-start.2 = (f32[256,128]{1,0:T(8,128)}, f32[256,128]{1,0:T(8,128)S(1)}, u32[]{:S(2)}) copy-start(f32[256,128]{1,0:T(8,128)S(1)} %convolution_add_fusion.4.enter_ref) | copy-start | bytes 393220
  44.4 5.6 %collective-permute-start.5 = (f32[256,128]{1,0:T(8,128)S(1)}, f32[256,128]{1,0:T(8,128)S(1)}, u32[]{:S(2)}, u32[]{:S(2)}) collective-permute-start(f32[256,128]{1,0:T(8,128)S(1)} %convolution_add_fusion.3), channel_id=1, source_target_pairs={{0,1},{2,3},{4,5},{6,7},{8,9},{10,11},{12,13},{14,15},{1,0},{3,2},... | collective-permute-start | bytes 393224 | tf_op jit(solution)/shard_map/ppermute | solution.py:168
  50.0 0.7 %copy-start.3 = (f32[256,128]{1,0:T(8,128)}, f32[256,128]{1,0:T(8,128)S(1)}, u32[]{:S(2)}) copy-start(f32[256,128]{1,0:T(8,128)S(1)} %collective-permute-done.5.other_ref) | copy-start | bytes 393220

commit v9 on v6

--- a/solution.py
+++ b/solution.py
@@ -135,6 +135,53 @@
     return enter, other
 
 
+def group_shift(value, axis, groups, shift):
+    pairs = [(4 * g + 2, 4 * (g + shift) + 2) for g in range(groups - shift)]
+    pairs += [(4 * g + 1, 4 * (g - shift) + 1) for g in range(shift, groups)]
+    return lax.ppermute(value, axis, pairs)
+
+
+def scan_groups(own, give, axis):
+    count = lax.axis_size(axis)
+    groups = count // 4
+    rank = own.shape[0]
+    place = lax.axis_index(axis) % 4
+    zeros = jnp.zeros((rank, rank), F32)
+    partner = [(2 * c, 2 * c + 1) for c in range(count // 2)]
+    partner += [(2 * c + 1, 2 * c) for c in range(count // 2)]
+    got = lax.ppermute(give, axis, partner)
+    both = jnp.dot(got[:, :rank], own, precision=HIGHEST) + jnp.concatenate(
+        [zeros, got[:, rank:]], axis=1
+    )
+    pair = [(4 * g, 4 * g + 2) for g in range(groups)]
+    pair += [(4 * g + 3, 4 * g + 1) for g in range(groups)]
+    beside = lax.ppermute(both, axis, pair)
+    both = jnp.dot(both[:, :rank], beside, precision=HIGHEST) + jnp.concatenate(
+        [zeros, both[:, rank:]], axis=1
+    )
+    rounds = 0
+    while 2 ** (rounds + 1) < groups - 1:
+        rounds += 1
+    shift = 1
+    for _ in range(rounds):
+        got = group_shift(both, axis, groups, shift)
+        tail = jnp.concatenate([zeros, both[:, rank:]], axis=1)
+        both = jnp.dot(both[:, :rank], got, precision=HIGHEST) + tail
+        shift *= 2
+    near = group_shift(both, axis, groups, 1)
+    far = group_shift(both[:, rank:], axis, groups, 1 + shift)
+    start = jnp.dot(near[:, :rank], far, precision=HIGHEST) + near[:, rank:]
+    back = [(4 * g + 2, 4 * g) for g in range(groups)]
+    back += [(4 * g + 1, 4 * g + 3) for g in range(groups)]
+    sent = lax.ppermute(start, axis, back)
+    mine = jnp.dot(beside[:, :rank], start, precision=HIGHEST) + beside[:, rank:]
+    holder = jnp.logical_or(place == 1, place == 2)
+    enter = jnp.where(holder, mine, sent)
+    send = jnp.dot(own[:, :rank], enter, precision=HIGHEST) + own[:, rank:]
+    other = lax.ppermute(send, axis, partner)
+    return enter, other
+
+
 def shards(
     right_sides,
     diagonal_blocks,
@@ -161,7 +208,13 @@
         "kab,kbc->kac", diagonal_blocks, right_sides, preferred_element_type=F32
     )
     count_row = lax.axis_size("row")
-    if count_row % 2 == 0 and count_row >= 4:
+    if count_row % 4 == 0 and count_row >= 8:
+        first = lax.axis_index("row") % 2 == 0
+        enter, other = scan_groups(
+            jnp.where(first, lboth, uboth), jnp.where(first, uboth, lboth), "row"
+        )
+        flag = jnp.full((1,), lax.axis_index("row") % 2, jnp.int32)
+    elif count_row % 2 == 0 and count_row >= 4:
         enter, other = scan_chips(lboth, uboth, "row")
         flag = jnp.full((1,), lax.axis_index("row") % 2, jnp.int32)
     else:

time: 57.3 us -> 58 us (1.012)
    ppermute x6 -> x7, starting transfers between devices: 9.56 us -> 10 us  [the longest x3 3.88 us: group_shift(): return lax.ppermute(value, axis, pairs)]
    dot_general x5 -> x6, matrix products: 2.55 us -> 2.93 us  [the longest x1 0.6 us: scan_groups(): jnp.dot(got[:, :rank], own, precision=HIGHEST)]
    ppermute x6 -> x7, waiting for transfers between devices: 28.5 us -> 28.5 us  [the longest x3 17.4 us: group_shift(): return lax.ppermute(value, axis, pairs)]
  transfers between devices with their start and end apart: 6 -> 7, of which waited for: 5 -> 5; matrix products, arithmetic and copies ran while one was open for 3% -> 2% of each run, Pallas kernels for 0% -> 0%
where the time goes in v9:
time: 58 us; the launch traced here: 57.8 us
  waiting for transfers between devices  28.5 us (49%)
  Pallas kernels  12.7 us (22%)
  starting transfers between devices  10 us (17%)
  matrix products  4.32 us (7%)
  other arithmetic  1.17 us (2%)
  local copies, waits for them, and re-layouts  0.96 us (2%)
    ppermute x3, waiting for transfers between devices, group_shift(): return lax.ppermute(value, axis, pairs)  17.4 us
    ppermute x1, waiting for transfers between devices, scan_groups(): beside = lax.ppermute(both, axis, pair)  7.48 us
    pallas_call x1, Pallas kernels, shards(): pl.pallas_call(sweep_kernel, out_shape=(jax.ShapeDtypeStruct((rank, rank...  6.43 us
    pallas_call x1, Pallas kernels, shards(): pl.pallas_call(apply_kernel, out_shape=jax.ShapeDtypeStruct((count, rows,...  6.27 us
    ppermute x3, starting transfers between devices, group_shift(): return lax.ppermute(value, axis, pairs)  3.88 us
    ppermute x1, starting transfers between devices, scan_groups(): other = lax.ppermute(send, axis, partner)  3.46 us
    ppermute x1, waiting for transfers between devices, scan_groups(): sent = lax.ppermute(start, axis, back)  1.89 us
    ppermute x1, waiting for transfers between devices, scan_groups(): got = lax.ppermute(give, axis, partner)  1.71 us
  transfers between devices with their start and end apart: 7, of which 5 were waited for; matrix products, arithmetic and copies ran while one was open for 2% of the time, Pallas kernels for 0%

profile of v9, /device:TPU:1, one launch (start us, length us, event | category | flops | bytes accessed | tf_op | source)
XLA Modules:
  0.0 57.8 jit_solution(11073494325718241049)
XLA Ops:
  0.0 0.0 copy-start
  0.0 6.4 %sweep.1 = (f32[256,384]{1,0:T(8,128)}, f32[8,256,128]{2,1,0:T(8,128)}, f32[256,384]{1,0:T(8,128)}, f32[8,256,128]{2,1,0:T(8,128)}) custom-call(bf16[8,256,128]{2,1,0:T(8,128)(2,1)} %rhs_ref.1, bf16[8,256,256]{2,1,0:T(8,128)(2,1)} %lcols_ref.1, bf16[8,256,256]{2,1,0:T(8,128)(2,1)} %ltrans_ref.3, bf16[8,256,256]{2,1,0:T(8,128)(2,1)} %ucols_ref.1, ...), custom_call_target="tpu_custom_call" | custom-call | tf_op jit(solution)/shard_map/sweep/pallas_call | solution.py:197
  6.4 1.2 %broadcast_select_fusion.1 = (f32[256,384]{1,0:T(8,128)S(1)}, f32[256,384]{1,0:T(8,128)S(1)}) fusion(f32[256,384]{1,0:T(8,128)} %get-tuple-element.9, f32[256,384]{1,0:T(8,128)} %get-tuple-element.10, pred[]{:T(512)S(6)} %eq.15), kind=kLoop, calls=%fused_computation.14 | loop fusion | flops 196608 | bytes 1572865 | tf_op jit(solution)/shard_map/jit(_where)/select_n | solution.py:214
  7.6 0.1 collective-permute-start
  7.7 1.7 %collective-permute-done = f32[256,384]{1,0:T(8,128)S(1)} collective-permute-done((f32[256,384]{1,0:T(8,128)S(1)}, f32[256,384]{1,0:T(8,128)S(1)}, u32[]{:S(2)}, u32[]{:S(2)}) %collective-permute-start) | collective-permute-done | bytes 393248 | tf_op jit(solution)/shard_map/ppermute | solution.py:152
  9.4 0.6 %convolution_add_fusion.2 = f32[256,384]{1,0:T(8,128)S(1)} fusion(f32[256,384]{1,0:T(8,128)S(1)} %get-tuple-element.14, f32[256,128]{1,0:T(8,128)S(1)} %slice.53, f32[256,384]{1,0:T(8,128)S(1)} %collective-permute-done), kind=kOutput, calls=%fused_computation.2 | convolution fusion | flops 302088192 | bytes 1179648 | tf_op jit(solution)/shard_map/dot_general | solution.py:153
  10.0 1.3 %collective-permute-start.1 = (f32[256,384]{1,0:T(8,128)S(1)}, f32[256,384]{1,0:T(8,128)S(1)}, u32[]{:S(2)}, u32[]{:S(2)}) collective-permute-start(f32[256,384]{1,0:T(8,128)S(1)} %convolution_add_fusion.2), channel_id=1, source_target_pairs={{0,2},{4,6},{8,10},{12,14},{3,1},{7,5},{11,9},{15,13},{16,18},{20,... | collective-permute-start | bytes 1179656 | tf_op jit(solution)/shard_map/ppermute | solution.py:158
  11.3 7.5 %collective-permute-done.1 = f32[256,384]{1,0:T(8,128)S(1)} collective-permute-done((f32[256,384]{1,0:T(8,128)S(1)}, f32[256,384]{1,0:T(8,128)S(1)}, u32[]{:S(2)}, u32[]{:S(2)}) %collective-permute-start.1) | collective-permute-done | bytes 393248 | tf_op jit(solution)/shard_map/ppermute | solution.py:158
  18.8 0.6 %convolution_add_fusion.1 = f32[256,384]{1,0:T(8,128)S(1)} fusion(f32[256,384]{1,0:T(8,128)S(1)} %collective-permute-done.1, f32[256,128]{1,0:T(8,128)S(1)} %slice.56, f32[256,384]{1,0:T(8,128)S(1)} %convolution_add_fusion.2), kind=kOutput, calls=%fused_computation.1 | convolution fusion | flops 302088192 | bytes 1179648 | tf_op jit(solution)/shard_map/dot_general | solution.py:159
  19.4 1.3 %collective-permute-start.2 = (f32[256,384]{1,0:T(8,128)S(1)}, f32[256,384]{1,0:T(8,128)S(1)}, u32[]{:S(2)}, u32[]{:S(2)}) collective-permute-start(f32[256,384]{1,0:T(8,128)S(1)} %convolution_add_fusion.1), channel_id=1, source_target_pairs={{2,6},{6,10},{10,14},{5,1},{9,5},{13,9},{18,22},{22,26},{26,30},{2... | collective-permute-start | bytes 1179656 | tf_op jit(solution)/shard_map/ppermute | solution.py:141
  20.7 7.9 %collective-permute-done.2 = f32[256,384]{1,0:T(8,128)S(1)} collective-permute-done((f32[256,384]{1,0:T(8,128)S(1)}, f32[256,384]{1,0:T(8,128)S(1)}, u32[]{:S(2)}, u32[]{:S(2)}) %collective-permute-start.2) | collective-permute-done | bytes 393248 | tf_op jit(solution)/shard_map/ppermute | solution.py:141
  28.6 0.6 %convolution_add_fusion = f32[256,384]{1,0:T(8,128)S(1)} fusion(f32[256,384]{1,0:T(8,128)S(1)} %collective-permute-done.2, f32[256,128]{1,0:T(8,128)S(1)} %slice.58, f32[256,384]{1,0:T(8,128)S(1)} %convolution_add_fusion.1), kind=kOutput, calls=%fused_computation | convolution fusion | flops 302088192 | bytes 1179648 | tf_op jit(solution)/shard_map/dot_general | solution.py:169
  29.2 1.3 %collective-permute-start.3 = (f32[256,384]{1,0:T(8,128)S(1)}, f32[256,384]{1,0:T(8,128)S(1)}, u32[]{:S(2)}, u32[]{:S(2)}) collective-permute-start(f32[256,384]{1,0:T(8,128)S(1)} %convolution_add_fusion), channel_id=1, source_target_pairs={{2,6},{6,10},{10,14},{5,1},{9,5},{13,9},{18,22},{22,26},{26,30},{2... | collective-permute-start | bytes 1179656 | tf_op jit(solution)/shard_map/ppermute | solution.py:141
  30.5 1.3 %collective-permute-start.4 = (f32[256,128]{1,0:T(8,128)S(1)}, f32[256,128]{1,0:T(8,128)S(1)}, u32[]{:S(2)}, u32[]{:S(2)}) collective-permute-start(f32[256,128]{1,0:T(8,128)S(1)} %slice.60), channel_id=1, source_target_pairs={{2,14},{13,1},{18,30},{29,17}} | collective-permute-start | bytes 393224 | tf_op jit(solution)/shard_map/ppermute | solution.py:141
  31.8 9.5 %collective-permute-done.4 = f32[256,128]{1,0:T(8,128)S(1)} collective-permute-done((f32[256,128]{1,0:T(8,128)S(1)}, f32[256,128]{1,0:T(8,128)S(1)}, u32[]{:S(2)}, u32[]{:S(2)}) %collective-permute-start.4) | collective-permute-done | bytes 131104 | tf_op jit(solution)/shard_map/ppermute | solution.py:141
  41.3 0.0 collective-permute-done.3
  41.3 0.4 convolution_add_fusion.5
  41.7 1.3 %collective-permute-start.5 = (f32[256,128]{1,0:T(8,128)S(1)}, f32[256,128]{1,0:T(8,128)S(1)}, u32[]{:S(2)}, u32[]{:S(2)}) collective-permute-start(f32[256,128]{1,0:T(8,128)S(1)} %convolution_add_fusion.5), channel_id=1, source_target_pairs={{2,0},{6,4},{10,8},{14,12},{1,3},{5,7},{9,11},{13,15},{18,16},{22,... | collective-permute-start | bytes 393224 | tf_op jit(solution)/shard_map/ppermute | solution.py:176
  43.0 0.0 copy-start.1
  43.1 1.9 %collective-permute-done.5 = f32[256,128]{1,0:T(8,128)S(1)} collective-permute-done((f32[256,128]{1,0:T(8,128)S(1)}, f32[256,128]{1,0:T(8,128)S(1)}, u32[]{:S(2)}, u32[]{:S(2)}) %collective-permute-start.5) | collective-permute-done | bytes 131104 | tf_op jit(solution)/shard_map/ppermute | solution.py:176
  45.0 0.4 fusion.enter_ref
  45.3 0.0 copy-start.2
  45.3 0.4 convolution_add_fusion.3
  45.7 0.3 copy-done.2
  46.0 3.5 %collective-permute-start.6 = (f32[256,128]{1,0:T(8,128)S(1)}, f32[256,128]{1,0:T(8,128)S(1)}, u32[]{:S(2)}, u32[]{:S(2)}) collective-permute-start(f32[256,128]{1,0:T(8,128)S(1)} %convolution_add_fusion.3), channel_id=1, source_target_pairs={{0,1},{2,3},{4,5},{6,7},{8,9},{10,11},{12,13},{14,15},{1,0},{3,2},... | collective-permute-start | bytes 393224 | tf_op jit(solution)/shard_map/ppermute | solution.py:181
  49.4 0.0 copy-done
  49.4 0.0 copy-done.1
  49.5 1.4 %fusion.7.diag_ref = f32[8,256,128]{2,1,0:T(8,128)} fusion(bf16[8,256,256]{2,1,0:T(8,128)(2,1)S(1)} %copy-done, bf16[8,256,128]{2,1,0:T(8,128)(2,1)S(1)} %copy-done.1), kind=kOutput, calls=%fused_computation.15 | convolution fusion | flops 134217728 | bytes 2621440 | tf_op jit(solution)/shard_map/kab,kbc->kac/dot_general | solution.py:207
  50.8 0.0 collective-permute-done.6.other_ref
  50.9 0.0 copy-start.3
  50.9 0.6 %copy-done.3 = f32[256,128]{1,0:T(8,128)} copy-done((f32[256,128]{1,0:T(8,128)}, f32[256,128]{1,0:T(8,128)S(1)}, u32[]{:S(2)}) %copy-start.3) | copy-done | bytes 131096
  51.5 6.3 %apply.1 = bf16[8,256,128]{2,1,0:T(8,128)(2,1)} custom-call(s32[1]{0:T(128)} %bitcast.flag_ref, f32[256,128]{1,0:T(8,128)} %copy-done.2, f32[256,128]{1,0:T(8,128)} %copy-done.3, bf16[8,256,256]{2,1,0:T(8,128)(2,1)} %ltrans_ref.3, bf16[8,256,256]{2,1,0:T(8,128)(2,1)} %utrans_ref.3, f32[8,256,128]{2,1,0:T(8,128)} %get-tuple-element.11.lsrc_ref, ...), custom_call_target="tpu_custom_call" | custom-call | tf_op jit(solution)/shard_map/apply/pallas_call | solution.py:225
  (4 shorter events, 0.0 us)
Async XLA Ops:
  0.0 49.4 %copy-start = (bf16[8,256,256]{2,1,0:T(8,128)(2,1)S(1)}, bf16[8,256,256]{2,1,0:T(8,128)(2,1)}, u32[]{:S(2)}) copy-start(bf16[8,256,256]{2,1,0:T(8,128)(2,1)} %param.9) | copy-start | bytes 3145732
  7.6 1.8 %collective-permute-start = (f32[256,384]{1,0:T(8,128)S(1)}, f32[256,384]{1,0:T(8,128)S(1)}, u32[]{:S(2)}, u32[]{:S(2)}) collective-permute-start(f32[256,384]{1,0:T(8,128)S(1)} %get-tuple-element.13), channel_id=1, source_target_pairs={{0,1},{2,3},{4,5},{6,7},{8,9},{10,11},{12,13},{14,15},{1,0},{3,2},... | collective-permute-start | bytes 1179656 | tf_op jit(solution)/shard_map/ppermute | solution.py:152
  10.0 8.8 %collective-permute-start.1 = (f32[256,384]{1,0:T(8,128)S(1)}, f32[256,384]{1,0:T(8,128)S(1)}, u32[]{:S(2)}, u32[]{:S(2)}) collective-permute-start(f32[256,384]{1,0:T(8,128)S(1)} %convolution_add_fusion.2), channel_id=1, source_target_pairs={{0,2},{4,6},{8,10},{12,14},{3,1},{7,5},{11,9},{15,13},{16,18},{20,... | collective-permute-start | bytes 1179656 | tf_op jit(solution)/shard_map/ppermute | solution.py:158
  19.4 9.2 %collective-permute-start.2 = (f32[256,384]{1,0:T(8,128)S(1)}, f32[256,384]{1,0:T(8,128)S(1)}, u32[]{:S(2)}, u32[]{:S(2)}) collective-permute-start(f32[256,384]{1,0:T(8,128)S(1)} %convolution_add_fusion.1), channel_id=1, source_target_pairs={{2,6},{6,10},{10,14},{5,1},{9,5},{13,9},{18,22},{22,26},{26,30},{2... | collective-permute-start | bytes 1179656 | tf_op jit(solution)/shard_map/ppermute | solution.py:141
  29.2 12.1 %collective-permute-start.3 = (f32[256,384]{1,0:T(8,128)S(1)}, f32[256,384]{1,0:T(8,128)S(1)}, u32[]{:S(2)}, u32[]{:S(2)}) collective-permute-start(f32[256,384]{1,0:T(8,128)S(1)} %convolution_add_fusion), channel_id=1, source_target_pairs={{2,6},{6,10},{10,14},{5,1},{9,5},{13,9},{18,22},{22,26},{26,30},{2... | collective-permute-start | bytes 1179656 | tf_op jit(solution)/shard_map/ppermute | solution.py:141
  30.5 10.8 %collective-permute-start.4 = (f32[256,128]{1,0:T(8,128)S(1)}, f32[256,128]{1,0:T(8,128)S(1)}, u32[]{:S(2)}, u32[]{:S(2)}) collective-permute-start(f32[256,128]{1,0:T(8,128)S(1)} %slice.60), channel_id=1, source_target_pairs={{2,14},{13,1},{18,30},{29,17}} | collective-permute-start | bytes 393224 | tf_op jit(solution)/shard_map/ppermute | solution.py:141
  41.7 3.2 %collective-permute-start.5 = (f32[256,128]{1,0:T(8,128)S(1)}, f32[256,128]{1,0:T(8,128)S(1)}, u32[]{:S(2)}, u32[]{:S(2)}) collective-permute-start(f32[256,128]{1,0:T(8,128)S(1)} %convolution_add_fusion.5), channel_id=1, source_target_pairs={{2,0},{6,4},{10,8},{14,12},{1,3},{5,7},{9,11},{13,15},{18,16},{22,... | collective-permute-start | bytes 393224 | tf_op jit(solution)/shard_map/ppermute | solution.py:176
  43.0 6.4 %copy-start.1 = (bf16[8,256,128]{2,1,0:T(8,128)(2,1)S(1)}, bf16[8,256,128]{2,1,0:T(8,128)(2,1)}, u32[]{:S(2)}) copy-start(bf16[8,256,128]{2,1,0:T(8,128)(2,1)} %rhs_ref.1) | copy-start | bytes 1572868
  45.3 0.7 %copy-start.2 = (f32[256,128]{1,0:T(8,128)}, f32[256,128]{1,0:T(8,128)S(1)}, u32[]{:S(2)}) copy-start(f32[256,128]{1,0:T(8,128)S(1)} %fusion.enter_ref) | copy-start | bytes 393220
  46.0 4.9 %collective-permute-start.6 = (f32[256,128]{1,0:T(8,128)S(1)}, f32[256,128]{1,0:T(8,128)S(1)}, u32[]{:S(2)}, u32[]{:S(2)}) collective-permute-start(f32[256,128]{1,0:T(8,128)S(1)} %convolution_add_fusion.3), channel_id=1, source_target_pairs={{0,1},{2,3},{4,5},{6,7},{8,9},{10,11},{12,13},{14,15},{1,0},{3,2},... | collective-permute-start | bytes 393224 | tf_op jit(solution)/shard_map/ppermute | solution.py:181
  50.9 0.7 %copy-start.3 = (f32[256,128]{1,0:T(8,128)}, f32[256,128]{1,0:T(8,128)S(1)}, u32[]{:S(2)}) copy-start(f32[256,128]{1,0:T(8,128)S(1)} %collective-permute-done.6.other_ref) | copy-start | bytes 393220

commit v10 on v9

--- a/solution.py
+++ b/solution.py
@@ -159,18 +159,25 @@
     both = jnp.dot(both[:, :rank], beside, precision=HIGHEST) + jnp.concatenate(
         [zeros, both[:, rank:]], axis=1
     )
-    rounds = 0
-    while 2 ** (rounds + 1) < groups - 1:
-        rounds += 1
-    shift = 1
-    for _ in range(rounds):
-        got = group_shift(both, axis, groups, shift)
-        tail = jnp.concatenate([zeros, both[:, rank:]], axis=1)
-        both = jnp.dot(both[:, :rank], got, precision=HIGHEST) + tail
-        shift *= 2
-    near = group_shift(both, axis, groups, 1)
-    far = group_shift(both[:, rank:], axis, groups, 1 + shift)
-    start = jnp.dot(near[:, :rank], far, precision=HIGHEST) + near[:, rank:]
+    if groups <= 4:
+        out = both[:, rank:]
+        for step in range(groups - 1):
+            start = group_shift(out, axis, groups, 1)
+            if step + 2 < groups:
+                out = jnp.dot(both[:, :rank], start, precision=HIGHEST) + both[:, rank:]
+    else:
+        rounds = 0
+        while 2 ** (rounds + 1) < groups - 1:
+            rounds += 1
+        shift = 1
+        for _ in range(rounds):
+            got = group_shift(both, axis, groups, shift)
+            tail = jnp.concatenate([zeros, both[:, rank:]], axis=1)
+            both = jnp.dot(both[:, :rank], got, precision=HIGHEST) + tail
+            shift *= 2
+        near = group_shift(both, axis, groups, 1)
+        far = group_shift(both[:, rank:], axis, groups, 1 + shift)
+        start = jnp.dot(near[:, :rank], far, precision=HIGHEST) + near[:, rank:]
     back = [(4 * g + 2, 4 * g) for g in range(groups)]
     back += [(4 * g + 1, 4 * g + 3) for g in range(groups)]
     sent = lax.ppermute(start, axis, back)

time: 58 us -> 57.6 us (level)
  waiting for transfers between devices: 28.5 us -> 25 us
  starting transfers between devices: 10 us -> 13.3 us
    ppermute x3, waiting for transfers between devices: 17.4 us -> 13.9 us  [group_shift(): return lax.ppermute(value, axis, pairs)]
    ppermute x1, starting transfers between devices: 3.46 us -> 6.77 us  [scan_groups(): other = lax.ppermute(send, axis, partner)]
  transfers between devices with their start and end apart: 7 -> 7, of which waited for: 5 -> 6; matrix products, arithmetic and copies ran while one was open for 2% -> 2% of each run, Pallas kernels for 0% -> 0%
where the time goes in v10:
time: 57.6 us; the launch traced here: 57.4 us
  waiting for transfers between devices  25 us (43%)
  starting transfers between devices  13.3 us (23%)
  Pallas kernels  12.7 us (22%)
  matrix products  4.1 us (7%)
  other arithmetic  1.17 us (2%)
  local copies, waits for them, and re-layouts  0.95 us (2%)
    ppermute x3, waiting for transfers between devices, group_shift(): return lax.ppermute(value, axis, pairs)  13.9 us
    ppermute x1, waiting for transfers between devices, scan_groups(): beside = lax.ppermute(both, axis, pair)  7.48 us
    ppermute x1, starting transfers between devices, scan_groups(): other = lax.ppermute(send, axis, partner)  6.77 us
    pallas_call x1, Pallas kernels, shards(): pl.pallas_call(sweep_kernel, out_shape=(jax.ShapeDtypeStruct((rank, rank...  6.43 us
    pallas_call x1, Pallas kernels, shards(): pl.pallas_call(apply_kernel, out_shape=jax.ShapeDtypeStruct((count, rows,...  6.27 us
    ppermute x3, starting transfers between devices, group_shift(): return lax.ppermute(value, axis, pairs)  3.88 us
    ppermute x1, waiting for transfers between devices, scan_groups(): sent = lax.ppermute(start, axis, back)  1.89 us
    ppermute x1, waiting for transfers between devices, scan_groups(): got = lax.ppermute(give, axis, partner)  1.71 us
  transfers between devices with their start and end apart: 7, of which 6 were waited for; matrix products, arithmetic and copies ran while one was open for 2% of the time, Pallas kernels for 0%

profile of v10, /device:TPU:1, one launch (start us, length us, event | category | flops | bytes accessed | tf_op | source)
XLA Modules:
  0.0 57.4 jit_solution(10826213409935711408)
XLA Ops:
  0.0 0.0 copy-start
  0.0 6.4 %sweep.1 = (f32[256,384]{1,0:T(8,128)}, f32[8,256,128]{2,1,0:T(8,128)}, f32[256,384]{1,0:T(8,128)}, f32[8,256,128]{2,1,0:T(8,128)}) custom-call(bf16[8,256,128]{2,1,0:T(8,128)(2,1)} %rhs_ref.1, bf16[8,256,256]{2,1,0:T(8,128)(2,1)} %lcols_ref.1, bf16[8,256,256]{2,1,0:T(8,128)(2,1)} %ltrans_ref.3, bf16[8,256,256]{2,1,0:T(8,128)(2,1)} %ucols_ref.1, ...), custom_call_target="tpu_custom_call" | custom-call | tf_op jit(solution)/shard_map/sweep/pallas_call | solution.py:204
  6.4 1.2 %broadcast_select_fusion.1 = (f32[256,384]{1,0:T(8,128)S(1)}, f32[256,384]{1,0:T(8,128)S(1)}) fusion(f32[256,384]{1,0:T(8,128)} %get-tuple-element.9, f32[256,384]{1,0:T(8,128)} %get-tuple-element.10, pred[]{:T(512)S(6)} %eq.15), kind=kLoop, calls=%fused_computation.14 | loop fusion | flops 196608 | bytes 1572865 | tf_op jit(solution)/shard_map/jit(_where)/select_n | solution.py:221
  7.6 0.1 collective-permute-start
  7.7 1.7 %collective-permute-done = f32[256,384]{1,0:T(8,128)S(1)} collective-permute-done((f32[256,384]{1,0:T(8,128)S(1)}, f32[256,384]{1,0:T(8,128)S(1)}, u32[]{:S(2)}, u32[]{:S(2)}) %collective-permute-start) | collective-permute-done | bytes 393248 | tf_op jit(solution)/shard_map/ppermute | solution.py:152
  9.4 0.6 %convolution_add_fusion.1 = f32[256,384]{1,0:T(8,128)S(1)} fusion(f32[256,384]{1,0:T(8,128)S(1)} %get-tuple-element.14, f32[256,128]{1,0:T(8,128)S(1)} %slice.44, f32[256,384]{1,0:T(8,128)S(1)} %collective-permute-done), kind=kOutput, calls=%fused_computation.1 | convolution fusion | flops 302088192 | bytes 1179648 | tf_op jit(solution)/shard_map/dot_general | solution.py:153
  10.0 1.3 %collective-permute-start.1 = (f32[256,384]{1,0:T(8,128)S(1)}, f32[256,384]{1,0:T(8,128)S(1)}, u32[]{:S(2)}, u32[]{:S(2)}) collective-permute-start(f32[256,384]{1,0:T(8,128)S(1)} %convolution_add_fusion.1), channel_id=1, source_target_pairs={{0,2},{4,6},{8,10},{12,14},{3,1},{7,5},{11,9},{15,13},{16,18},{20,... | collective-permute-start | bytes 1179656 | tf_op jit(solution)/shard_map/ppermute | solution.py:158
  11.3 7.5 %collective-permute-done.1 = f32[256,384]{1,0:T(8,128)S(1)} collective-permute-done((f32[256,384]{1,0:T(8,128)S(1)}, f32[256,384]{1,0:T(8,128)S(1)}, u32[]{:S(2)}, u32[]{:S(2)}) %collective-permute-start.1) | collective-permute-done | bytes 393248 | tf_op jit(solution)/shard_map/ppermute | solution.py:158
  18.8 0.6 %convolution_add_fusion = f32[256,384]{1,0:T(8,128)S(1)} fusion(f32[256,384]{1,0:T(8,128)S(1)} %collective-permute-done.1, f32[256,128]{1,0:T(8,128)S(1)} %slice.47, f32[256,384]{1,0:T(8,128)S(1)} %convolution_add_fusion.1), kind=kOutput, calls=%fused_computation | convolution fusion | flops 302088192 | bytes 1179648 | tf_op jit(solution)/shard_map/dot_general | solution.py:159
  19.4 1.3 %collective-permute-start.2 = (f32[256,128]{1,0:T(8,128)S(1)}, f32[256,128]{1,0:T(8,128)S(1)}, u32[]{:S(2)}, u32[]{:S(2)}) collective-permute-start(f32[256,128]{1,0:T(8,128)S(1)} %slice.49), channel_id=1, source_target_pairs={{2,6},{6,10},{10,14},{5,1},{9,5},{13,9},{18,22},{22,26},{26,30},{2... | collective-permute-start | bytes 393224 | tf_op jit(solution)/shard_map/ppermute | solution.py:141
  20.7 5.1 %collective-permute-done.2 = f32[256,128]{1,0:T(8,128)S(1)} collective-permute-done((f32[256,128]{1,0:T(8,128)S(1)}, f32[256,128]{1,0:T(8,128)S(1)}, u32[]{:S(2)}, u32[]{:S(2)}) %collective-permute-start.2) | collective-permute-done | bytes 131104 | tf_op jit(solution)/shard_map/ppermute | solution.py:141
  25.8 0.4 convolution_add_fusion.5
  26.2 1.3 %collective-permute-start.3 = (f32[256,128]{1,0:T(8,128)S(1)}, f32[256,128]{1,0:T(8,128)S(1)}, u32[]{:S(2)}, u32[]{:S(2)}) collective-permute-start(f32[256,128]{1,0:T(8,128)S(1)} %convolution_add_fusion.5), channel_id=1, source_target_pairs={{2,6},{6,10},{10,14},{5,1},{9,5},{13,9},{18,22},{22,26},{26,30},{2... | collective-permute-start | bytes 393224 | tf_op jit(solution)/shard_map/ppermute | solution.py:141
  27.5 4.4 %collective-permute-done.3 = f32[256,128]{1,0:T(8,128)S(1)} collective-permute-done((f32[256,128]{1,0:T(8,128)S(1)}, f32[256,128]{1,0:T(8,128)S(1)}, u32[]{:S(2)}, u32[]{:S(2)}) %collective-permute-start.3) | collective-permute-done | bytes 131104 | tf_op jit(solution)/shard_map/ppermute | solution.py:141
  31.9 0.4 convolution_add_fusion.4
  32.3 1.3 %collective-permute-start.4 = (f32[256,128]{1,0:T(8,128)S(1)}, f32[256,128]{1,0:T(8,128)S(1)}, u32[]{:S(2)}, u32[]{:S(2)}) collective-permute-start(f32[256,128]{1,0:T(8,128)S(1)} %convolution_add_fusion.4), channel_id=1, source_target_pairs={{2,6},{6,10},{10,14},{5,1},{9,5},{13,9},{18,22},{22,26},{26,30},{2... | collective-permute-start | bytes 393224 | tf_op jit(solution)/shard_map/ppermute | solution.py:141
  33.6 4.4 %collective-permute-done.4 = f32[256,128]{1,0:T(8,128)S(1)} collective-permute-done((f32[256,128]{1,0:T(8,128)S(1)}, f32[256,128]{1,0:T(8,128)S(1)}, u32[]{:S(2)}, u32[]{:S(2)}) %collective-permute-start.4) | collective-permute-done | bytes 131104 | tf_op jit(solution)/shard_map/ppermute | solution.py:141
  38.0 1.3 %collective-permute-start.5 = (f32[256,128]{1,0:T(8,128)S(1)}, f32[256,128]{1,0:T(8,128)S(1)}, u32[]{:S(2)}, u32[]{:S(2)}) collective-permute-start(f32[256,128]{1,0:T(8,128)S(1)} %collective-permute-done.4), channel_id=1, source_target_pairs={{2,0},{6,4},{10,8},{14,12},{1,3},{5,7},{9,11},{13,15},{18,16},{22,... | collective-permute-start | bytes 393224 | tf_op jit(solution)/shard_map/ppermute | solution.py:183
  39.3 0.0 copy-start.1
  39.3 1.9 %collective-permute-done.5 = f32[256,128]{1,0:T(8,128)S(1)} collective-permute-done((f32[256,128]{1,0:T(8,128)S(1)}, f32[256,128]{1,0:T(8,128)S(1)}, u32[]{:S(2)}, u32[]{:S(2)}) %collective-permute-start.5) | collective-permute-done | bytes 131104 | tf_op jit(solution)/shard_map/ppermute | solution.py:183
  41.2 0.4 fusion.enter_ref
  41.6 0.0 copy-start.2
  41.6 0.4 convolution_add_fusion.2
  42.0 0.3 copy-done.2
  42.3 6.8 %collective-permute-start.6 = (f32[256,128]{1,0:T(8,128)S(1)}, f32[256,128]{1,0:T(8,128)S(1)}, u32[]{:S(2)}, u32[]{:S(2)}) collective-permute-start(f32[256,128]{1,0:T(8,128)S(1)} %convolution_add_fusion.2), channel_id=1, source_target_pairs={{0,1},{2,3},{4,5},{6,7},{8,9},{10,11},{12,13},{14,15},{1,0},{3,2},... | collective-permute-start | bytes 393224 | tf_op jit(solution)/shard_map/ppermute | solution.py:188
  49.0 0.0 copy-done
  49.1 0.0 copy-done.1
  49.1 1.4 %fusion.7.diag_ref = f32[8,256,128]{2,1,0:T(8,128)} fusion(bf16[8,256,256]{2,1,0:T(8,128)(2,1)S(1)} %copy-done, bf16[8,256,128]{2,1,0:T(8,128)(2,1)S(1)} %copy-done.1), kind=kOutput, calls=%fused_computation.15 | convolution fusion | flops 134217728 | bytes 2621440 | tf_op jit(solution)/shard_map/kab,kbc->kac/dot_general | solution.py:214
  50.5 0.0 collective-permute-done.6.other_ref
  50.5 0.0 copy-start.3
  50.5 0.6 %copy-done.3 = f32[256,128]{1,0:T(8,128)} copy-done((f32[256,128]{1,0:T(8,128)}, f32[256,128]{1,0:T(8,128)S(1)}, u32[]{:S(2)}) %copy-start.3) | copy-done | bytes 131096
  51.1 6.3 %apply.1 = bf16[8,256,128]{2,1,0:T(8,128)(2,1)} custom-call(s32[1]{0:T(128)} %bitcast.flag_ref, f32[256,128]{1,0:T(8,128)} %copy-done.2, f32[256,128]{1,0:T(8,128)} %copy-done.3, bf16[8,256,256]{2,1,0:T(8,128)(2,1)} %ltrans_ref.3, bf16[8,256,256]{2,1,0:T(8,128)(2,1)} %utrans_ref.3, f32[8,256,128]{2,1,0:T(8,128)} %get-tuple-element.11.lsrc_ref, ...), custom_call_target="tpu_custom_call" | custom-call | tf_op jit(solution)/shard_map/apply/pallas_call | solution.py:232
  (3 shorter events, 0.0 us)
Async XLA Ops:
  0.0 49.1 %copy-start = (bf16[8,256,256]{2,1,0:T(8,128)(2,1)S(1)}, bf16[8,256,256]{2,1,0:T(8,128)(2,1)}, u32[]{:S(2)}) copy-start(bf16[8,256,256]{2,1,0:T(8,128)(2,1)} %param.9) | copy-start | bytes 3145732
  7.6 1.8 %collective-permute-start = (f32[256,384]{1,0:T(8,128)S(1)}, f32[256,384]{1,0:T(8,128)S(1)}, u32[]{:S(2)}, u32[]{:S(2)}) collective-permute-start(f32[256,384]{1,0:T(8,128)S(1)} %get-tuple-element.13), channel_id=1, source_target_pairs={{0,1},{2,3},{4,5},{6,7},{8,9},{10,11},{12,13},{14,15},{1,0},{3,2},... | collective-permute-start | bytes 1179656 | tf_op jit(solution)/shard_map/ppermute | solution.py:152
  10.0 8.8 %collective-permute-start.1 = (f32[256,384]{1,0:T(8,128)S(1)}, f32[256,384]{1,0:T(8,128)S(1)}, u32[]{:S(2)}, u32[]{:S(2)}) collective-permute-start(f32[256,384]{1,0:T(8,128)S(1)} %convolution_add_fusion.1), channel_id=1, source_target_pairs={{0,2},{4,6},{8,10},{12,14},{3,1},{7,5},{11,9},{15,13},{16,18},{20,... | collective-permute-start | bytes 1179656 | tf_op jit(solution)/shard_map/ppermute | solution.py:158
  19.4 6.4 %collective-permute-start.2 = (f32[256,128]{1,0:T(8,128)S(1)}, f32[256,128]{1,0:T(8,128)S(1)}, u32[]{:S(2)}, u32[]{:S(2)}) collective-permute-start(f32[256,128]{1,0:T(8,128)S(1)} %slice.49), channel_id=1, source_target_pairs={{2,6},{6,10},{10,14},{5,1},{9,5},{13,9},{18,22},{22,26},{26,30},{2... | collective-permute-start | bytes 393224 | tf_op jit(solution)/shard_map/ppermute | solution.py:141
  26.2 5.7 %collective-permute-start.3 = (f32[256,128]{1,0:T(8,128)S(1)}, f32[256,128]{1,0:T(8,128)S(1)}, u32[]{:S(2)}, u32[]{:S(2)}) collective-permute-start(f32[256,128]{1,0:T(8,128)S(1)} %convolution_add_fusion.5), channel_id=1, source_target_pairs={{2,6},{6,10},{10,14},{5,1},{9,5},{13,9},{18,22},{22,26},{26,30},{2... | collective-permute-start | bytes 393224 | tf_op jit(solution)/shard_map/ppermute | solution.py:141
  32.3 5.7 %collective-permute-start.4 = (f32[256,128]{1,0:T(8,128)S(1)}, f32[256,128]{1,0:T(8,128)S(1)}, u32[]{:S(2)}, u32[]{:S(2)}) collective-permute-start(f32[256,128]{1,0:T(8,128)S(1)} %convolution_add_fusion.4), channel_id=1, source_target_pairs={{2,6},{6,10},{10,14},{5,1},{9,5},{13,9},{18,22},{22,26},{26,30},{2... | collective-permute-start | bytes 393224 | tf_op jit(solution)/shard_map/ppermute | solution.py:141
  38.0 3.2 %collective-permute-start.5 = (f32[256,128]{1,0:T(8,128)S(1)}, f32[256,128]{1,0:T(8,128)S(1)}, u32[]{:S(2)}, u32[]{:S(2)}) collective-permute-start(f32[256,128]{1,0:T(8,128)S(1)} %collective-permute-done.4), channel_id=1, source_target_pairs={{2,0},{6,4},{10,8},{14,12},{1,3},{5,7},{9,11},{13,15},{18,16},{22,... | collective-permute-start | bytes 393224 | tf_op jit(solution)/shard_map/ppermute | solution.py:183
  39.3 9.7 %copy-start.1 = (bf16[8,256,128]{2,1,0:T(8,128)(2,1)S(1)}, bf16[8,256,128]{2,1,0:T(8,128)(2,1)}, u32[]{:S(2)}) copy-start(bf16[8,256,128]{2,1,0:T(8,128)(2,1)} %rhs_ref.1) | copy-start | bytes 1572868
  41.6 0.7 %copy-start.2 = (f32[256,128]{1,0:T(8,128)}, f32[256,128]{1,0:T(8,128)S(1)}, u32[]{:S(2)}) copy-start(f32[256,128]{1,0:T(8,128)S(1)} %fusion.enter_ref) | copy-start | bytes 393220
  42.3 8.2 %collective-permute-start.6 = (f32[256,128]{1,0:T(8,128)S(1)}, f32[256,128]{1,0:T(8,128)S(1)}, u32[]{:S(2)}, u32[]{:S(2)}) collective-permute-start(f32[256,128]{1,0:T(8,128)S(1)} %convolution_add_fusion.2), channel_id=1, source_target_pairs={{0,1},{2,3},{4,5},{6,7},{8,9},{10,11},{12,13},{14,15},{1,0},{3,2},... | collective-permute-start | bytes 393224 | tf_op jit(solution)/shard_map/ppermute | solution.py:188
  50.5 0.7 %copy-start.3 = (f32[256,128]{1,0:T(8,128)}, f32[256,128]{1,0:T(8,128)S(1)}, u32[]{:S(2)}) copy-start(f32[256,128]{1,0:T(8,128)S(1)} %collective-permute-done.6.other_ref) | copy-start | bytes 393220

commit v11 on v10

--- a/solution.py
+++ b/solution.py
@@ -50,27 +50,59 @@
     umap_ref[:, rank:] = ustate
 
 
-def apply_kernel(
-    flag_ref, enter_ref, other_ref, ltrans_ref, utrans_ref, lsrc_ref, usrc_ref,
-    diag_ref, lrows_ref, urows_ref, out_ref, lround_ref, uround_ref,
+def wide_dot(left, right):
+    left_high = left.astype(BF16)
+    left_low = (left - left_high.astype(F32)).astype(BF16)
+    right_high = right.astype(BF16)
+    right_low = (right - right_high.astype(F32)).astype(BF16)
+    total = jnp.dot(left_high, right_high, preferred_element_type=F32)
+    total = total + jnp.dot(left_high, right_low, preferred_element_type=F32)
+    return total + jnp.dot(left_low, right_high, preferred_element_type=F32)
+
+
+def prefix_kernel(
+    ltrans_ref, utrans_ref, lsrc_ref, usrc_ref, lpre_ref, lloc_ref, upre_ref, uloc_ref,
 ):
-    count = ltrans_ref.shape[0]
-    first = flag_ref[0] == 0
-    lstate = jnp.where(first, enter_ref[...], other_ref[...])
-    ustate = jnp.where(first, other_ref[...], enter_ref[...])
+    count, rank, _ = ltrans_ref.shape
+    rows = lax.broadcasted_iota(jnp.int32, (rank, rank), 0)
+    cols = lax.broadcasted_iota(jnp.int32, (rank, rank), 1)
+    eye = jnp.where(rows == cols, 1.0, 0.0).astype(F32)
+    zero = jnp.zeros(lloc_ref.shape[1:], F32)
+    lpre = upre = eye
+    lloc = uloc = zero
     for step in range(count):
         lk = step
         uk = count - 1 - step
-        lround_ref[lk] = lstate.astype(BF16)
-        uround_ref[uk] = ustate.astype(BF16)
+        lpre_ref[lk] = lpre
+        lloc_ref[lk] = lloc
+        upre_ref[uk] = upre
+        uloc_ref[uk] = uloc
         if step + 1 < count:
-            lstate = split_dot(ltrans_ref[lk], lstate) + lsrc_ref[lk]
-            ustate = split_dot(utrans_ref[uk], ustate) + usrc_ref[uk]
-    for k in range(count):
-        total = diag_ref[k]
-        total = total + jnp.dot(lrows_ref[k], lround_ref[k], preferred_element_type=F32)
-        total = total + jnp.dot(urows_ref[k], uround_ref[k], preferred_element_type=F32)
-        out_ref[k] = total.astype(out_ref.dtype)
+            if step == 0:
+                lpre = ltrans_ref[lk].astype(F32)
+                upre = utrans_ref[uk].astype(F32)
+                lloc = lsrc_ref[lk]
+                uloc = usrc_ref[uk]
+            else:
+                lpre = split_dot(ltrans_ref[lk], lpre)
+                upre = split_dot(utrans_ref[uk], upre)
+                lloc = split_dot(ltrans_ref[lk], lloc) + lsrc_ref[lk]
+                uloc = split_dot(utrans_ref[uk], uloc) + usrc_ref[uk]
+
+
+def apply_kernel(
+    flag_ref, enter_ref, other_ref, lpre_ref, lloc_ref, upre_ref, uloc_ref,
+    diag_ref, lrows_ref, urows_ref, out_ref,
+):
+    first = flag_ref[0] == 0
+    lenter = jnp.where(first, enter_ref[...], other_ref[...])
+    uenter = jnp.where(first, other_ref[...], enter_ref[...])
+    lstate = lloc_ref[0] + wide_dot(lpre_ref[0], lenter)
+    ustate = uloc_ref[0] + wide_dot(upre_ref[0], uenter)
+    total = diag_ref[0]
+    total = total + jnp.dot(lrows_ref[0], lstate.astype(BF16), preferred_element_type=F32)
+    total = total + jnp.dot(urows_ref[0], ustate.astype(BF16), preferred_element_type=F32)
+    out_ref[0] = total.astype(out_ref.dtype)
 
 
 def shifted(value, axis, count, shift, reverse):
@@ -229,16 +261,37 @@
         other = scan_enter(uboth[:, :rank], uboth[:, rank:], "row", True)
         flag = jnp.zeros((1,), jnp.int32)
     vmem = pl.BlockSpec(memory_space=pltpu.VMEM)
+    lpre, lloc, upre, uloc = pl.pallas_call(
+        prefix_kernel,
+        out_shape=(
+            jax.ShapeDtypeStruct((count, rank, rank), F32),
+            jax.ShapeDtypeStruct((count, rank, rhs), F32),
+            jax.ShapeDtypeStruct((count, rank, rank), F32),
+            jax.ShapeDtypeStruct((count, rank, rhs), F32),
+        ),
+        name="prefix",
+    )(lower_trans, upper_trans, lsrc, usrc)
+    whole = lambda k: (0, 0)
+    block = lambda k: (k, 0, 0)
     return pl.pallas_call(
         apply_kernel,
         out_shape=jax.ShapeDtypeStruct((count, rows, rhs), BF16),
-        scratch_shapes=[
-            pltpu.VMEM((count, rank, rhs), BF16),
-            pltpu.VMEM((count, rank, rhs), BF16),
+        grid=(count,),
+        in_specs=[
+            pl.BlockSpec(memory_space=pltpu.SMEM),
+            pl.BlockSpec((rank, rhs), whole),
+            pl.BlockSpec((rank, rhs), whole),
+            pl.BlockSpec((1, rank, rank), block),
+            pl.BlockSpec((1, rank, rhs), block),
+            pl.BlockSpec((1, rank, rank), block),
+            pl.BlockSpec((1, rank, rhs), block),
+            pl.BlockSpec((1, rows, rhs), block),
+            pl.BlockSpec((1, rows, rank), block),
+            pl.BlockSpec((1, rows, rank), block),
         ],
-        in_specs=[pl.BlockSpec(memory_space=pltpu.SMEM)] + [vmem] * 9,
+        out_specs=pl.BlockSpec((1, rows, rhs), block),
         name="apply",
-    )(flag, enter, other, lower_trans, upper_trans, lsrc, usrc, diag, lower_rows, upper_rows)
+    )(flag, enter, other, lpre, lloc, upre, uloc, diag, lower_rows, upper_rows)
 
 
 def solution(mesh):

time: 57.6 us -> 67.2 us (1.17)
  Pallas kernels: 12.7 us -> 22.1 us
    pallas_call x0 -> x1, Pallas kernels: none -> 6.56 us  [shards(): pl.pallas_call(prefix_kernel, out_shape=(jax.ShapeDtypeStruct((count, ran...]
    pallas_call x1, Pallas kernels: 6.27 us -> 9.09 us  [shards(): pl.pallas_call(apply_kernel, out_shape=jax.ShapeDtypeStruct((count, rows,...]
  transfers between devices with their start and end apart: 7 -> 7, of which waited for: 6 -> 6; matrix products, arithmetic and copies ran while one was open for 2% -> 2% of each run, Pallas kernels for 0% -> 10%
where the time goes in v11:
time: 67.2 us; the launch traced here: 66.7 us
  waiting for transfers between devices  25 us (37%)
  Pallas kernels  22.1 us (33%)
  starting transfers between devices  13.5 us (20%)
  matrix products  4.12 us (6%)
  other arithmetic  1.17 us (2%)
  local copies, waits for them, and re-layouts  0.69 us (1%)
    ppermute x3, waiting for transfers between devices, group_shift(): return lax.ppermute(value, axis, pairs)  13.9 us
    pallas_call x1, Pallas kernels, shards(): pl.pallas_call(apply_kernel, out_shape=jax.ShapeDtypeStruct((count, rows,...  9.09 us
    ppermute x1, waiting for transfers between devices, scan_groups(): beside = lax.ppermute(both, axis, pair)  7.48 us
    ppermute x1, starting transfers between devices, scan_groups(): other = lax.ppermute(send, axis, partner)  6.83 us
    pallas_call x1, Pallas kernels, shards(): pl.pallas_call(prefix_kernel, out_shape=(jax.ShapeDtypeStruct((count, ran...  6.56 us
    pallas_call x1, Pallas kernels, shards(): pl.pallas_call(sweep_kernel, out_shape=(jax.ShapeDtypeStruct((rank, rank...  6.43 us
    ppermute x3, starting transfers between devices, group_shift(): return lax.ppermute(value, axis, pairs)  3.88 us
    ppermute x1, waiting for transfers between devices, scan_groups(): sent = lax.ppermute(start, axis, back)  1.91 us
  transfers between devices with their start and end apart: 7, of which 6 were waited for; matrix products, arithmetic and copies ran while one was open for 2% of the time, Pallas kernels for 10%

profile of v11, /device:TPU:1, one launch (start us, length us, event | category | flops | bytes accessed | tf_op | source)
XLA Modules:
  0.0 66.7 jit_solution(13415246999877390329)
XLA Ops:
  0.0 0.0 copy-start
  0.0 6.4 %sweep.1 = (f32[256,384]{1,0:T(8,128)}, f32[8,256,128]{2,1,0:T(8,128)}, f32[256,384]{1,0:T(8,128)}, f32[8,256,128]{2,1,0:T(8,128)}) custom-call(bf16[8,256,128]{2,1,0:T(8,128)(2,1)} %rhs_ref.1, bf16[8,256,256]{2,1,0:T(8,128)(2,1)} %lcols_ref.1, bf16[8,256,256]{2,1,0:T(8,128)(2,1)} %ltrans_ref.3, bf16[8,256,256]{2,1,0:T(8,128)(2,1)} %ucols_ref.1, ...), custom_call_target="tpu_custom_call" | custom-call | tf_op jit(solution)/shard_map/sweep/pallas_call | solution.py:236
  6.4 1.2 %broadcast_select_fusion.1 = (f32[256,384]{1,0:T(8,128)S(1)}, f32[256,384]{1,0:T(8,128)S(1)}) fusion(f32[256,384]{1,0:T(8,128)} %get-tuple-element.13, f32[256,384]{1,0:T(8,128)} %get-tuple-element.14, pred[]{:T(512)S(6)} %eq.15), kind=kLoop, calls=%fused_computation.14 | loop fusion | flops 196608 | bytes 1572865 | tf_op jit(solution)/shard_map/jit(_where)/select_n | solution.py:253
  7.6 0.1 collective-permute-start
  7.7 1.7 %collective-permute-done = f32[256,384]{1,0:T(8,128)S(1)} collective-permute-done((f32[256,384]{1,0:T(8,128)S(1)}, f32[256,384]{1,0:T(8,128)S(1)}, u32[]{:S(2)}, u32[]{:S(2)}) %collective-permute-start) | collective-permute-done | bytes 393248 | tf_op jit(solution)/shard_map/ppermute | solution.py:184
  9.4 0.6 convolution_add_fusion.1
  10.0 0.0 copy-start.1
  10.0 1.4 %collective-permute-start.1 = (f32[256,384]{1,0:T(8,128)S(1)}, f32[256,384]{1,0:T(8,128)S(1)}, u32[]{:S(2)}, u32[]{:S(2)}) collective-permute-start(f32[256,384]{1,0:T(8,128)S(1)} %convolution_add_fusion.1), channel_id=1, source_target_pairs={{0,2},{4,6},{8,10},{12,14},{3,1},{7,5},{11,9},{15,13},{16,18},{20,... | collective-permute-start | bytes 1179656 | tf_op jit(solution)/shard_map/ppermute | solution.py:190
  11.5 7.5 %collective-permute-done.1 = f32[256,384]{1,0:T(8,128)S(1)} collective-permute-done((f32[256,384]{1,0:T(8,128)S(1)}, f32[256,384]{1,0:T(8,128)S(1)}, u32[]{:S(2)}, u32[]{:S(2)}) %collective-permute-start.1) | collective-permute-done | bytes 393248 | tf_op jit(solution)/shard_map/ppermute | solution.py:190
  19.0 0.6 convolution_add_fusion
  19.6 1.3 %collective-permute-start.2 = (f32[256,128]{1,0:T(8,128)S(1)}, f32[256,128]{1,0:T(8,128)S(1)}, u32[]{:S(2)}, u32[]{:S(2)}) collective-permute-start(f32[256,128]{1,0:T(8,128)S(1)} %slice.49), channel_id=1, source_target_pairs={{2,6},{6,10},{10,14},{5,1},{9,5},{13,9},{18,22},{22,26},{26,30},{2... | collective-permute-start | bytes 393224 | tf_op jit(solution)/shard_map/ppermute | solution.py:173
  20.9 5.1 %collective-permute-done.2 = f32[256,128]{1,0:T(8,128)S(1)} collective-permute-done((f32[256,128]{1,0:T(8,128)S(1)}, f32[256,128]{1,0:T(8,128)S(1)}, u32[]{:S(2)}, u32[]{:S(2)}) %collective-permute-start.2) | collective-permute-done | bytes 131104 | tf_op jit(solution)/shard_map/ppermute | solution.py:173
  26.0 0.4 convolution_add_fusion.5
  26.4 1.3 %collective-permute-start.3 = (f32[256,128]{1,0:T(8,128)S(1)}, f32[256,128]{1,0:T(8,128)S(1)}, u32[]{:S(2)}, u32[]{:S(2)}) collective-permute-start(f32[256,128]{1,0:T(8,128)S(1)} %convolution_add_fusion.5), channel_id=1, source_target_pairs={{2,6},{6,10},{10,14},{5,1},{9,5},{13,9},{18,22},{22,26},{26,30},{2... | collective-permute-start | bytes 393224 | tf_op jit(solution)/shard_map/ppermute | solution.py:173
  27.7 4.4 %collective-permute-done.3 = f32[256,128]{1,0:T(8,128)S(1)} collective-permute-done((f32[256,128]{1,0:T(8,128)S(1)}, f32[256,128]{1,0:T(8,128)S(1)}, u32[]{:S(2)}, u32[]{:S(2)}) %collective-permute-start.3) | collective-permute-done | bytes 131104 | tf_op jit(solution)/shard_map/ppermute | solution.py:173
  32.1 0.4 convolution_add_fusion.4
  32.5 1.3 %collective-permute-start.4 = (f32[256,128]{1,0:T(8,128)S(1)}, f32[256,128]{1,0:T(8,128)S(1)}, u32[]{:S(2)}, u32[]{:S(2)}) collective-permute-start(f32[256,128]{1,0:T(8,128)S(1)} %convolution_add_fusion.4), channel_id=1, source_target_pairs={{2,6},{6,10},{10,14},{5,1},{9,5},{13,9},{18,22},{22,26},{26,30},{2... | collective-permute-start | bytes 393224 | tf_op jit(solution)/shard_map/ppermute | solution.py:173
  33.8 4.4 %collective-permute-done.4 = f32[256,128]{1,0:T(8,128)S(1)} collective-permute-done((f32[256,128]{1,0:T(8,128)S(1)}, f32[256,128]{1,0:T(8,128)S(1)}, u32[]{:S(2)}, u32[]{:S(2)}) %collective-permute-start.4) | collective-permute-done | bytes 131104 | tf_op jit(solution)/shard_map/ppermute | solution.py:173
  38.2 1.3 %collective-permute-start.5 = (f32[256,128]{1,0:T(8,128)S(1)}, f32[256,128]{1,0:T(8,128)S(1)}, u32[]{:S(2)}, u32[]{:S(2)}) collective-permute-start(f32[256,128]{1,0:T(8,128)S(1)} %collective-permute-done.4), channel_id=1, source_target_pairs={{2,0},{6,4},{10,8},{14,12},{1,3},{5,7},{9,11},{13,15},{18,16},{22,... | collective-permute-start | bytes 393224 | tf_op jit(solution)/shard_map/ppermute | solution.py:215
  39.5 1.9 %collective-permute-done.5 = f32[256,128]{1,0:T(8,128)S(1)} collective-permute-done((f32[256,128]{1,0:T(8,128)S(1)}, f32[256,128]{1,0:T(8,128)S(1)}, u32[]{:S(2)}, u32[]{:S(2)}) %collective-permute-start.5) | collective-permute-done | bytes 131104 | tf_op jit(solution)/shard_map/ppermute | solution.py:215
  41.4 0.4 fusion.enter_ref
  41.8 0.0 copy-start.2
  41.8 0.4 convolution_add_fusion.2
  42.2 6.8 %collective-permute-start.6 = (f32[256,128]{1,0:T(8,128)S(1)}, f32[256,128]{1,0:T(8,128)S(1)}, u32[]{:S(2)}, u32[]{:S(2)}) collective-permute-start(f32[256,128]{1,0:T(8,128)S(1)} %convolution_add_fusion.2), channel_id=1, source_target_pairs={{0,1},{2,3},{4,5},{6,7},{8,9},{10,11},{12,13},{14,15},{1,0},{3,2},... | collective-permute-start | bytes 393224 | tf_op jit(solution)/shard_map/ppermute | solution.py:220
  49.0 0.0 copy-done
  49.0 0.0 copy-done.1
  49.0 1.4 %fusion.7.diag_ref = f32[8,256,128]{2,1,0:T(8,128)} fusion(bf16[8,256,256]{2,1,0:T(8,128)(2,1)S(1)} %copy-done, bf16[8,256,128]{2,1,0:T(8,128)(2,1)S(1)} %copy-done.1), kind=kOutput, calls=%fused_computation.15 | convolution fusion | flops 134217728 | bytes 2621440 | tf_op jit(solution)/shard_map/kab,kbc->kac/dot_general | solution.py:246
  50.4 6.6 %prefix.1 = (f32[8,256,256]{2,1,0:T(8,128)}, f32[8,256,128]{2,1,0:T(8,128)}, f32[8,256,256]{2,1,0:T(8,128)}, f32[8,256,128]{2,1,0:T(8,128)}) custom-call(bf16[8,256,256]{2,1,0:T(8,128)(2,1)} %ltrans_ref.3, bf16[8,256,256]{2,1,0:T(8,128)(2,1)} %utrans_ref.3, f32[8,256,128]{2,1,0:T(8,128)} %get-tuple-element.15.lsrc_ref, f32[8,256,128]{2,1,0:T(8,128)} %get-tuple-element.16.usrc_ref), custom_call_target="tpu_custom_call" | custom-call | tf_op jit(solution)/shard_map/prefix/pallas_call | solution.py:264
  57.0 0.0 copy-done.2
  57.0 0.0 collective-permute-done.6.other_ref
  57.0 0.0 copy-start.3
  57.0 0.6 copy-done.3
  57.6 9.1 %apply.1 = bf16[8,256,128]{2,1,0:T(8,128)(2,1)} custom-call(s32[1]{0:T(128)} %bitcast.flag_ref, f32[256,128]{1,0:T(8,128)} %copy-done.2, f32[256,128]{1,0:T(8,128)} %copy-done.3, f32[8,256,256]{2,1,0:T(8,128)} %get-tuple-element.17.lpre_ref, f32[8,256,128]{2,1,0:T(8,128)} %get-tuple-element.18.lloc_ref, f32[8,256,256]{2,1,0:T(8,128)} %get-tuple-element.19.upre_ref, ...), custom_call_target="tpu_custom_call" | custom-call | tf_op jit(solution)/shard_map/apply/pallas_call | solution.py:276
  (3 shorter events, 0.0 us)
Async XLA Ops:
  0.0 49.0 %copy-start = (bf16[8,256,256]{2,1,0:T(8,128)(2,1)S(1)}, bf16[8,256,256]{2,1,0:T(8,128)(2,1)}, u32[]{:S(2)}) copy-start(bf16[8,256,256]{2,1,0:T(8,128)(2,1)} %param.9) | copy-start | bytes 3145732
  7.6 1.8 %collective-permute-start = (f32[256,384]{1,0:T(8,128)S(1)}, f32[256,384]{1,0:T(8,128)S(1)}, u32[]{:S(2)}, u32[]{:S(2)}) collective-permute-start(f32[256,384]{1,0:T(8,128)S(1)} %get-tuple-element.21), channel_id=1, source_target_pairs={{0,1},{2,3},{4,5},{6,7},{8,9},{10,11},{12,13},{14,15},{1,0},{3,2},... | collective-permute-start | bytes 1179656 | tf_op jit(solution)/shard_map/ppermute | solution.py:184
  10.0 39.0 %copy-start.1 = (bf16[8,256,128]{2,1,0:T(8,128)(2,1)S(1)}, bf16[8,256,128]{2,1,0:T(8,128)(2,1)}, u32[]{:S(2)}) copy-start(bf16[8,256,128]{2,1,0:T(8,128)(2,1)} %rhs_ref.1) | copy-start | bytes 1572868
  10.0 8.9 %collective-permute-start.1 = (f32[256,384]{1,0:T(8,128)S(1)}, f32[256,384]{1,0:T(8,128)S(1)}, u32[]{:S(2)}, u32[]{:S(2)}) collective-permute-start(f32[256,384]{1,0:T(8,128)S(1)} %convolution_add_fusion.1), channel_id=1, source_target_pairs={{0,2},{4,6},{8,10},{12,14},{3,1},{7,5},{11,9},{15,13},{16,18},{20,... | collective-permute-start | bytes 1179656 | tf_op jit(solution)/shard_map/ppermute | solution.py:190
  19.6 6.4 %collective-permute-start.2 = (f32[256,128]{1,0:T(8,128)S(1)}, f32[256,128]{1,0:T(8,128)S(1)}, u32[]{:S(2)}, u32[]{:S(2)}) collective-permute-start(f32[256,128]{1,0:T(8,128)S(1)} %slice.49), channel_id=1, source_target_pairs={{2,6},{6,10},{10,14},{5,1},{9,5},{13,9},{18,22},{22,26},{26,30},{2... | collective-permute-start | bytes 393224 | tf_op jit(solution)/shard_map/ppermute | solution.py:173
  26.4 5.7 %collective-permute-start.3 = (f32[256,128]{1,0:T(8,128)S(1)}, f32[256,128]{1,0:T(8,128)S(1)}, u32[]{:S(2)}, u32[]{:S(2)}) collective-permute-start(f32[256,128]{1,0:T(8,128)S(1)} %convolution_add_fusion.5), channel_id=1, source_target_pairs={{2,6},{6,10},{10,14},{5,1},{9,5},{13,9},{18,22},{22,26},{26,30},{2... | collective-permute-start | bytes 393224 | tf_op jit(solution)/shard_map/ppermute | solution.py:173
  32.5 5.7 %collective-permute-start.4 = (f32[256,128]{1,0:T(8,128)S(1)}, f32[256,128]{1,0:T(8,128)S(1)}, u32[]{:S(2)}, u32[]{:S(2)}) collective-permute-start(f32[256,128]{1,0:T(8,128)S(1)} %convolution_add_fusion.4), channel_id=1, source_target_pairs={{2,6},{6,10},{10,14},{5,1},{9,5},{13,9},{18,22},{22,26},{26,30},{2... | collective-permute-start | bytes 393224 | tf_op jit(solution)/shard_map/ppermute | solution.py:173
  38.2 3.2 %collective-permute-start.5 = (f32[256,128]{1,0:T(8,128)S(1)}, f32[256,128]{1,0:T(8,128)S(1)}, u32[]{:S(2)}, u32[]{:S(2)}) collective-permute-start(f32[256,128]{1,0:T(8,128)S(1)} %collective-permute-done.4), channel_id=1, source_target_pairs={{2,0},{6,4},{10,8},{14,12},{1,3},{5,7},{9,11},{13,15},{18,16},{22,... | collective-permute-start | bytes 393224 | tf_op jit(solution)/shard_map/ppermute | solution.py:215
  41.8 15.2 %copy-start.2 = (f32[256,128]{1,0:T(8,128)}, f32[256,128]{1,0:T(8,128)S(1)}, u32[]{:S(2)}) copy-start(f32[256,128]{1,0:T(8,128)S(1)} %fusion.enter_ref) | copy-start | bytes 393220
  42.2 14.8 %collective-permute-start.6 = (f32[256,128]{1,0:T(8,128)S(1)}, f32[256,128]{1,0:T(8,128)S(1)}, u32[]{:S(2)}, u32[]{:S(2)}) collective-permute-start(f32[256,128]{1,0:T(8,128)S(1)} %convolution_add_fusion.2), channel_id=1, source_target_pairs={{0,1},{2,3},{4,5},{6,7},{8,9},{10,11},{12,13},{14,15},{1,0},{3,2},... | collective-permute-start | bytes 393224 | tf_op jit(solution)/shard_map/ppermute | solution.py:220
  57.0 0.7 copy-start.3

commit v12 on v10

--- a/solution.py
+++ b/solution.py
@@ -8,6 +8,7 @@
 F32 = jnp.float32
 BF16 = jnp.bfloat16
 HIGHEST = lax.Precision.HIGHEST
+LIMIT = 20 * 1024 * 1024
 
 
 def split_dot(matrix, value):
@@ -209,6 +210,7 @@
             jax.ShapeDtypeStruct((rank, rank + rhs), F32),
             jax.ShapeDtypeStruct((count, rank, rhs), F32),
         ),
+        compiler_params=pltpu.CompilerParams(vmem_limit_bytes=LIMIT),
         name="sweep",
     )(right_sides, lower_cols, lower_trans, upper_cols, upper_trans)
     diag = jnp.einsum(
@@ -237,6 +239,7 @@
             pltpu.VMEM((count, rank, rhs), BF16),
         ],
         in_specs=[pl.BlockSpec(memory_space=pltpu.SMEM)] + [vmem] * 9,
+        compiler_params=pltpu.CompilerParams(vmem_limit_bytes=LIMIT),
         name="apply",
     )(flag, enter, other, lower_trans, upper_trans, lsrc, usrc, diag, lower_rows, upper_rows)
 

time: 57.6 us -> 57.9 us (level); the launches traced: 57.4 us -> 57 us
  Pallas kernels: 12.7 us -> 5.77 us
  local copies, waits for them, and re-layouts: 0.95 us -> 7.45 us
  other arithmetic: 1.17 us -> 0.06 us
  starting transfers between devices: 13.3 us -> 14 us
    unnamed x8 -> x28, local copies, waits for them, and re-layouts: 0.92 us -> 7.42 us
    pallas_call x1, Pallas kernels: 6.43 us -> 2.72 us  [shards(): pl.pallas_call(sweep_kernel, out_shape=(jax.ShapeDtypeStruct((rank, rank...]
    pallas_call x1, Pallas kernels: 6.27 us -> 3.05 us  [shards(): pl.pallas_call(apply_kernel, out_shape=jax.ShapeDtypeStruct((count, rows,...]
    select_n x1, other arithmetic: 1.17 us -> 0.06 us  [shards(): jnp.where(first, uboth, lboth)]
    dot_general x1, matrix products: 0.37 us -> 1.43 us  [scan_groups(): jnp.dot(beside[:, :rank], start, precision=HIGHEST) + beside[:, rank:]]
    dot_general x1, matrix products: 1.4 us -> 0.42 us  [shards(): jnp.einsum('kab,kbc->kac', diagonal_blocks, right_sides, preferred_elemen...]
    ppermute x1, starting transfers between devices: 1.29 us -> 1.94 us  [scan_groups(): sent = lax.ppermute(start, axis, back)]
  transfers between devices with their start and end apart: 7 -> 7, of which waited for: 6 -> 7; matrix products, arithmetic and copies ran while one was open for 2% -> 1% of each run, Pallas kernels for 0% -> 0%
where the time goes in v12:
time: 57.9 us; the launch traced here: 57 us
  waiting for transfers between devices  25.4 us (44%)
  starting transfers between devices  14 us (24%)
  local copies, waits for them, and re-layouts  7.45 us (13%)
  Pallas kernels  5.77 us (10%)
  matrix products  4.18 us (7%)
    ppermute x3, waiting for transfers between devices, group_shift(): return lax.ppermute(value, axis, pairs)  14 us
    ppermute x1, waiting for transfers between devices, scan_groups(): beside = lax.ppermute(both, axis, pair)  7.48 us
    unnamed x28, local copies, waits for them, and re-layouts  7.42 us
    ppermute x1, starting transfers between devices, scan_groups(): other = lax.ppermute(send, axis, partner)  6.79 us
    ppermute x3, starting transfers between devices, group_shift(): return lax.ppermute(value, axis, pairs)  3.88 us
    pallas_call x1, Pallas kernels, shards(): pl.pallas_call(apply_kernel, out_shape=jax.ShapeDtypeStruct((count, rows,...  3.05 us
    pallas_call x1, Pallas kernels, shards(): pl.pallas_call(sweep_kernel, out_shape=(jax.ShapeDtypeStruct((rank, rank...  2.72 us
    ppermute x1, starting transfers between devices, scan_groups(): sent = lax.ppermute(start, axis, back)  1.94 us
  transfers between devices with their start and end apart: 7, of which 7 were waited for; matrix products, arithmetic and copies ran while one was open for 1% of the time, Pallas kernels for 0%

profile of v12, /device:TPU:1, one launch (start us, length us, event | category | flops | bytes accessed | tf_op | source)
XLA Modules:
  0.0 57.0 jit_solution(5367763578817633942)
XLA Ops:
  0.0 0.0 copy-start
  0.0 0.0 copy-start.1
  0.0 1.3 %copy-done.1 = bf16[8,256,256]{2,1,0:T(8,128)(2,1)S(1)} copy-done((bf16[8,256,256]{2,1,0:T(8,128)(2,1)S(1)}, bf16[8,256,256]{2,1,0:T(8,128)(2,1)}, u32[]{:S(2)}) %copy-start.1) | copy-done | bytes 1048600
  1.3 0.0 copy-start.3
  1.3 1.2 %copy-done.3 = bf16[8,256,256]{2,1,0:T(8,128)(2,1)S(1)} copy-done((bf16[8,256,256]{2,1,0:T(8,128)(2,1)S(1)}, bf16[8,256,256]{2,1,0:T(8,128)(2,1)}, u32[]{:S(2)}) %copy-start.3) | copy-done | bytes 1048600
  2.5 0.0 copy-start.5
  2.5 1.0 %copy-done.5 = bf16[8,256,128]{2,1,0:T(8,128)(2,1)S(1)} copy-done((bf16[8,256,128]{2,1,0:T(8,128)(2,1)S(1)}, bf16[8,256,128]{2,1,0:T(8,128)(2,1)}, u32[]{:S(2)}) %copy-start.5) | copy-done | bytes 524312
  3.6 0.0 copy-start.7
  3.6 1.2 %copy-done.7 = bf16[8,256,256]{2,1,0:T(8,128)(2,1)S(1)} copy-done((bf16[8,256,256]{2,1,0:T(8,128)(2,1)S(1)}, bf16[8,256,256]{2,1,0:T(8,128)(2,1)}, u32[]{:S(2)}) %copy-start.7) | copy-done | bytes 1048600
  4.8 1.2 %copy-done.8 = bf16[8,256,256]{2,1,0:T(8,128)(2,1)S(1)} copy-done((bf16[8,256,256]{2,1,0:T(8,128)(2,1)S(1)}, bf16[8,256,256]{2,1,0:T(8,128)(2,1)}, u32[]{:S(2)}) %copy-start.8) | copy-done | bytes 1048600
  6.0 2.7 %sweep.1 = (f32[256,384]{1,0:T(8,128)S(1)}, f32[8,256,128]{2,1,0:T(8,128)S(1)}, f32[256,384]{1,0:T(8,128)S(1)}, f32[8,256,128]{2,1,0:T(8,128)S(1)}) custom-call(bf16[8,256,128]{2,1,0:T(8,128)(2,1)S(1)} %copy-done.5, bf16[8,256,256]{2,1,0:T(8,128)(2,1)S(1)} %copy-done.7, bf16[8,256,256]{2,1,0:T(8,128)(2,1)S(1)} %copy-done.1, ...), custom_call_target="tpu_custom_call" | custom-call | tf_op jit(solution)/shard_map/sweep/pallas_call | solution.py:205
  8.8 0.0 copy-start.11
  8.8 0.1 broadcast_select_fusion.1
  8.8 0.1 collective-permute-start
  8.9 1.7 %collective-permute-done = f32[256,384]{1,0:T(8,128)S(1)} collective-permute-done((f32[256,384]{1,0:T(8,128)S(1)}, f32[256,384]{1,0:T(8,128)S(1)}, u32[]{:S(2)}, u32[]{:S(2)}) %collective-permute-start) | collective-permute-done | bytes 393248 | tf_op jit(solution)/shard_map/ppermute | solution.py:153
  10.6 0.6 %convolution_add_fusion.1 = f32[256,384]{1,0:T(8,128)S(1)} fusion(f32[256,384]{1,0:T(8,128)S(1)} %get-tuple-element.14, f32[256,128]{1,0:T(8,128)S(1)} %slice.44, f32[256,384]{1,0:T(8,128)S(1)} %collective-permute-done), kind=kOutput, calls=%fused_computation.1 | convolution fusion | flops 302088192 | bytes 1179648 | tf_op jit(solution)/shard_map/dot_general | solution.py:154
  11.2 0.0 copy-done.11
  11.3 1.3 %collective-permute-start.1 = (f32[256,384]{1,0:T(8,128)S(1)}, f32[256,384]{1,0:T(8,128)S(1)}, u32[]{:S(2)}, u32[]{:S(2)}) collective-permute-start(f32[256,384]{1,0:T(8,128)S(1)} %convolution_add_fusion.1), channel_id=1, source_target_pairs={{0,2},{4,6},{8,10},{12,14},{3,1},{7,5},{11,9},{15,13},{16,18},{20,... | collective-permute-start | bytes 1179656 | tf_op jit(solution)/shard_map/ppermute | solution.py:159
  12.6 7.5 %collective-permute-done.1 = f32[256,384]{1,0:T(8,128)S(1)} collective-permute-done((f32[256,384]{1,0:T(8,128)S(1)}, f32[256,384]{1,0:T(8,128)S(1)}, u32[]{:S(2)}, u32[]{:S(2)}) %collective-permute-start.1) | collective-permute-done | bytes 393248 | tf_op jit(solution)/shard_map/ppermute | solution.py:159
  20.1 0.6 %convolution_add_fusion = f32[256,384]{1,0:T(8,128)S(1)} fusion(f32[256,384]{1,0:T(8,128)S(1)} %collective-permute-done.1, f32[256,128]{1,0:T(8,128)S(1)} %slice.47, f32[256,384]{1,0:T(8,128)S(1)} %convolution_add_fusion.1), kind=kOutput, calls=%fused_computation | convolution fusion | flops 302088192 | bytes 1179648 | tf_op jit(solution)/shard_map/dot_general | solution.py:160
  20.7 0.1 copy-done.13
  20.8 1.3 %collective-permute-start.2 = (f32[256,128]{1,0:T(8,128)S(1)}, f32[256,128]{1,0:T(8,128)S(1)}, u32[]{:S(2)}, u32[]{:S(2)}) collective-permute-start(f32[256,128]{1,0:T(8,128)S(1)} %slice.49), channel_id=1, source_target_pairs={{2,6},{6,10},{10,14},{5,1},{9,5},{13,9},{18,22},{22,26},{26,30},{2... | collective-permute-start | bytes 393224 | tf_op jit(solution)/shard_map/ppermute | solution.py:142
  22.1 5.1 %collective-permute-done.2 = f32[256,128]{1,0:T(8,128)S(1)} collective-permute-done((f32[256,128]{1,0:T(8,128)S(1)}, f32[256,128]{1,0:T(8,128)S(1)}, u32[]{:S(2)}, u32[]{:S(2)}) %collective-permute-start.2) | collective-permute-done | bytes 131104 | tf_op jit(solution)/shard_map/ppermute | solution.py:142
  27.2 0.4 convolution_add_fusion.5
  27.6 1.3 %collective-permute-start.3 = (f32[256,128]{1,0:T(8,128)S(1)}, f32[256,128]{1,0:T(8,128)S(1)}, u32[]{:S(2)}, u32[]{:S(2)}) collective-permute-start(f32[256,128]{1,0:T(8,128)S(1)} %convolution_add_fusion.5), channel_id=1, source_target_pairs={{2,6},{6,10},{10,14},{5,1},{9,5},{13,9},{18,22},{22,26},{26,30},{2... | collective-permute-start | bytes 393224 | tf_op jit(solution)/shard_map/ppermute | solution.py:142
  28.9 4.4 %collective-permute-done.3 = f32[256,128]{1,0:T(8,128)S(1)} collective-permute-done((f32[256,128]{1,0:T(8,128)S(1)}, f32[256,128]{1,0:T(8,128)S(1)}, u32[]{:S(2)}, u32[]{:S(2)}) %collective-permute-start.3) | collective-permute-done | bytes 131104 | tf_op jit(solution)/shard_map/ppermute | solution.py:142
  33.3 0.4 convolution_add_fusion.4
  33.7 1.3 %collective-permute-start.4 = (f32[256,128]{1,0:T(8,128)S(1)}, f32[256,128]{1,0:T(8,128)}, u32[]{:S(2)}, u32[]{:S(2)}) collective-permute-start(f32[256,128]{1,0:T(8,128)S(1)} %convolution_add_fusion.4), channel_id=1, source_target_pairs={{2,6},{6,10},{10,14},{5,1},{9,5},{13,9},{18,22},{22,26},{26,30},{2... | collective-permute-start | bytes 393224 | tf_op jit(solution)/shard_map/ppermute | solution.py:142
  35.0 4.5 %collective-permute-done.4 = f32[256,128]{1,0:T(8,128)} collective-permute-done((f32[256,128]{1,0:T(8,128)S(1)}, f32[256,128]{1,0:T(8,128)}, u32[]{:S(2)}, u32[]{:S(2)}) %collective-permute-start.4) | collective-permute-done | bytes 131104 | tf_op jit(solution)/shard_map/ppermute | solution.py:142
  39.5 1.9 %collective-permute-start.5 = (f32[256,128]{1,0:T(8,128)}, f32[256,128]{1,0:T(8,128)}, u32[]{:S(2)}, u32[]{:S(2)}) collective-permute-start(f32[256,128]{1,0:T(8,128)} %collective-permute-done.4), channel_id=1, source_target_pairs={{2,0},{6,4},{10,8},{14,12},{1,3},{5,7},{9,11},{13,15},{18,16},{22,... | collective-permute-start | bytes 393224 | tf_op jit(solution)/shard_map/ppermute | solution.py:184
  41.4 1.6 %collective-permute-done.5 = f32[256,128]{1,0:T(8,128)} collective-permute-done((f32[256,128]{1,0:T(8,128)}, f32[256,128]{1,0:T(8,128)}, u32[]{:S(2)}, u32[]{:S(2)}) %collective-permute-start.5) | collective-permute-done | bytes 131104 | tf_op jit(solution)/shard_map/ppermute | solution.py:184
  43.0 1.4 %fusion.enter_ref = f32[256,128]{1,0:T(8,128)S(1)} fusion(f32[256,128]{1,0:T(8,128)} %collective-permute-done.5, f32[256,128]{1,0:T(8,128)} %collective-permute-done.4, f32[256,384]{1,0:T(8,128)} %copy-done.13, pred[]{:T(512)S(6)} %or.3), kind=kOutput, calls=%fused_computation.4 | convolution fusion | flops 100728832 | bytes 786433 | tf_op jit(solution)/shard_map/dot_general | solution.py:185
  44.5 0.0 copy-start.9
  44.5 0.4 convolution_add_fusion.2
  44.9 0.0 copy-start.2
  44.9 0.0 copy-start.4
  44.9 6.8 %collective-permute-start.6 = (f32[256,128]{1,0:T(8,128)S(1)}, f32[256,128]{1,0:T(8,128)S(1)}, u32[]{:S(2)}, u32[]{:S(2)}) collective-permute-start(f32[256,128]{1,0:T(8,128)S(1)} %convolution_add_fusion.2), channel_id=1, source_target_pairs={{0,1},{2,3},{4,5},{6,7},{8,9},{10,11},{12,13},{14,15},{1,0},{3,2},... | collective-permute-start | bytes 393224 | tf_op jit(solution)/shard_map/ppermute | solution.py:189
  51.7 0.0 copy-done
  51.7 0.0 copy-done.6
  51.7 0.4 fusion.7.diag_ref
  52.1 0.6 collective-permute-done.6.other_ref
  52.7 0.0 copy-done.10
  52.7 0.0 copy-done.9
  52.7 0.0 copy-done.2
  52.7 0.0 copy-done.4
  52.7 0.0 copy-start.12
  52.7 1.2 %copy-done.12 = f32[8,256,128]{2,1,0:T(8,128)S(1)} copy-done((f32[8,256,128]{2,1,0:T(8,128)S(1)}, f32[8,256,128]{2,1,0:T(8,128)}, u32[]{:S(2)}) %copy-start.12) | copy-done | bytes 1048600
  53.9 3.1 %apply.1 = bf16[8,256,128]{2,1,0:T(8,128)(2,1)} custom-call(s32[1]{0:T(128)} %bitcast.flag_ref, f32[256,128]{1,0:T(8,128)S(1)} %fusion.enter_ref, f32[256,128]{1,0:T(8,128)S(1)} %collective-permute-done.6.other_ref, bf16[8,256,256]{2,1,0:T(8,128)(2,1)S(1)} %copy-done.2, bf16[8,256,256]{2,1,0:T(8,128)(2,1)S(1)} %copy-done.4, ...), custom_call_target="tpu_custom_call" | custom-call | tf_op jit(solution)/shard_map/apply/pallas_call | solution.py:234
  (7 shorter events, 0.0 us)
Async XLA Ops:
  0.0 51.7 %copy-start = (bf16[8,256,256]{2,1,0:T(8,128)(2,1)S(1)}, bf16[8,256,256]{2,1,0:T(8,128)(2,1)}, u32[]{:S(2)}) copy-start(bf16[8,256,256]{2,1,0:T(8,128)(2,1)} %param.9) | copy-start | bytes 3145732
  0.0 1.3 %copy-start.1 = (bf16[8,256,256]{2,1,0:T(8,128)(2,1)S(1)}, bf16[8,256,256]{2,1,0:T(8,128)(2,1)}, u32[]{:S(2)}) copy-start(bf16[8,256,256]{2,1,0:T(8,128)(2,1)} %ltrans_ref.3) | copy-start | bytes 3145732
  1.3 1.2 %copy-start.3 = (bf16[8,256,256]{2,1,0:T(8,128)(2,1)S(1)}, bf16[8,256,256]{2,1,0:T(8,128)(2,1)}, u32[]{:S(2)}) copy-start(bf16[8,256,256]{2,1,0:T(8,128)(2,1)} %utrans_ref.3) | copy-start | bytes 3145732
  2.5 1.0 %copy-start.5 = (bf16[8,256,128]{2,1,0:T(8,128)(2,1)S(1)}, bf16[8,256,128]{2,1,0:T(8,128)(2,1)}, u32[]{:S(2)}) copy-start(bf16[8,256,128]{2,1,0:T(8,128)(2,1)} %rhs_ref.1) | copy-start | bytes 1572868
  3.6 1.2 %copy-start.7 = (bf16[8,256,256]{2,1,0:T(8,128)(2,1)S(1)}, bf16[8,256,256]{2,1,0:T(8,128)(2,1)}, u32[]{:S(2)}) copy-start(bf16[8,256,256]{2,1,0:T(8,128)(2,1)} %lcols_ref.1) | copy-start | bytes 3145732
  4.8 1.2 %copy-start.8 = (bf16[8,256,256]{2,1,0:T(8,128)(2,1)S(1)}, bf16[8,256,256]{2,1,0:T(8,128)(2,1)}, u32[]{:S(2)}) copy-start(bf16[8,256,256]{2,1,0:T(8,128)(2,1)} %ucols_ref.1) | copy-start | bytes 3145732
  8.8 2.5 %copy-start.11 = (f32[8,256,128]{2,1,0:T(8,128)}, f32[8,256,128]{2,1,0:T(8,128)S(1)}, u32[]{:S(2)}) copy-start(f32[8,256,128]{2,1,0:T(8,128)S(1)} %get-tuple-element.12.usrc_ref) | copy-start | bytes 3145732
  8.8 1.8 %collective-permute-start = (f32[256,384]{1,0:T(8,128)S(1)}, f32[256,384]{1,0:T(8,128)S(1)}, u32[]{:S(2)}, u32[]{:S(2)}) collective-permute-start(f32[256,384]{1,0:T(8,128)S(1)} %get-tuple-element.13), channel_id=1, source_target_pairs={{0,1},{2,3},{4,5},{6,7},{8,9},{10,11},{12,13},{14,15},{1,0},{3,2},... | collective-permute-start | bytes 1179656 | tf_op jit(solution)/shard_map/ppermute | solution.py:153
  11.3 8.8 %collective-permute-start.1 = (f32[256,384]{1,0:T(8,128)S(1)}, f32[256,384]{1,0:T(8,128)S(1)}, u32[]{:S(2)}, u32[]{:S(2)}) collective-permute-start(f32[256,384]{1,0:T(8,128)S(1)} %convolution_add_fusion.1), channel_id=1, source_target_pairs={{0,2},{4,6},{8,10},{12,14},{3,1},{7,5},{11,9},{15,13},{16,18},{20,... | collective-permute-start | bytes 1179656 | tf_op jit(solution)/shard_map/ppermute | solution.py:159
  20.1 0.7 %copy-start.13 = (f32[256,384]{1,0:T(8,128)}, f32[256,384]{1,0:T(8,128)S(1)}, u32[]{:S(2)}) copy-start(f32[256,384]{1,0:T(8,128)S(1)} %collective-permute-done.1) | copy-start | bytes 1179652
  20.8 6.4 %collective-permute-start.2 = (f32[256,128]{1,0:T(8,128)S(1)}, f32[256,128]{1,0:T(8,128)S(1)}, u32[]{:S(2)}, u32[]{:S(2)}) collective-permute-start(f32[256,128]{1,0:T(8,128)S(1)} %slice.49), channel_id=1, source_target_pairs={{2,6},{6,10},{10,14},{5,1},{9,5},{13,9},{18,22},{22,26},{26,30},{2... | collective-permute-start | bytes 393224 | tf_op jit(solution)/shard_map/ppermute | solution.py:142
  27.2 25.5 %copy-start.10 = (bf16[8,256,256]{2,1,0:T(8,128)(2,1)S(1)}, bf16[8,256,256]{2,1,0:T(8,128)(2,1)}, u32[]{:S(2)}) copy-start(bf16[8,256,256]{2,1,0:T(8,128)(2,1)} %urows_ref.1) | copy-start | bytes 3145732
  27.6 5.7 %collective-permute-start.3 = (f32[256,128]{1,0:T(8,128)S(1)}, f32[256,128]{1,0:T(8,128)S(1)}, u32[]{:S(2)}, u32[]{:S(2)}) collective-permute-start(f32[256,128]{1,0:T(8,128)S(1)} %convolution_add_fusion.5), channel_id=1, source_target_pairs={{2,6},{6,10},{10,14},{5,1},{9,5},{13,9},{18,22},{22,26},{26,30},{2... | collective-permute-start | bytes 393224 | tf_op jit(solution)/shard_map/ppermute | solution.py:142
  33.7 5.8 %collective-permute-start.4 = (f32[256,128]{1,0:T(8,128)S(1)}, f32[256,128]{1,0:T(8,128)}, u32[]{:S(2)}, u32[]{:S(2)}) collective-permute-start(f32[256,128]{1,0:T(8,128)S(1)} %convolution_add_fusion.4), channel_id=1, source_target_pairs={{2,6},{6,10},{10,14},{5,1},{9,5},{13,9},{18,22},{22,26},{26,30},{2... | collective-permute-start | bytes 393224 | tf_op jit(solution)/shard_map/ppermute | solution.py:142
  39.5 3.5 %collective-permute-start.5 = (f32[256,128]{1,0:T(8,128)}, f32[256,128]{1,0:T(8,128)}, u32[]{:S(2)}, u32[]{:S(2)}) collective-permute-start(f32[256,128]{1,0:T(8,128)} %collective-permute-done.4), channel_id=1, source_target_pairs={{2,0},{6,4},{10,8},{14,12},{1,3},{5,7},{9,11},{13,15},{18,16},{22,... | collective-permute-start | bytes 393224 | tf_op jit(solution)/shard_map/ppermute | solution.py:184
  41.4 10.2 %copy-start.6 = (bf16[8,256,128]{2,1,0:T(8,128)(2,1)S(1)}, bf16[8,256,128]{2,1,0:T(8,128)(2,1)}, u32[]{:S(2)}) copy-start(bf16[8,256,128]{2,1,0:T(8,128)(2,1)} %rhs_ref.1) | copy-start | bytes 1572868
  44.5 8.2 %copy-start.9 = (bf16[8,256,256]{2,1,0:T(8,128)(2,1)S(1)}, bf16[8,256,256]{2,1,0:T(8,128)(2,1)}, u32[]{:S(2)}) copy-start(bf16[8,256,256]{2,1,0:T(8,128)(2,1)} %lrows_ref.1) | copy-start | bytes 3145732
  44.9 7.8 %copy-start.2 = (bf16[8,256,256]{2,1,0:T(8,128)(2,1)S(1)}, bf16[8,256,256]{2,1,0:T(8,128)(2,1)}, u32[]{:S(2)}) copy-start(bf16[8,256,256]{2,1,0:T(8,128)(2,1)} %ltrans_ref.3) | copy-start | bytes 3145732
  44.9 7.8 %copy-start.4 = (bf16[8,256,256]{2,1,0:T(8,128)(2,1)S(1)}, bf16[8,256,256]{2,1,0:T(8,128)(2,1)}, u32[]{:S(2)}) copy-start(bf16[8,256,256]{2,1,0:T(8,128)(2,1)} %utrans_ref.3) | copy-start | bytes 3145732
  44.9 7.8 %collective-permute-start.6 = (f32[256,128]{1,0:T(8,128)S(1)}, f32[256,128]{1,0:T(8,128)S(1)}, u32[]{:S(2)}, u32[]{:S(2)}) collective-permute-start(f32[256,128]{1,0:T(8,128)S(1)} %convolution_add_fusion.2), channel_id=1, source_target_pairs={{0,1},{2,3},{4,5},{6,7},{8,9},{10,11},{12,13},{14,15},{1,0},{3,2},... | collective-permute-start | bytes 393224 | tf_op jit(solution)/shard_map/ppermute | solution.py:189
  52.7 1.2 %copy-start.12 = (f32[8,256,128]{2,1,0:T(8,128)S(1)}, f32[8,256,128]{2,1,0:T(8,128)}, u32[]{:S(2)}) copy-start(f32[8,256,128]{2,1,0:T(8,128)} %copy-done.11) | copy-start | bytes 3145732

commit v13 on v12

--- a/solution.py
+++ b/solution.py
@@ -210,7 +210,6 @@
             jax.ShapeDtypeStruct((rank, rank + rhs), F32),
             jax.ShapeDtypeStruct((count, rank, rhs), F32),
         ),
-        compiler_params=pltpu.CompilerParams(vmem_limit_bytes=LIMIT),
         name="sweep",
     )(right_sides, lower_cols, lower_trans, upper_cols, upper_trans)
     diag = jnp.einsum(

time: 57.9 us -> 56.7 us (0.979)
  local copies, waits for them, and re-layouts: 7.45 us -> 1.42 us
  Pallas kernels: 5.77 us -> 9.48 us
  other arithmetic: 0.06 us -> 1.17 us
  matrix products: 4.18 us -> 5.21 us
  waiting for transfers between devices: 25.4 us -> 24.8 us
    unnamed x28 -> x16, local copies, waits for them, and re-layouts: 7.42 us -> 1.39 us
    pallas_call x1, Pallas kernels: 2.72 us -> 6.43 us  [shards(): pl.pallas_call(sweep_kernel, out_shape=(jax.ShapeDtypeStruct((rank, rank...]
    select_n x1, other arithmetic: 0.06 us -> 1.17 us  [shards(): jnp.where(first, uboth, lboth)]
    dot_general x1, matrix products: 0.42 us -> 1.46 us  [shards(): jnp.einsum('kab,kbc->kac', diagonal_blocks, right_sides, preferred_elemen...]
  transfers between devices with their start and end apart: 7 -> 7, of which waited for: 7 -> 6; matrix products, arithmetic and copies ran while one was open for 1% -> 3% of each run, Pallas kernels for 0% -> 0%
where the time goes in v13:
time: 56.7 us; the launch traced here: 56.3 us
  waiting for transfers between devices  24.8 us (44%)
  starting transfers between devices  14 us (25%)
  Pallas kernels  9.48 us (17%)
  matrix products  5.21 us (9%)
  local copies, waits for them, and re-layouts  1.42 us (3%)
  other arithmetic  1.17 us (2%)
    ppermute x3, waiting for transfers between devices, group_shift(): return lax.ppermute(value, axis, pairs)  14 us
    ppermute x1, waiting for transfers between devices, scan_groups(): beside = lax.ppermute(both, axis, pair)  7.48 us
    ppermute x1, starting transfers between devices, scan_groups(): other = lax.ppermute(send, axis, partner)  6.8 us
    pallas_call x1, Pallas kernels, shards(): pl.pallas_call(sweep_kernel, out_shape=(jax.ShapeDtypeStruct((rank, rank...  6.43 us
    ppermute x3, starting transfers between devices, group_shift(): return lax.ppermute(value, axis, pairs)  3.88 us
    pallas_call x1, Pallas kernels, shards(): pl.pallas_call(apply_kernel, out_shape=jax.ShapeDtypeStruct((count, rows,...  3.06 us
    ppermute x1, starting transfers between devices, scan_groups(): sent = lax.ppermute(start, axis, back)  1.95 us
    ppermute x1, waiting for transfers between devices, scan_groups(): got = lax.ppermute(give, axis, partner)  1.71 us
  transfers between devices with their start and end apart: 7, of which 6 were waited for; matrix products, arithmetic and copies ran while one was open for 3% of the time, Pallas kernels for 0%

profile of v13, /device:TPU:1, one launch (start us, length us, event | category | flops | bytes accessed | tf_op | source)
XLA Modules:
  0.0 56.3 jit_solution(16469714387097828746)
XLA Ops:
  0.0 0.0 copy-start
  0.0 6.4 %sweep.1 = (f32[256,384]{1,0:T(8,128)}, f32[8,256,128]{2,1,0:T(8,128)}, f32[256,384]{1,0:T(8,128)}, f32[8,256,128]{2,1,0:T(8,128)}) custom-call(bf16[8,256,128]{2,1,0:T(8,128)(2,1)} %rhs_ref.1, bf16[8,256,256]{2,1,0:T(8,128)(2,1)} %lcols_ref.1, bf16[8,256,256]{2,1,0:T(8,128)(2,1)} %ltrans_ref.3, bf16[8,256,256]{2,1,0:T(8,128)(2,1)} %ucols_ref.1, ...), custom_call_target="tpu_custom_call" | custom-call | tf_op jit(solution)/shard_map/sweep/pallas_call | solution.py:205
  6.4 1.2 %broadcast_select_fusion.1 = (f32[256,384]{1,0:T(8,128)S(1)}, f32[256,384]{1,0:T(8,128)S(1)}) fusion(f32[256,384]{1,0:T(8,128)} %get-tuple-element.9, f32[256,384]{1,0:T(8,128)} %get-tuple-element.10, pred[]{:T(512)S(6)} %eq.15), kind=kLoop, calls=%fused_computation.14 | loop fusion | flops 196608 | bytes 1572865 | tf_op jit(solution)/shard_map/jit(_where)/select_n | solution.py:222
  7.6 0.1 collective-permute-start
  7.7 1.7 %collective-permute-done = f32[256,384]{1,0:T(8,128)S(1)} collective-permute-done((f32[256,384]{1,0:T(8,128)S(1)}, f32[256,384]{1,0:T(8,128)S(1)}, u32[]{:S(2)}, u32[]{:S(2)}) %collective-permute-start) | collective-permute-done | bytes 393248 | tf_op jit(solution)/shard_map/ppermute | solution.py:153
  9.4 0.6 %convolution_add_fusion.1 = f32[256,384]{1,0:T(8,128)S(1)} fusion(f32[256,384]{1,0:T(8,128)S(1)} %get-tuple-element.14, f32[256,128]{1,0:T(8,128)S(1)} %slice.44, f32[256,384]{1,0:T(8,128)S(1)} %collective-permute-done), kind=kOutput, calls=%fused_computation.1 | convolution fusion | flops 302088192 | bytes 1179648 | tf_op jit(solution)/shard_map/dot_general | solution.py:154
  10.0 1.3 %collective-permute-start.1 = (f32[256,384]{1,0:T(8,128)S(1)}, f32[256,384]{1,0:T(8,128)S(1)}, u32[]{:S(2)}, u32[]{:S(2)}) collective-permute-start(f32[256,384]{1,0:T(8,128)S(1)} %convolution_add_fusion.1), channel_id=1, source_target_pairs={{0,2},{4,6},{8,10},{12,14},{3,1},{7,5},{11,9},{15,13},{16,18},{20,... | collective-permute-start | bytes 1179656 | tf_op jit(solution)/shard_map/ppermute | solution.py:159
  11.3 7.5 %collective-permute-done.1 = f32[256,384]{1,0:T(8,128)S(1)} collective-permute-done((f32[256,384]{1,0:T(8,128)S(1)}, f32[256,384]{1,0:T(8,128)S(1)}, u32[]{:S(2)}, u32[]{:S(2)}) %collective-permute-start.1) | collective-permute-done | bytes 393248 | tf_op jit(solution)/shard_map/ppermute | solution.py:159
  18.8 0.0 copy-start.7
  18.8 0.0 copy-start.5
  18.8 0.6 %convolution_add_fusion = f32[256,384]{1,0:T(8,128)S(1)} fusion(f32[256,384]{1,0:T(8,128)S(1)} %collective-permute-done.1, f32[256,128]{1,0:T(8,128)S(1)} %slice.47, f32[256,384]{1,0:T(8,128)S(1)} %convolution_add_fusion.1), kind=kOutput, calls=%fused_computation | convolution fusion | flops 302088192 | bytes 1179648 | tf_op jit(solution)/shard_map/dot_general | solution.py:160
  19.4 0.1 copy-done.7
  19.6 1.3 %collective-permute-start.2 = (f32[256,128]{1,0:T(8,128)S(1)}, f32[256,128]{1,0:T(8,128)S(1)}, u32[]{:S(2)}, u32[]{:S(2)}) collective-permute-start(f32[256,128]{1,0:T(8,128)S(1)} %slice.49), channel_id=1, source_target_pairs={{2,6},{6,10},{10,14},{5,1},{9,5},{13,9},{18,22},{22,26},{26,30},{2... | collective-permute-start | bytes 393224 | tf_op jit(solution)/shard_map/ppermute | solution.py:142
  20.9 5.1 %collective-permute-done.2 = f32[256,128]{1,0:T(8,128)S(1)} collective-permute-done((f32[256,128]{1,0:T(8,128)S(1)}, f32[256,128]{1,0:T(8,128)S(1)}, u32[]{:S(2)}, u32[]{:S(2)}) %collective-permute-start.2) | collective-permute-done | bytes 131104 | tf_op jit(solution)/shard_map/ppermute | solution.py:142
  26.0 0.4 convolution_add_fusion.5
  26.3 1.3 %collective-permute-start.3 = (f32[256,128]{1,0:T(8,128)S(1)}, f32[256,128]{1,0:T(8,128)S(1)}, u32[]{:S(2)}, u32[]{:S(2)}) collective-permute-start(f32[256,128]{1,0:T(8,128)S(1)} %convolution_add_fusion.5), channel_id=1, source_target_pairs={{2,6},{6,10},{10,14},{5,1},{9,5},{13,9},{18,22},{22,26},{26,30},{2... | collective-permute-start | bytes 393224 | tf_op jit(solution)/shard_map/ppermute | solution.py:142
  27.6 4.4 %collective-permute-done.3 = f32[256,128]{1,0:T(8,128)S(1)} collective-permute-done((f32[256,128]{1,0:T(8,128)S(1)}, f32[256,128]{1,0:T(8,128)S(1)}, u32[]{:S(2)}, u32[]{:S(2)}) %collective-permute-start.3) | collective-permute-done | bytes 131104 | tf_op jit(solution)/shard_map/ppermute | solution.py:142
  32.1 0.0 copy-start.4
  32.1 0.4 convolution_add_fusion.4
  32.4 1.3 %collective-permute-start.4 = (f32[256,128]{1,0:T(8,128)S(1)}, f32[256,128]{1,0:T(8,128)}, u32[]{:S(2)}, u32[]{:S(2)}) collective-permute-start(f32[256,128]{1,0:T(8,128)S(1)} %convolution_add_fusion.4), channel_id=1, source_target_pairs={{2,6},{6,10},{10,14},{5,1},{9,5},{13,9},{18,22},{22,26},{26,30},{2... | collective-permute-start | bytes 393224 | tf_op jit(solution)/shard_map/ppermute | solution.py:142
  33.7 4.5 %collective-permute-done.4 = f32[256,128]{1,0:T(8,128)} collective-permute-done((f32[256,128]{1,0:T(8,128)S(1)}, f32[256,128]{1,0:T(8,128)}, u32[]{:S(2)}, u32[]{:S(2)}) %collective-permute-start.4) | collective-permute-done | bytes 131104 | tf_op jit(solution)/shard_map/ppermute | solution.py:142
  38.3 1.9 %collective-permute-start.5 = (f32[256,128]{1,0:T(8,128)}, f32[256,128]{1,0:T(8,128)}, u32[]{:S(2)}, u32[]{:S(2)}) collective-permute-start(f32[256,128]{1,0:T(8,128)} %collective-permute-done.4), channel_id=1, source_target_pairs={{2,0},{6,4},{10,8},{14,12},{1,3},{5,7},{9,11},{13,15},{18,16},{22,... | collective-permute-start | bytes 393224 | tf_op jit(solution)/shard_map/ppermute | solution.py:184
  40.2 1.6 %collective-permute-done.5 = f32[256,128]{1,0:T(8,128)} collective-permute-done((f32[256,128]{1,0:T(8,128)}, f32[256,128]{1,0:T(8,128)}, u32[]{:S(2)}, u32[]{:S(2)}) %collective-permute-start.5) | collective-permute-done | bytes 131104 | tf_op jit(solution)/shard_map/ppermute | solution.py:184
  41.8 1.4 %fusion.enter_ref = f32[256,128]{1,0:T(8,128)S(1)} fusion(f32[256,128]{1,0:T(8,128)} %collective-permute-done.5, f32[256,128]{1,0:T(8,128)} %collective-permute-done.4, f32[256,384]{1,0:T(8,128)} %copy-done.7, pred[]{:T(512)S(6)} %or.3), kind=kOutput, calls=%fused_computation.4 | convolution fusion | flops 100728832 | bytes 786433 | tf_op jit(solution)/shard_map/dot_general | solution.py:185
  43.2 0.0 copy-start.3
  43.2 0.4 convolution_add_fusion.2
  43.6 0.0 copy-start.1
  43.6 0.0 copy-start.2
  43.7 6.8 %collective-permute-start.6 = (f32[256,128]{1,0:T(8,128)S(1)}, f32[256,128]{1,0:T(8,128)S(1)}, u32[]{:S(2)}, u32[]{:S(2)}) collective-permute-start(f32[256,128]{1,0:T(8,128)S(1)} %convolution_add_fusion.2), channel_id=1, source_target_pairs={{0,1},{2,3},{4,5},{6,7},{8,9},{10,11},{12,13},{14,15},{1,0},{3,2},... | collective-permute-start | bytes 393224 | tf_op jit(solution)/shard_map/ppermute | solution.py:189
  50.5 0.0 copy-done
  50.5 1.5 %fusion.7.diag_ref = f32[8,256,128]{2,1,0:T(8,128)S(1)} fusion(bf16[8,256,256]{2,1,0:T(8,128)(2,1)S(1)} %copy-done, bf16[8,256,128]{2,1,0:T(8,128)(2,1)} %rhs_ref.1), kind=kOutput, calls=%fused_computation.15 | convolution fusion | flops 134217728 | bytes 2621440 | tf_op jit(solution)/shard_map/kab,kbc->kac/dot_general | solution.py:215
  51.9 0.0 collective-permute-done.6.other_ref
  51.9 0.0 copy-done.5
  51.9 0.0 copy-done.4
  52.0 0.0 copy-done.3
  52.0 0.0 copy-done.1
  52.0 0.0 copy-done.2
  52.0 0.0 copy-start.6
  52.0 1.2 %copy-done.6 = f32[8,256,128]{2,1,0:T(8,128)S(1)} copy-done((f32[8,256,128]{2,1,0:T(8,128)S(1)}, f32[8,256,128]{2,1,0:T(8,128)}, u32[]{:S(2)}) %copy-start.6) | copy-done | bytes 1048600
  53.2 3.1 %apply.1 = bf16[8,256,128]{2,1,0:T(8,128)(2,1)} custom-call(s32[1]{0:T(128)} %bitcast.flag_ref, f32[256,128]{1,0:T(8,128)S(1)} %fusion.enter_ref, f32[256,128]{1,0:T(8,128)S(1)} %collective-permute-done.6.other_ref, bf16[8,256,256]{2,1,0:T(8,128)(2,1)S(1)} %copy-done.1, bf16[8,256,256]{2,1,0:T(8,128)(2,1)S(1)} %copy-done.2, f32[8,256,128]{2,1,0:T(8,128)S(1)} %copy-done.5, ...), custom_call_target="tpu_custom_call" | custom-call | tf_op jit(solution)/shard_map/apply/pallas_call | solution.py:233
  (3 shorter events, 0.0 us)
Async XLA Ops:
  0.0 50.5 %copy-start = (bf16[8,256,256]{2,1,0:T(8,128)(2,1)S(1)}, bf16[8,256,256]{2,1,0:T(8,128)(2,1)}, u32[]{:S(2)}) copy-start(bf16[8,256,256]{2,1,0:T(8,128)(2,1)} %param.9) | copy-start | bytes 3145732
  7.6 1.8 %collective-permute-start = (f32[256,384]{1,0:T(8,128)S(1)}, f32[256,384]{1,0:T(8,128)S(1)}, u32[]{:S(2)}, u32[]{:S(2)}) collective-permute-start(f32[256,384]{1,0:T(8,128)S(1)} %get-tuple-element.13), channel_id=1, source_target_pairs={{0,1},{2,3},{4,5},{6,7},{8,9},{10,11},{12,13},{14,15},{1,0},{3,2},... | collective-permute-start | bytes 1179656 | tf_op jit(solution)/shard_map/ppermute | solution.py:153
  10.0 8.8 %collective-permute-start.1 = (f32[256,384]{1,0:T(8,128)S(1)}, f32[256,384]{1,0:T(8,128)S(1)}, u32[]{:S(2)}, u32[]{:S(2)}) collective-permute-start(f32[256,384]{1,0:T(8,128)S(1)} %convolution_add_fusion.1), channel_id=1, source_target_pairs={{0,2},{4,6},{8,10},{12,14},{3,1},{7,5},{11,9},{15,13},{16,18},{20,... | collective-permute-start | bytes 1179656 | tf_op jit(solution)/shard_map/ppermute | solution.py:159
  18.8 0.7 %copy-start.7 = (f32[256,384]{1,0:T(8,128)}, f32[256,384]{1,0:T(8,128)S(1)}, u32[]{:S(2)}) copy-start(f32[256,384]{1,0:T(8,128)S(1)} %collective-permute-done.1) | copy-start | bytes 1179652
  18.8 33.1 %copy-start.5 = (f32[8,256,128]{2,1,0:T(8,128)S(1)}, f32[8,256,128]{2,1,0:T(8,128)}, u32[]{:S(2)}) copy-start(f32[8,256,128]{2,1,0:T(8,128)} %get-tuple-element.11.lsrc_ref) | copy-start | bytes 3145732
  19.6 6.4 %collective-permute-start.2 = (f32[256,128]{1,0:T(8,128)S(1)}, f32[256,128]{1,0:T(8,128)S(1)}, u32[]{:S(2)}, u32[]{:S(2)}) collective-permute-start(f32[256,128]{1,0:T(8,128)S(1)} %slice.49), channel_id=1, source_target_pairs={{2,6},{6,10},{10,14},{5,1},{9,5},{13,9},{18,22},{22,26},{26,30},{2... | collective-permute-start | bytes 393224 | tf_op jit(solution)/shard_map/ppermute | solution.py:142
  26.3 5.7 %collective-permute-start.3 = (f32[256,128]{1,0:T(8,128)S(1)}, f32[256,128]{1,0:T(8,128)S(1)}, u32[]{:S(2)}, u32[]{:S(2)}) collective-permute-start(f32[256,128]{1,0:T(8,128)S(1)} %convolution_add_fusion.5), channel_id=1, source_target_pairs={{2,6},{6,10},{10,14},{5,1},{9,5},{13,9},{18,22},{22,26},{26,30},{2... | collective-permute-start | bytes 393224 | tf_op jit(solution)/shard_map/ppermute | solution.py:142
  32.1 19.9 %copy-start.4 = (bf16[8,256,256]{2,1,0:T(8,128)(2,1)S(1)}, bf16[8,256,256]{2,1,0:T(8,128)(2,1)}, u32[]{:S(2)}) copy-start(bf16[8,256,256]{2,1,0:T(8,128)(2,1)} %urows_ref.1) | copy-start | bytes 3145732
  32.4 5.8 %collective-permute-start.4 = (f32[256,128]{1,0:T(8,128)S(1)}, f32[256,128]{1,0:T(8,128)}, u32[]{:S(2)}, u32[]{:S(2)}) collective-permute-start(f32[256,128]{1,0:T(8,128)S(1)} %convolution_add_fusion.4), channel_id=1, source_target_pairs={{2,6},{6,10},{10,14},{5,1},{9,5},{13,9},{18,22},{22,26},{26,30},{2... | collective-permute-start | bytes 393224 | tf_op jit(solution)/shard_map/ppermute | solution.py:142
  38.3 3.5 %collective-permute-start.5 = (f32[256,128]{1,0:T(8,128)}, f32[256,128]{1,0:T(8,128)}, u32[]{:S(2)}, u32[]{:S(2)}) collective-permute-start(f32[256,128]{1,0:T(8,128)} %collective-permute-done.4), channel_id=1, source_target_pairs={{2,0},{6,4},{10,8},{14,12},{1,3},{5,7},{9,11},{13,15},{18,16},{22,... | collective-permute-start | bytes 393224 | tf_op jit(solution)/shard_map/ppermute | solution.py:184
  43.2 8.7 %copy-start.3 = (bf16[8,256,256]{2,1,0:T(8,128)(2,1)S(1)}, bf16[8,256,256]{2,1,0:T(8,128)(2,1)}, u32[]{:S(2)}) copy-start(bf16[8,256,256]{2,1,0:T(8,128)(2,1)} %lrows_ref.1) | copy-start | bytes 3145732
  43.6 8.3 %copy-start.1 = (bf16[8,256,256]{2,1,0:T(8,128)(2,1)S(1)}, bf16[8,256,256]{2,1,0:T(8,128)(2,1)}, u32[]{:S(2)}) copy-start(bf16[8,256,256]{2,1,0:T(8,128)(2,1)} %ltrans_ref.3) | copy-start | bytes 3145732
  43.6 8.3 %copy-start.2 = (bf16[8,256,256]{2,1,0:T(8,128)(2,1)S(1)}, bf16[8,256,256]{2,1,0:T(8,128)(2,1)}, u32[]{:S(2)}) copy-start(bf16[8,256,256]{2,1,0:T(8,128)(2,1)} %utrans_ref.3) | copy-start | bytes 3145732
  43.7 8.3 %collective-permute-start.6 = (f32[256,128]{1,0:T(8,128)S(1)}, f32[256,128]{1,0:T(8,128)S(1)}, u32[]{:S(2)}, u32[]{:S(2)}) collective-permute-start(f32[256,128]{1,0:T(8,128)S(1)} %convolution_add_fusion.2), channel_id=1, source_target_pairs={{0,1},{2,3},{4,5},{6,7},{8,9},{10,11},{12,13},{14,15},{1,0},{3,2},... | collective-permute-start | bytes 393224 | tf_op jit(solution)/shard_map/ppermute | solution.py:189
  52.0 1.2 %copy-start.6 = (f32[8,256,128]{2,1,0:T(8,128)S(1)}, f32[8,256,128]{2,1,0:T(8,128)}, u32[]{:S(2)}) copy-start(f32[8,256,128]{2,1,0:T(8,128)} %get-tuple-element.12.usrc_ref) | copy-start | bytes 3145732

commit v14 on v13

--- a/solution.py
+++ b/solution.py
@@ -53,7 +53,7 @@
 
 def apply_kernel(
     flag_ref, enter_ref, other_ref, ltrans_ref, utrans_ref, lsrc_ref, usrc_ref,
-    diag_ref, lrows_ref, urows_ref, out_ref, lround_ref, uround_ref,
+    diag_ref, rhs_ref, lrows_ref, urows_ref, out_ref, lround_ref, uround_ref,
 ):
     count = ltrans_ref.shape[0]
     first = flag_ref[0] == 0
@@ -68,7 +68,7 @@
             lstate = split_dot(ltrans_ref[lk], lstate) + lsrc_ref[lk]
             ustate = split_dot(utrans_ref[uk], ustate) + usrc_ref[uk]
     for k in range(count):
-        total = diag_ref[k]
+        total = jnp.dot(diag_ref[k], rhs_ref[k], preferred_element_type=F32)
         total = total + jnp.dot(lrows_ref[k], lround_ref[k], preferred_element_type=F32)
         total = total + jnp.dot(urows_ref[k], uround_ref[k], preferred_element_type=F32)
         out_ref[k] = total.astype(out_ref.dtype)
@@ -183,6 +183,7 @@
     back += [(4 * g + 1, 4 * g + 3) for g in range(groups)]
     sent = lax.ppermute(start, axis, back)
     mine = jnp.dot(beside[:, :rank], start, precision=HIGHEST) + beside[:, rank:]
+    mine, sent = lax.optimization_barrier((mine, sent))
     holder = jnp.logical_or(place == 1, place == 2)
     enter = jnp.where(holder, mine, sent)
     send = jnp.dot(own[:, :rank], enter, precision=HIGHEST) + own[:, rank:]
@@ -212,9 +213,6 @@
         ),
         name="sweep",
     )(right_sides, lower_cols, lower_trans, upper_cols, upper_trans)
-    diag = jnp.einsum(
-        "kab,kbc->kac", diagonal_blocks, right_sides, preferred_element_type=F32
-    )
     count_row = lax.axis_size("row")
     if count_row % 4 == 0 and count_row >= 8:
         first = lax.axis_index("row") % 2 == 0
@@ -237,10 +235,10 @@
             pltpu.VMEM((count, rank, rhs), BF16),
             pltpu.VMEM((count, rank, rhs), BF16),
         ],
-        in_specs=[pl.BlockSpec(memory_space=pltpu.SMEM)] + [vmem] * 9,
+        in_specs=[pl.BlockSpec(memory_space=pltpu.SMEM)] + [vmem] * 10,
         compiler_params=pltpu.CompilerParams(vmem_limit_bytes=LIMIT),
         name="apply",
-    )(flag, enter, other, lower_trans, upper_trans, lsrc, usrc, diag, lower_rows, upper_rows)
+    )(flag, enter, other, lower_trans, upper_trans, lsrc, usrc, diagonal_blocks, right_sides, lower_rows, upper_rows)
 
 
 def solution(mesh):

time: 56.7 us -> 60.8 us (1.072)
  local copies, waits for them, and re-layouts: 1.42 us -> 6.16 us
  matrix products: 5.21 us -> 3.36 us
  waiting for transfers between devices: 24.8 us -> 25.8 us
    unnamed x16, local copies, waits for them, and re-layouts: 1.39 us -> 6.13 us
    dot_general x1 -> x0, matrix products: 1.46 us -> none  [shards(): jnp.einsum('kab,kbc->kac', diagonal_blocks, right_sides, preferred_elemen...]
    dot_general x1, matrix products: 1.43 us -> 0.38 us  [scan_groups(): jnp.dot(beside[:, :rank], start, precision=HIGHEST) + beside[:, rank:]]
    ppermute x1, waiting for transfers between devices: 0.01 us -> 0.99 us  [scan_groups(): other = lax.ppermute(send, axis, partner)]
    ppermute x1, starting transfers between devices: 1.95 us -> 1.29 us  [scan_groups(): sent = lax.ppermute(start, axis, back)]
    dot_general x2, matrix products: 0.75 us -> 1.41 us  [scan_groups(): out = jnp.dot(both[:, :rank], start, precision=HIGHEST) + both[:, rank:]]
  transfers between devices with their start and end apart: 7 -> 7, of which waited for: 6 -> 7; matrix products, arithmetic and copies ran while one was open for 3% -> 1% of each run, Pallas kernels for 0% -> 0%
where the time goes in v14:
time: 60.8 us; the launch traced here: 60 us
  waiting for transfers between devices  25.8 us (42%)
  starting transfers between devices  13.7 us (23%)
  Pallas kernels  9.61 us (16%)
  local copies, waits for them, and re-layouts  6.16 us (10%)
  matrix products  3.36 us (6%)
  other arithmetic  1.18 us (2%)
    ppermute x3, waiting for transfers between devices, group_shift(): return lax.ppermute(value, axis, pairs)  14.1 us
    ppermute x1, waiting for transfers between devices, scan_groups(): beside = lax.ppermute(both, axis, pair)  7.48 us
    ppermute x1, starting transfers between devices, scan_groups(): other = lax.ppermute(send, axis, partner)  6.94 us
    pallas_call x1, Pallas kernels, shards(): pl.pallas_call(sweep_kernel, out_shape=(jax.ShapeDtypeStruct((rank, rank...  6.34 us
    unnamed x16, local copies, waits for them, and re-layouts  6.13 us
    ppermute x3, starting transfers between devices, group_shift(): return lax.ppermute(value, axis, pairs)  4.13 us
    pallas_call x1, Pallas kernels, shards(): pl.pallas_call(apply_kernel, out_shape=jax.ShapeDtypeStruct((count, rows,...  3.27 us
    ppermute x1, waiting for transfers between devices, scan_groups(): got = lax.ppermute(give, axis, partner)  1.71 us
  transfers between devices with their start and end apart: 7, of which 7 were waited for; matrix products, arithmetic and copies ran while one was open for 1% of the time, Pallas kernels for 0%

profile of v14, /device:TPU:1, one launch (start us, length us, event | category | flops | bytes accessed | tf_op | source)
XLA Modules:
  0.0 60.0 jit_solution(2121810133247351849)
XLA Ops:
  0.0 6.3 %sweep.1 = (f32[256,384]{1,0:T(8,128)}, f32[8,256,128]{2,1,0:T(8,128)}, f32[256,384]{1,0:T(8,128)}, f32[8,256,128]{2,1,0:T(8,128)}) custom-call(bf16[8,256,128]{2,1,0:T(8,128)(2,1)} %rhs_ref.3, bf16[8,256,256]{2,1,0:T(8,128)(2,1)} %lcols_ref.1, bf16[8,256,256]{2,1,0:T(8,128)(2,1)} %ltrans_ref.3, bf16[8,256,256]{2,1,0:T(8,128)(2,1)} %ucols_ref.1, ...), custom_call_target="tpu_custom_call" | custom-call | tf_op jit(solution)/shard_map/sweep/pallas_call | solution.py:206
  6.3 1.2 %broadcast_select_fusion.1 = (f32[256,384]{1,0:T(8,128)S(1)}, f32[256,384]{1,0:T(8,128)S(1)}) fusion(f32[256,384]{1,0:T(8,128)} %get-tuple-element.11, f32[256,384]{1,0:T(8,128)} %get-tuple-element.12, pred[]{:T(512)S(6)} %eq.15), kind=kLoop, calls=%fused_computation.13 | loop fusion | flops 196608 | bytes 1572865 | tf_op jit(solution)/shard_map/jit(_where)/select_n | solution.py:220
  7.5 0.1 collective-permute-start
  7.6 1.7 %collective-permute-done = f32[256,384]{1,0:T(8,128)S(1)} collective-permute-done((f32[256,384]{1,0:T(8,128)S(1)}, f32[256,384]{1,0:T(8,128)S(1)}, u32[]{:S(2)}, u32[]{:S(2)}) %collective-permute-start) | collective-permute-done | bytes 393248 | tf_op jit(solution)/shard_map/ppermute | solution.py:153
  9.3 0.6 convolution_add_fusion.1
  9.9 1.3 %collective-permute-start.1 = (f32[256,384]{1,0:T(8,128)S(1)}, f32[256,384]{1,0:T(8,128)S(1)}, u32[]{:S(2)}, u32[]{:S(2)}) collective-permute-start(f32[256,384]{1,0:T(8,128)S(1)} %convolution_add_fusion.1), channel_id=1, source_target_pairs={{0,2},{4,6},{8,10},{12,14},{3,1},{7,5},{11,9},{15,13},{16,18},{20,... | collective-permute-start | bytes 1179656 | tf_op jit(solution)/shard_map/ppermute | solution.py:159
  11.2 7.5 %collective-permute-done.1 = f32[256,384]{1,0:T(8,128)S(1)} collective-permute-done((f32[256,384]{1,0:T(8,128)S(1)}, f32[256,384]{1,0:T(8,128)S(1)}, u32[]{:S(2)}, u32[]{:S(2)}) %collective-permute-start.1) | collective-permute-done | bytes 393248 | tf_op jit(solution)/shard_map/ppermute | solution.py:159
  18.7 0.6 convolution_add_fusion
  19.3 0.0 copy-start.2
  19.4 1.4 %collective-permute-start.2 = (f32[256,128]{1,0:T(8,128)S(1)}, f32[256,128]{1,0:T(8,128)S(1)}, u32[]{:S(2)}, u32[]{:S(2)}) collective-permute-start(f32[256,128]{1,0:T(8,128)S(1)} %slice.49), channel_id=1, source_target_pairs={{2,6},{6,10},{10,14},{5,1},{9,5},{13,9},{18,22},{22,26},{26,30},{2... | collective-permute-start | bytes 393224 | tf_op jit(solution)/shard_map/ppermute | solution.py:142
  20.8 5.1 %collective-permute-done.2 = f32[256,128]{1,0:T(8,128)S(1)} collective-permute-done((f32[256,128]{1,0:T(8,128)S(1)}, f32[256,128]{1,0:T(8,128)S(1)}, u32[]{:S(2)}, u32[]{:S(2)}) %collective-permute-start.2) | collective-permute-done | bytes 131104 | tf_op jit(solution)/shard_map/ppermute | solution.py:142
  25.9 0.0 copy-start.1
  25.9 0.4 convolution_add_fusion.5
  26.3 0.0 copy-start
  26.3 1.4 %collective-permute-start.3 = (f32[256,128]{1,0:T(8,128)S(1)}, f32[256,128]{1,0:T(8,128)S(1)}, u32[]{:S(2)}, u32[]{:S(2)}) collective-permute-start(f32[256,128]{1,0:T(8,128)S(1)} %convolution_add_fusion.5), channel_id=1, source_target_pairs={{2,6},{6,10},{10,14},{5,1},{9,5},{13,9},{18,22},{22,26},{26,30},{2... | collective-permute-start | bytes 393224 | tf_op jit(solution)/shard_map/ppermute | solution.py:142
  27.7 4.4 %collective-permute-done.3 = f32[256,128]{1,0:T(8,128)S(1)} collective-permute-done((f32[256,128]{1,0:T(8,128)S(1)}, f32[256,128]{1,0:T(8,128)S(1)}, u32[]{:S(2)}, u32[]{:S(2)}) %collective-permute-start.3) | collective-permute-done | bytes 131104 | tf_op jit(solution)/shard_map/ppermute | solution.py:142
  32.1 1.0 %convolution_add_fusion.4 = f32[256,128]{1,0:T(8,128)} fusion(f32[256,128]{1,0:T(8,128)S(1)} %collective-permute-done.3, f32[256,384]{1,0:T(8,128)S(1)} %convolution_add_fusion), kind=kOutput, calls=%fused_computation.4 | convolution fusion | flops 100696064 | bytes 655360 | tf_op jit(solution)/shard_map/dot_general | solution.py:168
  33.2 1.3 %collective-permute-start.4 = (f32[256,128]{1,0:T(8,128)}, f32[256,128]{1,0:T(8,128)S(1)}, u32[]{:S(2)}, u32[]{:S(2)}) collective-permute-start(f32[256,128]{1,0:T(8,128)} %convolution_add_fusion.4), channel_id=1, source_target_pairs={{2,6},{6,10},{10,14},{5,1},{9,5},{13,9},{18,22},{22,26},{26,30},{2... | collective-permute-start | bytes 393224 | tf_op jit(solution)/shard_map/ppermute | solution.py:142
  34.5 4.6 %collective-permute-done.4 = f32[256,128]{1,0:T(8,128)S(1)} collective-permute-done((f32[256,128]{1,0:T(8,128)}, f32[256,128]{1,0:T(8,128)S(1)}, u32[]{:S(2)}, u32[]{:S(2)}) %collective-permute-start.4) | collective-permute-done | bytes 131104 | tf_op jit(solution)/shard_map/ppermute | solution.py:142
  39.1 1.3 %collective-permute-start.5 = (f32[256,128]{1,0:T(8,128)S(1)}, f32[256,128]{1,0:T(8,128)S(1)}, u32[]{:S(2)}, u32[]{:S(2)}) collective-permute-start(f32[256,128]{1,0:T(8,128)S(1)} %collective-permute-done.4), channel_id=1, source_target_pairs={{2,0},{6,4},{10,8},{14,12},{1,3},{5,7},{9,11},{13,15},{18,16},{22,... | collective-permute-start | bytes 393224 | tf_op jit(solution)/shard_map/ppermute | solution.py:184
  40.4 0.4 convolution_add_fusion.3
  40.8 1.5 %collective-permute-done.5 = f32[256,128]{1,0:T(8,128)S(1)} collective-permute-done((f32[256,128]{1,0:T(8,128)S(1)}, f32[256,128]{1,0:T(8,128)S(1)}, u32[]{:S(2)}, u32[]{:S(2)}) %collective-permute-start.5) | collective-permute-done | bytes 131104 | tf_op jit(solution)/shard_map/ppermute | solution.py:184
  42.3 0.4 convolution_add_fusion.2
  42.7 6.9 %collective-permute-start.6 = (f32[256,128]{1,0:T(8,128)S(1)}, f32[256,128]{1,0:T(8,128)S(1)}, u32[]{:S(2)}, u32[]{:S(2)}) collective-permute-start(f32[256,128]{1,0:T(8,128)S(1)} %convolution_add_fusion.2), channel_id=1, source_target_pairs={{0,1},{2,3},{4,5},{6,7},{8,9},{10,11},{12,13},{14,15},{1,0},{3,2},... | collective-permute-start | bytes 393224 | tf_op jit(solution)/shard_map/ppermute | solution.py:190
  49.6 1.0 %collective-permute-done.6.other_ref = f32[256,128]{1,0:T(8,128)S(1)} collective-permute-done((f32[256,128]{1,0:T(8,128)S(1)}, f32[256,128]{1,0:T(8,128)S(1)}, u32[]{:S(2)}, u32[]{:S(2)}) %collective-permute-start.6) | collective-permute-done | bytes 131104 | tf_op jit(solution)/shard_map/ppermute | solution.py:190
  50.6 0.0 copy-done.2
  50.6 0.0 copy-done.1
  50.6 0.0 copy-done
  50.6 0.0 copy-start.3
  50.6 1.2 %copy-done.3 = bf16[8,256,256]{2,1,0:T(8,128)(2,1)S(1)} copy-done((bf16[8,256,256]{2,1,0:T(8,128)(2,1)S(1)}, bf16[8,256,256]{2,1,0:T(8,128)(2,1)}, u32[]{:S(2)}) %copy-start.3) | copy-done | bytes 1048600
  51.9 0.0 copy-start.4
  51.9 1.2 %copy-done.4 = bf16[8,256,256]{2,1,0:T(8,128)(2,1)S(1)} copy-done((bf16[8,256,256]{2,1,0:T(8,128)(2,1)S(1)}, bf16[8,256,256]{2,1,0:T(8,128)(2,1)}, u32[]{:S(2)}) %copy-start.4) | copy-done | bytes 1048600
  53.1 0.0 copy-start.5
  53.1 1.2 %copy-done.5 = bf16[8,256,256]{2,1,0:T(8,128)(2,1)S(1)} copy-done((bf16[8,256,256]{2,1,0:T(8,128)(2,1)S(1)}, bf16[8,256,256]{2,1,0:T(8,128)(2,1)}, u32[]{:S(2)}) %copy-start.5) | copy-done | bytes 1048600
  54.3 0.0 copy-start.6
  54.3 1.2 %copy-done.6 = f32[8,256,128]{2,1,0:T(8,128)S(1)} copy-done((f32[8,256,128]{2,1,0:T(8,128)S(1)}, f32[8,256,128]{2,1,0:T(8,128)}, u32[]{:S(2)}) %copy-start.6) | copy-done | bytes 1048600
  55.5 0.0 copy-start.7
  55.5 1.2 %copy-done.7 = f32[8,256,128]{2,1,0:T(8,128)S(1)} copy-done((f32[8,256,128]{2,1,0:T(8,128)S(1)}, f32[8,256,128]{2,1,0:T(8,128)}, u32[]{:S(2)}) %copy-start.7) | copy-done | bytes 1048600
  56.8 3.3 %apply.1 = bf16[8,256,128]{2,1,0:T(8,128)(2,1)} custom-call(s32[1]{0:T(128)} %bitcast.flag_ref, f32[256,128]{1,0:T(8,128)S(1)} %broadcast_select_fusion.2.enter_ref, f32[256,128]{1,0:T(8,128)S(1)} %collective-permute-done.6.other_ref, bf16[8,256,256]{2,1,0:T(8,128)(2,1)S(1)} %copy-done, bf16[8,256,256]{2,1,0:T(8,128)(2,1)S(1)} %copy-done.1, ...), custom_call_target="tpu_custom_call" | custom-call | tf_op jit(solution)/shard_map/apply/pallas_call | solution.py:231
  (4 shorter events, 0.0 us)
Async XLA Ops:
  7.5 1.8 %collective-permute-start = (f32[256,384]{1,0:T(8,128)S(1)}, f32[256,384]{1,0:T(8,128)S(1)}, u32[]{:S(2)}, u32[]{:S(2)}) collective-permute-start(f32[256,384]{1,0:T(8,128)S(1)} %get-tuple-element.17), channel_id=1, source_target_pairs={{0,1},{2,3},{4,5},{6,7},{8,9},{10,11},{12,13},{14,15},{1,0},{3,2},... | collective-permute-start | bytes 1179656 | tf_op jit(solution)/shard_map/ppermute | solution.py:153
  9.9 8.8 %collective-permute-start.1 = (f32[256,384]{1,0:T(8,128)S(1)}, f32[256,384]{1,0:T(8,128)S(1)}, u32[]{:S(2)}, u32[]{:S(2)}) collective-permute-start(f32[256,384]{1,0:T(8,128)S(1)} %convolution_add_fusion.1), channel_id=1, source_target_pairs={{0,2},{4,6},{8,10},{12,14},{3,1},{7,5},{11,9},{15,13},{16,18},{20,... | collective-permute-start | bytes 1179656 | tf_op jit(solution)/shard_map/ppermute | solution.py:159
  19.3 31.3 %copy-start.2 = (bf16[8,256,128]{2,1,0:T(8,128)(2,1)S(1)}, bf16[8,256,128]{2,1,0:T(8,128)(2,1)}, u32[]{:S(2)}) copy-start(bf16[8,256,128]{2,1,0:T(8,128)(2,1)} %rhs_ref.3) | copy-start | bytes 1572868
  19.4 6.5 %collective-permute-start.2 = (f32[256,128]{1,0:T(8,128)S(1)}, f32[256,128]{1,0:T(8,128)S(1)}, u32[]{:S(2)}, u32[]{:S(2)}) collective-permute-start(f32[256,128]{1,0:T(8,128)S(1)} %slice.49), channel_id=1, source_target_pairs={{2,6},{6,10},{10,14},{5,1},{9,5},{13,9},{18,22},{22,26},{26,30},{2... | collective-permute-start | bytes 393224 | tf_op jit(solution)/shard_map/ppermute | solution.py:142
  25.9 24.7 %copy-start.1 = (bf16[8,256,256]{2,1,0:T(8,128)(2,1)S(1)}, bf16[8,256,256]{2,1,0:T(8,128)(2,1)}, u32[]{:S(2)}) copy-start(bf16[8,256,256]{2,1,0:T(8,128)(2,1)} %utrans_ref.3) | copy-start | bytes 3145732
  26.3 24.4 %copy-start = (bf16[8,256,256]{2,1,0:T(8,128)(2,1)S(1)}, bf16[8,256,256]{2,1,0:T(8,128)(2,1)}, u32[]{:S(2)}) copy-start(bf16[8,256,256]{2,1,0:T(8,128)(2,1)} %ltrans_ref.3) | copy-start | bytes 3145732
  26.3 5.8 %collective-permute-start.3 = (f32[256,128]{1,0:T(8,128)S(1)}, f32[256,128]{1,0:T(8,128)S(1)}, u32[]{:S(2)}, u32[]{:S(2)}) collective-permute-start(f32[256,128]{1,0:T(8,128)S(1)} %convolution_add_fusion.5), channel_id=1, source_target_pairs={{2,6},{6,10},{10,14},{5,1},{9,5},{13,9},{18,22},{22,26},{26,30},{2... | collective-permute-start | bytes 393224 | tf_op jit(solution)/shard_map/ppermute | solution.py:142
  33.2 5.9 %collective-permute-start.4 = (f32[256,128]{1,0:T(8,128)}, f32[256,128]{1,0:T(8,128)S(1)}, u32[]{:S(2)}, u32[]{:S(2)}) collective-permute-start(f32[256,128]{1,0:T(8,128)} %convolution_add_fusion.4), channel_id=1, source_target_pairs={{2,6},{6,10},{10,14},{5,1},{9,5},{13,9},{18,22},{22,26},{26,30},{2... | collective-permute-start | bytes 393224 | tf_op jit(solution)/shard_map/ppermute | solution.py:142
  39.1 3.2 %collective-permute-start.5 = (f32[256,128]{1,0:T(8,128)S(1)}, f32[256,128]{1,0:T(8,128)S(1)}, u32[]{:S(2)}, u32[]{:S(2)}) collective-permute-start(f32[256,128]{1,0:T(8,128)S(1)} %collective-permute-done.4), channel_id=1, source_target_pairs={{2,0},{6,4},{10,8},{14,12},{1,3},{5,7},{9,11},{13,15},{18,16},{22,... | collective-permute-start | bytes 393224 | tf_op jit(solution)/shard_map/ppermute | solution.py:184
  42.7 7.9 %collective-permute-start.6 = (f32[256,128]{1,0:T(8,128)S(1)}, f32[256,128]{1,0:T(8,128)S(1)}, u32[]{:S(2)}, u32[]{:S(2)}) collective-permute-start(f32[256,128]{1,0:T(8,128)S(1)} %convolution_add_fusion.2), channel_id=1, source_target_pairs={{0,1},{2,3},{4,5},{6,7},{8,9},{10,11},{12,13},{14,15},{1,0},{3,2},... | collective-permute-start | bytes 393224 | tf_op jit(solution)/shard_map/ppermute | solution.py:190
  50.6 1.2 %copy-start.3 = (bf16[8,256,256]{2,1,0:T(8,128)(2,1)S(1)}, bf16[8,256,256]{2,1,0:T(8,128)(2,1)}, u32[]{:S(2)}) copy-start(bf16[8,256,256]{2,1,0:T(8,128)(2,1)} %diag_ref.1) | copy-start | bytes 3145732
  51.9 1.2 %copy-start.4 = (bf16[8,256,256]{2,1,0:T(8,128)(2,1)S(1)}, bf16[8,256,256]{2,1,0:T(8,128)(2,1)}, u32[]{:S(2)}) copy-start(bf16[8,256,256]{2,1,0:T(8,128)(2,1)} %lrows_ref.1) | copy-start | bytes 3145732
  53.1 1.2 %copy-start.5 = (bf16[8,256,256]{2,1,0:T(8,128)(2,1)S(1)}, bf16[8,256,256]{2,1,0:T(8,128)(2,1)}, u32[]{:S(2)}) copy-start(bf16[8,256,256]{2,1,0:T(8,128)(2,1)} %urows_ref.1) | copy-start | bytes 3145732
  54.3 1.2 %copy-start.6 = (f32[8,256,128]{2,1,0:T(8,128)S(1)}, f32[8,256,128]{2,1,0:T(8,128)}, u32[]{:S(2)}) copy-start(f32[8,256,128]{2,1,0:T(8,128)} %get-tuple-element.15.lsrc_ref) | copy-start | bytes 3145732
  55.5 1.2 %copy-start.7 = (f32[8,256,128]{2,1,0:T(8,128)S(1)}, f32[8,256,128]{2,1,0:T(8,128)}, u32[]{:S(2)}) copy-start(f32[8,256,128]{2,1,0:T(8,128)} %get-tuple-element.16.usrc_ref) | copy-start | bytes 3145732

commit v15 on v13

--- a/solution.py
+++ b/solution.py
@@ -21,9 +21,11 @@
 
 def sweep_kernel(
     rhs_ref, lcols_ref, ltrans_ref, ucols_ref, utrans_ref,
-    lmap_ref, lsrc_ref, umap_ref, usrc_ref,
+    lmap_ref, lsrc_hbm, umap_ref, usrc_hbm,
+    lsrc_ref, usrc_ref, sems,
 ):
     count = rhs_ref.shape[0]
+    copies = []
     lmap = lstate = umap = ustate = None
     for step in range(count):
         lk = step
@@ -32,6 +34,10 @@
         usrc = lax.dot_general(ucols_ref[uk], rhs_ref[uk], (((0,), (0,)), ((), ())), preferred_element_type=F32)
         lsrc_ref[lk] = lsrc
         usrc_ref[uk] = usrc
+        for target, source, k, side in ((lsrc_hbm, lsrc_ref, lk, 0), (usrc_hbm, usrc_ref, uk, 1)):
+            copy = pltpu.make_async_copy(source.at[k], target.at[k], sems.at[side, k])
+            copy.start()
+            copies.append(copy)
         ltrans = ltrans_ref[lk]
         utrans = utrans_ref[uk]
         if step == 0:
@@ -44,6 +50,8 @@
             ustate = split_dot(utrans, ustate) + usrc
             lmap = split_dot(ltrans, lmap)
             umap = split_dot(utrans, umap)
+    for copy in copies:
+        copy.wait()
     rank = lmap.shape[0]
     lmap_ref[:, :rank] = lmap
     lmap_ref[:, rank:] = lstate
@@ -210,6 +218,17 @@
             jax.ShapeDtypeStruct((rank, rank + rhs), F32),
             jax.ShapeDtypeStruct((count, rank, rhs), F32),
         ),
+        out_specs=(
+            pl.BlockSpec(memory_space=pltpu.VMEM),
+            pl.BlockSpec(memory_space=pl.ANY),
+            pl.BlockSpec(memory_space=pltpu.VMEM),
+            pl.BlockSpec(memory_space=pl.ANY),
+        ),
+        scratch_shapes=[
+            pltpu.VMEM((count, rank, rhs), F32),
+            pltpu.VMEM((count, rank, rhs), F32),
+            pltpu.SemaphoreType.DMA((2, count)),
+        ],
         name="sweep",
     )(right_sides, lower_cols, lower_trans, upper_cols, upper_trans)
     diag = jnp.einsum(

time: 56.7 us -> 56.9 us (level)
  no operation moved by 1% of the time
where the time goes in v15:
time: 56.9 us; the launch traced here: 56.5 us
  waiting for transfers between devices  24.8 us (44%)
  starting transfers between devices  14 us (25%)
  Pallas kernels  9.67 us (17%)
  matrix products  5.21 us (9%)
  local copies, waits for them, and re-layouts  1.42 us (2%)
  other arithmetic  1.17 us (2%)
    ppermute x3, waiting for transfers between devices, group_shift(): return lax.ppermute(value, axis, pairs)  14 us
    ppermute x1, waiting for transfers between devices, scan_groups(): beside = lax.ppermute(both, axis, pair)  7.48 us
    ppermute x1, starting transfers between devices, scan_groups(): other = lax.ppermute(send, axis, partner)  6.79 us
    pallas_call x1, Pallas kernels, shards(): pl.pallas_call(sweep_kernel, out_shape=(jax.ShapeDtypeStruct((rank, rank...  6.62 us
    ppermute x3, starting transfers between devices, group_shift(): return lax.ppermute(value, axis, pairs)  3.88 us
    pallas_call x1, Pallas kernels, shards(): pl.pallas_call(apply_kernel, out_shape=jax.ShapeDtypeStruct((count, rows,...  3.05 us
    ppermute x1, starting transfers between devices, scan_groups(): sent = lax.ppermute(start, axis, back)  1.95 us
    ppermute x1, waiting for transfers between devices, scan_groups(): got = lax.ppermute(give, axis, partner)  1.71 us
  transfers between devices with their start and end apart: 7, of which 6 were waited for; matrix products, arithmetic and copies ran while one was open for 3% of the time, Pallas kernels for 0%

profile of v15, /device:TPU:1, one launch (start us, length us, event | category | flops | bytes accessed | tf_op | source)
XLA Modules:
  0.0 56.5 jit_solution(15457973423285279224)
XLA Ops:
  0.0 0.0 copy-start
  0.0 6.6 %sweep.1 = (f32[256,384]{1,0:T(8,128)}, f32[8,256,128]{2,1,0:T(8,128)}, f32[256,384]{1,0:T(8,128)}, f32[8,256,128]{2,1,0:T(8,128)}) custom-call(bf16[8,256,128]{2,1,0:T(8,128)(2,1)} %rhs_ref.1, bf16[8,256,256]{2,1,0:T(8,128)(2,1)} %lcols_ref.1, bf16[8,256,256]{2,1,0:T(8,128)(2,1)} %ltrans_ref.3, bf16[8,256,256]{2,1,0:T(8,128)(2,1)} %ucols_ref.1, ...), custom_call_target="tpu_custom_call" | custom-call | tf_op jit(solution)/shard_map/sweep/pallas_call | solution.py:213
  6.6 1.2 %broadcast_select_fusion.1 = (f32[256,384]{1,0:T(8,128)S(1)}, f32[256,384]{1,0:T(8,128)S(1)}) fusion(f32[256,384]{1,0:T(8,128)} %get-tuple-element.9, f32[256,384]{1,0:T(8,128)} %get-tuple-element.10, pred[]{:T(512)S(6)} %eq.15), kind=kLoop, calls=%fused_computation.14 | loop fusion | flops 196608 | bytes 1572865 | tf_op jit(solution)/shard_map/jit(_where)/select_n | solution.py:241
  7.8 0.1 collective-permute-start
  7.9 1.7 %collective-permute-done = f32[256,384]{1,0:T(8,128)S(1)} collective-permute-done((f32[256,384]{1,0:T(8,128)S(1)}, f32[256,384]{1,0:T(8,128)S(1)}, u32[]{:S(2)}, u32[]{:S(2)}) %collective-permute-start) | collective-permute-done | bytes 393248 | tf_op jit(solution)/shard_map/ppermute | solution.py:161
  9.6 0.6 %convolution_add_fusion.1 = f32[256,384]{1,0:T(8,128)S(1)} fusion(f32[256,384]{1,0:T(8,128)S(1)} %get-tuple-element.14, f32[256,128]{1,0:T(8,128)S(1)} %slice.44, f32[256,384]{1,0:T(8,128)S(1)} %collective-permute-done), kind=kOutput, calls=%fused_computation.1 | convolution fusion | flops 302088192 | bytes 1179648 | tf_op jit(solution)/shard_map/dot_general | solution.py:162
  10.2 1.3 %collective-permute-start.1 = (f32[256,384]{1,0:T(8,128)S(1)}, f32[256,384]{1,0:T(8,128)S(1)}, u32[]{:S(2)}, u32[]{:S(2)}) collective-permute-start(f32[256,384]{1,0:T(8,128)S(1)} %convolution_add_fusion.1), channel_id=1, source_target_pairs={{0,2},{4,6},{8,10},{12,14},{3,1},{7,5},{11,9},{15,13},{16,18},{20,... | collective-permute-start | bytes 1179656 | tf_op jit(solution)/shard_map/ppermute | solution.py:167
  11.5 7.5 %collective-permute-done.1 = f32[256,384]{1,0:T(8,128)S(1)} collective-permute-done((f32[256,384]{1,0:T(8,128)S(1)}, f32[256,384]{1,0:T(8,128)S(1)}, u32[]{:S(2)}, u32[]{:S(2)}) %collective-permute-start.1) | collective-permute-done | bytes 393248 | tf_op jit(solution)/shard_map/ppermute | solution.py:167
  19.0 0.0 copy-start.7
  19.0 0.0 copy-start.5
  19.0 0.6 %convolution_add_fusion = f32[256,384]{1,0:T(8,128)S(1)} fusion(f32[256,384]{1,0:T(8,128)S(1)} %collective-permute-done.1, f32[256,128]{1,0:T(8,128)S(1)} %slice.47, f32[256,384]{1,0:T(8,128)S(1)} %convolution_add_fusion.1), kind=kOutput, calls=%fused_computation | convolution fusion | flops 302088192 | bytes 1179648 | tf_op jit(solution)/shard_map/dot_general | solution.py:168
  19.6 0.1 copy-done.7
  19.8 1.3 %collective-permute-start.2 = (f32[256,128]{1,0:T(8,128)S(1)}, f32[256,128]{1,0:T(8,128)S(1)}, u32[]{:S(2)}, u32[]{:S(2)}) collective-permute-start(f32[256,128]{1,0:T(8,128)S(1)} %slice.49), channel_id=1, source_target_pairs={{2,6},{6,10},{10,14},{5,1},{9,5},{13,9},{18,22},{22,26},{26,30},{2... | collective-permute-start | bytes 393224 | tf_op jit(solution)/shard_map/ppermute | solution.py:150
  21.1 5.1 %collective-permute-done.2 = f32[256,128]{1,0:T(8,128)S(1)} collective-permute-done((f32[256,128]{1,0:T(8,128)S(1)}, f32[256,128]{1,0:T(8,128)S(1)}, u32[]{:S(2)}, u32[]{:S(2)}) %collective-permute-start.2) | collective-permute-done | bytes 131104 | tf_op jit(solution)/shard_map/ppermute | solution.py:150
  26.2 0.4 convolution_add_fusion.5
  26.5 1.3 %collective-permute-start.3 = (f32[256,128]{1,0:T(8,128)S(1)}, f32[256,128]{1,0:T(8,128)S(1)}, u32[]{:S(2)}, u32[]{:S(2)}) collective-permute-start(f32[256,128]{1,0:T(8,128)S(1)} %convolution_add_fusion.5), channel_id=1, source_target_pairs={{2,6},{6,10},{10,14},{5,1},{9,5},{13,9},{18,22},{22,26},{26,30},{2... | collective-permute-start | bytes 393224 | tf_op jit(solution)/shard_map/ppermute | solution.py:150
  27.8 4.4 %collective-permute-done.3 = f32[256,128]{1,0:T(8,128)S(1)} collective-permute-done((f32[256,128]{1,0:T(8,128)S(1)}, f32[256,128]{1,0:T(8,128)S(1)}, u32[]{:S(2)}, u32[]{:S(2)}) %collective-permute-start.3) | collective-permute-done | bytes 131104 | tf_op jit(solution)/shard_map/ppermute | solution.py:150
  32.3 0.0 copy-start.4
  32.3 0.4 convolution_add_fusion.4
  32.6 1.3 %collective-permute-start.4 = (f32[256,128]{1,0:T(8,128)S(1)}, f32[256,128]{1,0:T(8,128)}, u32[]{:S(2)}, u32[]{:S(2)}) collective-permute-start(f32[256,128]{1,0:T(8,128)S(1)} %convolution_add_fusion.4), channel_id=1, source_target_pairs={{2,6},{6,10},{10,14},{5,1},{9,5},{13,9},{18,22},{22,26},{26,30},{2... | collective-permute-start | bytes 393224 | tf_op jit(solution)/shard_map/ppermute | solution.py:150
  33.9 4.5 %collective-permute-done.4 = f32[256,128]{1,0:T(8,128)} collective-permute-done((f32[256,128]{1,0:T(8,128)S(1)}, f32[256,128]{1,0:T(8,128)}, u32[]{:S(2)}, u32[]{:S(2)}) %collective-permute-start.4) | collective-permute-done | bytes 131104 | tf_op jit(solution)/shard_map/ppermute | solution.py:150
  38.5 1.9 %collective-permute-start.5 = (f32[256,128]{1,0:T(8,128)}, f32[256,128]{1,0:T(8,128)}, u32[]{:S(2)}, u32[]{:S(2)}) collective-permute-start(f32[256,128]{1,0:T(8,128)} %collective-permute-done.4), channel_id=1, source_target_pairs={{2,0},{6,4},{10,8},{14,12},{1,3},{5,7},{9,11},{13,15},{18,16},{22,... | collective-permute-start | bytes 393224 | tf_op jit(solution)/shard_map/ppermute | solution.py:192
  40.4 1.6 %collective-permute-done.5 = f32[256,128]{1,0:T(8,128)} collective-permute-done((f32[256,128]{1,0:T(8,128)}, f32[256,128]{1,0:T(8,128)}, u32[]{:S(2)}, u32[]{:S(2)}) %collective-permute-start.5) | collective-permute-done | bytes 131104 | tf_op jit(solution)/shard_map/ppermute | solution.py:192
  42.0 1.4 %fusion.enter_ref = f32[256,128]{1,0:T(8,128)S(1)} fusion(f32[256,128]{1,0:T(8,128)} %collective-permute-done.5, f32[256,128]{1,0:T(8,128)} %collective-permute-done.4, f32[256,384]{1,0:T(8,128)} %copy-done.7, pred[]{:T(512)S(6)} %or.3), kind=kOutput, calls=%fused_computation.4 | convolution fusion | flops 100728832 | bytes 786433 | tf_op jit(solution)/shard_map/dot_general | solution.py:193
  43.4 0.0 copy-start.3
  43.4 0.4 convolution_add_fusion.2
  43.8 0.0 copy-start.1
  43.8 0.0 copy-start.2
  43.9 6.8 %collective-permute-start.6 = (f32[256,128]{1,0:T(8,128)S(1)}, f32[256,128]{1,0:T(8,128)S(1)}, u32[]{:S(2)}, u32[]{:S(2)}) collective-permute-start(f32[256,128]{1,0:T(8,128)S(1)} %convolution_add_fusion.2), channel_id=1, source_target_pairs={{0,1},{2,3},{4,5},{6,7},{8,9},{10,11},{12,13},{14,15},{1,0},{3,2},... | collective-permute-start | bytes 393224 | tf_op jit(solution)/shard_map/ppermute | solution.py:197
  50.6 0.0 copy-done
  50.7 1.5 %fusion.7.diag_ref = f32[8,256,128]{2,1,0:T(8,128)S(1)} fusion(bf16[8,256,256]{2,1,0:T(8,128)(2,1)S(1)} %copy-done, bf16[8,256,128]{2,1,0:T(8,128)(2,1)} %rhs_ref.1), kind=kOutput, calls=%fused_computation.15 | convolution fusion | flops 134217728 | bytes 2621440 | tf_op jit(solution)/shard_map/kab,kbc->kac/dot_general | solution.py:234
  52.1 0.0 collective-permute-done.6.other_ref
  52.1 0.0 copy-done.5
  52.1 0.0 copy-done.4
  52.2 0.0 copy-done.3
  52.2 0.0 copy-done.1
  52.2 0.0 copy-done.2
  52.2 0.0 copy-start.6
  52.2 1.2 %copy-done.6 = f32[8,256,128]{2,1,0:T(8,128)S(1)} copy-done((f32[8,256,128]{2,1,0:T(8,128)S(1)}, f32[8,256,128]{2,1,0:T(8,128)}, u32[]{:S(2)}) %copy-start.6) | copy-done | bytes 1048600
  53.4 3.1 %apply.1 = bf16[8,256,128]{2,1,0:T(8,128)(2,1)} custom-call(s32[1]{0:T(128)} %bitcast.flag_ref, f32[256,128]{1,0:T(8,128)S(1)} %fusion.enter_ref, f32[256,128]{1,0:T(8,128)S(1)} %collective-permute-done.6.other_ref, bf16[8,256,256]{2,1,0:T(8,128)(2,1)S(1)} %copy-done.1, bf16[8,256,256]{2,1,0:T(8,128)(2,1)S(1)} %copy-done.2, f32[8,256,128]{2,1,0:T(8,128)S(1)} %copy-done.5, ...), custom_call_target="tpu_custom_call" | custom-call | tf_op jit(solution)/shard_map/apply/pallas_call | solution.py:252
  (3 shorter events, 0.0 us)
Async XLA Ops:
  0.0 50.7 %copy-start = (bf16[8,256,256]{2,1,0:T(8,128)(2,1)S(1)}, bf16[8,256,256]{2,1,0:T(8,128)(2,1)}, u32[]{:S(2)}) copy-start(bf16[8,256,256]{2,1,0:T(8,128)(2,1)} %param.9) | copy-start | bytes 3145732
  7.8 1.8 %collective-permute-start = (f32[256,384]{1,0:T(8,128)S(1)}, f32[256,384]{1,0:T(8,128)S(1)}, u32[]{:S(2)}, u32[]{:S(2)}) collective-permute-start(f32[256,384]{1,0:T(8,128)S(1)} %get-tuple-element.13), channel_id=1, source_target_pairs={{0,1},{2,3},{4,5},{6,7},{8,9},{10,11},{12,13},{14,15},{1,0},{3,2},... | collective-permute-start | bytes 1179656 | tf_op jit(solution)/shard_map/ppermute | solution.py:161
  10.2 8.8 %collective-permute-start.1 = (f32[256,384]{1,0:T(8,128)S(1)}, f32[256,384]{1,0:T(8,128)S(1)}, u32[]{:S(2)}, u32[]{:S(2)}) collective-permute-start(f32[256,384]{1,0:T(8,128)S(1)} %convolution_add_fusion.1), channel_id=1, source_target_pairs={{0,2},{4,6},{8,10},{12,14},{3,1},{7,5},{11,9},{15,13},{16,18},{20,... | collective-permute-start | bytes 1179656 | tf_op jit(solution)/shard_map/ppermute | solution.py:167
  19.0 0.7 %copy-start.7 = (f32[256,384]{1,0:T(8,128)}, f32[256,384]{1,0:T(8,128)S(1)}, u32[]{:S(2)}) copy-start(f32[256,384]{1,0:T(8,128)S(1)} %collective-permute-done.1) | copy-start | bytes 1179652
  19.0 33.1 %copy-start.5 = (f32[8,256,128]{2,1,0:T(8,128)S(1)}, f32[8,256,128]{2,1,0:T(8,128)}, u32[]{:S(2)}) copy-start(f32[8,256,128]{2,1,0:T(8,128)} %get-tuple-element.11.lsrc_ref) | copy-start | bytes 3145732
  19.8 6.4 %collective-permute-start.2 = (f32[256,128]{1,0:T(8,128)S(1)}, f32[256,128]{1,0:T(8,128)S(1)}, u32[]{:S(2)}, u32[]{:S(2)}) collective-permute-start(f32[256,128]{1,0:T(8,128)S(1)} %slice.49), channel_id=1, source_target_pairs={{2,6},{6,10},{10,14},{5,1},{9,5},{13,9},{18,22},{22,26},{26,30},{2... | collective-permute-start | bytes 393224 | tf_op jit(solution)/shard_map/ppermute | solution.py:150
  26.5 5.7 %collective-permute-start.3 = (f32[256,128]{1,0:T(8,128)S(1)}, f32[256,128]{1,0:T(8,128)S(1)}, u32[]{:S(2)}, u32[]{:S(2)}) collective-permute-start(f32[256,128]{1,0:T(8,128)S(1)} %convolution_add_fusion.5), channel_id=1, source_target_pairs={{2,6},{6,10},{10,14},{5,1},{9,5},{13,9},{18,22},{22,26},{26,30},{2... | collective-permute-start | bytes 393224 | tf_op jit(solution)/shard_map/ppermute | solution.py:150
  32.3 19.9 %copy-start.4 = (bf16[8,256,256]{2,1,0:T(8,128)(2,1)S(1)}, bf16[8,256,256]{2,1,0:T(8,128)(2,1)}, u32[]{:S(2)}) copy-start(bf16[8,256,256]{2,1,0:T(8,128)(2,1)} %urows_ref.1) | copy-start | bytes 3145732
  32.6 5.8 %collective-permute-start.4 = (f32[256,128]{1,0:T(8,128)S(1)}, f32[256,128]{1,0:T(8,128)}, u32[]{:S(2)}, u32[]{:S(2)}) collective-permute-start(f32[256,128]{1,0:T(8,128)S(1)} %convolution_add_fusion.4), channel_id=1, source_target_pairs={{2,6},{6,10},{10,14},{5,1},{9,5},{13,9},{18,22},{22,26},{26,30},{2... | collective-permute-start | bytes 393224 | tf_op jit(solution)/shard_map/ppermute | solution.py:150
  38.5 3.5 %collective-permute-start.5 = (f32[256,128]{1,0:T(8,128)}, f32[256,128]{1,0:T(8,128)}, u32[]{:S(2)}, u32[]{:S(2)}) collective-permute-start(f32[256,128]{1,0:T(8,128)} %collective-permute-done.4), channel_id=1, source_target_pairs={{2,0},{6,4},{10,8},{14,12},{1,3},{5,7},{9,11},{13,15},{18,16},{22,... | collective-permute-start | bytes 393224 | tf_op jit(solution)/shard_map/ppermute | solution.py:192
  43.4 8.7 %copy-start.3 = (bf16[8,256,256]{2,1,0:T(8,128)(2,1)S(1)}, bf16[8,256,256]{2,1,0:T(8,128)(2,1)}, u32[]{:S(2)}) copy-start(bf16[8,256,256]{2,1,0:T(8,128)(2,1)} %lrows_ref.1) | copy-start | bytes 3145732
  43.8 8.3 %copy-start.1 = (bf16[8,256,256]{2,1,0:T(8,128)(2,1)S(1)}, bf16[8,256,256]{2,1,0:T(8,128)(2,1)}, u32[]{:S(2)}) copy-start(bf16[8,256,256]{2,1,0:T(8,128)(2,1)} %ltrans_ref.3) | copy-start | bytes 3145732
  43.8 8.3 %copy-start.2 = (bf16[8,256,256]{2,1,0:T(8,128)(2,1)S(1)}, bf16[8,256,256]{2,1,0:T(8,128)(2,1)}, u32[]{:S(2)}) copy-start(bf16[8,256,256]{2,1,0:T(8,128)(2,1)} %utrans_ref.3) | copy-start | bytes 3145732
  43.9 8.3 %collective-permute-start.6 = (f32[256,128]{1,0:T(8,128)S(1)}, f32[256,128]{1,0:T(8,128)S(1)}, u32[]{:S(2)}, u32[]{:S(2)}) collective-permute-start(f32[256,128]{1,0:T(8,128)S(1)} %convolution_add_fusion.2), channel_id=1, source_target_pairs={{0,1},{2,3},{4,5},{6,7},{8,9},{10,11},{12,13},{14,15},{1,0},{3,2},... | collective-permute-start | bytes 393224 | tf_op jit(solution)/shard_map/ppermute | solution.py:197
  52.2 1.2 %copy-start.6 = (f32[8,256,128]{2,1,0:T(8,128)S(1)}, f32[8,256,128]{2,1,0:T(8,128)}, u32[]{:S(2)}) copy-start(f32[8,256,128]{2,1,0:T(8,128)} %get-tuple-element.12.usrc_ref) | copy-start | bytes 3145732

commit v16 on v13

--- a/solution.py
+++ b/solution.py
@@ -156,16 +156,18 @@
     )
     pair = [(4 * g, 4 * g + 2) for g in range(groups)]
     pair += [(4 * g + 3, 4 * g + 1) for g in range(groups)]
-    beside = lax.ppermute(both, axis, pair)
-    both = jnp.dot(both[:, :rank], beside, precision=HIGHEST) + jnp.concatenate(
-        [zeros, both[:, rank:]], axis=1
-    )
+    beside_state = lax.ppermute(both[:, rank:], axis, pair)
+    beside_map = lax.ppermute(both[:, :rank], axis, pair)
+    group_state = jnp.dot(both[:, :rank], beside_state, precision=HIGHEST) + both[:, rank:]
+    group_map = jnp.dot(both[:, :rank], beside_map, precision=HIGHEST)
+    beside = jnp.concatenate([beside_map, beside_state], axis=1)
+    both = jnp.concatenate([group_map, group_state], axis=1)
     if groups <= 4:
-        out = both[:, rank:]
+        out = group_state
         for step in range(groups - 1):
             start = group_shift(out, axis, groups, 1)
             if step + 2 < groups:
-                out = jnp.dot(both[:, :rank], start, precision=HIGHEST) + both[:, rank:]
+                out = jnp.dot(group_map, start, precision=HIGHEST) + group_state
     else:
         rounds = 0
         while 2 ** (rounds + 1) < groups - 1:
@@ -182,7 +184,7 @@
     back = [(4 * g + 2, 4 * g) for g in range(groups)]
     back += [(4 * g + 1, 4 * g + 3) for g in range(groups)]
     sent = lax.ppermute(start, axis, back)
-    mine = jnp.dot(beside[:, :rank], start, precision=HIGHEST) + beside[:, rank:]
+    mine = jnp.dot(beside_map, start, precision=HIGHEST) + beside_state
     holder = jnp.logical_or(place == 1, place == 2)
     enter = jnp.where(holder, mine, sent)
     send = jnp.dot(own[:, :rank], enter, precision=HIGHEST) + own[:, rank:]

time: 56.7 us -> 53.9 us (0.951)
  waiting for transfers between devices: 24.8 us -> 20 us
  starting transfers between devices: 14 us -> 15.3 us
    ppermute x1 -> x2, waiting for transfers between devices: 7.48 us -> 4.23 us  [the longest x1 3.37 us: scan_groups(): beside_state = lax.ppermute(both[:, rank:], axis, pair)]
    ppermute x3, waiting for transfers between devices: 14 us -> 12.5 us  [group_shift(): return lax.ppermute(value, axis, pairs)]
    ppermute x1 -> x2, starting transfers between devices: 1.29 us -> 2.58 us  [the longest x1 1.29 us: scan_groups(): beside_state = lax.ppermute(both[:, rank:], axis, pair)]
    unnamed x16 -> x18, local copies, waits for them, and re-layouts: 1.39 us -> 1.84 us
    dot_general x4 -> x5, matrix products: 2.78 us -> 2.93 us  [the longest x1 1.42 us: scan_groups(): mine = jnp.dot(beside_map, start, precision=HIGHEST) + beside_state]
  transfers between devices with their start and end apart: 7 -> 8, of which waited for: 6 -> 7; matrix products, arithmetic and copies ran while one was open for 3% -> 4% of each run, Pallas kernels for 0% -> 0%
where the time goes in v16:
time: 53.9 us; the launch traced here: 53.4 us
  waiting for transfers between devices  20 us (37%)
  starting transfers between devices  15.3 us (28%)
  Pallas kernels  9.48 us (18%)
  matrix products  5.36 us (10%)
  local copies, waits for them, and re-layouts  1.88 us (3%)
  other arithmetic  1.17 us (2%)
    ppermute x3, waiting for transfers between devices, group_shift(): return lax.ppermute(value, axis, pairs)  12.5 us
    ppermute x1, starting transfers between devices, scan_groups(): other = lax.ppermute(send, axis, partner)  6.8 us
    pallas_call x1, Pallas kernels, shards(): pl.pallas_call(sweep_kernel, out_shape=(jax.ShapeDtypeStruct((rank, rank...  6.43 us
    ppermute x3, starting transfers between devices, group_shift(): return lax.ppermute(value, axis, pairs)  3.86 us
    ppermute x1, waiting for transfers between devices, scan_groups(): beside_state = lax.ppermute(both[:, rank:], axis, pair)  3.37 us
    pallas_call x1, Pallas kernels, shards(): pl.pallas_call(apply_kernel, out_shape=jax.ShapeDtypeStruct((count, rows,...  3.05 us
    ppermute x1, starting transfers between devices, scan_groups(): sent = lax.ppermute(start, axis, back)  1.94 us
    unnamed x18, local copies, waits for them, and re-layouts  1.84 us
  transfers between devices with their start and end apart: 8, of which 7 were waited for; matrix products, arithmetic and copies ran while one was open for 4% of the time, Pallas kernels for 0%

profile of v16, /device:TPU:1, one launch (start us, length us, event | category | flops | bytes accessed | tf_op | source)
XLA Modules:
  0.0 53.4 jit_solution(10048944154819990989)
XLA Ops:
  0.0 0.0 copy-start
  0.0 6.4 %sweep.1 = (f32[256,384]{1,0:T(8,128)}, f32[8,256,128]{2,1,0:T(8,128)}, f32[256,384]{1,0:T(8,128)}, f32[8,256,128]{2,1,0:T(8,128)}) custom-call(bf16[8,256,128]{2,1,0:T(8,128)(2,1)} %rhs_ref.1, bf16[8,256,256]{2,1,0:T(8,128)(2,1)} %lcols_ref.1, bf16[8,256,256]{2,1,0:T(8,128)(2,1)} %ltrans_ref.3, bf16[8,256,256]{2,1,0:T(8,128)(2,1)} %ucols_ref.1, ...), custom_call_target="tpu_custom_call" | custom-call | tf_op jit(solution)/shard_map/sweep/pallas_call | solution.py:207
  6.4 1.2 %broadcast_select_fusion.1 = (f32[256,384]{1,0:T(8,128)S(1)}, f32[256,384]{1,0:T(8,128)S(1)}) fusion(f32[256,384]{1,0:T(8,128)} %get-tuple-element.9, f32[256,384]{1,0:T(8,128)} %get-tuple-element.10, pred[]{:T(512)S(6)} %eq.15), kind=kLoop, calls=%fused_computation.10 | loop fusion | flops 196608 | bytes 1572865 | tf_op jit(solution)/shard_map/jit(_where)/select_n | solution.py:224
  7.6 0.1 collective-permute-start
  7.7 1.7 %collective-permute-done = f32[256,384]{1,0:T(8,128)S(1)} collective-permute-done((f32[256,384]{1,0:T(8,128)S(1)}, f32[256,384]{1,0:T(8,128)S(1)}, u32[]{:S(2)}, u32[]{:S(2)}) %collective-permute-start) | collective-permute-done | bytes 393248 | tf_op jit(solution)/shard_map/ppermute | solution.py:153
  9.4 0.6 %convolution_add_fusion = f32[256,384]{1,0:T(8,128)S(1)} fusion(f32[256,384]{1,0:T(8,128)S(1)} %get-tuple-element.14, f32[256,128]{1,0:T(8,128)S(1)} %slice.28, f32[256,384]{1,0:T(8,128)S(1)} %collective-permute-done), kind=kOutput, calls=%fused_computation | convolution fusion | flops 302088192 | bytes 1179648 | tf_op jit(solution)/shard_map/dot_general | solution.py:154
  10.0 1.3 %collective-permute-start.2 = (f32[256,128]{1,0:T(8,128)S(1)}, f32[256,128]{1,0:T(8,128)S(1)}, u32[]{:S(2)}, u32[]{:S(2)}) collective-permute-start(f32[256,128]{1,0:T(8,128)S(1)} %slice.30), channel_id=1, source_target_pairs={{0,2},{4,6},{8,10},{12,14},{3,1},{7,5},{11,9},{15,13},{16,18},{20,... | collective-permute-start | bytes 393224 | tf_op jit(solution)/shard_map/ppermute | solution.py:159
  11.4 1.3 %collective-permute-start.1 = (f32[256,256]{1,0:T(8,128)S(1)}, f32[256,256]{1,0:T(8,128)S(1)}, u32[]{:S(2)}, u32[]{:S(2)}) collective-permute-start(f32[256,256]{1,0:T(8,128)S(1)} %slice.29), channel_id=1, source_target_pairs={{0,2},{4,6},{8,10},{12,14},{3,1},{7,5},{11,9},{15,13},{16,18},{20,... | collective-permute-start | bytes 786440 | tf_op jit(solution)/shard_map/ppermute | solution.py:160
  12.7 3.4 %collective-permute-done.2 = f32[256,128]{1,0:T(8,128)S(1)} collective-permute-done((f32[256,128]{1,0:T(8,128)S(1)}, f32[256,128]{1,0:T(8,128)S(1)}, u32[]{:S(2)}, u32[]{:S(2)}) %collective-permute-start.2) | collective-permute-done | bytes 131104 | tf_op jit(solution)/shard_map/ppermute | solution.py:159
  16.0 0.0 copy-start.8
  16.0 0.4 convolution_add_fusion.5
  16.4 0.3 copy-done.8
  16.7 1.3 %collective-permute-start.3 = (f32[256,128]{1,0:T(8,128)S(1)}, f32[256,128]{1,0:T(8,128)S(1)}, u32[]{:S(2)}, u32[]{:S(2)}) collective-permute-start(f32[256,128]{1,0:T(8,128)S(1)} %convolution_add_fusion.5), channel_id=1, source_target_pairs={{2,6},{6,10},{10,14},{5,1},{9,5},{13,9},{18,22},{22,26},{26,30},{2... | collective-permute-start | bytes 393224 | tf_op jit(solution)/shard_map/ppermute | solution.py:142
  18.0 0.9 %collective-permute-done.1 = f32[256,256]{1,0:T(8,128)S(1)} collective-permute-done((f32[256,256]{1,0:T(8,128)S(1)}, f32[256,256]{1,0:T(8,128)S(1)}, u32[]{:S(2)}, u32[]{:S(2)}) %collective-permute-start.1) | collective-permute-done | bytes 262176 | tf_op jit(solution)/shard_map/ppermute | solution.py:160
  18.8 0.0 copy-start.7
  18.8 0.4 fusion.4
  19.2 0.3 copy-done.7
  19.5 3.5 %collective-permute-done.3 = f32[256,128]{1,0:T(8,128)S(1)} collective-permute-done((f32[256,128]{1,0:T(8,128)S(1)}, f32[256,128]{1,0:T(8,128)S(1)}, u32[]{:S(2)}, u32[]{:S(2)}) %collective-permute-start.3) | collective-permute-done | bytes 131104 | tf_op jit(solution)/shard_map/ppermute | solution.py:142
  23.1 0.0 copy-start.5
  23.1 0.4 convolution_add_fusion.4
  23.4 1.3 %collective-permute-start.4 = (f32[256,128]{1,0:T(8,128)S(1)}, f32[256,128]{1,0:T(8,128)S(1)}, u32[]{:S(2)}, u32[]{:S(2)}) collective-permute-start(f32[256,128]{1,0:T(8,128)S(1)} %convolution_add_fusion.4), channel_id=1, source_target_pairs={{2,6},{6,10},{10,14},{5,1},{9,5},{13,9},{18,22},{22,26},{26,30},{2... | collective-permute-start | bytes 393224 | tf_op jit(solution)/shard_map/ppermute | solution.py:142
  24.7 4.4 %collective-permute-done.4 = f32[256,128]{1,0:T(8,128)S(1)} collective-permute-done((f32[256,128]{1,0:T(8,128)S(1)}, f32[256,128]{1,0:T(8,128)S(1)}, u32[]{:S(2)}, u32[]{:S(2)}) %collective-permute-start.4) | collective-permute-done | bytes 131104 | tf_op jit(solution)/shard_map/ppermute | solution.py:142
  29.2 0.0 copy-start.4
  29.2 0.4 convolution_add_fusion.3
  29.5 1.3 %collective-permute-start.5 = (f32[256,128]{1,0:T(8,128)S(1)}, f32[256,128]{1,0:T(8,128)}, u32[]{:S(2)}, u32[]{:S(2)}) collective-permute-start(f32[256,128]{1,0:T(8,128)S(1)} %convolution_add_fusion.3), channel_id=1, source_target_pairs={{2,6},{6,10},{10,14},{5,1},{9,5},{13,9},{18,22},{22,26},{26,30},{2... | collective-permute-start | bytes 393224 | tf_op jit(solution)/shard_map/ppermute | solution.py:142
  30.8 4.5 %collective-permute-done.5 = f32[256,128]{1,0:T(8,128)} collective-permute-done((f32[256,128]{1,0:T(8,128)S(1)}, f32[256,128]{1,0:T(8,128)}, u32[]{:S(2)}, u32[]{:S(2)}) %collective-permute-start.5) | collective-permute-done | bytes 131104 | tf_op jit(solution)/shard_map/ppermute | solution.py:142
  35.4 1.9 %collective-permute-start.6 = (f32[256,128]{1,0:T(8,128)}, f32[256,128]{1,0:T(8,128)}, u32[]{:S(2)}, u32[]{:S(2)}) collective-permute-start(f32[256,128]{1,0:T(8,128)} %collective-permute-done.5), channel_id=1, source_target_pairs={{2,0},{6,4},{10,8},{14,12},{1,3},{5,7},{9,11},{13,15},{18,16},{22,... | collective-permute-start | bytes 393224 | tf_op jit(solution)/shard_map/ppermute | solution.py:186
  37.3 1.6 %collective-permute-done.6 = f32[256,128]{1,0:T(8,128)} collective-permute-done((f32[256,128]{1,0:T(8,128)}, f32[256,128]{1,0:T(8,128)}, u32[]{:S(2)}, u32[]{:S(2)}) %collective-permute-start.6) | collective-permute-done | bytes 131104 | tf_op jit(solution)/shard_map/ppermute | solution.py:186
  38.9 1.4 %fusion.enter_ref = f32[256,128]{1,0:T(8,128)S(1)} fusion(f32[256,128]{1,0:T(8,128)} %collective-permute-done.6, f32[256,128]{1,0:T(8,128)} %copy-done.8, f32[256,256]{1,0:T(8,128)} %copy-done.7, f32[256,128]{1,0:T(8,128)} %collective-permute-done.5, pred[]{:T(512)S(6)} %or.3), kind=kOutput, calls=%fused_computation.3 | convolution fusion | flops 100728832 | bytes 786433 | tf_op jit(solution)/shard_map/dot_general | solution.py:187
  40.3 0.0 copy-start.3
  40.3 0.4 convolution_add_fusion.1
  40.7 0.0 copy-start.1
  40.7 0.0 copy-start.2
  40.7 6.8 %collective-permute-start.7 = (f32[256,128]{1,0:T(8,128)S(1)}, f32[256,128]{1,0:T(8,128)S(1)}, u32[]{:S(2)}, u32[]{:S(2)}) collective-permute-start(f32[256,128]{1,0:T(8,128)S(1)} %convolution_add_fusion.1), channel_id=1, source_target_pairs={{0,1},{2,3},{4,5},{6,7},{8,9},{10,11},{12,13},{14,15},{1,0},{3,2},... | collective-permute-start | bytes 393224 | tf_op jit(solution)/shard_map/ppermute | solution.py:191
  47.6 0.0 copy-done
  47.6 1.5 %fusion.6.diag_ref = f32[8,256,128]{2,1,0:T(8,128)S(1)} fusion(bf16[8,256,256]{2,1,0:T(8,128)(2,1)S(1)} %copy-done, bf16[8,256,128]{2,1,0:T(8,128)(2,1)} %rhs_ref.1), kind=kOutput, calls=%fused_computation.14 | convolution fusion | flops 134217728 | bytes 2621440 | tf_op jit(solution)/shard_map/kab,kbc->kac/dot_general | solution.py:217
  49.0 0.0 collective-permute-done.7.other_ref
  49.0 0.0 copy-done.5
  49.0 0.0 copy-done.4
  49.1 0.0 copy-done.3
  49.1 0.0 copy-done.1
  49.1 0.0 copy-done.2
  49.1 0.0 copy-start.6
  49.1 1.2 %copy-done.6 = f32[8,256,128]{2,1,0:T(8,128)S(1)} copy-done((f32[8,256,128]{2,1,0:T(8,128)S(1)}, f32[8,256,128]{2,1,0:T(8,128)}, u32[]{:S(2)}) %copy-start.6) | copy-done | bytes 1048600
  50.3 3.1 %apply.1 = bf16[8,256,128]{2,1,0:T(8,128)(2,1)} custom-call(s32[1]{0:T(128)} %bitcast.flag_ref, f32[256,128]{1,0:T(8,128)S(1)} %fusion.enter_ref, f32[256,128]{1,0:T(8,128)S(1)} %collective-permute-done.7.other_ref, bf16[8,256,256]{2,1,0:T(8,128)(2,1)S(1)} %copy-done.1, bf16[8,256,256]{2,1,0:T(8,128)(2,1)S(1)} %copy-done.2, f32[8,256,128]{2,1,0:T(8,128)S(1)} %copy-done.5, ...), custom_call_target="tpu_custom_call" | custom-call | tf_op jit(solution)/shard_map/apply/pallas_call | solution.py:235
  (3 shorter events, 0.0 us)
Async XLA Ops:
  0.0 47.6 %copy-start = (bf16[8,256,256]{2,1,0:T(8,128)(2,1)S(1)}, bf16[8,256,256]{2,1,0:T(8,128)(2,1)}, u32[]{:S(2)}) copy-start(bf16[8,256,256]{2,1,0:T(8,128)(2,1)} %param.9) | copy-start | bytes 3145732
  7.6 1.8 %collective-permute-start = (f32[256,384]{1,0:T(8,128)S(1)}, f32[256,384]{1,0:T(8,128)S(1)}, u32[]{:S(2)}, u32[]{:S(2)}) collective-permute-start(f32[256,384]{1,0:T(8,128)S(1)} %get-tuple-element.13), channel_id=1, source_target_pairs={{0,1},{2,3},{4,5},{6,7},{8,9},{10,11},{12,13},{14,15},{1,0},{3,2},... | collective-permute-start | bytes 1179656 | tf_op jit(solution)/shard_map/ppermute | solution.py:153
  10.0 6.0 %collective-permute-start.2 = (f32[256,128]{1,0:T(8,128)S(1)}, f32[256,128]{1,0:T(8,128)S(1)}, u32[]{:S(2)}, u32[]{:S(2)}) collective-permute-start(f32[256,128]{1,0:T(8,128)S(1)} %slice.30), channel_id=1, source_target_pairs={{0,2},{4,6},{8,10},{12,14},{3,1},{7,5},{11,9},{15,13},{16,18},{20,... | collective-permute-start | bytes 393224 | tf_op jit(solution)/shard_map/ppermute | solution.py:159
  11.4 7.5 %collective-permute-start.1 = (f32[256,256]{1,0:T(8,128)S(1)}, f32[256,256]{1,0:T(8,128)S(1)}, u32[]{:S(2)}, u32[]{:S(2)}) collective-permute-start(f32[256,256]{1,0:T(8,128)S(1)} %slice.29), channel_id=1, source_target_pairs={{0,2},{4,6},{8,10},{12,14},{3,1},{7,5},{11,9},{15,13},{16,18},{20,... | collective-permute-start | bytes 786440 | tf_op jit(solution)/shard_map/ppermute | solution.py:160
  16.0 0.7 %copy-start.8 = (f32[256,128]{1,0:T(8,128)}, f32[256,128]{1,0:T(8,128)S(1)}, u32[]{:S(2)}) copy-start(f32[256,128]{1,0:T(8,128)S(1)} %collective-permute-done.2) | copy-start | bytes 393220
  16.7 6.4 %collective-permute-start.3 = (f32[256,128]{1,0:T(8,128)S(1)}, f32[256,128]{1,0:T(8,128)S(1)}, u32[]{:S(2)}, u32[]{:S(2)}) collective-permute-start(f32[256,128]{1,0:T(8,128)S(1)} %convolution_add_fusion.5), channel_id=1, source_target_pairs={{2,6},{6,10},{10,14},{5,1},{9,5},{13,9},{18,22},{22,26},{26,30},{2... | collective-permute-start | bytes 393224 | tf_op jit(solution)/shard_map/ppermute | solution.py:142
  18.8 0.7 %copy-start.7 = (f32[256,256]{1,0:T(8,128)}, f32[256,256]{1,0:T(8,128)S(1)}, u32[]{:S(2)}) copy-start(f32[256,256]{1,0:T(8,128)S(1)} %collective-permute-done.1) | copy-start | bytes 786436
  23.1 26.0 %copy-start.5 = (f32[8,256,128]{2,1,0:T(8,128)S(1)}, f32[8,256,128]{2,1,0:T(8,128)}, u32[]{:S(2)}) copy-start(f32[8,256,128]{2,1,0:T(8,128)} %get-tuple-element.11.lsrc_ref) | copy-start | bytes 3145732
  23.4 5.7 %collective-permute-start.4 = (f32[256,128]{1,0:T(8,128)S(1)}, f32[256,128]{1,0:T(8,128)S(1)}, u32[]{:S(2)}, u32[]{:S(2)}) collective-permute-start(f32[256,128]{1,0:T(8,128)S(1)} %convolution_add_fusion.4), channel_id=1, source_target_pairs={{2,6},{6,10},{10,14},{5,1},{9,5},{13,9},{18,22},{22,26},{26,30},{2... | collective-permute-start | bytes 393224 | tf_op jit(solution)/shard_map/ppermute | solution.py:142
  29.2 19.9 %copy-start.4 = (bf16[8,256,256]{2,1,0:T(8,128)(2,1)S(1)}, bf16[8,256,256]{2,1,0:T(8,128)(2,1)}, u32[]{:S(2)}) copy-start(bf16[8,256,256]{2,1,0:T(8,128)(2,1)} %urows_ref.1) | copy-start | bytes 3145732
  29.5 5.8 %collective-permute-start.5 = (f32[256,128]{1,0:T(8,128)S(1)}, f32[256,128]{1,0:T(8,128)}, u32[]{:S(2)}, u32[]{:S(2)}) collective-permute-start(f32[256,128]{1,0:T(8,128)S(1)} %convolution_add_fusion.3), channel_id=1, source_target_pairs={{2,6},{6,10},{10,14},{5,1},{9,5},{13,9},{18,22},{22,26},{26,30},{2... | collective-permute-start | bytes 393224 | tf_op jit(solution)/shard_map/ppermute | solution.py:142
  35.4 3.5 %collective-permute-start.6 = (f32[256,128]{1,0:T(8,128)}, f32[256,128]{1,0:T(8,128)}, u32[]{:S(2)}, u32[]{:S(2)}) collective-permute-start(f32[256,128]{1,0:T(8,128)} %collective-permute-done.5), channel_id=1, source_target_pairs={{2,0},{6,4},{10,8},{14,12},{1,3},{5,7},{9,11},{13,15},{18,16},{22,... | collective-permute-start | bytes 393224 | tf_op jit(solution)/shard_map/ppermute | solution.py:186
  40.3 8.7 %copy-start.3 = (bf16[8,256,256]{2,1,0:T(8,128)(2,1)S(1)}, bf16[8,256,256]{2,1,0:T(8,128)(2,1)}, u32[]{:S(2)}) copy-start(bf16[8,256,256]{2,1,0:T(8,128)(2,1)} %lrows_ref.1) | copy-start | bytes 3145732
  40.7 8.3 %copy-start.1 = (bf16[8,256,256]{2,1,0:T(8,128)(2,1)S(1)}, bf16[8,256,256]{2,1,0:T(8,128)(2,1)}, u32[]{:S(2)}) copy-start(bf16[8,256,256]{2,1,0:T(8,128)(2,1)} %ltrans_ref.3) | copy-start | bytes 3145732
  40.7 8.3 %copy-start.2 = (bf16[8,256,256]{2,1,0:T(8,128)(2,1)S(1)}, bf16[8,256,256]{2,1,0:T(8,128)(2,1)}, u32[]{:S(2)}) copy-start(bf16[8,256,256]{2,1,0:T(8,128)(2,1)} %utrans_ref.3) | copy-start | bytes 3145732
  40.7 8.3 %collective-permute-start.7 = (f32[256,128]{1,0:T(8,128)S(1)}, f32[256,128]{1,0:T(8,128)S(1)}, u32[]{:S(2)}, u32[]{:S(2)}) collective-permute-start(f32[256,128]{1,0:T(8,128)S(1)} %convolution_add_fusion.1), channel_id=1, source_target_pairs={{0,1},{2,3},{4,5},{6,7},{8,9},{10,11},{12,13},{14,15},{1,0},{3,2},... | collective-permute-start | bytes 393224 | tf_op jit(solution)/shard_map/ppermute | solution.py:191
  49.1 1.2 %copy-start.6 = (f32[8,256,128]{2,1,0:T(8,128)S(1)}, f32[8,256,128]{2,1,0:T(8,128)}, u32[]{:S(2)}) copy-start(f32[8,256,128]{2,1,0:T(8,128)} %get-tuple-element.12.usrc_ref) | copy-start | bytes 3145732

commit v17 on v16

--- a/solution.py
+++ b/solution.py
@@ -156,6 +156,9 @@
     )
     pair = [(4 * g, 4 * g + 2) for g in range(groups)]
     pair += [(4 * g + 3, 4 * g + 1) for g in range(groups)]
+    early = [(4 * g, 4 * g + 2) for g in range(groups)]
+    early += [(4 * g + 3, 4 * g + 1) for g in range(groups)]
+    far_own = lax.ppermute(own, axis, early)
     beside_state = lax.ppermute(both[:, rank:], axis, pair)
     beside_map = lax.ppermute(both[:, :rank], axis, pair)
     group_state = jnp.dot(both[:, :rank], beside_state, precision=HIGHEST) + both[:, rank:]
@@ -183,12 +186,19 @@
         start = jnp.dot(near[:, :rank], far, precision=HIGHEST) + near[:, rank:]
     back = [(4 * g + 2, 4 * g) for g in range(groups)]
     back += [(4 * g + 1, 4 * g + 3) for g in range(groups)]
+    cross = [(4 * g + 2, 4 * g + 1) for g in range(groups)]
+    cross += [(4 * g + 1, 4 * g + 2) for g in range(groups)]
+    inner = [(4 * g + 2, 4 * g + 3) for g in range(groups)]
+    inner += [(4 * g + 1, 4 * g) for g in range(groups)]
+    mine = jnp.dot(beside_map, start, precision=HIGHEST) + beside_state
+    crossed = jnp.dot(far_own[:, :rank], start, precision=HIGHEST) + far_own[:, rank:]
+    inside = jnp.dot(own[:, :rank], mine, precision=HIGHEST) + own[:, rank:]
     sent = lax.ppermute(start, axis, back)
-    mine = jnp.dot(beside_map, start, precision=HIGHEST) + beside_state
+    got_cross = lax.ppermute(crossed, axis, cross)
+    got_inner = lax.ppermute(inside, axis, inner)
     holder = jnp.logical_or(place == 1, place == 2)
     enter = jnp.where(holder, mine, sent)
-    send = jnp.dot(own[:, :rank], enter, precision=HIGHEST) + own[:, rank:]
-    other = lax.ppermute(send, axis, partner)
+    other = jnp.where(holder, got_cross, got_inner)
     return enter, other
 
 

time: 53.9 us -> 59.4 us (1.10)
  local copies, waits for them, and re-layouts: 1.88 us -> 4.3 us
  starting transfers between devices: 15.3 us -> 17.7 us
  matrix products: 5.36 us -> 6.49 us
  waiting for transfers between devices: 20 us -> 19.4 us
    ppermute x1 -> x3, starting transfers between devices: 6.8 us -> 9.88 us  [the longest x1 6.12 us: scan_groups(): got_cross = lax.ppermute(crossed, axis, cross)]
    ppermute x1 -> x3, waiting for transfers between devices: 0.01 us -> 2.59 us  [the longest x1 2.59 us: scan_groups(): got_cross = lax.ppermute(crossed, axis, cross)]
    unnamed x18 -> x20, local copies, waits for them, and re-layouts: 1.84 us -> 4.26 us
    ppermute x3, waiting for transfers between devices: 12.5 us -> 10.9 us  [group_shift(): return lax.ppermute(value, axis, pairs)]
    ppermute x1, waiting for transfers between devices: 1.59 us -> 0.01 us  [scan_groups(): sent = lax.ppermute(start, axis, back)]
    dot_general x1 -> x2, matrix products: 0.38 us -> 1.8 us  [the longest x1 1.42 us: scan_groups(): jnp.dot(far_own[:, :rank], start, precision=HIGHEST) + far_own[:, rank:]]
    dot_general x1, matrix products: 1.46 us -> 0.42 us  [shards(): jnp.einsum('kab,kbc->kac', diagonal_blocks, right_sides, preferred_elemen...]
    dot_general x2, matrix products: 0.75 us -> 1.41 us  [scan_groups(): out = jnp.dot(group_map, start, precision=HIGHEST) + group_state]
  transfers between devices with their start and end apart: 8 -> 10, of which waited for: 7 -> 7; matrix products, arithmetic and copies ran while one was open for 4% -> 9% of each run, Pallas kernels for 0% -> 0%
where the time goes in v17:
time: 59.4 us; the launch traced here: 58.9 us
  waiting for transfers between devices  19.4 us (33%)
  starting transfers between devices  17.7 us (30%)
  Pallas kernels  9.48 us (16%)
  matrix products  6.49 us (11%)
  local copies, waits for them, and re-layouts  4.3 us (7%)
  other arithmetic  1.2 us (2%)
    ppermute x3, waiting for transfers between devices, group_shift(): return lax.ppermute(value, axis, pairs)  10.9 us
    pallas_call x1, Pallas kernels, shards(): pl.pallas_call(sweep_kernel, out_shape=(jax.ShapeDtypeStruct((rank, rank...  6.43 us
    ppermute x1, starting transfers between devices, scan_groups(): got_cross = lax.ppermute(crossed, axis, cross)  6.12 us
    unnamed x20, local copies, waits for them, and re-layouts  4.26 us
    ppermute x3, starting transfers between devices, group_shift(): return lax.ppermute(value, axis, pairs)  3.85 us
    ppermute x1, waiting for transfers between devices, scan_groups(): beside_state = lax.ppermute(both[:, rank:], axis, pair)  3.37 us
    pallas_call x1, Pallas kernels, shards(): pl.pallas_call(apply_kernel, out_shape=jax.ShapeDtypeStruct((count, rows,...  3.06 us
    ppermute x1, waiting for transfers between devices, scan_groups(): got_cross = lax.ppermute(crossed, axis, cross)  2.59 us
  transfers between devices with their start and end apart: 10, of which 7 were waited for; matrix products, arithmetic and copies ran while one was open for 9% of the time, Pallas kernels for 0%

profile of v17, /device:TPU:1, one launch (start us, length us, event | category | flops | bytes accessed | tf_op | source)
XLA Modules:
  0.0 58.9 jit_solution(8571453074587148728)
XLA Ops:
  0.0 0.0 copy-start
  0.0 6.4 %sweep.1 = (f32[256,384]{1,0:T(8,128)}, f32[8,256,128]{2,1,0:T(8,128)}, f32[256,384]{1,0:T(8,128)}, f32[8,256,128]{2,1,0:T(8,128)}) custom-call(bf16[8,256,128]{2,1,0:T(8,128)(2,1)} %rhs_ref.1, bf16[8,256,256]{2,1,0:T(8,128)(2,1)} %lcols_ref.1, bf16[8,256,256]{2,1,0:T(8,128)(2,1)} %ltrans_ref.3, bf16[8,256,256]{2,1,0:T(8,128)(2,1)} %ucols_ref.1, ...), custom_call_target="tpu_custom_call" | custom-call | tf_op jit(solution)/shard_map/sweep/pallas_call | solution.py:217
  6.4 1.2 %broadcast_select_fusion.1 = (f32[256,384]{1,0:T(8,128)S(1)}, f32[256,384]{1,0:T(8,128)S(1)}) fusion(f32[256,384]{1,0:T(8,128)} %get-tuple-element.9, f32[256,384]{1,0:T(8,128)} %get-tuple-element.10, pred[]{:T(512)S(6)} %eq.15), kind=kLoop, calls=%fused_computation.11 | loop fusion | flops 196608 | bytes 1572865 | tf_op jit(solution)/shard_map/jit(_where)/select_n | solution.py:234
  7.6 0.1 collective-permute-start
  7.7 1.7 %collective-permute-done = f32[256,384]{1,0:T(8,128)S(1)} collective-permute-done((f32[256,384]{1,0:T(8,128)S(1)}, f32[256,384]{1,0:T(8,128)S(1)}, u32[]{:S(2)}, u32[]{:S(2)}) %collective-permute-start) | collective-permute-done | bytes 393248 | tf_op jit(solution)/shard_map/ppermute | solution.py:153
  9.4 0.6 %convolution_add_fusion = f32[256,384]{1,0:T(8,128)S(1)} fusion(f32[256,384]{1,0:T(8,128)S(1)} %get-tuple-element.14, f32[256,128]{1,0:T(8,128)S(1)} %slice.36, f32[256,384]{1,0:T(8,128)S(1)} %collective-permute-done), kind=kOutput, calls=%fused_computation | convolution fusion | flops 302088192 | bytes 1179648 | tf_op jit(solution)/shard_map/dot_general | solution.py:154
  10.0 1.3 %collective-permute-start.2 = (f32[256,128]{1,0:T(8,128)S(1)}, f32[256,128]{1,0:T(8,128)S(1)}, u32[]{:S(2)}, u32[]{:S(2)}) collective-permute-start(f32[256,128]{1,0:T(8,128)S(1)} %slice.38), channel_id=1, source_target_pairs={{0,2},{4,6},{8,10},{12,14},{3,1},{7,5},{11,9},{15,13},{16,18},{20,... | collective-permute-start | bytes 393224 | tf_op jit(solution)/shard_map/ppermute | solution.py:162
  11.4 1.3 %collective-permute-start.1 = (f32[256,256]{1,0:T(8,128)S(1)}, f32[256,256]{1,0:T(8,128)S(1)}, u32[]{:S(2)}, u32[]{:S(2)}) collective-permute-start(f32[256,256]{1,0:T(8,128)S(1)} %slice.37), channel_id=1, source_target_pairs={{0,2},{4,6},{8,10},{12,14},{3,1},{7,5},{11,9},{15,13},{16,18},{20,... | collective-permute-start | bytes 786440 | tf_op jit(solution)/shard_map/ppermute | solution.py:163
  12.7 3.4 %collective-permute-done.2 = f32[256,128]{1,0:T(8,128)S(1)} collective-permute-done((f32[256,128]{1,0:T(8,128)S(1)}, f32[256,128]{1,0:T(8,128)S(1)}, u32[]{:S(2)}, u32[]{:S(2)}) %collective-permute-start.2) | collective-permute-done | bytes 131104 | tf_op jit(solution)/shard_map/ppermute | solution.py:162
  16.0 0.4 convolution_add_fusion.6
  16.4 0.3 copy-done.9
  16.7 1.3 %collective-permute-start.3 = (f32[256,128]{1,0:T(8,128)S(1)}, f32[256,128]{1,0:T(8,128)S(1)}, u32[]{:S(2)}, u32[]{:S(2)}) collective-permute-start(f32[256,128]{1,0:T(8,128)S(1)} %convolution_add_fusion.6), channel_id=1, source_target_pairs={{2,6},{6,10},{10,14},{5,1},{9,5},{13,9},{18,22},{22,26},{26,30},{2... | collective-permute-start | bytes 393224 | tf_op jit(solution)/shard_map/ppermute | solution.py:142
  17.9 0.9 %collective-permute-done.1 = f32[256,256]{1,0:T(8,128)S(1)} collective-permute-done((f32[256,256]{1,0:T(8,128)S(1)}, f32[256,256]{1,0:T(8,128)S(1)}, u32[]{:S(2)}, u32[]{:S(2)}) %collective-permute-start.1) | collective-permute-done | bytes 262176 | tf_op jit(solution)/shard_map/ppermute | solution.py:163
  18.8 0.0 copy-start.8
  18.8 0.4 fusion.4
  19.2 0.3 copy-done.8
  19.5 0.0 copy-start.7
  19.5 3.5 %collective-permute-done.3 = f32[256,128]{1,0:T(8,128)S(1)} collective-permute-done((f32[256,128]{1,0:T(8,128)S(1)}, f32[256,128]{1,0:T(8,128)S(1)}, u32[]{:S(2)}, u32[]{:S(2)}) %collective-permute-start.3) | collective-permute-done | bytes 131104 | tf_op jit(solution)/shard_map/ppermute | solution.py:142
  23.0 0.4 convolution_add_fusion.5
  23.4 1.3 %collective-permute-start.4 = (f32[256,128]{1,0:T(8,128)S(1)}, f32[256,128]{1,0:T(8,128)S(1)}, u32[]{:S(2)}, u32[]{:S(2)}) collective-permute-start(f32[256,128]{1,0:T(8,128)S(1)} %convolution_add_fusion.5), channel_id=1, source_target_pairs={{2,6},{6,10},{10,14},{5,1},{9,5},{13,9},{18,22},{22,26},{26,30},{2... | collective-permute-start | bytes 393224 | tf_op jit(solution)/shard_map/ppermute | solution.py:142
  24.7 1.3 %collective-permute-start.7 = (f32[256,384]{1,0:T(8,128)S(1)}, f32[256,384]{1,0:T(8,128)}, u32[]{:S(2)}, u32[]{:S(2)}) collective-permute-start(f32[256,384]{1,0:T(8,128)S(1)} %get-tuple-element.14), channel_id=1, source_target_pairs={{0,2},{4,6},{8,10},{12,14},{3,1},{7,5},{11,9},{15,13},{16,18},{20,... | collective-permute-start | bytes 1179656 | tf_op jit(solution)/shard_map/ppermute | solution.py:161
  26.0 3.1 %collective-permute-done.4 = f32[256,128]{1,0:T(8,128)S(1)} collective-permute-done((f32[256,128]{1,0:T(8,128)S(1)}, f32[256,128]{1,0:T(8,128)S(1)}, u32[]{:S(2)}, u32[]{:S(2)}) %collective-permute-start.4) | collective-permute-done | bytes 131104 | tf_op jit(solution)/shard_map/ppermute | solution.py:142
  29.1 1.0 %convolution_add_fusion.4 = f32[256,128]{1,0:T(8,128)} fusion(f32[256,128]{1,0:T(8,128)S(1)} %convolution_add_fusion.6, f32[256,256]{1,0:T(8,128)S(1)} %fusion.4, f32[256,128]{1,0:T(8,128)S(1)} %collective-permute-done.4), kind=kOutput, calls=%fused_computation.4 | convolution fusion | flops 100696064 | bytes 655360 | tf_op jit(solution)/shard_map/dot_general | solution.py:173
  30.2 1.3 %collective-permute-start.5 = (f32[256,128]{1,0:T(8,128)}, f32[256,128]{1,0:T(8,128)}, u32[]{:S(2)}, u32[]{:S(2)}) collective-permute-start(f32[256,128]{1,0:T(8,128)} %convolution_add_fusion.4), channel_id=1, source_target_pairs={{2,6},{6,10},{10,14},{5,1},{9,5},{13,9},{18,22},{22,26},{26,30},{2... | collective-permute-start | bytes 393224 | tf_op jit(solution)/shard_map/ppermute | solution.py:142
  31.5 0.0 copy-done
  31.5 0.0 copy-done.7
  31.5 0.0 copy-start.3
  31.5 0.4 fusion.6.diag_ref
  31.9 4.3 %collective-permute-done.5 = f32[256,128]{1,0:T(8,128)} collective-permute-done((f32[256,128]{1,0:T(8,128)}, f32[256,128]{1,0:T(8,128)}, u32[]{:S(2)}, u32[]{:S(2)}) %collective-permute-start.5) | collective-permute-done | bytes 131104 | tf_op jit(solution)/shard_map/ppermute | solution.py:142
  36.2 1.5 %convolution_add_fusion.3 = f32[256,128]{1,0:T(8,128)S(1)} fusion(f32[256,128]{1,0:T(8,128)} %copy-done.9, f32[256,256]{1,0:T(8,128)} %copy-done.8, f32[256,128]{1,0:T(8,128)} %collective-permute-done.5), kind=kOutput, calls=%fused_computation.3 | convolution fusion | flops 100696064 | bytes 655360 | tf_op jit(solution)/shard_map/dot_general | solution.py:193
  37.7 0.0 copy-start.1
  37.7 0.4 convolution_add_fusion.1
  38.1 2.5 %collective-permute-start.9 = (f32[256,128]{1,0:T(8,128)S(1)}, f32[256,128]{1,0:T(8,128)S(1)}, u32[]{:S(2)}, u32[]{:S(2)}) collective-permute-start(f32[256,128]{1,0:T(8,128)S(1)} %convolution_add_fusion.1), channel_id=1, source_target_pairs={{2,3},{6,7},{10,11},{14,15},{1,0},{5,4},{9,8},{13,12},{18,19},{22,... | collective-permute-start | bytes 393224 | tf_op jit(solution)/shard_map/ppermute | solution.py:198
  40.6 1.3 %collective-permute-start.6 = (f32[256,128]{1,0:T(8,128)}, f32[256,128]{1,0:T(8,128)S(1)}, u32[]{:S(2)}, u32[]{:S(2)}) collective-permute-start(f32[256,128]{1,0:T(8,128)} %collective-permute-done.5), channel_id=1, source_target_pairs={{2,0},{6,4},{10,8},{14,12},{1,3},{5,7},{9,11},{13,15},{18,16},{22,... | collective-permute-start | bytes 393224 | tf_op jit(solution)/shard_map/ppermute | solution.py:196
  41.9 0.0 collective-permute-done.7
  41.9 1.4 %convolution_add_fusion.2 = f32[256,128]{1,0:T(8,128)S(1)} fusion(f32[256,128]{1,0:T(8,128)} %collective-permute-done.5, f32[256,384]{1,0:T(8,128)} %collective-permute-done.7), kind=kOutput, calls=%fused_computation.2 | convolution fusion | flops 100696064 | bytes 655360 | tf_op jit(solution)/shard_map/dot_general | solution.py:194
  43.3 6.1 %collective-permute-start.8 = (f32[256,128]{1,0:T(8,128)S(1)}, f32[256,128]{1,0:T(8,128)S(1)}, u32[]{:S(2)}, u32[]{:S(2)}) collective-permute-start(f32[256,128]{1,0:T(8,128)S(1)} %convolution_add_fusion.2), channel_id=1, source_target_pairs={{2,1},{6,5},{10,9},{14,13},{1,2},{5,6},{9,10},{13,14},{18,17},{22,... | collective-permute-start | bytes 393224 | tf_op jit(solution)/shard_map/ppermute | solution.py:197
  49.4 0.0 collective-permute-done.6
  49.5 0.0 collective-permute-done.9
  49.5 2.6 %collective-permute-done.8 = f32[256,128]{1,0:T(8,128)S(1)} collective-permute-done((f32[256,128]{1,0:T(8,128)S(1)}, f32[256,128]{1,0:T(8,128)S(1)}, u32[]{:S(2)}, u32[]{:S(2)}) %collective-permute-start.8) | collective-permute-done | bytes 131104 | tf_op jit(solution)/shard_map/ppermute | solution.py:197
  52.1 0.0 copy-done.3
  52.1 0.0 copy-done.2
  52.1 0.0 copy-done.1
  52.1 0.0 copy-start.4
  52.1 1.2 %copy-done.4 = bf16[8,256,256]{2,1,0:T(8,128)(2,1)S(1)} copy-done((bf16[8,256,256]{2,1,0:T(8,128)(2,1)S(1)}, bf16[8,256,256]{2,1,0:T(8,128)(2,1)}, u32[]{:S(2)}) %copy-start.4) | copy-done | bytes 1048600
  53.4 1.2 %copy-done.5 = f32[8,256,128]{2,1,0:T(8,128)S(1)} copy-done((f32[8,256,128]{2,1,0:T(8,128)S(1)}, f32[8,256,128]{2,1,0:T(8,128)}, u32[]{:S(2)}) %copy-start.5) | copy-done | bytes 1048600
  54.6 1.2 %copy-done.6 = f32[8,256,128]{2,1,0:T(8,128)S(1)} copy-done((f32[8,256,128]{2,1,0:T(8,128)S(1)}, f32[8,256,128]{2,1,0:T(8,128)}, u32[]{:S(2)}) %copy-start.6) | copy-done | bytes 1048600
  55.8 3.1 %apply.1 = bf16[8,256,128]{2,1,0:T(8,128)(2,1)} custom-call(s32[1]{0:T(128)} %bitcast.flag_ref, f32[256,128]{1,0:T(8,128)S(1)} %broadcast_select_fusion.3.enter_ref, f32[256,128]{1,0:T(8,128)S(1)} %broadcast_select_fusion.2.other_ref, bf16[8,256,256]{2,1,0:T(8,128)(2,1)S(1)} %copy-done.1, bf16[8,256,256]{2,1,0:T(8,128)(2,1)S(1)} %copy-done.2, ...), custom_call_target="tpu_custom_call" | custom-call | tf_op jit(solution)/shard_map/apply/pallas_call | solution.py:245
  (9 shorter events, 0.1 us)
Async XLA Ops:
  0.0 31.5 %copy-start = (bf16[8,256,256]{2,1,0:T(8,128)(2,1)S(1)}, bf16[8,256,256]{2,1,0:T(8,128)(2,1)}, u32[]{:S(2)}) copy-start(bf16[8,256,256]{2,1,0:T(8,128)(2,1)} %param.9) | copy-start | bytes 3145732
  7.6 1.8 %collective-permute-start = (f32[256,384]{1,0:T(8,128)S(1)}, f32[256,384]{1,0:T(8,128)S(1)}, u32[]{:S(2)}, u32[]{:S(2)}) collective-permute-start(f32[256,384]{1,0:T(8,128)S(1)} %get-tuple-element.13), channel_id=1, source_target_pairs={{0,1},{2,3},{4,5},{6,7},{8,9},{10,11},{12,13},{14,15},{1,0},{3,2},... | collective-permute-start | bytes 1179656 | tf_op jit(solution)/shard_map/ppermute | solution.py:153
  10.0 6.0 %collective-permute-start.2 = (f32[256,128]{1,0:T(8,128)S(1)}, f32[256,128]{1,0:T(8,128)S(1)}, u32[]{:S(2)}, u32[]{:S(2)}) collective-permute-start(f32[256,128]{1,0:T(8,128)S(1)} %slice.38), channel_id=1, source_target_pairs={{0,2},{4,6},{8,10},{12,14},{3,1},{7,5},{11,9},{15,13},{16,18},{20,... | collective-permute-start | bytes 393224 | tf_op jit(solution)/shard_map/ppermute | solution.py:162
  11.4 7.5 %collective-permute-start.1 = (f32[256,256]{1,0:T(8,128)S(1)}, f32[256,256]{1,0:T(8,128)S(1)}, u32[]{:S(2)}, u32[]{:S(2)}) collective-permute-start(f32[256,256]{1,0:T(8,128)S(1)} %slice.37), channel_id=1, source_target_pairs={{0,2},{4,6},{8,10},{12,14},{3,1},{7,5},{11,9},{15,13},{16,18},{20,... | collective-permute-start | bytes 786440 | tf_op jit(solution)/shard_map/ppermute | solution.py:163
  16.0 0.6 %copy-start.9 = (f32[256,128]{1,0:T(8,128)}, f32[256,128]{1,0:T(8,128)S(1)}, u32[]{:S(2)}) copy-start(f32[256,128]{1,0:T(8,128)S(1)} %collective-permute-done.2) | copy-start | bytes 393220
  16.7 6.4 %collective-permute-start.3 = (f32[256,128]{1,0:T(8,128)S(1)}, f32[256,128]{1,0:T(8,128)S(1)}, u32[]{:S(2)}, u32[]{:S(2)}) collective-permute-start(f32[256,128]{1,0:T(8,128)S(1)} %convolution_add_fusion.6), channel_id=1, source_target_pairs={{2,6},{6,10},{10,14},{5,1},{9,5},{13,9},{18,22},{22,26},{26,30},{2... | collective-permute-start | bytes 393224 | tf_op jit(solution)/shard_map/ppermute | solution.py:142
  18.8 0.7 %copy-start.8 = (f32[256,256]{1,0:T(8,128)}, f32[256,256]{1,0:T(8,128)S(1)}, u32[]{:S(2)}) copy-start(f32[256,256]{1,0:T(8,128)S(1)} %collective-permute-done.1) | copy-start | bytes 786436
  19.5 11.9 %copy-start.7 = (bf16[8,256,128]{2,1,0:T(8,128)(2,1)S(1)}, bf16[8,256,128]{2,1,0:T(8,128)(2,1)}, u32[]{:S(2)}) copy-start(bf16[8,256,128]{2,1,0:T(8,128)(2,1)} %rhs_ref.1) | copy-start | bytes 1572868
  23.4 5.7 %collective-permute-start.4 = (f32[256,128]{1,0:T(8,128)S(1)}, f32[256,128]{1,0:T(8,128)S(1)}, u32[]{:S(2)}, u32[]{:S(2)}) collective-permute-start(f32[256,128]{1,0:T(8,128)S(1)} %convolution_add_fusion.5), channel_id=1, source_target_pairs={{2,6},{6,10},{10,14},{5,1},{9,5},{13,9},{18,22},{22,26},{26,30},{2... | collective-permute-start | bytes 393224 | tf_op jit(solution)/shard_map/ppermute | solution.py:142
  24.7 17.1 %collective-permute-start.7 = (f32[256,384]{1,0:T(8,128)S(1)}, f32[256,384]{1,0:T(8,128)}, u32[]{:S(2)}, u32[]{:S(2)}) collective-permute-start(f32[256,384]{1,0:T(8,128)S(1)} %get-tuple-element.14), channel_id=1, source_target_pairs={{0,2},{4,6},{8,10},{12,14},{3,1},{7,5},{11,9},{15,13},{16,18},{20,... | collective-permute-start | bytes 1179656 | tf_op jit(solution)/shard_map/ppermute | solution.py:161
  30.2 6.0 %collective-permute-start.5 = (f32[256,128]{1,0:T(8,128)}, f32[256,128]{1,0:T(8,128)}, u32[]{:S(2)}, u32[]{:S(2)}) collective-permute-start(f32[256,128]{1,0:T(8,128)} %convolution_add_fusion.4), channel_id=1, source_target_pairs={{2,6},{6,10},{10,14},{5,1},{9,5},{13,9},{18,22},{22,26},{26,30},{2... | collective-permute-start | bytes 393224 | tf_op jit(solution)/shard_map/ppermute | solution.py:142
  31.5 20.6 %copy-start.3 = (bf16[8,256,256]{2,1,0:T(8,128)(2,1)S(1)}, bf16[8,256,256]{2,1,0:T(8,128)(2,1)}, u32[]{:S(2)}) copy-start(bf16[8,256,256]{2,1,0:T(8,128)(2,1)} %lrows_ref.1) | copy-start | bytes 3145732
  36.2 15.9 %copy-start.2 = (bf16[8,256,256]{2,1,0:T(8,128)(2,1)S(1)}, bf16[8,256,256]{2,1,0:T(8,128)(2,1)}, u32[]{:S(2)}) copy-start(bf16[8,256,256]{2,1,0:T(8,128)(2,1)} %utrans_ref.3) | copy-start | bytes 3145732
  37.7 14.4 %copy-start.1 = (bf16[8,256,256]{2,1,0:T(8,128)(2,1)S(1)}, bf16[8,256,256]{2,1,0:T(8,128)(2,1)}, u32[]{:S(2)}) copy-start(bf16[8,256,256]{2,1,0:T(8,128)(2,1)} %ltrans_ref.3) | copy-start | bytes 3145732
  38.1 11.4 %collective-permute-start.9 = (f32[256,128]{1,0:T(8,128)S(1)}, f32[256,128]{1,0:T(8,128)S(1)}, u32[]{:S(2)}, u32[]{:S(2)}) collective-permute-start(f32[256,128]{1,0:T(8,128)S(1)} %convolution_add_fusion.1), channel_id=1, source_target_pairs={{2,3},{6,7},{10,11},{14,15},{1,0},{5,4},{9,8},{13,12},{18,19},{22,... | collective-permute-start | bytes 393224 | tf_op jit(solution)/shard_map/ppermute | solution.py:198
  40.6 8.9 %collective-permute-start.6 = (f32[256,128]{1,0:T(8,128)}, f32[256,128]{1,0:T(8,128)S(1)}, u32[]{:S(2)}, u32[]{:S(2)}) collective-permute-start(f32[256,128]{1,0:T(8,128)} %collective-permute-done.5), channel_id=1, source_target_pairs={{2,0},{6,4},{10,8},{14,12},{1,3},{5,7},{9,11},{13,15},{18,16},{22,... | collective-permute-start | bytes 393224 | tf_op jit(solution)/shard_map/ppermute | solution.py:196
  43.3 8.8 %collective-permute-start.8 = (f32[256,128]{1,0:T(8,128)S(1)}, f32[256,128]{1,0:T(8,128)S(1)}, u32[]{:S(2)}, u32[]{:S(2)}) collective-permute-start(f32[256,128]{1,0:T(8,128)S(1)} %convolution_add_fusion.2), channel_id=1, source_target_pairs={{2,1},{6,5},{10,9},{14,13},{1,2},{5,6},{9,10},{13,14},{18,17},{22,... | collective-permute-start | bytes 393224 | tf_op jit(solution)/shard_map/ppermute | solution.py:197
  52.1 1.2 %copy-start.4 = (bf16[8,256,256]{2,1,0:T(8,128)(2,1)S(1)}, bf16[8,256,256]{2,1,0:T(8,128)(2,1)}, u32[]{:S(2)}) copy-start(bf16[8,256,256]{2,1,0:T(8,128)(2,1)} %urows_ref.1) | copy-start | bytes 3145732
  53.4 1.2 %copy-start.5 = (f32[8,256,128]{2,1,0:T(8,128)S(1)}, f32[8,256,128]{2,1,0:T(8,128)}, u32[]{:S(2)}) copy-start(f32[8,256,128]{2,1,0:T(8,128)} %get-tuple-element.11.lsrc_ref) | copy-start | bytes 3145732
  54.6 1.2 %copy-start.6 = (f32[8,256,128]{2,1,0:T(8,128)S(1)}, f32[8,256,128]{2,1,0:T(8,128)}, u32[]{:S(2)}) copy-start(f32[8,256,128]{2,1,0:T(8,128)} %get-tuple-element.12.usrc_ref) | copy-start | bytes 3145732

commit v18 on v16

--- a/solution.py
+++ b/solution.py
@@ -20,7 +20,7 @@
 
 
 def sweep_kernel(
-    rhs_ref, lcols_ref, ltrans_ref, ucols_ref, utrans_ref,
+    flag_ref, rhs_ref, lcols_ref, ltrans_ref, ucols_ref, utrans_ref,
     lmap_ref, lsrc_ref, umap_ref, usrc_ref,
 ):
     count = rhs_ref.shape[0]
@@ -45,10 +45,21 @@
             lmap = split_dot(ltrans, lmap)
             umap = split_dot(utrans, umap)
     rank = lmap.shape[0]
-    lmap_ref[:, :rank] = lmap
-    lmap_ref[:, rank:] = lstate
-    umap_ref[:, :rank] = umap
-    umap_ref[:, rank:] = ustate
+    first = flag_ref[0] == 0
+
+    @pl.when(first)
+    def _():
+        lmap_ref[:, :rank] = lmap
+        lmap_ref[:, rank:] = lstate
+        umap_ref[:, :rank] = umap
+        umap_ref[:, rank:] = ustate
+
+    @pl.when(jnp.logical_not(first))
+    def _():
+        lmap_ref[:, :rank] = umap
+        lmap_ref[:, rank:] = ustate
+        umap_ref[:, :rank] = lmap
+        umap_ref[:, rank:] = lstate
 
 
 def apply_kernel(
@@ -185,6 +196,7 @@
     back += [(4 * g + 1, 4 * g + 3) for g in range(groups)]
     sent = lax.ppermute(start, axis, back)
     mine = jnp.dot(beside_map, start, precision=HIGHEST) + beside_state
+    mine, sent = lax.optimization_barrier((mine, sent))
     holder = jnp.logical_or(place == 1, place == 2)
     enter = jnp.where(holder, mine, sent)
     send = jnp.dot(own[:, :rank], enter, precision=HIGHEST) + own[:, rank:]
@@ -204,6 +216,12 @@
 ):
     count, rows, rhs = right_sides.shape
     rank = lower_trans.shape[1]
+    count_row = lax.axis_size("row")
+    grouped = count_row % 4 == 0 and count_row >= 8
+    if grouped:
+        flag = jnp.full((1,), lax.axis_index("row") % 2, jnp.int32)
+    else:
+        flag = jnp.zeros((1,), jnp.int32)
     lboth, lsrc, uboth, usrc = pl.pallas_call(
         sweep_kernel,
         out_shape=(
@@ -212,18 +230,15 @@
             jax.ShapeDtypeStruct((rank, rank + rhs), F32),
             jax.ShapeDtypeStruct((count, rank, rhs), F32),
         ),
+        in_specs=[pl.BlockSpec(memory_space=pltpu.SMEM)] + [pl.BlockSpec(memory_space=pltpu.VMEM)] * 5,
         name="sweep",
-    )(right_sides, lower_cols, lower_trans, upper_cols, upper_trans)
+    )(flag, right_sides, lower_cols, lower_trans, upper_cols, upper_trans)
     diag = jnp.einsum(
         "kab,kbc->kac", diagonal_blocks, right_sides, preferred_element_type=F32
     )
     count_row = lax.axis_size("row")
-    if count_row % 4 == 0 and count_row >= 8:
-        first = lax.axis_index("row") % 2 == 0
-        enter, other = scan_groups(
-            jnp.where(first, lboth, uboth), jnp.where(first, uboth, lboth), "row"
-        )
-        flag = jnp.full((1,), lax.axis_index("row") % 2, jnp.int32)
+    if grouped:
+        enter, other = scan_groups(lboth, uboth, "row")
     elif count_row % 2 == 0 and count_row >= 4:
         enter, other = scan_chips(lboth, uboth, "row")
         flag = jnp.full((1,), lax.axis_index("row") % 2, jnp.int32)

time: 53.9 us -> 52.3 us (0.970)
  matrix products: 5.36 us -> 7.1 us
  local copies, waits for them, and re-layouts: 1.88 us -> 0.67 us
  other arithmetic: 1.17 us -> 0.02 us
  starting transfers between devices: 15.3 us -> 14.5 us
    unnamed x18 -> x20, local copies, waits for them, and re-layouts: 1.84 us -> 0.63 us
    select_n x1, other arithmetic: 1.17 us -> 0.02 us  [scan_groups(): enter = jnp.where(holder, mine, sent)]
    dot_general x1, matrix products: 0.6 us -> 1.59 us  [scan_groups(): jnp.dot(got[:, :rank], own, precision=HIGHEST)]
    ppermute x1, waiting for transfers between devices: 1.59 us -> 0.71 us  [scan_groups(): sent = lax.ppermute(start, axis, back)]
    dot_general x2, matrix products: 0.75 us -> 1.41 us  [scan_groups(): out = jnp.dot(group_map, start, precision=HIGHEST) + group_state]
    ppermute x1, starting transfers between devices: 1.94 us -> 1.29 us  [scan_groups(): sent = lax.ppermute(start, axis, back)]
  transfers between devices with their start and end apart: 8 -> 8, of which waited for: 7 -> 7; matrix products, arithmetic and copies ran while one was open for 4% -> 7% of each run, Pallas kernels for 0% -> 0%
where the time goes in v18:
time: 52.3 us; the launch traced here: 51.8 us
  waiting for transfers between devices  19.5 us (37%)
  starting transfers between devices  14.5 us (28%)
  Pallas kernels  9.85 us (19%)
  matrix products  7.1 us (14%)
  local copies, waits for them, and re-layouts  0.67 us (1%)
    ppermute x3, waiting for transfers between devices, group_shift(): return lax.ppermute(value, axis, pairs)  12.6 us
    pallas_call x1, Pallas kernels, shards(): pl.pallas_call(sweep_kernel, out_shape=(jax.ShapeDtypeStruct((rank, rank...  6.79 us
    ppermute x1, starting transfers between devices, scan_groups(): other = lax.ppermute(send, axis, partner)  6.73 us
    ppermute x3, starting transfers between devices, group_shift(): return lax.ppermute(value, axis, pairs)  3.85 us
    ppermute x1, waiting for transfers between devices, scan_groups(): beside_state = lax.ppermute(both[:, rank:], axis, pair)  3.35 us
    pallas_call x1, Pallas kernels, shards(): pl.pallas_call(apply_kernel, out_shape=jax.ShapeDtypeStruct((count, rows,...  3.06 us
    ppermute x1, waiting for transfers between devices, scan_groups(): got = lax.ppermute(give, axis, partner)  1.93 us
    dot_general x1, matrix products, scan_groups(): jnp.dot(got[:, :rank], own, precision=HIGHEST)  1.59 us
  transfers between devices with their start and end apart: 8, of which 7 were waited for; matrix products, arithmetic and copies ran while one was open for 7% of the time, Pallas kernels for 0%

profile of v18, /device:TPU:1, one launch (start us, length us, event | category | flops | bytes accessed | tf_op | source)
XLA Modules:
  0.0 51.8 jit_solution(13210972736646986680)
XLA Ops:
  0.0 0.0 copy-start
  0.0 6.8 %sweep.1 = (f32[256,384]{1,0:T(8,128)}, f32[8,256,128]{2,1,0:T(8,128)}, f32[256,384]{1,0:T(8,128)}, f32[8,256,128]{2,1,0:T(8,128)}) custom-call(s32[1]{0:T(128)} %bitcast.flag_ref, bf16[8,256,128]{2,1,0:T(8,128)(2,1)} %rhs_ref.1, bf16[8,256,256]{2,1,0:T(8,128)(2,1)} %lcols_ref.1, bf16[8,256,256]{2,1,0:T(8,128)(2,1)} %ltrans_ref.3, ...), custom_call_target="tpu_custom_call" | custom-call | tf_op jit(solution)/shard_map/sweep/pallas_call | solution.py:225
  6.8 0.0 collective-permute-start
  6.8 1.9 %collective-permute-done = f32[256,384]{1,0:T(8,128)S(1)} collective-permute-done((f32[256,384]{1,0:T(8,128)}, f32[256,384]{1,0:T(8,128)S(1)}, u32[]{:S(2)}, u32[]{:S(2)}) %collective-permute-start) | collective-permute-done | bytes 393248 | tf_op jit(solution)/shard_map/ppermute | solution.py:164
  8.7 1.6 %convolution_add_fusion = f32[256,384]{1,0:T(8,128)S(1)} fusion(f32[256,384]{1,0:T(8,128)} %get-tuple-element.12, f32[256,128]{1,0:T(8,128)S(1)} %slice.28, f32[256,384]{1,0:T(8,128)S(1)} %collective-permute-done), kind=kOutput, calls=%fused_computation | convolution fusion | flops 302088192 | bytes 1179648 | tf_op jit(solution)/shard_map/dot_general | solution.py:165
  10.4 1.3 %collective-permute-start.2 = (f32[256,128]{1,0:T(8,128)S(1)}, f32[256,128]{1,0:T(8,128)S(1)}, u32[]{:S(2)}, u32[]{:S(2)}) collective-permute-start(f32[256,128]{1,0:T(8,128)S(1)} %slice.30), channel_id=1, source_target_pairs={{0,2},{4,6},{8,10},{12,14},{3,1},{7,5},{11,9},{15,13},{16,18},{20,... | collective-permute-start | bytes 393224 | tf_op jit(solution)/shard_map/ppermute | solution.py:170
  11.7 1.3 %collective-permute-start.1 = (f32[256,256]{1,0:T(8,128)S(1)}, f32[256,256]{1,0:T(8,128)S(1)}, u32[]{:S(2)}, u32[]{:S(2)}) collective-permute-start(f32[256,256]{1,0:T(8,128)S(1)} %slice.29), channel_id=1, source_target_pairs={{0,2},{4,6},{8,10},{12,14},{3,1},{7,5},{11,9},{15,13},{16,18},{20,... | collective-permute-start | bytes 786440 | tf_op jit(solution)/shard_map/ppermute | solution.py:171
  13.0 3.4 %collective-permute-done.2 = f32[256,128]{1,0:T(8,128)S(1)} collective-permute-done((f32[256,128]{1,0:T(8,128)S(1)}, f32[256,128]{1,0:T(8,128)S(1)}, u32[]{:S(2)}, u32[]{:S(2)}) %collective-permute-start.2) | collective-permute-done | bytes 131104 | tf_op jit(solution)/shard_map/ppermute | solution.py:170
  16.3 0.0 copy-start.9
  16.3 0.0 copy-start.7
  16.3 0.4 convolution_add_fusion.5
  16.7 0.3 copy-done.9
  17.0 1.3 %collective-permute-start.3 = (f32[256,128]{1,0:T(8,128)S(1)}, f32[256,128]{1,0:T(8,128)S(1)}, u32[]{:S(2)}, u32[]{:S(2)}) collective-permute-start(f32[256,128]{1,0:T(8,128)S(1)} %convolution_add_fusion.5), channel_id=1, source_target_pairs={{2,6},{6,10},{10,14},{5,1},{9,5},{13,9},{18,22},{22,26},{26,30},{2... | collective-permute-start | bytes 393224 | tf_op jit(solution)/shard_map/ppermute | solution.py:153
  18.3 0.9 %collective-permute-done.1 = f32[256,256]{1,0:T(8,128)S(1)} collective-permute-done((f32[256,256]{1,0:T(8,128)S(1)}, f32[256,256]{1,0:T(8,128)S(1)}, u32[]{:S(2)}, u32[]{:S(2)}) %collective-permute-start.1) | collective-permute-done | bytes 262176 | tf_op jit(solution)/shard_map/ppermute | solution.py:171
  19.1 0.0 copy-start.8
  19.1 0.0 copy-start.6
  19.1 0.4 fusion.3
  19.5 0.3 copy-done.8
  19.9 3.5 %collective-permute-done.3 = f32[256,128]{1,0:T(8,128)S(1)} collective-permute-done((f32[256,128]{1,0:T(8,128)S(1)}, f32[256,128]{1,0:T(8,128)S(1)}, u32[]{:S(2)}, u32[]{:S(2)}) %collective-permute-start.3) | collective-permute-done | bytes 131104 | tf_op jit(solution)/shard_map/ppermute | solution.py:153
  23.4 0.0 copy-start.5
  23.4 0.4 convolution_add_fusion.4
  23.8 1.3 %collective-permute-start.4 = (f32[256,128]{1,0:T(8,128)S(1)}, f32[256,128]{1,0:T(8,128)S(1)}, u32[]{:S(2)}, u32[]{:S(2)}) collective-permute-start(f32[256,128]{1,0:T(8,128)S(1)} %convolution_add_fusion.4), channel_id=1, source_target_pairs={{2,6},{6,10},{10,14},{5,1},{9,5},{13,9},{18,22},{22,26},{26,30},{2... | collective-permute-start | bytes 393224 | tf_op jit(solution)/shard_map/ppermute | solution.py:153
  25.1 4.4 %collective-permute-done.4 = f32[256,128]{1,0:T(8,128)S(1)} collective-permute-done((f32[256,128]{1,0:T(8,128)S(1)}, f32[256,128]{1,0:T(8,128)S(1)}, u32[]{:S(2)}, u32[]{:S(2)}) %collective-permute-start.4) | collective-permute-done | bytes 131104 | tf_op jit(solution)/shard_map/ppermute | solution.py:153
  29.5 1.0 %convolution_add_fusion.3 = f32[256,128]{1,0:T(8,128)} fusion(f32[256,128]{1,0:T(8,128)S(1)} %convolution_add_fusion.5, f32[256,256]{1,0:T(8,128)S(1)} %fusion.3, f32[256,128]{1,0:T(8,128)S(1)} %collective-permute-done.4), kind=kOutput, calls=%fused_computation.3 | convolution fusion | flops 100696064 | bytes 655360 | tf_op jit(solution)/shard_map/dot_general | solution.py:181
  30.5 1.3 %collective-permute-start.5 = (f32[256,128]{1,0:T(8,128)}, f32[256,128]{1,0:T(8,128)}, u32[]{:S(2)}, u32[]{:S(2)}) collective-permute-start(f32[256,128]{1,0:T(8,128)} %convolution_add_fusion.3), channel_id=1, source_target_pairs={{2,6},{6,10},{10,14},{5,1},{9,5},{13,9},{18,22},{22,26},{26,30},{2... | collective-permute-start | bytes 393224 | tf_op jit(solution)/shard_map/ppermute | solution.py:153
  31.8 4.7 %collective-permute-done.5 = f32[256,128]{1,0:T(8,128)} collective-permute-done((f32[256,128]{1,0:T(8,128)}, f32[256,128]{1,0:T(8,128)}, u32[]{:S(2)}, u32[]{:S(2)}) %collective-permute-start.5) | collective-permute-done | bytes 131104 | tf_op jit(solution)/shard_map/ppermute | solution.py:153
  36.5 1.3 %collective-permute-start.6 = (f32[256,128]{1,0:T(8,128)}, f32[256,128]{1,0:T(8,128)S(1)}, u32[]{:S(2)}, u32[]{:S(2)}) collective-permute-start(f32[256,128]{1,0:T(8,128)} %collective-permute-done.5), channel_id=1, source_target_pairs={{2,0},{6,4},{10,8},{14,12},{1,3},{5,7},{9,11},{13,15},{18,16},{22,... | collective-permute-start | bytes 393224 | tf_op jit(solution)/shard_map/ppermute | solution.py:197
  37.8 0.0 copy-start.4
  37.8 1.5 %convolution_add_fusion.2 = f32[256,128]{1,0:T(8,128)S(1)} fusion(f32[256,128]{1,0:T(8,128)} %copy-done.9, f32[256,256]{1,0:T(8,128)} %copy-done.8, f32[256,128]{1,0:T(8,128)} %collective-permute-done.5), kind=kOutput, calls=%fused_computation.2 | convolution fusion | flops 100696064 | bytes 655360 | tf_op jit(solution)/shard_map/dot_general | solution.py:198
  39.3 0.7 %collective-permute-done.6 = f32[256,128]{1,0:T(8,128)S(1)} collective-permute-done((f32[256,128]{1,0:T(8,128)}, f32[256,128]{1,0:T(8,128)S(1)}, u32[]{:S(2)}, u32[]{:S(2)}) %collective-permute-start.6) | collective-permute-done | bytes 131104 | tf_op jit(solution)/shard_map/ppermute | solution.py:197
  40.1 0.0 copy-done.7
  40.1 0.0 copy-start.3
  40.1 0.4 convolution_add_fusion.1
  40.5 0.0 copy-start.1
  40.5 0.0 copy-start.2
  40.5 6.7 %collective-permute-start.7 = (f32[256,128]{1,0:T(8,128)S(1)}, f32[256,128]{1,0:T(8,128)S(1)}, u32[]{:S(2)}, u32[]{:S(2)}) collective-permute-start(f32[256,128]{1,0:T(8,128)S(1)} %convolution_add_fusion.1), channel_id=1, source_target_pairs={{0,1},{2,3},{4,5},{6,7},{8,9},{10,11},{12,13},{14,15},{1,0},{3,2},... | collective-permute-start | bytes 393224 | tf_op jit(solution)/shard_map/ppermute | solution.py:203
  47.2 0.0 copy-done
  47.2 1.5 %fusion.5.diag_ref = f32[8,256,128]{2,1,0:T(8,128)S(1)} fusion(bf16[8,256,256]{2,1,0:T(8,128)(2,1)S(1)} %copy-done, bf16[8,256,128]{2,1,0:T(8,128)(2,1)} %rhs_ref.1), kind=kOutput, calls=%fused_computation.12 | convolution fusion | flops 134217728 | bytes 2621440 | tf_op jit(solution)/shard_map/kab,kbc->kac/dot_general | solution.py:236
  48.7 0.0 collective-permute-done.7.other_ref
  48.7 0.0 copy-done.6
  48.7 0.0 copy-done.5
  48.7 0.0 copy-done.4
  48.7 0.0 copy-done.3
  48.8 0.0 copy-done.1
  48.8 0.0 copy-done.2
  48.8 3.1 %apply.1 = bf16[8,256,128]{2,1,0:T(8,128)(2,1)} custom-call(s32[1]{0:T(128)} %bitcast.flag_ref, f32[256,128]{1,0:T(8,128)S(1)} %broadcast_select_fusion.enter_ref, f32[256,128]{1,0:T(8,128)S(1)} %collective-permute-done.7.other_ref, bf16[8,256,256]{2,1,0:T(8,128)(2,1)S(1)} %copy-done.1, bf16[8,256,256]{2,1,0:T(8,128)(2,1)S(1)} %copy-done.2, ...), custom_call_target="tpu_custom_call" | custom-call | tf_op jit(solution)/shard_map/apply/pallas_call | solution.py:250
  (4 shorter events, 0.1 us)
Async XLA Ops:
  0.0 47.2 %copy-start = (bf16[8,256,256]{2,1,0:T(8,128)(2,1)S(1)}, bf16[8,256,256]{2,1,0:T(8,128)(2,1)}, u32[]{:S(2)}) copy-start(bf16[8,256,256]{2,1,0:T(8,128)(2,1)} %param.9) | copy-start | bytes 3145732
  6.8 1.9 %collective-permute-start = (f32[256,384]{1,0:T(8,128)}, f32[256,384]{1,0:T(8,128)S(1)}, u32[]{:S(2)}, u32[]{:S(2)}) collective-permute-start(f32[256,384]{1,0:T(8,128)} %get-tuple-element.11), channel_id=1, source_target_pairs={{0,1},{2,3},{4,5},{6,7},{8,9},{10,11},{12,13},{14,15},{1,0},{3,2},... | collective-permute-start | bytes 1179656 | tf_op jit(solution)/shard_map/ppermute | solution.py:164
  10.4 6.0 %collective-permute-start.2 = (f32[256,128]{1,0:T(8,128)S(1)}, f32[256,128]{1,0:T(8,128)S(1)}, u32[]{:S(2)}, u32[]{:S(2)}) collective-permute-start(f32[256,128]{1,0:T(8,128)S(1)} %slice.30), channel_id=1, source_target_pairs={{0,2},{4,6},{8,10},{12,14},{3,1},{7,5},{11,9},{15,13},{16,18},{20,... | collective-permute-start | bytes 393224 | tf_op jit(solution)/shard_map/ppermute | solution.py:170
  11.7 7.5 %collective-permute-start.1 = (f32[256,256]{1,0:T(8,128)S(1)}, f32[256,256]{1,0:T(8,128)S(1)}, u32[]{:S(2)}, u32[]{:S(2)}) collective-permute-start(f32[256,256]{1,0:T(8,128)S(1)} %slice.29), channel_id=1, source_target_pairs={{0,2},{4,6},{8,10},{12,14},{3,1},{7,5},{11,9},{15,13},{16,18},{20,... | collective-permute-start | bytes 786440 | tf_op jit(solution)/shard_map/ppermute | solution.py:171
  16.3 0.7 %copy-start.9 = (f32[256,128]{1,0:T(8,128)}, f32[256,128]{1,0:T(8,128)S(1)}, u32[]{:S(2)}) copy-start(f32[256,128]{1,0:T(8,128)S(1)} %collective-permute-done.2) | copy-start | bytes 393220
  16.3 23.7 %copy-start.7 = (f32[256,384]{1,0:T(8,128)S(1)}, f32[256,384]{1,0:T(8,128)}, u32[]{:S(2)}) copy-start(f32[256,384]{1,0:T(8,128)} %get-tuple-element.12) | copy-start | bytes 1179652
  17.0 6.4 %collective-permute-start.3 = (f32[256,128]{1,0:T(8,128)S(1)}, f32[256,128]{1,0:T(8,128)S(1)}, u32[]{:S(2)}, u32[]{:S(2)}) collective-permute-start(f32[256,128]{1,0:T(8,128)S(1)} %convolution_add_fusion.5), channel_id=1, source_target_pairs={{2,6},{6,10},{10,14},{5,1},{9,5},{13,9},{18,22},{22,26},{26,30},{2... | collective-permute-start | bytes 393224 | tf_op jit(solution)/shard_map/ppermute | solution.py:153
  19.1 0.7 %copy-start.8 = (f32[256,256]{1,0:T(8,128)}, f32[256,256]{1,0:T(8,128)S(1)}, u32[]{:S(2)}) copy-start(f32[256,256]{1,0:T(8,128)S(1)} %collective-permute-done.1) | copy-start | bytes 786436
  19.1 29.6 %copy-start.6 = (f32[8,256,128]{2,1,0:T(8,128)S(1)}, f32[8,256,128]{2,1,0:T(8,128)}, u32[]{:S(2)}) copy-start(f32[8,256,128]{2,1,0:T(8,128)} %get-tuple-element.16.usrc_ref) | copy-start | bytes 3145732
  23.4 25.3 %copy-start.5 = (f32[8,256,128]{2,1,0:T(8,128)S(1)}, f32[8,256,128]{2,1,0:T(8,128)}, u32[]{:S(2)}) copy-start(f32[8,256,128]{2,1,0:T(8,128)} %get-tuple-element.15.lsrc_ref) | copy-start | bytes 3145732
  23.8 5.7 %collective-permute-start.4 = (f32[256,128]{1,0:T(8,128)S(1)}, f32[256,128]{1,0:T(8,128)S(1)}, u32[]{:S(2)}, u32[]{:S(2)}) collective-permute-start(f32[256,128]{1,0:T(8,128)S(1)} %convolution_add_fusion.4), channel_id=1, source_target_pairs={{2,6},{6,10},{10,14},{5,1},{9,5},{13,9},{18,22},{22,26},{26,30},{2... | collective-permute-start | bytes 393224 | tf_op jit(solution)/shard_map/ppermute | solution.py:153
  30.5 6.0 %collective-permute-start.5 = (f32[256,128]{1,0:T(8,128)}, f32[256,128]{1,0:T(8,128)}, u32[]{:S(2)}, u32[]{:S(2)}) collective-permute-start(f32[256,128]{1,0:T(8,128)} %convolution_add_fusion.3), channel_id=1, source_target_pairs={{2,6},{6,10},{10,14},{5,1},{9,5},{13,9},{18,22},{22,26},{26,30},{2... | collective-permute-start | bytes 393224 | tf_op jit(solution)/shard_map/ppermute | solution.py:153
  36.5 3.5 %collective-permute-start.6 = (f32[256,128]{1,0:T(8,128)}, f32[256,128]{1,0:T(8,128)S(1)}, u32[]{:S(2)}, u32[]{:S(2)}) collective-permute-start(f32[256,128]{1,0:T(8,128)} %collective-permute-done.5), channel_id=1, source_target_pairs={{2,0},{6,4},{10,8},{14,12},{1,3},{5,7},{9,11},{13,15},{18,16},{22,... | collective-permute-start | bytes 393224 | tf_op jit(solution)/shard_map/ppermute | solution.py:197
  37.8 10.9 %copy-start.4 = (bf16[8,256,256]{2,1,0:T(8,128)(2,1)S(1)}, bf16[8,256,256]{2,1,0:T(8,128)(2,1)}, u32[]{:S(2)}) copy-start(bf16[8,256,256]{2,1,0:T(8,128)(2,1)} %urows_ref.1) | copy-start | bytes 3145732
  40.1 8.7 %copy-start.3 = (bf16[8,256,256]{2,1,0:T(8,128)(2,1)S(1)}, bf16[8,256,256]{2,1,0:T(8,128)(2,1)}, u32[]{:S(2)}) copy-start(bf16[8,256,256]{2,1,0:T(8,128)(2,1)} %lrows_ref.1) | copy-start | bytes 3145732
  40.5 8.3 %copy-start.1 = (bf16[8,256,256]{2,1,0:T(8,128)(2,1)S(1)}, bf16[8,256,256]{2,1,0:T(8,128)(2,1)}, u32[]{:S(2)}) copy-start(bf16[8,256,256]{2,1,0:T(8,128)(2,1)} %ltrans_ref.3) | copy-start | bytes 3145732
  40.5 8.3 %copy-start.2 = (bf16[8,256,256]{2,1,0:T(8,128)(2,1)S(1)}, bf16[8,256,256]{2,1,0:T(8,128)(2,1)}, u32[]{:S(2)}) copy-start(bf16[8,256,256]{2,1,0:T(8,128)(2,1)} %utrans_ref.3) | copy-start | bytes 3145732
  40.5 8.2 %collective-permute-start.7 = (f32[256,128]{1,0:T(8,128)S(1)}, f32[256,128]{1,0:T(8,128)S(1)}, u32[]{:S(2)}, u32[]{:S(2)}) collective-permute-start(f32[256,128]{1,0:T(8,128)S(1)} %convolution_add_fusion.1), channel_id=1, source_target_pairs={{0,1},{2,3},{4,5},{6,7},{8,9},{10,11},{12,13},{14,15},{1,0},{3,2},... | collective-permute-start | bytes 393224 | tf_op jit(solution)/shard_map/ppermute | solution.py:203

commit v19 on v18

--- a/solution.py
+++ b/solution.py
@@ -17,6 +17,27 @@
     return jnp.dot(matrix, high, preferred_element_type=F32) + jnp.dot(
         matrix, low, preferred_element_type=F32
     )
+
+
+def wide_kernel(left_ref, right_ref, add_ref, out_ref):
+    left = left_ref[...]
+    right = right_ref[...]
+    left_high = left.astype(BF16)
+    left_low = (left - left_high.astype(F32)).astype(BF16)
+    right_high = right.astype(BF16)
+    right_low = (right - right_high.astype(F32)).astype(BF16)
+    total = jnp.dot(left_high, right_high, preferred_element_type=F32)
+    total = total + jnp.dot(left_high, right_low, preferred_element_type=F32)
+    total = total + jnp.dot(left_low, right_high, preferred_element_type=F32)
+    out_ref[...] = total + add_ref[...]
+
+
+def wide(left, right, add):
+    return pl.pallas_call(
+        wide_kernel,
+        out_shape=jax.ShapeDtypeStruct((left.shape[0], right.shape[1]), F32),
+        name="wide",
+    )(left, right, add)
 
 
 def sweep_kernel(
@@ -162,15 +183,13 @@
     partner = [(2 * c, 2 * c + 1) for c in range(count // 2)]
     partner += [(2 * c + 1, 2 * c) for c in range(count // 2)]
     got = lax.ppermute(give, axis, partner)
-    both = jnp.dot(got[:, :rank], own, precision=HIGHEST) + jnp.concatenate(
-        [zeros, got[:, rank:]], axis=1
-    )
+    both = wide(got[:, :rank], own, jnp.concatenate([zeros, got[:, rank:]], axis=1))
     pair = [(4 * g, 4 * g + 2) for g in range(groups)]
     pair += [(4 * g + 3, 4 * g + 1) for g in range(groups)]
     beside_state = lax.ppermute(both[:, rank:], axis, pair)
     beside_map = lax.ppermute(both[:, :rank], axis, pair)
-    group_state = jnp.dot(both[:, :rank], beside_state, precision=HIGHEST) + both[:, rank:]
-    group_map = jnp.dot(both[:, :rank], beside_map, precision=HIGHEST)
+    group_state = wide(both[:, :rank], beside_state, both[:, rank:])
+    group_map = wide(both[:, :rank], beside_map, zeros)
     beside = jnp.concatenate([beside_map, beside_state], axis=1)
     both = jnp.concatenate([group_map, group_state], axis=1)
     if groups <= 4:
@@ -178,7 +197,7 @@
         for step in range(groups - 1):
             start = group_shift(out, axis, groups, 1)
             if step + 2 < groups:
-                out = jnp.dot(group_map, start, precision=HIGHEST) + group_state
+                out = wide(group_map, start, group_state)
     else:
         rounds = 0
         while 2 ** (rounds + 1) < groups - 1:
@@ -195,11 +214,11 @@
     back = [(4 * g + 2, 4 * g) for g in range(groups)]
     back += [(4 * g + 1, 4 * g + 3) for g in range(groups)]
     sent = lax.ppermute(start, axis, back)
-    mine = jnp.dot(beside_map, start, precision=HIGHEST) + beside_state
+    mine = wide(beside_map, start, beside_state)
     mine, sent = lax.optimization_barrier((mine, sent))
     holder = jnp.logical_or(place == 1, place == 2)
     enter = jnp.where(holder, mine, sent)
-    send = jnp.dot(own[:, :rank], enter, precision=HIGHEST) + own[:, rank:]
+    send = wide(own[:, :rank], enter, own[:, rank:])
     other = lax.ppermute(send, axis, partner)
     return enter, other
 

time: 52.3 us -> 69.3 us (1.33)
  Pallas kernels: 9.85 us -> 24.2 us
  local copies, waits for them, and re-layouts: 0.67 us -> 10 us
  matrix products: 7.1 us -> 1.46 us
  starting transfers between devices: 14.5 us -> 12.3 us
  other arithmetic: 0.02 us -> 1.59 us
    pallas_call x0 -> x7, Pallas kernels: none -> 14.4 us  [wide(): pl.pallas_call(wide_kernel, out_shape=jax.ShapeDtypeStruct((left.shape[0]...]
    dot_general x7 -> x0, matrix products: 5.65 us -> none  [the longest x1 1.59 us: scan_groups(): jnp.dot(got[:, :rank], own, precision=HIGHEST)]
    unnamed x20 -> x32, local copies, waits for them, and re-layouts: 0.63 us -> 4.5 us
    ppermute x1, starting transfers between devices: 6.73 us -> 4.41 us  [scan_groups(): other = lax.ppermute(send, axis, partner)]
    slice x0 -> x3, local copies, waits for them, and re-layouts: none -> 2.1 us  [the longest x2 1.38 us: scan_groups(): send = wide(own[:, :rank], enter, own[:, rank:])]
    ppermute x1, waiting for transfers between devices: 3.35 us -> 5.26 us  [scan_groups(): beside_state = lax.ppermute(both[:, rank:], axis, pair)]
    select_n x1, other arithmetic: 0.02 us -> 1.59 us  [scan_groups(): enter = jnp.where(holder, mine, sent)]
    ppermute x3, waiting for transfers between devices: 12.6 us -> 11.7 us  [group_shift(): return lax.ppermute(value, axis, pairs)]
  transfers between devices with their start and end apart: 8 -> 8, of which waited for: 7 -> 5; matrix products, arithmetic and copies ran while one was open for 7% -> 7% of each run, Pallas kernels for 0% -> 9%
where the time goes in v19:
time: 69.3 us; the launch traced here: 68.6 us
  Pallas kernels  24.2 us (35%)
  waiting for transfers between devices  18.9 us (27%)
  starting transfers between devices  12.3 us (18%)
  local copies, waits for them, and re-layouts  10 us (14%)
  other arithmetic  1.59 us (2%)
  matrix products  1.46 us (2%)
    pallas_call x7, Pallas kernels, wide(): pl.pallas_call(wide_kernel, out_shape=jax.ShapeDtypeStruct((left.shape[0]...  14.4 us
    ppermute x3, waiting for transfers between devices, group_shift(): return lax.ppermute(value, axis, pairs)  11.7 us
    pallas_call x1, Pallas kernels, shards(): pl.pallas_call(sweep_kernel, out_shape=(jax.ShapeDtypeStruct((rank, rank...  6.76 us
    ppermute x1, waiting for transfers between devices, scan_groups(): beside_state = lax.ppermute(both[:, rank:], axis, pair)  5.26 us
    unnamed x32, local copies, waits for them, and re-layouts  4.5 us
    ppermute x1, starting transfers between devices, scan_groups(): other = lax.ppermute(send, axis, partner)  4.41 us
    ppermute x3, starting transfers between devices, group_shift(): return lax.ppermute(value, axis, pairs)  3.97 us
    pallas_call x1, Pallas kernels, shards(): pl.pallas_call(apply_kernel, out_shape=jax.ShapeDtypeStruct((count, rows,...  3.06 us
  transfers between devices with their start and end apart: 8, of which 5 were waited for; matrix products, arithmetic and copies ran while one was open for 7% of the time, Pallas kernels for 9%

profile of v19, /device:TPU:1, one launch (start us, length us, event | category | flops | bytes accessed | tf_op | source)
XLA Modules:
  0.0 68.6 jit_solution(2177151545592909078)
XLA Ops:
  0.0 0.0 copy-start
  0.0 6.8 %sweep.1 = (f32[256,384]{1,0:T(8,128)}, f32[8,256,128]{2,1,0:T(8,128)}, f32[256,384]{1,0:T(8,128)}, f32[8,256,128]{2,1,0:T(8,128)}) custom-call(s32[1]{0:T(128)} %bitcast.flag_ref, bf16[8,256,128]{2,1,0:T(8,128)(2,1)} %rhs_ref.1, bf16[8,256,256]{2,1,0:T(8,128)(2,1)} %lcols_ref.1, bf16[8,256,256]{2,1,0:T(8,128)(2,1)} %ltrans_ref.3, ...), custom_call_target="tpu_custom_call" | custom-call | tf_op jit(solution)/shard_map/sweep/pallas_call | solution.py:244
  6.8 0.0 collective-permute-start
  6.8 1.9 %collective-permute-done = f32[256,384]{1,0:T(8,128)S(1)} collective-permute-done((f32[256,384]{1,0:T(8,128)}, f32[256,384]{1,0:T(8,128)S(1)}, u32[]{:S(2)}, u32[]{:S(2)}) %collective-permute-start) | collective-permute-done | bytes 393248 | tf_op jit(solution)/shard_map/ppermute | solution.py:185
  8.7 0.8 %concatenate.3.add_ref = f32[256,384]{1,0:T(8,128)} pad(f32[256,128]{1,0:T(8,128)S(1)} %slice.28, f32[]{:T(128)} %constant.29.clone.1), padding=0_0x256_0 | pad | bytes 524292 | tf_op jit(solution)/shard_map/concatenate | solution.py:186
  9.5 0.7 %slice.27.left_ref = f32[256,256]{1,0:T(8,128)} slice(f32[256,384]{1,0:T(8,128)S(1)} %collective-permute-done), slice={[0:256], [0:256]} | slice | bytes 524288 | tf_op jit(solution)/shard_map/slice | solution.py:186
  10.2 2.3 %wide.7 = f32[256,384]{1,0:T(8,128)} custom-call(f32[256,256]{1,0:T(8,128)} %slice.27.left_ref, f32[256,384]{1,0:T(8,128)} %get-tuple-element.12.right_ref, f32[256,384]{1,0:T(8,128)} %concatenate.3.add_ref), custom_call_target="tpu_custom_call" | custom-call | tf_op jit(solution)/shard_map/wide/pallas_call | solution.py:36
  12.5 1.0 %slice.29.left_ref = f32[256,256]{1,0:T(8,128)S(1)} slice(f32[256,384]{1,0:T(8,128)} %wide.7), slice={[0:256], [0:256]} | slice | bytes 524288 | tf_op jit(solution)/shard_map/slice | solution.py:190
  13.5 0.0 copy-start.8
  13.5 1.3 %collective-permute-start.1 = (f32[256,256]{1,0:T(8,128)S(1)}, f32[256,256]{1,0:T(8,128)S(1)}, u32[]{:S(2)}, u32[]{:S(2)}) collective-permute-start(f32[256,256]{1,0:T(8,128)S(1)} %slice.29.left_ref), channel_id=1, source_target_pairs={{0,2},{4,6},{8,10},{12,14},{3,1},{7,5},{11,9},{15,13},{16,18},{20,... | collective-permute-start | bytes 786440 | tf_op jit(solution)/shard_map/ppermute | solution.py:190
  14.8 0.9 %slice.30.add_ref = f32[256,128]{1,0:T(8,128)S(1)} slice(f32[256,384]{1,0:T(8,128)} %wide.7), slice={[0:256], [256:384]} | slice | bytes 262144 | tf_op jit(solution)/shard_map/slice | solution.py:189
  15.7 0.0 copy-start.12
  15.7 1.3 %collective-permute-start.2 = (f32[256,128]{1,0:T(8,128)S(1)}, f32[256,128]{1,0:T(8,128)S(1)}, u32[]{:S(2)}, u32[]{:S(2)}) collective-permute-start(f32[256,128]{1,0:T(8,128)S(1)} %slice.30.add_ref), channel_id=1, source_target_pairs={{0,2},{4,6},{8,10},{12,14},{3,1},{7,5},{11,9},{15,13},{16,18},{20,... | collective-permute-start | bytes 393224 | tf_op jit(solution)/shard_map/ppermute | solution.py:189
  17.0 5.3 %collective-permute-done.2.right_ref.add_ref = f32[256,128]{1,0:T(8,128)S(1)} collective-permute-done((f32[256,128]{1,0:T(8,128)S(1)}, f32[256,128]{1,0:T(8,128)S(1)}, u32[]{:S(2)}, u32[]{:S(2)}) %collective-permute-start.2) | collective-permute-done | bytes 131104 | tf_op jit(solution)/shard_map/ppermute | solution.py:189
  22.3 0.0 copy-done.8
  22.3 0.0 copy-done.12
  22.3 0.7 copy-done.11
  23.0 2.0 %wide.9.add_ref = f32[256,128]{1,0:T(8,128)} custom-call(f32[256,256]{1,0:T(8,128)} %copy-done.8, f32[256,128]{1,0:T(8,128)} %copy-done.11, f32[256,128]{1,0:T(8,128)} %copy-done.12), custom_call_target="tpu_custom_call" | custom-call | tf_op jit(solution)/shard_map/wide/pallas_call | solution.py:36
  24.9 1.3 %collective-permute-start.3 = (f32[256,128]{1,0:T(8,128)}, f32[256,128]{1,0:T(8,128)S(1)}, u32[]{:S(2)}, u32[]{:S(2)}) collective-permute-start(f32[256,128]{1,0:T(8,128)} %wide.9.add_ref), channel_id=1, source_target_pairs={{2,6},{6,10},{10,14},{5,1},{9,5},{13,9},{18,22},{22,26},{26,30},{2... | collective-permute-start | bytes 393224 | tf_op jit(solution)/shard_map/ppermute | solution.py:174
  26.2 0.0 collective-permute-done.1.right_ref.left_ref
  26.2 0.0 copy-start.10
  26.2 0.8 %broadcast_in_dim.7.add_ref = f32[256,256]{1,0:T(8,128)} broadcast(f32[]{:T(128)} %constant.29.clone.1), dimensions={} | broadcast | bytes 262148 | tf_op jit(solution)/shard_map/broadcast_in_dim | solution.py:182
  27.0 0.0 copy-done.10
  27.0 2.1 %wide.8.left_ref = f32[256,256]{1,0:T(8,128)} custom-call(f32[256,256]{1,0:T(8,128)} %copy-done.8, f32[256,256]{1,0:T(8,128)} %copy-done.10, f32[256,256]{1,0:T(8,128)} %broadcast_in_dim.7.add_ref), custom_call_target="tpu_custom_call" | custom-call | tf_op jit(solution)/shard_map/wide/pallas_call | solution.py:36
  29.1 2.4 %collective-permute-done.3.right_ref = f32[256,128]{1,0:T(8,128)S(1)} collective-permute-done((f32[256,128]{1,0:T(8,128)}, f32[256,128]{1,0:T(8,128)S(1)}, u32[]{:S(2)}, u32[]{:S(2)}) %collective-permute-start.3) | collective-permute-done | bytes 131104 | tf_op jit(solution)/shard_map/ppermute | solution.py:174
  31.5 0.7 copy-done.14
  32.2 1.9 %wide.10 = f32[256,128]{1,0:T(8,128)} custom-call(f32[256,256]{1,0:T(8,128)} %wide.8.left_ref, f32[256,128]{1,0:T(8,128)} %copy-done.14, f32[256,128]{1,0:T(8,128)} %wide.9.add_ref), custom_call_target="tpu_custom_call" | custom-call | tf_op jit(solution)/shard_map/wide/pallas_call | solution.py:36
  34.1 1.4 %collective-permute-start.4 = (f32[256,128]{1,0:T(8,128)}, f32[256,128]{1,0:T(8,128)S(1)}, u32[]{:S(2)}, u32[]{:S(2)}) collective-permute-start(f32[256,128]{1,0:T(8,128)} %wide.10), channel_id=1, source_target_pairs={{2,6},{6,10},{10,14},{5,1},{9,5},{13,9},{18,22},{22,26},{26,30},{2... | collective-permute-start | bytes 393224 | tf_op jit(solution)/shard_map/ppermute | solution.py:174
  35.6 4.6 %collective-permute-done.4.right_ref = f32[256,128]{1,0:T(8,128)S(1)} collective-permute-done((f32[256,128]{1,0:T(8,128)}, f32[256,128]{1,0:T(8,128)S(1)}, u32[]{:S(2)}, u32[]{:S(2)}) %collective-permute-start.4) | collective-permute-done | bytes 131104 | tf_op jit(solution)/shard_map/ppermute | solution.py:174
  40.2 0.7 copy-done.15
  40.9 1.9 %wide.11 = f32[256,128]{1,0:T(8,128)} custom-call(f32[256,256]{1,0:T(8,128)} %wide.8.left_ref, f32[256,128]{1,0:T(8,128)} %copy-done.15, f32[256,128]{1,0:T(8,128)} %wide.9.add_ref), custom_call_target="tpu_custom_call" | custom-call | tf_op jit(solution)/shard_map/wide/pallas_call | solution.py:36
  42.8 1.3 %collective-permute-start.5 = (f32[256,128]{1,0:T(8,128)}, f32[256,128]{1,0:T(8,128)S(1)}, u32[]{:S(2)}, u32[]{:S(2)}) collective-permute-start(f32[256,128]{1,0:T(8,128)} %wide.11), channel_id=1, source_target_pairs={{2,6},{6,10},{10,14},{5,1},{9,5},{13,9},{18,22},{22,26},{26,30},{2... | collective-permute-start | bytes 393224 | tf_op jit(solution)/shard_map/ppermute | solution.py:174
  44.1 4.6 %collective-permute-done.5.right_ref = f32[256,128]{1,0:T(8,128)S(1)} collective-permute-done((f32[256,128]{1,0:T(8,128)}, f32[256,128]{1,0:T(8,128)S(1)}, u32[]{:S(2)}, u32[]{:S(2)}) %collective-permute-start.5) | collective-permute-done | bytes 131104 | tf_op jit(solution)/shard_map/ppermute | solution.py:174
  48.7 1.3 %collective-permute-start.6 = (f32[256,128]{1,0:T(8,128)S(1)}, f32[256,128]{1,0:T(8,128)S(1)}, u32[]{:S(2)}, u32[]{:S(2)}) collective-permute-start(f32[256,128]{1,0:T(8,128)S(1)} %collective-permute-done.5.right_ref), channel_id=1, source_target_pairs={{2,0},{6,4},{10,8},{14,12},{1,3},{5,7},{9,11},{13,15},{18,16},{22,... | collective-permute-start | bytes 393224 | tf_op jit(solution)/shard_map/ppermute | solution.py:216
  50.0 0.0 copy-done.9
  50.0 0.7 %slice.25.left_ref = f32[256,256]{1,0:T(8,128)} slice(f32[256,384]{1,0:T(8,128)S(1)} %copy-done.9), slice={[0:256], [0:256]} | slice | bytes 524288 | tf_op jit(solution)/shard_map/slice | solution.py:221
  50.8 0.0 copy-done.13
  50.8 0.7 slice.26.add_ref
  51.4 2.1 %wide.12 = f32[256,128]{1,0:T(8,128)} custom-call(f32[256,256]{1,0:T(8,128)} %copy-done.10, f32[256,128]{1,0:T(8,128)} %copy-done.13, f32[256,128]{1,0:T(8,128)} %copy-done.11), custom_call_target="tpu_custom_call" | custom-call | tf_op jit(solution)/shard_map/wide/pallas_call | solution.py:36
  53.5 0.0 collective-permute-done.6
  53.5 1.6 %broadcast_select_fusion.right_ref.enter_ref = f32[256,128]{1,0:T(8,128)} fusion(f32[256,128]{1,0:T(8,128)} %wide.12, f32[256,128]{1,0:T(8,128)S(1)} %collective-permute-done.6, pred[]{:T(512)S(6)} %or.3), kind=kLoop, calls=%fused_computation | loop fusion | flops 32768 | bytes 393217 | tf_op jit(solution)/shard_map/jit(_where)/select_n | solution.py:220
  55.1 2.0 %wide.13 = f32[256,128]{1,0:T(8,128)} custom-call(f32[256,256]{1,0:T(8,128)} %slice.25.left_ref, f32[256,128]{1,0:T(8,128)} %broadcast_select_fusion.right_ref.enter_ref, f32[256,128]{1,0:T(8,128)} %slice.26.add_ref), custom_call_target="tpu_custom_call" | custom-call | tf_op jit(solution)/shard_map/wide/pallas_call | solution.py:36
  57.1 4.4 %collective-permute-start.7 = (f32[256,128]{1,0:T(8,128)}, f32[256,128]{1,0:T(8,128)S(1)}, u32[]{:S(2)}, u32[]{:S(2)}) collective-permute-start(f32[256,128]{1,0:T(8,128)} %wide.13), channel_id=1, source_target_pairs={{0,1},{2,3},{4,5},{6,7},{8,9},{10,11},{12,13},{14,15},{1,0},{3,2},... | collective-permute-start | bytes 393224 | tf_op jit(solution)/shard_map/ppermute | solution.py:222
  61.5 1.5 %fusion.diag_ref = f32[8,256,128]{2,1,0:T(8,128)S(1)} fusion(bf16[8,256,256]{2,1,0:T(8,128)(2,1)S(1)} %copy-done, bf16[8,256,128]{2,1,0:T(8,128)(2,1)} %rhs_ref.1), kind=kOutput, calls=%fused_computation.1 | convolution fusion | flops 134217728 | bytes 2621440 | tf_op jit(solution)/shard_map/kab,kbc->kac/dot_general | solution.py:255
  63.0 0.0 collective-permute-done.7.other_ref
  63.1 1.2 %copy-done.6 = f32[8,256,128]{2,1,0:T(8,128)S(1)} copy-done((f32[8,256,128]{2,1,0:T(8,128)S(1)}, f32[8,256,128]{2,1,0:T(8,128)}, u32[]{:S(2)}) %copy-start.6) | copy-done | bytes 1048600
  64.3 1.2 %copy-done.7 = f32[8,256,128]{2,1,0:T(8,128)S(1)} copy-done((f32[8,256,128]{2,1,0:T(8,128)S(1)}, f32[8,256,128]{2,1,0:T(8,128)}, u32[]{:S(2)}) %copy-start.7) | copy-done | bytes 1048600
  65.5 3.1 %apply.1 = bf16[8,256,128]{2,1,0:T(8,128)(2,1)} custom-call(s32[1]{0:T(128)} %bitcast.flag_ref, f32[256,128]{1,0:T(8,128)S(1)} %copy-done.3, f32[256,128]{1,0:T(8,128)S(1)} %collective-permute-done.7.other_ref, bf16[8,256,256]{2,1,0:T(8,128)(2,1)S(1)} %copy-done.1, bf16[8,256,256]{2,1,0:T(8,128)(2,1)S(1)} %copy-done.2, f32[8,256,128]{2,1,0:T(8,128)S(1)} %copy-done.6, ...), custom_call_target="tpu_custom_call" | custom-call | tf_op jit(solution)/shard_map/apply/pallas_call | solution.py:269
  (19 shorter events, 0.0 us)
Async XLA Ops:
  0.0 61.5 %copy-start = (bf16[8,256,256]{2,1,0:T(8,128)(2,1)S(1)}, bf16[8,256,256]{2,1,0:T(8,128)(2,1)}, u32[]{:S(2)}) copy-start(bf16[8,256,256]{2,1,0:T(8,128)(2,1)} %param.9) | copy-start | bytes 3145732
  6.8 1.9 %collective-permute-start = (f32[256,384]{1,0:T(8,128)}, f32[256,384]{1,0:T(8,128)S(1)}, u32[]{:S(2)}, u32[]{:S(2)}) collective-permute-start(f32[256,384]{1,0:T(8,128)} %get-tuple-element.11), channel_id=1, source_target_pairs={{0,1},{2,3},{4,5},{6,7},{8,9},{10,11},{12,13},{14,15},{1,0},{3,2},... | collective-permute-start | bytes 1179656 | tf_op jit(solution)/shard_map/ppermute | solution.py:185
  13.5 8.8 %copy-start.8 = (f32[256,256]{1,0:T(8,128)}, f32[256,256]{1,0:T(8,128)S(1)}, u32[]{:S(2)}) copy-start(f32[256,256]{1,0:T(8,128)S(1)} %slice.29.left_ref) | copy-start | bytes 786436
  13.5 12.7 %collective-permute-start.1 = (f32[256,256]{1,0:T(8,128)S(1)}, f32[256,256]{1,0:T(8,128)S(1)}, u32[]{:S(2)}, u32[]{:S(2)}) collective-permute-start(f32[256,256]{1,0:T(8,128)S(1)} %slice.29.left_ref), channel_id=1, source_target_pairs={{0,2},{4,6},{8,10},{12,14},{3,1},{7,5},{11,9},{15,13},{16,18},{20,... | collective-permute-start | bytes 786440 | tf_op jit(solution)/shard_map/ppermute | solution.py:190
  15.7 6.6 %copy-start.12 = (f32[256,128]{1,0:T(8,128)}, f32[256,128]{1,0:T(8,128)S(1)}, u32[]{:S(2)}) copy-start(f32[256,128]{1,0:T(8,128)S(1)} %slice.30.add_ref) | copy-start | bytes 393220
  15.7 6.6 %collective-permute-start.2 = (f32[256,128]{1,0:T(8,128)S(1)}, f32[256,128]{1,0:T(8,128)S(1)}, u32[]{:S(2)}, u32[]{:S(2)}) collective-permute-start(f32[256,128]{1,0:T(8,128)S(1)} %slice.30.add_ref), channel_id=1, source_target_pairs={{0,2},{4,6},{8,10},{12,14},{3,1},{7,5},{11,9},{15,13},{16,18},{20,... | collective-permute-start | bytes 393224 | tf_op jit(solution)/shard_map/ppermute | solution.py:189
  22.3 0.7 copy-start.11
  24.9 6.6 %collective-permute-start.3 = (f32[256,128]{1,0:T(8,128)}, f32[256,128]{1,0:T(8,128)S(1)}, u32[]{:S(2)}, u32[]{:S(2)}) collective-permute-start(f32[256,128]{1,0:T(8,128)} %wide.9.add_ref), channel_id=1, source_target_pairs={{2,6},{6,10},{10,14},{5,1},{9,5},{13,9},{18,22},{22,26},{26,30},{2... | collective-permute-start | bytes 393224 | tf_op jit(solution)/shard_map/ppermute | solution.py:174
  26.2 0.8 %copy-start.10 = (f32[256,256]{1,0:T(8,128)}, f32[256,256]{1,0:T(8,128)S(1)}, u32[]{:S(2)}) copy-start(f32[256,256]{1,0:T(8,128)S(1)} %collective-permute-done.1.right_ref.left_ref) | copy-start | bytes 786436
  31.5 0.7 copy-start.14
  34.1 15.9 %copy-start.9 = (f32[256,384]{1,0:T(8,128)S(1)}, f32[256,384]{1,0:T(8,128)}, u32[]{:S(2)}) copy-start(f32[256,384]{1,0:T(8,128)} %get-tuple-element.12.right_ref) | copy-start | bytes 1179652
  34.1 6.0 %collective-permute-start.4 = (f32[256,128]{1,0:T(8,128)}, f32[256,128]{1,0:T(8,128)S(1)}, u32[]{:S(2)}, u32[]{:S(2)}) collective-permute-start(f32[256,128]{1,0:T(8,128)} %wide.10), channel_id=1, source_target_pairs={{2,6},{6,10},{10,14},{5,1},{9,5},{13,9},{18,22},{22,26},{26,30},{2... | collective-permute-start | bytes 393224 | tf_op jit(solution)/shard_map/ppermute | solution.py:174
  40.2 0.7 copy-start.15
  42.8 5.9 %collective-permute-start.5 = (f32[256,128]{1,0:T(8,128)}, f32[256,128]{1,0:T(8,128)S(1)}, u32[]{:S(2)}, u32[]{:S(2)}) collective-permute-start(f32[256,128]{1,0:T(8,128)} %wide.11), channel_id=1, source_target_pairs={{2,6},{6,10},{10,14},{5,1},{9,5},{13,9},{18,22},{22,26},{26,30},{2... | collective-permute-start | bytes 393224 | tf_op jit(solution)/shard_map/ppermute | solution.py:174
  48.7 2.0 %copy-start.13 = (f32[256,128]{1,0:T(8,128)}, f32[256,128]{1,0:T(8,128)S(1)}, u32[]{:S(2)}) copy-start(f32[256,128]{1,0:T(8,128)S(1)} %collective-permute-done.5.right_ref) | copy-start | bytes 393220
  48.7 4.8 %collective-permute-start.6 = (f32[256,128]{1,0:T(8,128)S(1)}, f32[256,128]{1,0:T(8,128)S(1)}, u32[]{:S(2)}, u32[]{:S(2)}) collective-permute-start(f32[256,128]{1,0:T(8,128)S(1)} %collective-permute-done.5.right_ref), channel_id=1, source_target_pairs={{2,0},{6,4},{10,8},{14,12},{1,3},{5,7},{9,11},{13,15},{18,16},{22,... | collective-permute-start | bytes 393224 | tf_op jit(solution)/shard_map/ppermute | solution.py:216
  51.4 11.6 %copy-start.5 = (bf16[8,256,256]{2,1,0:T(8,128)(2,1)S(1)}, bf16[8,256,256]{2,1,0:T(8,128)(2,1)}, u32[]{:S(2)}) copy-start(bf16[8,256,256]{2,1,0:T(8,128)(2,1)} %urows_ref.1) | copy-start | bytes 3145732
  55.1 7.9 %copy-start.4 = (bf16[8,256,256]{2,1,0:T(8,128)(2,1)S(1)}, bf16[8,256,256]{2,1,0:T(8,128)(2,1)}, u32[]{:S(2)}) copy-start(bf16[8,256,256]{2,1,0:T(8,128)(2,1)} %lrows_ref.1) | copy-start | bytes 3145732
  57.1 5.9 %copy-start.1 = (bf16[8,256,256]{2,1,0:T(8,128)(2,1)S(1)}, bf16[8,256,256]{2,1,0:T(8,128)(2,1)}, u32[]{:S(2)}) copy-start(bf16[8,256,256]{2,1,0:T(8,128)(2,1)} %ltrans_ref.3) | copy-start | bytes 3145732
  57.1 5.9 %copy-start.2 = (bf16[8,256,256]{2,1,0:T(8,128)(2,1)S(1)}, bf16[8,256,256]{2,1,0:T(8,128)(2,1)}, u32[]{:S(2)}) copy-start(bf16[8,256,256]{2,1,0:T(8,128)(2,1)} %utrans_ref.3) | copy-start | bytes 3145732
  57.1 5.9 %copy-start.3 = (f32[256,128]{1,0:T(8,128)S(1)}, f32[256,128]{1,0:T(8,128)}, u32[]{:S(2)}) copy-start(f32[256,128]{1,0:T(8,128)} %broadcast_select_fusion.right_ref.enter_ref) | copy-start | bytes 393220
  57.1 5.9 %collective-permute-start.7 = (f32[256,128]{1,0:T(8,128)}, f32[256,128]{1,0:T(8,128)S(1)}, u32[]{:S(2)}, u32[]{:S(2)}) collective-permute-start(f32[256,128]{1,0:T(8,128)} %wide.13), channel_id=1, source_target_pairs={{0,1},{2,3},{4,5},{6,7},{8,9},{10,11},{12,13},{14,15},{1,0},{3,2},... | collective-permute-start | bytes 393224 | tf_op jit(solution)/shard_map/ppermute | solution.py:222
  63.1 1.2 %copy-start.6 = (f32[8,256,128]{2,1,0:T(8,128)S(1)}, f32[8,256,128]{2,1,0:T(8,128)}, u32[]{:S(2)}) copy-start(f32[8,256,128]{2,1,0:T(8,128)} %get-tuple-element.15.lsrc_ref) | copy-start | bytes 3145732
  64.3 1.2 %copy-start.7 = (f32[8,256,128]{2,1,0:T(8,128)S(1)}, f32[8,256,128]{2,1,0:T(8,128)}, u32[]{:S(2)}) copy-start(f32[8,256,128]{2,1,0:T(8,128)} %get-tuple-element.16.usrc_ref) | copy-start | bytes 3145732

commit v20 on v18

--- a/solution.py
+++ b/solution.py
@@ -19,9 +19,15 @@
     )
 
 
+def source_kernel(rhs_ref, lcols_ref, ucols_ref, lsrc_ref, usrc_ref):
+    for k in range(rhs_ref.shape[0]):
+        lsrc_ref[k] = lax.dot_general(lcols_ref[k], rhs_ref[k], (((0,), (0,)), ((), ())), preferred_element_type=F32)
+        usrc_ref[k] = lax.dot_general(ucols_ref[k], rhs_ref[k], (((0,), (0,)), ((), ())), preferred_element_type=F32)
+
+
 def sweep_kernel(
     flag_ref, rhs_ref, lcols_ref, ltrans_ref, ucols_ref, utrans_ref,
-    lmap_ref, lsrc_ref, umap_ref, usrc_ref,
+    lmap_ref, umap_ref,
 ):
     count = rhs_ref.shape[0]
     lmap = lstate = umap = ustate = None
@@ -30,8 +36,6 @@
         uk = count - 1 - step
         lsrc = lax.dot_general(lcols_ref[lk], rhs_ref[lk], (((0,), (0,)), ((), ())), preferred_element_type=F32)
         usrc = lax.dot_general(ucols_ref[uk], rhs_ref[uk], (((0,), (0,)), ((), ())), preferred_element_type=F32)
-        lsrc_ref[lk] = lsrc
-        usrc_ref[uk] = usrc
         ltrans = ltrans_ref[lk]
         utrans = utrans_ref[uk]
         if step == 0:
@@ -204,7 +208,7 @@
     return enter, other
 
 
-def shards(
+def shards_body(
     right_sides,
     diagonal_blocks,
     lower_rows,
@@ -222,17 +226,23 @@
         flag = jnp.full((1,), lax.axis_index("row") % 2, jnp.int32)
     else:
         flag = jnp.zeros((1,), jnp.int32)
-    lboth, lsrc, uboth, usrc = pl.pallas_call(
+    lboth, uboth = pl.pallas_call(
         sweep_kernel,
         out_shape=(
             jax.ShapeDtypeStruct((rank, rank + rhs), F32),
-            jax.ShapeDtypeStruct((count, rank, rhs), F32),
             jax.ShapeDtypeStruct((rank, rank + rhs), F32),
-            jax.ShapeDtypeStruct((count, rank, rhs), F32),
         ),
         in_specs=[pl.BlockSpec(memory_space=pltpu.SMEM)] + [pl.BlockSpec(memory_space=pltpu.VMEM)] * 5,
         name="sweep",
     )(flag, right_sides, lower_cols, lower_trans, upper_cols, upper_trans)
+    lsrc, usrc = pl.pallas_call(
+        source_kernel,
+        out_shape=(
+            jax.ShapeDtypeStruct((count, rank, rhs), F32),
+            jax.ShapeDtypeStruct((count, rank, rhs), F32),
+        ),
+        name="source",
+    )(right_sides, lower_cols, upper_cols)
     diag = jnp.einsum(
         "kab,kbc->kac", diagonal_blocks, right_sides, preferred_element_type=F32
     )
@@ -263,5 +273,5 @@
 def solution(mesh):
     spec = P(("sep", "row"), None, None)
     return jax.shard_map(
-        shards, mesh=mesh, in_specs=(spec,) * 8, out_specs=spec, check_vma=False
-    )
+        shards_body, mesh=mesh, in_specs=(spec,) * 8, out_specs=spec, check_vma=False
+    )

time: 52.3 us -> 60.1 us (1.15)
  local copies, waits for them, and re-layouts: 0.67 us -> 6.18 us
  Pallas kernels: 9.85 us -> 13.1 us
  matrix products: 7.1 us -> 5.24 us
  waiting for transfers between devices: 19.5 us -> 20.3 us
    unnamed x20, local copies, waits for them, and re-layouts: 0.63 us -> 6.14 us
    pallas_call x2 -> x3, Pallas kernels: 9.85 us -> 13.1 us  [the longest x1 6.06 us: shards_body(): pl.pallas_call(sweep_kernel, out_shape=(jax.ShapeDtypeStruct((rank, rank...]
    dot_general x1, matrix products: 1.51 us -> 0.38 us  [scan_groups(): mine = jnp.dot(beside_map, start, precision=HIGHEST) + beside_state]
    ppermute x1, waiting for transfers between devices: 0.71 us -> 1.53 us  [scan_groups(): sent = lax.ppermute(start, axis, back)]
    dot_general x2, matrix products: 1.41 us -> 0.75 us  [scan_groups(): out = jnp.dot(group_map, start, precision=HIGHEST) + group_state]
  transfers between devices with their start and end apart: 8 -> 8, of which waited for: 7 -> 7; matrix products, arithmetic and copies ran while one was open for 7% -> 4% of each run, Pallas kernels for 0% -> 7%
where the time goes in v20:
time: 60.1 us; the launch traced here: 59.6 us
  waiting for transfers between devices  20.3 us (34%)
  starting transfers between devices  14.6 us (24%)
  Pallas kernels  13.1 us (22%)
  local copies, waits for them, and re-layouts  6.18 us (10%)
  matrix products  5.24 us (9%)
    ppermute x3, waiting for transfers between devices, group_shift(): return lax.ppermute(value, axis, pairs)  12.4 us
    ppermute x1, starting transfers between devices, scan_groups(): other = lax.ppermute(send, axis, partner)  6.83 us
    unnamed x20, local copies, waits for them, and re-layouts  6.14 us
    pallas_call x1, Pallas kernels, shards_body(): pl.pallas_call(sweep_kernel, out_shape=(jax.ShapeDtypeStruct((rank, rank...  6.06 us
    pallas_call x1, Pallas kernels, shards_body(): pl.pallas_call(source_kernel, out_shape=(jax.ShapeDtypeStruct((count, ran...  3.93 us
    ppermute x3, starting transfers between devices, group_shift(): return lax.ppermute(value, axis, pairs)  3.88 us
    ppermute x1, waiting for transfers between devices, scan_groups(): beside_state = lax.ppermute(both[:, rank:], axis, pair)  3.35 us
    pallas_call x1, Pallas kernels, shards_body(): pl.pallas_call(apply_kernel, out_shape=jax.ShapeDtypeStruct((count, rows,...  3.09 us
  transfers between devices with their start and end apart: 8, of which 7 were waited for; matrix products, arithmetic and copies ran while one was open for 4% of the time, Pallas kernels for 7%

profile of v20, /device:TPU:1, one launch (start us, length us, event | category | flops | bytes accessed | tf_op | source)
XLA Modules:
  0.0 59.6 jit_solution(635647223440702331)
XLA Ops:
  0.0 0.0 copy-start
  0.0 6.1 %sweep.1 = (f32[256,384]{1,0:T(8,128)}, f32[256,384]{1,0:T(8,128)}) custom-call(s32[1]{0:T(128)} %bitcast.flag_ref, bf16[8,256,128]{2,1,0:T(8,128)(2,1)} %rhs_ref.3, bf16[8,256,256]{2,1,0:T(8,128)(2,1)} %lcols_ref.3, bf16[8,256,256]{2,1,0:T(8,128)(2,1)} %ltrans_ref.3, bf16[8,256,256]{2,1,0:T(8,128)(2,1)} %ucols_ref.3, bf16[8,256,256]{2,1,0:T(8,128)(2,1)} %utrans_ref.3), custom_call_target="tpu_custom_call" | custom-call | tf_op jit(solution)/shard_map/sweep/pallas_call | solution.py:229
  6.1 0.0 collective-permute-start
  6.1 1.9 %collective-permute-done = f32[256,384]{1,0:T(8,128)S(1)} collective-permute-done((f32[256,384]{1,0:T(8,128)}, f32[256,384]{1,0:T(8,128)S(1)}, u32[]{:S(2)}, u32[]{:S(2)}) %collective-permute-start) | collective-permute-done | bytes 393248 | tf_op jit(solution)/shard_map/ppermute | solution.py:168
  8.0 1.6 %convolution_add_fusion = f32[256,384]{1,0:T(8,128)S(1)} fusion(f32[256,384]{1,0:T(8,128)} %get-tuple-element.12, f32[256,128]{1,0:T(8,128)S(1)} %slice.28, f32[256,384]{1,0:T(8,128)S(1)} %collective-permute-done), kind=kOutput, calls=%fused_computation | convolution fusion | flops 302088192 | bytes 1179648 | tf_op jit(solution)/shard_map/dot_general | solution.py:169
  9.6 1.3 %collective-permute-start.2 = (f32[256,128]{1,0:T(8,128)S(1)}, f32[256,128]{1,0:T(8,128)S(1)}, u32[]{:S(2)}, u32[]{:S(2)}) collective-permute-start(f32[256,128]{1,0:T(8,128)S(1)} %slice.30), channel_id=1, source_target_pairs={{0,2},{4,6},{8,10},{12,14},{3,1},{7,5},{11,9},{15,13},{16,18},{20,... | collective-permute-start | bytes 393224 | tf_op jit(solution)/shard_map/ppermute | solution.py:174
  11.0 1.3 %collective-permute-start.1 = (f32[256,256]{1,0:T(8,128)S(1)}, f32[256,256]{1,0:T(8,128)S(1)}, u32[]{:S(2)}, u32[]{:S(2)}) collective-permute-start(f32[256,256]{1,0:T(8,128)S(1)} %slice.29), channel_id=1, source_target_pairs={{0,2},{4,6},{8,10},{12,14},{3,1},{7,5},{11,9},{15,13},{16,18},{20,... | collective-permute-start | bytes 786440 | tf_op jit(solution)/shard_map/ppermute | solution.py:175
  12.3 3.4 %collective-permute-done.2 = f32[256,128]{1,0:T(8,128)S(1)} collective-permute-done((f32[256,128]{1,0:T(8,128)S(1)}, f32[256,128]{1,0:T(8,128)S(1)}, u32[]{:S(2)}, u32[]{:S(2)}) %collective-permute-start.2) | collective-permute-done | bytes 131104 | tf_op jit(solution)/shard_map/ppermute | solution.py:174
  15.6 0.4 convolution_add_fusion.5
  16.0 1.3 %collective-permute-start.3 = (f32[256,128]{1,0:T(8,128)S(1)}, f32[256,128]{1,0:T(8,128)S(1)}, u32[]{:S(2)}, u32[]{:S(2)}) collective-permute-start(f32[256,128]{1,0:T(8,128)S(1)} %convolution_add_fusion.5), channel_id=1, source_target_pairs={{2,6},{6,10},{10,14},{5,1},{9,5},{13,9},{18,22},{22,26},{26,30},{2... | collective-permute-start | bytes 393224 | tf_op jit(solution)/shard_map/ppermute | solution.py:157
  17.3 1.1 %collective-permute-done.1 = f32[256,256]{1,0:T(8,128)S(1)} collective-permute-done((f32[256,256]{1,0:T(8,128)S(1)}, f32[256,256]{1,0:T(8,128)S(1)}, u32[]{:S(2)}, u32[]{:S(2)}) %collective-permute-start.1) | collective-permute-done | bytes 262176 | tf_op jit(solution)/shard_map/ppermute | solution.py:175
  18.4 0.4 fusion.3
  18.8 3.6 %collective-permute-done.3 = f32[256,128]{1,0:T(8,128)S(1)} collective-permute-done((f32[256,128]{1,0:T(8,128)S(1)}, f32[256,128]{1,0:T(8,128)S(1)}, u32[]{:S(2)}, u32[]{:S(2)}) %collective-permute-start.3) | collective-permute-done | bytes 131104 | tf_op jit(solution)/shard_map/ppermute | solution.py:157
  22.4 0.4 convolution_add_fusion.4
  22.8 1.3 %collective-permute-start.4 = (f32[256,128]{1,0:T(8,128)S(1)}, f32[256,128]{1,0:T(8,128)S(1)}, u32[]{:S(2)}, u32[]{:S(2)}) collective-permute-start(f32[256,128]{1,0:T(8,128)S(1)} %convolution_add_fusion.4), channel_id=1, source_target_pairs={{2,6},{6,10},{10,14},{5,1},{9,5},{13,9},{18,22},{22,26},{26,30},{2... | collective-permute-start | bytes 393224 | tf_op jit(solution)/shard_map/ppermute | solution.py:157
  24.1 4.4 %collective-permute-done.4 = f32[256,128]{1,0:T(8,128)S(1)} collective-permute-done((f32[256,128]{1,0:T(8,128)S(1)}, f32[256,128]{1,0:T(8,128)S(1)}, u32[]{:S(2)}, u32[]{:S(2)}) %collective-permute-start.4) | collective-permute-done | bytes 131104 | tf_op jit(solution)/shard_map/ppermute | solution.py:157
  28.5 0.4 convolution_add_fusion.3
  28.9 1.3 %collective-permute-start.5 = (f32[256,128]{1,0:T(8,128)S(1)}, f32[256,128]{1,0:T(8,128)S(1)}, u32[]{:S(2)}, u32[]{:S(2)}) collective-permute-start(f32[256,128]{1,0:T(8,128)S(1)} %convolution_add_fusion.3), channel_id=1, source_target_pairs={{2,6},{6,10},{10,14},{5,1},{9,5},{13,9},{18,22},{22,26},{26,30},{2... | collective-permute-start | bytes 393224 | tf_op jit(solution)/shard_map/ppermute | solution.py:157
  30.2 0.0 copy-start.9
  30.2 4.4 %collective-permute-done.5 = f32[256,128]{1,0:T(8,128)S(1)} collective-permute-done((f32[256,128]{1,0:T(8,128)S(1)}, f32[256,128]{1,0:T(8,128)S(1)}, u32[]{:S(2)}, u32[]{:S(2)}) %collective-permute-start.5) | collective-permute-done | bytes 131104 | tf_op jit(solution)/shard_map/ppermute | solution.py:157
  34.6 1.3 %collective-permute-start.6 = (f32[256,128]{1,0:T(8,128)S(1)}, f32[256,128]{1,0:T(8,128)S(1)}, u32[]{:S(2)}, u32[]{:S(2)}) collective-permute-start(f32[256,128]{1,0:T(8,128)S(1)} %collective-permute-done.5), channel_id=1, source_target_pairs={{2,0},{6,4},{10,8},{14,12},{1,3},{5,7},{9,11},{13,15},{18,16},{22,... | collective-permute-start | bytes 393224 | tf_op jit(solution)/shard_map/ppermute | solution.py:201
  35.9 0.4 convolution_add_fusion.2
  36.3 0.0 copy-start.8
  36.3 1.5 %collective-permute-done.6 = f32[256,128]{1,0:T(8,128)S(1)} collective-permute-done((f32[256,128]{1,0:T(8,128)S(1)}, f32[256,128]{1,0:T(8,128)S(1)}, u32[]{:S(2)}, u32[]{:S(2)}) %collective-permute-start.6) | collective-permute-done | bytes 131104 | tf_op jit(solution)/shard_map/ppermute | solution.py:201
  37.8 0.0 copy-done.9
  37.8 0.4 convolution_add_fusion.1
  38.2 6.8 %collective-permute-start.7 = (f32[256,128]{1,0:T(8,128)S(1)}, f32[256,128]{1,0:T(8,128)S(1)}, u32[]{:S(2)}, u32[]{:S(2)}) collective-permute-start(f32[256,128]{1,0:T(8,128)S(1)} %convolution_add_fusion.1), channel_id=1, source_target_pairs={{0,1},{2,3},{4,5},{6,7},{8,9},{10,11},{12,13},{14,15},{1,0},{3,2},... | collective-permute-start | bytes 393224 | tf_op jit(solution)/shard_map/ppermute | solution.py:207
  45.0 0.0 copy-done
  45.0 0.0 copy-done.8
  45.0 1.4 %fusion.5.diag_ref = f32[8,256,128]{2,1,0:T(8,128)} fusion(bf16[8,256,256]{2,1,0:T(8,128)(2,1)S(1)} %copy-done, bf16[8,256,128]{2,1,0:T(8,128)(2,1)S(1)} %copy-done.8), kind=kOutput, calls=%fused_computation.12 | convolution fusion | flops 134217728 | bytes 2621440 | tf_op jit(solution)/shard_map/kab,kbc->kac/dot_general | solution.py:246
  46.4 0.0 copy-start.1
  46.4 0.0 copy-start.2
  46.4 3.9 %source.1 = (f32[8,256,128]{2,1,0:T(8,128)}, f32[8,256,128]{2,1,0:T(8,128)}) custom-call(bf16[8,256,128]{2,1,0:T(8,128)(2,1)} %rhs_ref.3, bf16[8,256,256]{2,1,0:T(8,128)(2,1)} %lcols_ref.3, bf16[8,256,256]{2,1,0:T(8,128)(2,1)} %ucols_ref.3), custom_call_target="tpu_custom_call" | custom-call | tf_op jit(solution)/shard_map/source/pallas_call | solution.py:238
  50.4 0.0 collective-permute-done.7.other_ref
  50.4 0.0 copy-done.1
  50.4 0.0 copy-done.2
  50.4 0.0 copy-start.3
  50.4 1.2 %copy-done.3 = f32[8,256,128]{2,1,0:T(8,128)S(1)} copy-done((f32[8,256,128]{2,1,0:T(8,128)S(1)}, f32[8,256,128]{2,1,0:T(8,128)}, u32[]{:S(2)}) %copy-start.3) | copy-done | bytes 1048600
  51.6 0.0 copy-start.4
  51.6 1.2 %copy-done.4 = bf16[8,256,256]{2,1,0:T(8,128)(2,1)S(1)} copy-done((bf16[8,256,256]{2,1,0:T(8,128)(2,1)S(1)}, bf16[8,256,256]{2,1,0:T(8,128)(2,1)}, u32[]{:S(2)}) %copy-start.4) | copy-done | bytes 1048600
  52.8 0.0 copy-start.5
  52.8 1.2 %copy-done.5 = bf16[8,256,256]{2,1,0:T(8,128)(2,1)S(1)} copy-done((bf16[8,256,256]{2,1,0:T(8,128)(2,1)S(1)}, bf16[8,256,256]{2,1,0:T(8,128)(2,1)}, u32[]{:S(2)}) %copy-start.5) | copy-done | bytes 1048600
  54.1 0.0 copy-start.6
  54.1 1.2 %copy-done.6 = f32[8,256,128]{2,1,0:T(8,128)S(1)} copy-done((f32[8,256,128]{2,1,0:T(8,128)S(1)}, f32[8,256,128]{2,1,0:T(8,128)}, u32[]{:S(2)}) %copy-start.6) | copy-done | bytes 1048600
  55.3 0.0 copy-start.7
  55.3 1.2 %copy-done.7 = f32[8,256,128]{2,1,0:T(8,128)S(1)} copy-done((f32[8,256,128]{2,1,0:T(8,128)S(1)}, f32[8,256,128]{2,1,0:T(8,128)}, u32[]{:S(2)}) %copy-start.7) | copy-done | bytes 1048600
  56.5 3.1 %apply.1 = bf16[8,256,128]{2,1,0:T(8,128)(2,1)} custom-call(s32[1]{0:T(128)} %bitcast.flag_ref, f32[256,128]{1,0:T(8,128)S(1)} %broadcast_select_fusion.enter_ref, f32[256,128]{1,0:T(8,128)S(1)} %collective-permute-done.7.other_ref, bf16[8,256,256]{2,1,0:T(8,128)(2,1)S(1)} %copy-done.1, bf16[8,256,256]{2,1,0:T(8,128)(2,1)S(1)} %copy-done.2, ...), custom_call_target="tpu_custom_call" | custom-call | tf_op jit(solution)/shard_map/apply/pallas_call | solution.py:260
  (4 shorter events, 0.1 us)
Async XLA Ops:
  0.0 45.0 %copy-start = (bf16[8,256,256]{2,1,0:T(8,128)(2,1)S(1)}, bf16[8,256,256]{2,1,0:T(8,128)(2,1)}, u32[]{:S(2)}) copy-start(bf16[8,256,256]{2,1,0:T(8,128)(2,1)} %param.9) | copy-start | bytes 3145732
  6.1 1.9 %collective-permute-start = (f32[256,384]{1,0:T(8,128)}, f32[256,384]{1,0:T(8,128)S(1)}, u32[]{:S(2)}, u32[]{:S(2)}) collective-permute-start(f32[256,384]{1,0:T(8,128)} %get-tuple-element.11), channel_id=1, source_target_pairs={{0,1},{2,3},{4,5},{6,7},{8,9},{10,11},{12,13},{14,15},{1,0},{3,2},... | collective-permute-start | bytes 1179656 | tf_op jit(solution)/shard_map/ppermute | solution.py:168
  9.6 6.0 %collective-permute-start.2 = (f32[256,128]{1,0:T(8,128)S(1)}, f32[256,128]{1,0:T(8,128)S(1)}, u32[]{:S(2)}, u32[]{:S(2)}) collective-permute-start(f32[256,128]{1,0:T(8,128)S(1)} %slice.30), channel_id=1, source_target_pairs={{0,2},{4,6},{8,10},{12,14},{3,1},{7,5},{11,9},{15,13},{16,18},{20,... | collective-permute-start | bytes 393224 | tf_op jit(solution)/shard_map/ppermute | solution.py:174
  11.0 7.5 %collective-permute-start.1 = (f32[256,256]{1,0:T(8,128)S(1)}, f32[256,256]{1,0:T(8,128)S(1)}, u32[]{:S(2)}, u32[]{:S(2)}) collective-permute-start(f32[256,256]{1,0:T(8,128)S(1)} %slice.29), channel_id=1, source_target_pairs={{0,2},{4,6},{8,10},{12,14},{3,1},{7,5},{11,9},{15,13},{16,18},{20,... | collective-permute-start | bytes 786440 | tf_op jit(solution)/shard_map/ppermute | solution.py:175
  16.0 6.4 %collective-permute-start.3 = (f32[256,128]{1,0:T(8,128)S(1)}, f32[256,128]{1,0:T(8,128)S(1)}, u32[]{:S(2)}, u32[]{:S(2)}) collective-permute-start(f32[256,128]{1,0:T(8,128)S(1)} %convolution_add_fusion.5), channel_id=1, source_target_pairs={{2,6},{6,10},{10,14},{5,1},{9,5},{13,9},{18,22},{22,26},{26,30},{2... | collective-permute-start | bytes 393224 | tf_op jit(solution)/shard_map/ppermute | solution.py:157
  22.8 5.7 %collective-permute-start.4 = (f32[256,128]{1,0:T(8,128)S(1)}, f32[256,128]{1,0:T(8,128)S(1)}, u32[]{:S(2)}, u32[]{:S(2)}) collective-permute-start(f32[256,128]{1,0:T(8,128)S(1)} %convolution_add_fusion.4), channel_id=1, source_target_pairs={{2,6},{6,10},{10,14},{5,1},{9,5},{13,9},{18,22},{22,26},{26,30},{2... | collective-permute-start | bytes 393224 | tf_op jit(solution)/shard_map/ppermute | solution.py:157
  28.9 5.7 %collective-permute-start.5 = (f32[256,128]{1,0:T(8,128)S(1)}, f32[256,128]{1,0:T(8,128)S(1)}, u32[]{:S(2)}, u32[]{:S(2)}) collective-permute-start(f32[256,128]{1,0:T(8,128)S(1)} %convolution_add_fusion.3), channel_id=1, source_target_pairs={{2,6},{6,10},{10,14},{5,1},{9,5},{13,9},{18,22},{22,26},{26,30},{2... | collective-permute-start | bytes 393224 | tf_op jit(solution)/shard_map/ppermute | solution.py:157
  30.2 7.6 %copy-start.9 = (f32[256,384]{1,0:T(8,128)S(1)}, f32[256,384]{1,0:T(8,128)}, u32[]{:S(2)}) copy-start(f32[256,384]{1,0:T(8,128)} %get-tuple-element.12) | copy-start | bytes 1179652
  34.6 3.2 %collective-permute-start.6 = (f32[256,128]{1,0:T(8,128)S(1)}, f32[256,128]{1,0:T(8,128)S(1)}, u32[]{:S(2)}, u32[]{:S(2)}) collective-permute-start(f32[256,128]{1,0:T(8,128)S(1)} %collective-permute-done.5), channel_id=1, source_target_pairs={{2,0},{6,4},{10,8},{14,12},{1,3},{5,7},{9,11},{13,15},{18,16},{22,... | collective-permute-start | bytes 393224 | tf_op jit(solution)/shard_map/ppermute | solution.py:201
  36.3 8.8 %copy-start.8 = (bf16[8,256,128]{2,1,0:T(8,128)(2,1)S(1)}, bf16[8,256,128]{2,1,0:T(8,128)(2,1)}, u32[]{:S(2)}) copy-start(bf16[8,256,128]{2,1,0:T(8,128)(2,1)} %rhs_ref.3) | copy-start | bytes 1572868
  38.2 12.2 %collective-permute-start.7 = (f32[256,128]{1,0:T(8,128)S(1)}, f32[256,128]{1,0:T(8,128)S(1)}, u32[]{:S(2)}, u32[]{:S(2)}) collective-permute-start(f32[256,128]{1,0:T(8,128)S(1)} %convolution_add_fusion.1), channel_id=1, source_target_pairs={{0,1},{2,3},{4,5},{6,7},{8,9},{10,11},{12,13},{14,15},{1,0},{3,2},... | collective-permute-start | bytes 393224 | tf_op jit(solution)/shard_map/ppermute | solution.py:207
  46.4 3.9 %copy-start.1 = (bf16[8,256,256]{2,1,0:T(8,128)(2,1)S(1)}, bf16[8,256,256]{2,1,0:T(8,128)(2,1)}, u32[]{:S(2)}) copy-start(bf16[8,256,256]{2,1,0:T(8,128)(2,1)} %ltrans_ref.3) | copy-start | bytes 3145732
  46.4 3.9 %copy-start.2 = (bf16[8,256,256]{2,1,0:T(8,128)(2,1)S(1)}, bf16[8,256,256]{2,1,0:T(8,128)(2,1)}, u32[]{:S(2)}) copy-start(bf16[8,256,256]{2,1,0:T(8,128)(2,1)} %utrans_ref.3) | copy-start | bytes 3145732
  50.4 1.2 %copy-start.3 = (f32[8,256,128]{2,1,0:T(8,128)S(1)}, f32[8,256,128]{2,1,0:T(8,128)}, u32[]{:S(2)}) copy-start(f32[8,256,128]{2,1,0:T(8,128)} %fusion.5.diag_ref) | copy-start | bytes 3145732
  51.6 1.2 %copy-start.4 = (bf16[8,256,256]{2,1,0:T(8,128)(2,1)S(1)}, bf16[8,256,256]{2,1,0:T(8,128)(2,1)}, u32[]{:S(2)}) copy-start(bf16[8,256,256]{2,1,0:T(8,128)(2,1)} %lrows_ref.1) | copy-start | bytes 3145732
  52.8 1.2 %copy-start.5 = (bf16[8,256,256]{2,1,0:T(8,128)(2,1)S(1)}, bf16[8,256,256]{2,1,0:T(8,128)(2,1)}, u32[]{:S(2)}) copy-start(bf16[8,256,256]{2,1,0:T(8,128)(2,1)} %urows_ref.1) | copy-start | bytes 3145732
  54.1 1.2 %copy-start.6 = (f32[8,256,128]{2,1,0:T(8,128)S(1)}, f32[8,256,128]{2,1,0:T(8,128)}, u32[]{:S(2)}) copy-start(f32[8,256,128]{2,1,0:T(8,128)} %get-tuple-element.15.lsrc_ref) | copy-start | bytes 3145732
  55.3 1.2 %copy-start.7 = (f32[8,256,128]{2,1,0:T(8,128)S(1)}, f32[8,256,128]{2,1,0:T(8,128)}, u32[]{:S(2)}) copy-start(f32[8,256,128]{2,1,0:T(8,128)} %get-tuple-element.16.usrc_ref) | copy-start | bytes 3145732

commit v21 on v18

--- a/solution.py
+++ b/solution.py
@@ -21,7 +21,7 @@
 
 def sweep_kernel(
     flag_ref, rhs_ref, lcols_ref, ltrans_ref, ucols_ref, utrans_ref,
-    lmap_ref, lsrc_ref, umap_ref, usrc_ref,
+    lmap_ref, umap_ref,
 ):
     count = rhs_ref.shape[0]
     lmap = lstate = umap = ustate = None
@@ -30,8 +30,6 @@
         uk = count - 1 - step
         lsrc = lax.dot_general(lcols_ref[lk], rhs_ref[lk], (((0,), (0,)), ((), ())), preferred_element_type=F32)
         usrc = lax.dot_general(ucols_ref[uk], rhs_ref[uk], (((0,), (0,)), ((), ())), preferred_element_type=F32)
-        lsrc_ref[lk] = lsrc
-        usrc_ref[uk] = usrc
         ltrans = ltrans_ref[lk]
         utrans = utrans_ref[uk]
         if step == 0:
@@ -63,7 +61,7 @@
 
 
 def apply_kernel(
-    flag_ref, enter_ref, other_ref, ltrans_ref, utrans_ref, lsrc_ref, usrc_ref,
+    flag_ref, enter_ref, other_ref, ltrans_ref, utrans_ref, lcols_ref, ucols_ref, rhs_ref,
     diag_ref, lrows_ref, urows_ref, out_ref, lround_ref, uround_ref,
 ):
     count = ltrans_ref.shape[0]
@@ -76,8 +74,10 @@
         lround_ref[lk] = lstate.astype(BF16)
         uround_ref[uk] = ustate.astype(BF16)
         if step + 1 < count:
-            lstate = split_dot(ltrans_ref[lk], lstate) + lsrc_ref[lk]
-            ustate = split_dot(utrans_ref[uk], ustate) + usrc_ref[uk]
+            lsrc = lax.dot_general(lcols_ref[lk], rhs_ref[lk], (((0,), (0,)), ((), ())), preferred_element_type=F32)
+            usrc = lax.dot_general(ucols_ref[uk], rhs_ref[uk], (((0,), (0,)), ((), ())), preferred_element_type=F32)
+            lstate = split_dot(ltrans_ref[lk], lstate) + lsrc
+            ustate = split_dot(utrans_ref[uk], ustate) + usrc
     for k in range(count):
         total = diag_ref[k]
         total = total + jnp.dot(lrows_ref[k], lround_ref[k], preferred_element_type=F32)
@@ -222,13 +222,11 @@
         flag = jnp.full((1,), lax.axis_index("row") % 2, jnp.int32)
     else:
         flag = jnp.zeros((1,), jnp.int32)
-    lboth, lsrc, uboth, usrc = pl.pallas_call(
+    lboth, uboth = pl.pallas_call(
         sweep_kernel,
         out_shape=(
             jax.ShapeDtypeStruct((rank, rank + rhs), F32),
-            jax.ShapeDtypeStruct((count, rank, rhs), F32),
             jax.ShapeDtypeStruct((rank, rank + rhs), F32),
-            jax.ShapeDtypeStruct((count, rank, rhs), F32),
         ),
         in_specs=[pl.BlockSpec(memory_space=pltpu.SMEM)] + [pl.BlockSpec(memory_space=pltpu.VMEM)] * 5,
         name="sweep",
@@ -254,10 +252,10 @@
             pltpu.VMEM((count, rank, rhs), BF16),
             pltpu.VMEM((count, rank, rhs), BF16),
         ],
-        in_specs=[pl.BlockSpec(memory_space=pltpu.SMEM)] + [vmem] * 9,
+        in_specs=[pl.BlockSpec(memory_space=pltpu.SMEM)] + [vmem] * 10,
         compiler_params=pltpu.CompilerParams(vmem_limit_bytes=LIMIT),
         name="apply",
-    )(flag, enter, other, lower_trans, upper_trans, lsrc, usrc, diag, lower_rows, upper_rows)
+    )(flag, enter, other, lower_trans, upper_trans, lower_cols, upper_cols, right_sides, diag, lower_rows, upper_rows)
 
 
 def solution(mesh):

time: 52.3 us -> 52.6 us (level)
  local copies, waits for them, and re-layouts: 0.67 us -> 1.85 us
  matrix products: 7.1 us -> 6.05 us
  Pallas kernels: 9.85 us -> 9.19 us
  waiting for transfers between devices: 19.5 us -> 20.1 us
    unnamed x20 -> x22, local copies, waits for them, and re-layouts: 0.63 us -> 1.82 us
    dot_general x1, matrix products: 1.46 us -> 0.42 us  [shards(): jnp.einsum('kab,kbc->kac', diagonal_blocks, right_sides, preferred_elemen...]
    pallas_call x1, Pallas kernels: 6.79 us -> 6.06 us  [shards(): pl.pallas_call(sweep_kernel, out_shape=(jax.ShapeDtypeStruct((rank, rank...]
    ppermute x1, waiting for transfers between devices: 0.01 us -> 0.56 us  [scan_groups(): other = lax.ppermute(send, axis, partner)]
  transfers between devices with their start and end apart: 8 -> 8, of which waited for: 7 -> 8; matrix products, arithmetic and copies ran while one was open for 7% -> 5% of each run, Pallas kernels for 0% -> 0%
where the time goes in v21:
time: 52.6 us; the launch traced here: 51.8 us
  waiting for transfers between devices  20.1 us (38%)
  starting transfers between devices  14.5 us (28%)
  Pallas kernels  9.19 us (17%)
  matrix products  6.05 us (12%)
  local copies, waits for them, and re-layouts  1.85 us (4%)
    ppermute x3, waiting for transfers between devices, group_shift(): return lax.ppermute(value, axis, pairs)  12.7 us
    ppermute x1, starting transfers between devices, scan_groups(): other = lax.ppermute(send, axis, partner)  6.73 us
    pallas_call x1, Pallas kernels, shards(): pl.pallas_call(sweep_kernel, out_shape=(jax.ShapeDtypeStruct((rank, rank...  6.06 us
    ppermute x3, starting transfers between devices, group_shift(): return lax.ppermute(value, axis, pairs)  3.85 us
    ppermute x1, waiting for transfers between devices, scan_groups(): beside_state = lax.ppermute(both[:, rank:], axis, pair)  3.35 us
    pallas_call x1, Pallas kernels, shards(): pl.pallas_call(apply_kernel, out_shape=jax.ShapeDtypeStruct((count, rows,...  3.13 us
    ppermute x1, waiting for transfers between devices, scan_groups(): got = lax.ppermute(give, axis, partner)  1.93 us
    unnamed x22, local copies, waits for them, and re-layouts  1.82 us
  transfers between devices with their start and end apart: 8, of which 8 were waited for; matrix products, arithmetic and copies ran while one was open for 5% of the time, Pallas kernels for 0%

profile of v21, /device:TPU:1, one launch (start us, length us, event | category | flops | bytes accessed | tf_op | source)
XLA Modules:
  0.0 51.8 jit_solution(3525950689678439016)
XLA Ops:
  0.0 0.0 copy-start
  0.0 6.1 %sweep.1 = (f32[256,384]{1,0:T(8,128)}, f32[256,384]{1,0:T(8,128)}) custom-call(s32[1]{0:T(128)} %bitcast.flag_ref, bf16[8,256,128]{2,1,0:T(8,128)(2,1)} %rhs_ref.3, bf16[8,256,256]{2,1,0:T(8,128)(2,1)} %lcols_ref.3, bf16[8,256,256]{2,1,0:T(8,128)(2,1)} %ltrans_ref.3, bf16[8,256,256]{2,1,0:T(8,128)(2,1)} %ucols_ref.3, bf16[8,256,256]{2,1,0:T(8,128)(2,1)} %utrans_ref.3), custom_call_target="tpu_custom_call" | custom-call | tf_op jit(solution)/shard_map/sweep/pallas_call | solution.py:225
  6.1 0.0 collective-permute-start
  6.1 1.9 %collective-permute-done = f32[256,384]{1,0:T(8,128)S(1)} collective-permute-done((f32[256,384]{1,0:T(8,128)}, f32[256,384]{1,0:T(8,128)S(1)}, u32[]{:S(2)}, u32[]{:S(2)}) %collective-permute-start) | collective-permute-done | bytes 393248 | tf_op jit(solution)/shard_map/ppermute | solution.py:164
  8.0 1.6 %convolution_add_fusion = f32[256,384]{1,0:T(8,128)S(1)} fusion(f32[256,384]{1,0:T(8,128)} %get-tuple-element.10, f32[256,128]{1,0:T(8,128)S(1)} %slice.28, f32[256,384]{1,0:T(8,128)S(1)} %collective-permute-done), kind=kOutput, calls=%fused_computation | convolution fusion | flops 302088192 | bytes 1179648 | tf_op jit(solution)/shard_map/dot_general | solution.py:165
  9.6 1.3 %collective-permute-start.2 = (f32[256,128]{1,0:T(8,128)S(1)}, f32[256,128]{1,0:T(8,128)S(1)}, u32[]{:S(2)}, u32[]{:S(2)}) collective-permute-start(f32[256,128]{1,0:T(8,128)S(1)} %slice.30), channel_id=1, source_target_pairs={{0,2},{4,6},{8,10},{12,14},{3,1},{7,5},{11,9},{15,13},{16,18},{20,... | collective-permute-start | bytes 393224 | tf_op jit(solution)/shard_map/ppermute | solution.py:170
  11.0 1.3 %collective-permute-start.1 = (f32[256,256]{1,0:T(8,128)S(1)}, f32[256,256]{1,0:T(8,128)S(1)}, u32[]{:S(2)}, u32[]{:S(2)}) collective-permute-start(f32[256,256]{1,0:T(8,128)S(1)} %slice.29), channel_id=1, source_target_pairs={{0,2},{4,6},{8,10},{12,14},{3,1},{7,5},{11,9},{15,13},{16,18},{20,... | collective-permute-start | bytes 786440 | tf_op jit(solution)/shard_map/ppermute | solution.py:171
  12.3 3.4 %collective-permute-done.2 = f32[256,128]{1,0:T(8,128)S(1)} collective-permute-done((f32[256,128]{1,0:T(8,128)S(1)}, f32[256,128]{1,0:T(8,128)S(1)}, u32[]{:S(2)}, u32[]{:S(2)}) %collective-permute-start.2) | collective-permute-done | bytes 131104 | tf_op jit(solution)/shard_map/ppermute | solution.py:170
  15.6 0.0 copy-start.10
  15.6 0.0 copy-start.8
  15.6 0.4 convolution_add_fusion.5
  16.0 0.3 copy-done.10
  16.2 1.3 %collective-permute-start.3 = (f32[256,128]{1,0:T(8,128)S(1)}, f32[256,128]{1,0:T(8,128)S(1)}, u32[]{:S(2)}, u32[]{:S(2)}) collective-permute-start(f32[256,128]{1,0:T(8,128)S(1)} %convolution_add_fusion.5), channel_id=1, source_target_pairs={{2,6},{6,10},{10,14},{5,1},{9,5},{13,9},{18,22},{22,26},{26,30},{2... | collective-permute-start | bytes 393224 | tf_op jit(solution)/shard_map/ppermute | solution.py:153
  17.5 0.9 %collective-permute-done.1 = f32[256,256]{1,0:T(8,128)S(1)} collective-permute-done((f32[256,256]{1,0:T(8,128)S(1)}, f32[256,256]{1,0:T(8,128)S(1)}, u32[]{:S(2)}, u32[]{:S(2)}) %collective-permute-start.1) | collective-permute-done | bytes 262176 | tf_op jit(solution)/shard_map/ppermute | solution.py:171
  18.4 0.0 copy-start.9
  18.4 0.0 copy-start.6
  18.4 0.4 fusion.3
  18.8 0.3 copy-done.9
  19.1 3.5 %collective-permute-done.3 = f32[256,128]{1,0:T(8,128)S(1)} collective-permute-done((f32[256,128]{1,0:T(8,128)S(1)}, f32[256,128]{1,0:T(8,128)S(1)}, u32[]{:S(2)}, u32[]{:S(2)}) %collective-permute-start.3) | collective-permute-done | bytes 131104 | tf_op jit(solution)/shard_map/ppermute | solution.py:153
  22.6 0.0 copy-start.5
  22.6 0.4 convolution_add_fusion.4
  23.0 1.3 %collective-permute-start.4 = (f32[256,128]{1,0:T(8,128)S(1)}, f32[256,128]{1,0:T(8,128)S(1)}, u32[]{:S(2)}, u32[]{:S(2)}) collective-permute-start(f32[256,128]{1,0:T(8,128)S(1)} %convolution_add_fusion.4), channel_id=1, source_target_pairs={{2,6},{6,10},{10,14},{5,1},{9,5},{13,9},{18,22},{22,26},{26,30},{2... | collective-permute-start | bytes 393224 | tf_op jit(solution)/shard_map/ppermute | solution.py:153
  24.3 4.4 %collective-permute-done.4 = f32[256,128]{1,0:T(8,128)S(1)} collective-permute-done((f32[256,128]{1,0:T(8,128)S(1)}, f32[256,128]{1,0:T(8,128)S(1)}, u32[]{:S(2)}, u32[]{:S(2)}) %collective-permute-start.4) | collective-permute-done | bytes 131104 | tf_op jit(solution)/shard_map/ppermute | solution.py:153
  28.7 1.0 %convolution_add_fusion.3 = f32[256,128]{1,0:T(8,128)} fusion(f32[256,128]{1,0:T(8,128)S(1)} %convolution_add_fusion.5, f32[256,256]{1,0:T(8,128)S(1)} %fusion.3, f32[256,128]{1,0:T(8,128)S(1)} %collective-permute-done.4), kind=kOutput, calls=%fused_computation.3 | convolution fusion | flops 100696064 | bytes 655360 | tf_op jit(solution)/shard_map/dot_general | solution.py:181
  29.8 1.3 %collective-permute-start.5 = (f32[256,128]{1,0:T(8,128)}, f32[256,128]{1,0:T(8,128)}, u32[]{:S(2)}, u32[]{:S(2)}) collective-permute-start(f32[256,128]{1,0:T(8,128)} %convolution_add_fusion.3), channel_id=1, source_target_pairs={{2,6},{6,10},{10,14},{5,1},{9,5},{13,9},{18,22},{22,26},{26,30},{2... | collective-permute-start | bytes 393224 | tf_op jit(solution)/shard_map/ppermute | solution.py:153
  31.1 4.7 %collective-permute-done.5 = f32[256,128]{1,0:T(8,128)} collective-permute-done((f32[256,128]{1,0:T(8,128)}, f32[256,128]{1,0:T(8,128)}, u32[]{:S(2)}, u32[]{:S(2)}) %collective-permute-start.5) | collective-permute-done | bytes 131104 | tf_op jit(solution)/shard_map/ppermute | solution.py:153
  35.8 1.3 %collective-permute-start.6 = (f32[256,128]{1,0:T(8,128)}, f32[256,128]{1,0:T(8,128)S(1)}, u32[]{:S(2)}, u32[]{:S(2)}) collective-permute-start(f32[256,128]{1,0:T(8,128)} %collective-permute-done.5), channel_id=1, source_target_pairs={{2,0},{6,4},{10,8},{14,12},{1,3},{5,7},{9,11},{13,15},{18,16},{22,... | collective-permute-start | bytes 393224 | tf_op jit(solution)/shard_map/ppermute | solution.py:197
  37.1 0.0 copy-start.4
  37.1 1.5 %convolution_add_fusion.2 = f32[256,128]{1,0:T(8,128)S(1)} fusion(f32[256,128]{1,0:T(8,128)} %copy-done.10, f32[256,256]{1,0:T(8,128)} %copy-done.9, f32[256,128]{1,0:T(8,128)} %collective-permute-done.5), kind=kOutput, calls=%fused_computation.2 | convolution fusion | flops 100696064 | bytes 655360 | tf_op jit(solution)/shard_map/dot_general | solution.py:198
  38.6 0.0 copy-start.1
  38.6 0.7 %collective-permute-done.6 = f32[256,128]{1,0:T(8,128)S(1)} collective-permute-done((f32[256,128]{1,0:T(8,128)}, f32[256,128]{1,0:T(8,128)S(1)}, u32[]{:S(2)}, u32[]{:S(2)}) %collective-permute-start.6) | collective-permute-done | bytes 131104 | tf_op jit(solution)/shard_map/ppermute | solution.py:197
  39.3 0.0 copy-done.8
  39.3 0.4 convolution_add_fusion.1
  39.7 0.0 copy-start.2
  39.7 0.0 copy-start.3
  39.7 6.7 %collective-permute-start.7 = (f32[256,128]{1,0:T(8,128)S(1)}, f32[256,128]{1,0:T(8,128)S(1)}, u32[]{:S(2)}, u32[]{:S(2)}) collective-permute-start(f32[256,128]{1,0:T(8,128)S(1)} %convolution_add_fusion.1), channel_id=1, source_target_pairs={{0,1},{2,3},{4,5},{6,7},{8,9},{10,11},{12,13},{14,15},{1,0},{3,2},... | collective-permute-start | bytes 393224 | tf_op jit(solution)/shard_map/ppermute | solution.py:203
  46.5 0.0 copy-done
  46.5 0.0 copy-done.1
  46.5 0.4 fusion.5.diag_ref
  46.9 0.6 %collective-permute-done.7.other_ref = f32[256,128]{1,0:T(8,128)S(1)} collective-permute-done((f32[256,128]{1,0:T(8,128)S(1)}, f32[256,128]{1,0:T(8,128)S(1)}, u32[]{:S(2)}, u32[]{:S(2)}) %collective-permute-start.7) | collective-permute-done | bytes 131104 | tf_op jit(solution)/shard_map/ppermute | solution.py:203
  47.5 0.0 copy-done.6
  47.5 0.0 copy-done.5
  47.5 0.0 copy-done.4
  47.5 0.0 copy-done.2
  47.5 0.0 copy-done.3
  47.5 0.0 copy-start.7
  47.5 1.2 %copy-done.7 = bf16[8,256,256]{2,1,0:T(8,128)(2,1)S(1)} copy-done((bf16[8,256,256]{2,1,0:T(8,128)(2,1)S(1)}, bf16[8,256,256]{2,1,0:T(8,128)(2,1)}, u32[]{:S(2)}) %copy-start.7) | copy-done | bytes 1048600
  48.7 3.1 %apply.1 = bf16[8,256,128]{2,1,0:T(8,128)(2,1)} custom-call(s32[1]{0:T(128)} %bitcast.flag_ref, f32[256,128]{1,0:T(8,128)S(1)} %broadcast_select_fusion.enter_ref, f32[256,128]{1,0:T(8,128)S(1)} %collective-permute-done.7.other_ref, bf16[8,256,256]{2,1,0:T(8,128)(2,1)S(1)} %copy-done.3, bf16[8,256,256]{2,1,0:T(8,128)(2,1)S(1)} %copy-done.5, ...), custom_call_target="tpu_custom_call" | custom-call | tf_op jit(solution)/shard_map/apply/pallas_call | solution.py:248
  (4 shorter events, 0.1 us)
Async XLA Ops:
  0.0 46.5 %copy-start = (bf16[8,256,256]{2,1,0:T(8,128)(2,1)S(1)}, bf16[8,256,256]{2,1,0:T(8,128)(2,1)}, u32[]{:S(2)}) copy-start(bf16[8,256,256]{2,1,0:T(8,128)(2,1)} %param.9) | copy-start | bytes 3145732
  6.1 1.9 %collective-permute-start = (f32[256,384]{1,0:T(8,128)}, f32[256,384]{1,0:T(8,128)S(1)}, u32[]{:S(2)}, u32[]{:S(2)}) collective-permute-start(f32[256,384]{1,0:T(8,128)} %get-tuple-element.9), channel_id=1, source_target_pairs={{0,1},{2,3},{4,5},{6,7},{8,9},{10,11},{12,13},{14,15},{1,0},{3,2},... | collective-permute-start | bytes 1179656 | tf_op jit(solution)/shard_map/ppermute | solution.py:164
  9.6 6.0 %collective-permute-start.2 = (f32[256,128]{1,0:T(8,128)S(1)}, f32[256,128]{1,0:T(8,128)S(1)}, u32[]{:S(2)}, u32[]{:S(2)}) collective-permute-start(f32[256,128]{1,0:T(8,128)S(1)} %slice.30), channel_id=1, source_target_pairs={{0,2},{4,6},{8,10},{12,14},{3,1},{7,5},{11,9},{15,13},{16,18},{20,... | collective-permute-start | bytes 393224 | tf_op jit(solution)/shard_map/ppermute | solution.py:170
  11.0 7.5 %collective-permute-start.1 = (f32[256,256]{1,0:T(8,128)S(1)}, f32[256,256]{1,0:T(8,128)S(1)}, u32[]{:S(2)}, u32[]{:S(2)}) collective-permute-start(f32[256,256]{1,0:T(8,128)S(1)} %slice.29), channel_id=1, source_target_pairs={{0,2},{4,6},{8,10},{12,14},{3,1},{7,5},{11,9},{15,13},{16,18},{20,... | collective-permute-start | bytes 786440 | tf_op jit(solution)/shard_map/ppermute | solution.py:171
  15.6 0.6 %copy-start.10 = (f32[256,128]{1,0:T(8,128)}, f32[256,128]{1,0:T(8,128)S(1)}, u32[]{:S(2)}) copy-start(f32[256,128]{1,0:T(8,128)S(1)} %collective-permute-done.2) | copy-start | bytes 393220
  15.6 23.7 %copy-start.8 = (f32[256,384]{1,0:T(8,128)S(1)}, f32[256,384]{1,0:T(8,128)}, u32[]{:S(2)}) copy-start(f32[256,384]{1,0:T(8,128)} %get-tuple-element.10) | copy-start | bytes 1179652
  16.2 6.4 %collective-permute-start.3 = (f32[256,128]{1,0:T(8,128)S(1)}, f32[256,128]{1,0:T(8,128)S(1)}, u32[]{:S(2)}, u32[]{:S(2)}) collective-permute-start(f32[256,128]{1,0:T(8,128)S(1)} %convolution_add_fusion.5), channel_id=1, source_target_pairs={{2,6},{6,10},{10,14},{5,1},{9,5},{13,9},{18,22},{22,26},{26,30},{2... | collective-permute-start | bytes 393224 | tf_op jit(solution)/shard_map/ppermute | solution.py:153
  18.4 0.7 %copy-start.9 = (f32[256,256]{1,0:T(8,128)}, f32[256,256]{1,0:T(8,128)S(1)}, u32[]{:S(2)}) copy-start(f32[256,256]{1,0:T(8,128)S(1)} %collective-permute-done.1) | copy-start | bytes 786436
  18.4 29.0 %copy-start.6 = (bf16[8,256,256]{2,1,0:T(8,128)(2,1)S(1)}, bf16[8,256,256]{2,1,0:T(8,128)(2,1)}, u32[]{:S(2)}) copy-start(bf16[8,256,256]{2,1,0:T(8,128)(2,1)} %lrows_ref.1) | copy-start | bytes 3145732
  22.6 24.8 %copy-start.5 = (bf16[8,256,256]{2,1,0:T(8,128)(2,1)S(1)}, bf16[8,256,256]{2,1,0:T(8,128)(2,1)}, u32[]{:S(2)}) copy-start(bf16[8,256,256]{2,1,0:T(8,128)(2,1)} %utrans_ref.3) | copy-start | bytes 3145732
  23.0 5.7 %collective-permute-start.4 = (f32[256,128]{1,0:T(8,128)S(1)}, f32[256,128]{1,0:T(8,128)S(1)}, u32[]{:S(2)}, u32[]{:S(2)}) collective-permute-start(f32[256,128]{1,0:T(8,128)S(1)} %convolution_add_fusion.4), channel_id=1, source_target_pairs={{2,6},{6,10},{10,14},{5,1},{9,5},{13,9},{18,22},{22,26},{26,30},{2... | collective-permute-start | bytes 393224 | tf_op jit(solution)/shard_map/ppermute | solution.py:153
  29.8 6.0 %collective-permute-start.5 = (f32[256,128]{1,0:T(8,128)}, f32[256,128]{1,0:T(8,128)}, u32[]{:S(2)}, u32[]{:S(2)}) collective-permute-start(f32[256,128]{1,0:T(8,128)} %convolution_add_fusion.3), channel_id=1, source_target_pairs={{2,6},{6,10},{10,14},{5,1},{9,5},{13,9},{18,22},{22,26},{26,30},{2... | collective-permute-start | bytes 393224 | tf_op jit(solution)/shard_map/ppermute | solution.py:153
  35.8 3.5 %collective-permute-start.6 = (f32[256,128]{1,0:T(8,128)}, f32[256,128]{1,0:T(8,128)S(1)}, u32[]{:S(2)}, u32[]{:S(2)}) collective-permute-start(f32[256,128]{1,0:T(8,128)} %collective-permute-done.5), channel_id=1, source_target_pairs={{2,0},{6,4},{10,8},{14,12},{1,3},{5,7},{9,11},{13,15},{18,16},{22,... | collective-permute-start | bytes 393224 | tf_op jit(solution)/shard_map/ppermute | solution.py:197
  37.1 10.4 %copy-start.4 = (bf16[8,256,256]{2,1,0:T(8,128)(2,1)S(1)}, bf16[8,256,256]{2,1,0:T(8,128)(2,1)}, u32[]{:S(2)}) copy-start(bf16[8,256,256]{2,1,0:T(8,128)(2,1)} %ucols_ref.3) | copy-start | bytes 3145732
  38.6 7.9 %copy-start.1 = (bf16[8,256,128]{2,1,0:T(8,128)(2,1)S(1)}, bf16[8,256,128]{2,1,0:T(8,128)(2,1)}, u32[]{:S(2)}) copy-start(bf16[8,256,128]{2,1,0:T(8,128)(2,1)} %rhs_ref.3) | copy-start | bytes 1572868
  39.7 7.8 %copy-start.2 = (bf16[8,256,256]{2,1,0:T(8,128)(2,1)S(1)}, bf16[8,256,256]{2,1,0:T(8,128)(2,1)}, u32[]{:S(2)}) copy-start(bf16[8,256,256]{2,1,0:T(8,128)(2,1)} %lcols_ref.3) | copy-start | bytes 3145732
  39.7 7.7 %copy-start.3 = (bf16[8,256,256]{2,1,0:T(8,128)(2,1)S(1)}, bf16[8,256,256]{2,1,0:T(8,128)(2,1)}, u32[]{:S(2)}) copy-start(bf16[8,256,256]{2,1,0:T(8,128)(2,1)} %ltrans_ref.3) | copy-start | bytes 3145732
  39.7 7.7 %collective-permute-start.7 = (f32[256,128]{1,0:T(8,128)S(1)}, f32[256,128]{1,0:T(8,128)S(1)}, u32[]{:S(2)}, u32[]{:S(2)}) collective-permute-start(f32[256,128]{1,0:T(8,128)S(1)} %convolution_add_fusion.1), channel_id=1, source_target_pairs={{0,1},{2,3},{4,5},{6,7},{8,9},{10,11},{12,13},{14,15},{1,0},{3,2},... | collective-permute-start | bytes 393224 | tf_op jit(solution)/shard_map/ppermute | solution.py:203
  47.5 1.2 %copy-start.7 = (bf16[8,256,256]{2,1,0:T(8,128)(2,1)S(1)}, bf16[8,256,256]{2,1,0:T(8,128)(2,1)}, u32[]{:S(2)}) copy-start(bf16[8,256,256]{2,1,0:T(8,128)(2,1)} %urows_ref.1) | copy-start | bytes 3145732

commit v22 on v18

--- a/solution.py
+++ b/solution.py
@@ -162,15 +162,15 @@
     partner = [(2 * c, 2 * c + 1) for c in range(count // 2)]
     partner += [(2 * c + 1, 2 * c) for c in range(count // 2)]
     got = lax.ppermute(give, axis, partner)
-    both = jnp.dot(got[:, :rank], own, precision=HIGHEST) + jnp.concatenate(
+    both = jnp.dot(got[:, :rank], own, precision=lax.Precision.HIGH) + jnp.concatenate(
         [zeros, got[:, rank:]], axis=1
     )
     pair = [(4 * g, 4 * g + 2) for g in range(groups)]
     pair += [(4 * g + 3, 4 * g + 1) for g in range(groups)]
     beside_state = lax.ppermute(both[:, rank:], axis, pair)
     beside_map = lax.ppermute(both[:, :rank], axis, pair)
-    group_state = jnp.dot(both[:, :rank], beside_state, precision=HIGHEST) + both[:, rank:]
-    group_map = jnp.dot(both[:, :rank], beside_map, precision=HIGHEST)
+    group_state = jnp.dot(both[:, :rank], beside_state, precision=lax.Precision.HIGH) + both[:, rank:]
+    group_map = jnp.dot(both[:, :rank], beside_map, precision=lax.Precision.HIGH)
     beside = jnp.concatenate([beside_map, beside_state], axis=1)
     both = jnp.concatenate([group_map, group_state], axis=1)
     if groups <= 4:
@@ -178,7 +178,7 @@
         for step in range(groups - 1):
             start = group_shift(out, axis, groups, 1)
             if step + 2 < groups:
-                out = jnp.dot(group_map, start, precision=HIGHEST) + group_state
+                out = jnp.dot(group_map, start, precision=lax.Precision.HIGH) + group_state
     else:
         rounds = 0
         while 2 ** (rounds + 1) < groups - 1:
@@ -187,19 +187,19 @@
         for _ in range(rounds):
             got = group_shift(both, axis, groups, shift)
             tail = jnp.concatenate([zeros, both[:, rank:]], axis=1)
-            both = jnp.dot(both[:, :rank], got, precision=HIGHEST) + tail
+            both = jnp.dot(both[:, :rank], got, precision=lax.Precision.HIGH) + tail
             shift *= 2
         near = group_shift(both, axis, groups, 1)
         far = group_shift(both[:, rank:], axis, groups, 1 + shift)
-        start = jnp.dot(near[:, :rank], far, precision=HIGHEST) + near[:, rank:]
+        start = jnp.dot(near[:, :rank], far, precision=lax.Precision.HIGH) + near[:, rank:]
     back = [(4 * g + 2, 4 * g) for g in range(groups)]
     back += [(4 * g + 1, 4 * g + 3) for g in range(groups)]
     sent = lax.ppermute(start, axis, back)
-    mine = jnp.dot(beside_map, start, precision=HIGHEST) + beside_state
+    mine = jnp.dot(beside_map, start, precision=lax.Precision.HIGH) + beside_state
     mine, sent = lax.optimization_barrier((mine, sent))
     holder = jnp.logical_or(place == 1, place == 2)
     enter = jnp.where(holder, mine, sent)
-    send = jnp.dot(own[:, :rank], enter, precision=HIGHEST) + own[:, rank:]
+    send = jnp.dot(own[:, :rank], enter, precision=lax.Precision.HIGH) + own[:, rank:]
     other = lax.ppermute(send, axis, partner)
     return enter, other
 

time: 52.3 us -> 51.9 us (level)
  matrix products: 7.1 us -> 6.26 us
    dot_general x7, matrix products: 5.65 us -> 4.81 us  [the longest x1 1.41 us: scan_groups(): jnp.dot(beside_map, start, precision=lax.Precision.HIGH) + beside_state]
where the time goes in v22:
time: 51.9 us; the launch traced here: 51.4 us
  waiting for transfers between devices  19.6 us (38%)
  starting transfers between devices  14.6 us (28%)
  Pallas kernels  9.85 us (19%)
  matrix products  6.26 us (12%)
  local copies, waits for them, and re-layouts  0.88 us (2%)
    ppermute x3, waiting for transfers between devices, group_shift(): return lax.ppermute(value, axis, pairs)  12.6 us
    pallas_call x1, Pallas kernels, shards(): pl.pallas_call(sweep_kernel, out_shape=(jax.ShapeDtypeStruct((rank, rank...  6.79 us
    ppermute x1, starting transfers between devices, scan_groups(): other = lax.ppermute(send, axis, partner)  6.74 us
    ppermute x3, starting transfers between devices, group_shift(): return lax.ppermute(value, axis, pairs)  3.98 us
    ppermute x1, waiting for transfers between devices, scan_groups(): beside_state = lax.ppermute(both[:, rank:], axis, pair)  3.35 us
    pallas_call x1, Pallas kernels, shards(): pl.pallas_call(apply_kernel, out_shape=jax.ShapeDtypeStruct((count, rows,...  3.06 us
    ppermute x1, waiting for transfers between devices, scan_groups(): got = lax.ppermute(give, axis, partner)  1.93 us
    dot_general x1, matrix products, shards(): jnp.einsum('kab,kbc->kac', diagonal_blocks, right_sides, preferred_elemen...  1.46 us
  transfers between devices with their start and end apart: 8, of which 7 were waited for; matrix products, arithmetic and copies ran while one was open for 7% of the time, Pallas kernels for 0%

profile of v22, /device:TPU:1, one launch (start us, length us, event | category | flops | bytes accessed | tf_op | source)
XLA Modules:
  0.0 51.4 jit_solution(3211431356696877581)
XLA Ops:
  0.0 0.0 copy-start
  0.0 6.8 %sweep.1 = (f32[256,384]{1,0:T(8,128)}, f32[8,256,128]{2,1,0:T(8,128)}, f32[256,384]{1,0:T(8,128)}, f32[8,256,128]{2,1,0:T(8,128)}) custom-call(s32[1]{0:T(128)} %bitcast.flag_ref, bf16[8,256,128]{2,1,0:T(8,128)(2,1)} %rhs_ref.1, bf16[8,256,256]{2,1,0:T(8,128)(2,1)} %lcols_ref.1, bf16[8,256,256]{2,1,0:T(8,128)(2,1)} %ltrans_ref.3, ...), custom_call_target="tpu_custom_call" | custom-call | tf_op jit(solution)/shard_map/sweep/pallas_call | solution.py:225
  6.8 0.0 collective-permute-start
  6.8 1.9 %collective-permute-done = f32[256,384]{1,0:T(8,128)S(1)} collective-permute-done((f32[256,384]{1,0:T(8,128)}, f32[256,384]{1,0:T(8,128)S(1)}, u32[]{:S(2)}, u32[]{:S(2)}) %collective-permute-start) | collective-permute-done | bytes 393248 | tf_op jit(solution)/shard_map/ppermute | solution.py:164
  8.7 1.4 %convolution_add_fusion = f32[256,384]{1,0:T(8,128)S(1)} fusion(f32[256,384]{1,0:T(8,128)} %get-tuple-element.12, f32[256,128]{1,0:T(8,128)S(1)} %slice.28, f32[256,384]{1,0:T(8,128)S(1)} %collective-permute-done), kind=kOutput, calls=%fused_computation | convolution fusion | flops 151093248 | bytes 1179648 | tf_op jit(solution)/shard_map/dot_general | solution.py:165
  10.1 1.3 %collective-permute-start.2 = (f32[256,128]{1,0:T(8,128)S(1)}, f32[256,128]{1,0:T(8,128)S(1)}, u32[]{:S(2)}, u32[]{:S(2)}) collective-permute-start(f32[256,128]{1,0:T(8,128)S(1)} %slice.30), channel_id=1, source_target_pairs={{0,2},{4,6},{8,10},{12,14},{3,1},{7,5},{11,9},{15,13},{16,18},{20,... | collective-permute-start | bytes 393224 | tf_op jit(solution)/shard_map/ppermute | solution.py:170
  11.5 1.3 %collective-permute-start.1 = (f32[256,256]{1,0:T(8,128)S(1)}, f32[256,256]{1,0:T(8,128)S(1)}, u32[]{:S(2)}, u32[]{:S(2)}) collective-permute-start(f32[256,256]{1,0:T(8,128)S(1)} %slice.29), channel_id=1, source_target_pairs={{0,2},{4,6},{8,10},{12,14},{3,1},{7,5},{11,9},{15,13},{16,18},{20,... | collective-permute-start | bytes 786440 | tf_op jit(solution)/shard_map/ppermute | solution.py:171
  12.8 3.4 %collective-permute-done.2 = f32[256,128]{1,0:T(8,128)S(1)} collective-permute-done((f32[256,128]{1,0:T(8,128)S(1)}, f32[256,128]{1,0:T(8,128)S(1)}, u32[]{:S(2)}, u32[]{:S(2)}) %collective-permute-start.2) | collective-permute-done | bytes 131104 | tf_op jit(solution)/shard_map/ppermute | solution.py:170
  16.1 0.0 copy-start.9
  16.1 0.0 copy-start.7
  16.1 0.3 convolution_add_fusion.5
  16.4 0.4 copy-done.9
  16.8 1.3 %collective-permute-start.3 = (f32[256,128]{1,0:T(8,128)S(1)}, f32[256,128]{1,0:T(8,128)S(1)}, u32[]{:S(2)}, u32[]{:S(2)}) collective-permute-start(f32[256,128]{1,0:T(8,128)S(1)} %convolution_add_fusion.5), channel_id=1, source_target_pairs={{2,6},{6,10},{10,14},{5,1},{9,5},{13,9},{18,22},{22,26},{26,30},{2... | collective-permute-start | bytes 393224 | tf_op jit(solution)/shard_map/ppermute | solution.py:153
  18.1 0.9 %collective-permute-done.1 = f32[256,256]{1,0:T(8,128)S(1)} collective-permute-done((f32[256,256]{1,0:T(8,128)S(1)}, f32[256,256]{1,0:T(8,128)S(1)}, u32[]{:S(2)}, u32[]{:S(2)}) %collective-permute-start.1) | collective-permute-done | bytes 262176 | tf_op jit(solution)/shard_map/ppermute | solution.py:171
  18.9 0.0 copy-start.8
  18.9 0.0 copy-start.6
  18.9 0.3 fusion.3
  19.2 0.4 copy-done.8
  19.6 3.5 %collective-permute-done.3 = f32[256,128]{1,0:T(8,128)S(1)} collective-permute-done((f32[256,128]{1,0:T(8,128)S(1)}, f32[256,128]{1,0:T(8,128)S(1)}, u32[]{:S(2)}, u32[]{:S(2)}) %collective-permute-start.3) | collective-permute-done | bytes 131104 | tf_op jit(solution)/shard_map/ppermute | solution.py:153
  23.2 0.0 copy-start.5
  23.2 0.3 convolution_add_fusion.4
  23.4 1.4 %collective-permute-start.4 = (f32[256,128]{1,0:T(8,128)S(1)}, f32[256,128]{1,0:T(8,128)S(1)}, u32[]{:S(2)}, u32[]{:S(2)}) collective-permute-start(f32[256,128]{1,0:T(8,128)S(1)} %convolution_add_fusion.4), channel_id=1, source_target_pairs={{2,6},{6,10},{10,14},{5,1},{9,5},{13,9},{18,22},{22,26},{26,30},{2... | collective-permute-start | bytes 393224 | tf_op jit(solution)/shard_map/ppermute | solution.py:153
  24.9 4.4 %collective-permute-done.4 = f32[256,128]{1,0:T(8,128)S(1)} collective-permute-done((f32[256,128]{1,0:T(8,128)S(1)}, f32[256,128]{1,0:T(8,128)S(1)}, u32[]{:S(2)}, u32[]{:S(2)}) %collective-permute-start.4) | collective-permute-done | bytes 131104 | tf_op jit(solution)/shard_map/ppermute | solution.py:153
  29.3 0.9 %convolution_add_fusion.3 = f32[256,128]{1,0:T(8,128)} fusion(f32[256,128]{1,0:T(8,128)S(1)} %convolution_add_fusion.5, f32[256,256]{1,0:T(8,128)S(1)} %fusion.3, f32[256,128]{1,0:T(8,128)S(1)} %collective-permute-done.4), kind=kOutput, calls=%fused_computation.3 | convolution fusion | flops 50364416 | bytes 655360 | tf_op jit(solution)/shard_map/dot_general | solution.py:181
  30.2 1.3 %collective-permute-start.5 = (f32[256,128]{1,0:T(8,128)}, f32[256,128]{1,0:T(8,128)}, u32[]{:S(2)}, u32[]{:S(2)}) collective-permute-start(f32[256,128]{1,0:T(8,128)} %convolution_add_fusion.3), channel_id=1, source_target_pairs={{2,6},{6,10},{10,14},{5,1},{9,5},{13,9},{18,22},{22,26},{26,30},{2... | collective-permute-start | bytes 393224 | tf_op jit(solution)/shard_map/ppermute | solution.py:153
  31.5 4.7 %collective-permute-done.5 = f32[256,128]{1,0:T(8,128)} collective-permute-done((f32[256,128]{1,0:T(8,128)}, f32[256,128]{1,0:T(8,128)}, u32[]{:S(2)}, u32[]{:S(2)}) %collective-permute-start.5) | collective-permute-done | bytes 131104 | tf_op jit(solution)/shard_map/ppermute | solution.py:153
  36.2 1.3 %collective-permute-start.6 = (f32[256,128]{1,0:T(8,128)}, f32[256,128]{1,0:T(8,128)S(1)}, u32[]{:S(2)}, u32[]{:S(2)}) collective-permute-start(f32[256,128]{1,0:T(8,128)} %collective-permute-done.5), channel_id=1, source_target_pairs={{2,0},{6,4},{10,8},{14,12},{1,3},{5,7},{9,11},{13,15},{18,16},{22,... | collective-permute-start | bytes 393224 | tf_op jit(solution)/shard_map/ppermute | solution.py:197
  37.5 0.0 copy-start.4
  37.5 1.4 %convolution_add_fusion.2 = f32[256,128]{1,0:T(8,128)S(1)} fusion(f32[256,128]{1,0:T(8,128)} %copy-done.9, f32[256,256]{1,0:T(8,128)} %copy-done.8, f32[256,128]{1,0:T(8,128)} %collective-permute-done.5), kind=kOutput, calls=%fused_computation.2 | convolution fusion | flops 50364416 | bytes 655360 | tf_op jit(solution)/shard_map/dot_general | solution.py:198
  39.0 0.8 %collective-permute-done.6 = f32[256,128]{1,0:T(8,128)S(1)} collective-permute-done((f32[256,128]{1,0:T(8,128)}, f32[256,128]{1,0:T(8,128)S(1)}, u32[]{:S(2)}, u32[]{:S(2)}) %collective-permute-start.6) | collective-permute-done | bytes 131104 | tf_op jit(solution)/shard_map/ppermute | solution.py:197
  39.8 0.0 copy-done.7
  39.8 0.0 copy-start.3
  39.8 0.3 convolution_add_fusion.1
  40.1 0.0 copy-start.1
  40.1 0.0 copy-start.2
  40.1 6.7 %collective-permute-start.7 = (f32[256,128]{1,0:T(8,128)S(1)}, f32[256,128]{1,0:T(8,128)S(1)}, u32[]{:S(2)}, u32[]{:S(2)}) collective-permute-start(f32[256,128]{1,0:T(8,128)S(1)} %convolution_add_fusion.1), channel_id=1, source_target_pairs={{0,1},{2,3},{4,5},{6,7},{8,9},{10,11},{12,13},{14,15},{1,0},{3,2},... | collective-permute-start | bytes 393224 | tf_op jit(solution)/shard_map/ppermute | solution.py:203
  46.9 0.0 copy-done
  46.9 1.5 %fusion.5.diag_ref = f32[8,256,128]{2,1,0:T(8,128)S(1)} fusion(bf16[8,256,256]{2,1,0:T(8,128)(2,1)S(1)} %copy-done, bf16[8,256,128]{2,1,0:T(8,128)(2,1)} %rhs_ref.1), kind=kOutput, calls=%fused_computation.12 | convolution fusion | flops 134217728 | bytes 2621440 | tf_op jit(solution)/shard_map/kab,kbc->kac/dot_general | solution.py:236
  48.3 0.0 collective-permute-done.7.other_ref
  48.3 0.0 copy-done.6
  48.3 0.0 copy-done.5
  48.3 0.0 copy-done.4
  48.4 0.0 copy-done.3
  48.4 0.0 copy-done.1
  48.4 0.0 copy-done.2
  48.4 3.1 %apply.1 = bf16[8,256,128]{2,1,0:T(8,128)(2,1)} custom-call(s32[1]{0:T(128)} %bitcast.flag_ref, f32[256,128]{1,0:T(8,128)S(1)} %broadcast_select_fusion.enter_ref, f32[256,128]{1,0:T(8,128)S(1)} %collective-permute-done.7.other_ref, bf16[8,256,256]{2,1,0:T(8,128)(2,1)S(1)} %copy-done.1, bf16[8,256,256]{2,1,0:T(8,128)(2,1)S(1)} %copy-done.2, ...), custom_call_target="tpu_custom_call" | custom-call | tf_op jit(solution)/shard_map/apply/pallas_call | solution.py:250
  (4 shorter events, 0.1 us)
Async XLA Ops:
  0.0 46.9 %copy-start = (bf16[8,256,256]{2,1,0:T(8,128)(2,1)S(1)}, bf16[8,256,256]{2,1,0:T(8,128)(2,1)}, u32[]{:S(2)}) copy-start(bf16[8,256,256]{2,1,0:T(8,128)(2,1)} %param.9) | copy-start | bytes 3145732
  6.8 1.9 %collective-permute-start = (f32[256,384]{1,0:T(8,128)}, f32[256,384]{1,0:T(8,128)S(1)}, u32[]{:S(2)}, u32[]{:S(2)}) collective-permute-start(f32[256,384]{1,0:T(8,128)} %get-tuple-element.11), channel_id=1, source_target_pairs={{0,1},{2,3},{4,5},{6,7},{8,9},{10,11},{12,13},{14,15},{1,0},{3,2},... | collective-permute-start | bytes 1179656 | tf_op jit(solution)/shard_map/ppermute | solution.py:164
  10.1 6.0 %collective-permute-start.2 = (f32[256,128]{1,0:T(8,128)S(1)}, f32[256,128]{1,0:T(8,128)S(1)}, u32[]{:S(2)}, u32[]{:S(2)}) collective-permute-start(f32[256,128]{1,0:T(8,128)S(1)} %slice.30), channel_id=1, source_target_pairs={{0,2},{4,6},{8,10},{12,14},{3,1},{7,5},{11,9},{15,13},{16,18},{20,... | collective-permute-start | bytes 393224 | tf_op jit(solution)/shard_map/ppermute | solution.py:170
  11.5 7.5 %collective-permute-start.1 = (f32[256,256]{1,0:T(8,128)S(1)}, f32[256,256]{1,0:T(8,128)S(1)}, u32[]{:S(2)}, u32[]{:S(2)}) collective-permute-start(f32[256,256]{1,0:T(8,128)S(1)} %slice.29), channel_id=1, source_target_pairs={{0,2},{4,6},{8,10},{12,14},{3,1},{7,5},{11,9},{15,13},{16,18},{20,... | collective-permute-start | bytes 786440 | tf_op jit(solution)/shard_map/ppermute | solution.py:171
  16.1 0.7 %copy-start.9 = (f32[256,128]{1,0:T(8,128)}, f32[256,128]{1,0:T(8,128)S(1)}, u32[]{:S(2)}) copy-start(f32[256,128]{1,0:T(8,128)S(1)} %collective-permute-done.2) | copy-start | bytes 393220
  16.1 23.7 %copy-start.7 = (f32[256,384]{1,0:T(8,128)S(1)}, f32[256,384]{1,0:T(8,128)}, u32[]{:S(2)}) copy-start(f32[256,384]{1,0:T(8,128)} %get-tuple-element.12) | copy-start | bytes 1179652
  16.8 6.4 %collective-permute-start.3 = (f32[256,128]{1,0:T(8,128)S(1)}, f32[256,128]{1,0:T(8,128)S(1)}, u32[]{:S(2)}, u32[]{:S(2)}) collective-permute-start(f32[256,128]{1,0:T(8,128)S(1)} %convolution_add_fusion.5), channel_id=1, source_target_pairs={{2,6},{6,10},{10,14},{5,1},{9,5},{13,9},{18,22},{22,26},{26,30},{2... | collective-permute-start | bytes 393224 | tf_op jit(solution)/shard_map/ppermute | solution.py:153
  18.9 0.7 %copy-start.8 = (f32[256,256]{1,0:T(8,128)}, f32[256,256]{1,0:T(8,128)S(1)}, u32[]{:S(2)}) copy-start(f32[256,256]{1,0:T(8,128)S(1)} %collective-permute-done.1) | copy-start | bytes 786436
  18.9 29.4 %copy-start.6 = (f32[8,256,128]{2,1,0:T(8,128)S(1)}, f32[8,256,128]{2,1,0:T(8,128)}, u32[]{:S(2)}) copy-start(f32[8,256,128]{2,1,0:T(8,128)} %get-tuple-element.16.usrc_ref) | copy-start | bytes 3145732
  23.2 25.2 %copy-start.5 = (f32[8,256,128]{2,1,0:T(8,128)S(1)}, f32[8,256,128]{2,1,0:T(8,128)}, u32[]{:S(2)}) copy-start(f32[8,256,128]{2,1,0:T(8,128)} %get-tuple-element.15.lsrc_ref) | copy-start | bytes 3145732
  23.4 5.8 %collective-permute-start.4 = (f32[256,128]{1,0:T(8,128)S(1)}, f32[256,128]{1,0:T(8,128)S(1)}, u32[]{:S(2)}, u32[]{:S(2)}) collective-permute-start(f32[256,128]{1,0:T(8,128)S(1)} %convolution_add_fusion.4), channel_id=1, source_target_pairs={{2,6},{6,10},{10,14},{5,1},{9,5},{13,9},{18,22},{22,26},{26,30},{2... | collective-permute-start | bytes 393224 | tf_op jit(solution)/shard_map/ppermute | solution.py:153
  30.2 6.0 %collective-permute-start.5 = (f32[256,128]{1,0:T(8,128)}, f32[256,128]{1,0:T(8,128)}, u32[]{:S(2)}, u32[]{:S(2)}) collective-permute-start(f32[256,128]{1,0:T(8,128)} %convolution_add_fusion.3), channel_id=1, source_target_pairs={{2,6},{6,10},{10,14},{5,1},{9,5},{13,9},{18,22},{22,26},{26,30},{2... | collective-permute-start | bytes 393224 | tf_op jit(solution)/shard_map/ppermute | solution.py:153
  36.2 3.5 %collective-permute-start.6 = (f32[256,128]{1,0:T(8,128)}, f32[256,128]{1,0:T(8,128)S(1)}, u32[]{:S(2)}, u32[]{:S(2)}) collective-permute-start(f32[256,128]{1,0:T(8,128)} %collective-permute-done.5), channel_id=1, source_target_pairs={{2,0},{6,4},{10,8},{14,12},{1,3},{5,7},{9,11},{13,15},{18,16},{22,... | collective-permute-start | bytes 393224 | tf_op jit(solution)/shard_map/ppermute | solution.py:197
  37.5 10.8 %copy-start.4 = (bf16[8,256,256]{2,1,0:T(8,128)(2,1)S(1)}, bf16[8,256,256]{2,1,0:T(8,128)(2,1)}, u32[]{:S(2)}) copy-start(bf16[8,256,256]{2,1,0:T(8,128)(2,1)} %urows_ref.1) | copy-start | bytes 3145732
  39.8 8.6 %copy-start.3 = (bf16[8,256,256]{2,1,0:T(8,128)(2,1)S(1)}, bf16[8,256,256]{2,1,0:T(8,128)(2,1)}, u32[]{:S(2)}) copy-start(bf16[8,256,256]{2,1,0:T(8,128)(2,1)} %lrows_ref.1) | copy-start | bytes 3145732
  40.1 8.3 %copy-start.1 = (bf16[8,256,256]{2,1,0:T(8,128)(2,1)S(1)}, bf16[8,256,256]{2,1,0:T(8,128)(2,1)}, u32[]{:S(2)}) copy-start(bf16[8,256,256]{2,1,0:T(8,128)(2,1)} %ltrans_ref.3) | copy-start | bytes 3145732
  40.1 8.3 %copy-start.2 = (bf16[8,256,256]{2,1,0:T(8,128)(2,1)S(1)}, bf16[8,256,256]{2,1,0:T(8,128)(2,1)}, u32[]{:S(2)}) copy-start(bf16[8,256,256]{2,1,0:T(8,128)(2,1)} %utrans_ref.3) | copy-start | bytes 3145732
  40.1 8.2 %collective-permute-start.7 = (f32[256,128]{1,0:T(8,128)S(1)}, f32[256,128]{1,0:T(8,128)S(1)}, u32[]{:S(2)}, u32[]{:S(2)}) collective-permute-start(f32[256,128]{1,0:T(8,128)S(1)} %convolution_add_fusion.1), channel_id=1, source_target_pairs={{0,1},{2,3},{4,5},{6,7},{8,9},{10,11},{12,13},{14,15},{1,0},{3,2},... | collective-permute-start | bytes 393224 | tf_op jit(solution)/shard_map/ppermute | solution.py:203

commit v23 on v21

--- a/solution.py
+++ b/solution.py
@@ -162,15 +162,15 @@
     partner = [(2 * c, 2 * c + 1) for c in range(count // 2)]
     partner += [(2 * c + 1, 2 * c) for c in range(count // 2)]
     got = lax.ppermute(give, axis, partner)
-    both = jnp.dot(got[:, :rank], own, precision=HIGHEST) + jnp.concatenate(
+    both = jnp.dot(got[:, :rank], own, precision=lax.Precision.HIGH) + jnp.concatenate(
         [zeros, got[:, rank:]], axis=1
     )
     pair = [(4 * g, 4 * g + 2) for g in range(groups)]
     pair += [(4 * g + 3, 4 * g + 1) for g in range(groups)]
     beside_state = lax.ppermute(both[:, rank:], axis, pair)
     beside_map = lax.ppermute(both[:, :rank], axis, pair)
-    group_state = jnp.dot(both[:, :rank], beside_state, precision=HIGHEST) + both[:, rank:]
-    group_map = jnp.dot(both[:, :rank], beside_map, precision=HIGHEST)
+    group_state = jnp.dot(both[:, :rank], beside_state, precision=lax.Precision.HIGH) + both[:, rank:]
+    group_map = jnp.dot(both[:, :rank], beside_map, precision=lax.Precision.HIGH)
     beside = jnp.concatenate([beside_map, beside_state], axis=1)
     both = jnp.concatenate([group_map, group_state], axis=1)
     if groups <= 4:
@@ -178,7 +178,7 @@
         for step in range(groups - 1):
             start = group_shift(out, axis, groups, 1)
             if step + 2 < groups:
-                out = jnp.dot(group_map, start, precision=HIGHEST) + group_state
+                out = jnp.dot(group_map, start, precision=lax.Precision.HIGH) + group_state
     else:
         rounds = 0
         while 2 ** (rounds + 1) < groups - 1:
@@ -187,19 +187,19 @@
         for _ in range(rounds):
             got = group_shift(both, axis, groups, shift)
             tail = jnp.concatenate([zeros, both[:, rank:]], axis=1)
-            both = jnp.dot(both[:, :rank], got, precision=HIGHEST) + tail
+            both = jnp.dot(both[:, :rank], got, precision=lax.Precision.HIGH) + tail
             shift *= 2
         near = group_shift(both, axis, groups, 1)
         far = group_shift(both[:, rank:], axis, groups, 1 + shift)
-        start = jnp.dot(near[:, :rank], far, precision=HIGHEST) + near[:, rank:]
+        start = jnp.dot(near[:, :rank], far, precision=lax.Precision.HIGH) + near[:, rank:]
     back = [(4 * g + 2, 4 * g) for g in range(groups)]
     back += [(4 * g + 1, 4 * g + 3) for g in range(groups)]
     sent = lax.ppermute(start, axis, back)
-    mine = jnp.dot(beside_map, start, precision=HIGHEST) + beside_state
+    mine = jnp.dot(beside_map, start, precision=lax.Precision.HIGH) + beside_state
     mine, sent = lax.optimization_barrier((mine, sent))
     holder = jnp.logical_or(place == 1, place == 2)
     enter = jnp.where(holder, mine, sent)
-    send = jnp.dot(own[:, :rank], enter, precision=HIGHEST) + own[:, rank:]
+    send = jnp.dot(own[:, :rank], enter, precision=lax.Precision.HIGH) + own[:, rank:]
     other = lax.ppermute(send, axis, partner)
     return enter, other
 

time: 52.6 us -> 52.2 us (level)
  matrix products: 6.05 us -> 5.21 us
    dot_general x7, matrix products: 5.63 us -> 4.79 us  [the longest x1 1.41 us: scan_groups(): jnp.dot(beside_map, start, precision=lax.Precision.HIGH) + beside_state]
where the time goes in v23:
time: 52.2 us; the launch traced here: 51.5 us
  waiting for transfers between devices  20.2 us (39%)
  starting transfers between devices  14.6 us (28%)
  Pallas kernels  9.19 us (18%)
  matrix products  5.21 us (10%)
  local copies, waits for them, and re-layouts  2.07 us (4%)
    ppermute x3, waiting for transfers between devices, group_shift(): return lax.ppermute(value, axis, pairs)  12.6 us
    ppermute x1, starting transfers between devices, scan_groups(): other = lax.ppermute(send, axis, partner)  6.74 us
    pallas_call x1, Pallas kernels, shards(): pl.pallas_call(sweep_kernel, out_shape=(jax.ShapeDtypeStruct((rank, rank...  6.06 us
    ppermute x3, starting transfers between devices, group_shift(): return lax.ppermute(value, axis, pairs)  3.98 us
    ppermute x1, waiting for transfers between devices, scan_groups(): beside_state = lax.ppermute(both[:, rank:], axis, pair)  3.35 us
    pallas_call x1, Pallas kernels, shards(): pl.pallas_call(apply_kernel, out_shape=jax.ShapeDtypeStruct((count, rows,...  3.13 us
    unnamed x22, local copies, waits for them, and re-layouts  2.03 us
    ppermute x1, waiting for transfers between devices, scan_groups(): got = lax.ppermute(give, axis, partner)  1.93 us
  transfers between devices with their start and end apart: 8, of which 8 were waited for; matrix products, arithmetic and copies ran while one was open for 5% of the time, Pallas kernels for 0%

profile of v23, /device:TPU:1, one launch (start us, length us, event | category | flops | bytes accessed | tf_op | source)
XLA Modules:
  0.0 51.5 jit_solution(18195173286608428335)
XLA Ops:
  0.0 0.0 copy-start
  0.0 6.1 %sweep.1 = (f32[256,384]{1,0:T(8,128)}, f32[256,384]{1,0:T(8,128)}) custom-call(s32[1]{0:T(128)} %bitcast.flag_ref, bf16[8,256,128]{2,1,0:T(8,128)(2,1)} %rhs_ref.3, bf16[8,256,256]{2,1,0:T(8,128)(2,1)} %lcols_ref.3, bf16[8,256,256]{2,1,0:T(8,128)(2,1)} %ltrans_ref.3, bf16[8,256,256]{2,1,0:T(8,128)(2,1)} %ucols_ref.3, bf16[8,256,256]{2,1,0:T(8,128)(2,1)} %utrans_ref.3), custom_call_target="tpu_custom_call" | custom-call | tf_op jit(solution)/shard_map/sweep/pallas_call | solution.py:225
  6.1 0.0 collective-permute-start
  6.1 1.9 %collective-permute-done = f32[256,384]{1,0:T(8,128)S(1)} collective-permute-done((f32[256,384]{1,0:T(8,128)}, f32[256,384]{1,0:T(8,128)S(1)}, u32[]{:S(2)}, u32[]{:S(2)}) %collective-permute-start) | collective-permute-done | bytes 393248 | tf_op jit(solution)/shard_map/ppermute | solution.py:164
  8.0 1.4 %convolution_add_fusion = f32[256,384]{1,0:T(8,128)S(1)} fusion(f32[256,384]{1,0:T(8,128)} %get-tuple-element.10, f32[256,128]{1,0:T(8,128)S(1)} %slice.28, f32[256,384]{1,0:T(8,128)S(1)} %collective-permute-done), kind=kOutput, calls=%fused_computation | convolution fusion | flops 151093248 | bytes 1179648 | tf_op jit(solution)/shard_map/dot_general | solution.py:165
  9.4 1.3 %collective-permute-start.2 = (f32[256,128]{1,0:T(8,128)S(1)}, f32[256,128]{1,0:T(8,128)S(1)}, u32[]{:S(2)}, u32[]{:S(2)}) collective-permute-start(f32[256,128]{1,0:T(8,128)S(1)} %slice.30), channel_id=1, source_target_pairs={{0,2},{4,6},{8,10},{12,14},{3,1},{7,5},{11,9},{15,13},{16,18},{20,... | collective-permute-start | bytes 393224 | tf_op jit(solution)/shard_map/ppermute | solution.py:170
  10.7 1.3 %collective-permute-start.1 = (f32[256,256]{1,0:T(8,128)S(1)}, f32[256,256]{1,0:T(8,128)S(1)}, u32[]{:S(2)}, u32[]{:S(2)}) collective-permute-start(f32[256,256]{1,0:T(8,128)S(1)} %slice.29), channel_id=1, source_target_pairs={{0,2},{4,6},{8,10},{12,14},{3,1},{7,5},{11,9},{15,13},{16,18},{20,... | collective-permute-start | bytes 786440 | tf_op jit(solution)/shard_map/ppermute | solution.py:171
  12.0 3.3 %collective-permute-done.2 = f32[256,128]{1,0:T(8,128)S(1)} collective-permute-done((f32[256,128]{1,0:T(8,128)S(1)}, f32[256,128]{1,0:T(8,128)S(1)}, u32[]{:S(2)}, u32[]{:S(2)}) %collective-permute-start.2) | collective-permute-done | bytes 131104 | tf_op jit(solution)/shard_map/ppermute | solution.py:170
  15.4 0.0 copy-start.10
  15.4 0.0 copy-start.8
  15.4 0.3 convolution_add_fusion.5
  15.7 0.4 copy-done.10
  16.0 1.3 %collective-permute-start.3 = (f32[256,128]{1,0:T(8,128)S(1)}, f32[256,128]{1,0:T(8,128)S(1)}, u32[]{:S(2)}, u32[]{:S(2)}) collective-permute-start(f32[256,128]{1,0:T(8,128)S(1)} %convolution_add_fusion.5), channel_id=1, source_target_pairs={{2,6},{6,10},{10,14},{5,1},{9,5},{13,9},{18,22},{22,26},{26,30},{2... | collective-permute-start | bytes 393224 | tf_op jit(solution)/shard_map/ppermute | solution.py:153
  17.3 0.9 %collective-permute-done.1 = f32[256,256]{1,0:T(8,128)S(1)} collective-permute-done((f32[256,256]{1,0:T(8,128)S(1)}, f32[256,256]{1,0:T(8,128)S(1)}, u32[]{:S(2)}, u32[]{:S(2)}) %collective-permute-start.1) | collective-permute-done | bytes 262176 | tf_op jit(solution)/shard_map/ppermute | solution.py:171
  18.2 0.0 copy-start.9
  18.2 0.0 copy-start.6
  18.2 0.3 fusion.3
  18.5 0.4 copy-done.9
  18.9 3.5 %collective-permute-done.3 = f32[256,128]{1,0:T(8,128)S(1)} collective-permute-done((f32[256,128]{1,0:T(8,128)S(1)}, f32[256,128]{1,0:T(8,128)S(1)}, u32[]{:S(2)}, u32[]{:S(2)}) %collective-permute-start.3) | collective-permute-done | bytes 131104 | tf_op jit(solution)/shard_map/ppermute | solution.py:153
  22.4 0.0 copy-start.5
  22.4 0.3 convolution_add_fusion.4
  22.7 1.4 %collective-permute-start.4 = (f32[256,128]{1,0:T(8,128)S(1)}, f32[256,128]{1,0:T(8,128)S(1)}, u32[]{:S(2)}, u32[]{:S(2)}) collective-permute-start(f32[256,128]{1,0:T(8,128)S(1)} %convolution_add_fusion.4), channel_id=1, source_target_pairs={{2,6},{6,10},{10,14},{5,1},{9,5},{13,9},{18,22},{22,26},{26,30},{2... | collective-permute-start | bytes 393224 | tf_op jit(solution)/shard_map/ppermute | solution.py:153
  24.1 4.4 %collective-permute-done.4 = f32[256,128]{1,0:T(8,128)S(1)} collective-permute-done((f32[256,128]{1,0:T(8,128)S(1)}, f32[256,128]{1,0:T(8,128)S(1)}, u32[]{:S(2)}, u32[]{:S(2)}) %collective-permute-start.4) | collective-permute-done | bytes 131104 | tf_op jit(solution)/shard_map/ppermute | solution.py:153
  28.5 0.9 %convolution_add_fusion.3 = f32[256,128]{1,0:T(8,128)} fusion(f32[256,128]{1,0:T(8,128)S(1)} %convolution_add_fusion.5, f32[256,256]{1,0:T(8,128)S(1)} %fusion.3, f32[256,128]{1,0:T(8,128)S(1)} %collective-permute-done.4), kind=kOutput, calls=%fused_computation.3 | convolution fusion | flops 50364416 | bytes 655360 | tf_op jit(solution)/shard_map/dot_general | solution.py:181
  29.5 1.3 %collective-permute-start.5 = (f32[256,128]{1,0:T(8,128)}, f32[256,128]{1,0:T(8,128)}, u32[]{:S(2)}, u32[]{:S(2)}) collective-permute-start(f32[256,128]{1,0:T(8,128)} %convolution_add_fusion.3), channel_id=1, source_target_pairs={{2,6},{6,10},{10,14},{5,1},{9,5},{13,9},{18,22},{22,26},{26,30},{2... | collective-permute-start | bytes 393224 | tf_op jit(solution)/shard_map/ppermute | solution.py:153
  30.8 4.7 %collective-permute-done.5 = f32[256,128]{1,0:T(8,128)} collective-permute-done((f32[256,128]{1,0:T(8,128)}, f32[256,128]{1,0:T(8,128)}, u32[]{:S(2)}, u32[]{:S(2)}) %collective-permute-start.5) | collective-permute-done | bytes 131104 | tf_op jit(solution)/shard_map/ppermute | solution.py:153
  35.5 1.3 %collective-permute-start.6 = (f32[256,128]{1,0:T(8,128)}, f32[256,128]{1,0:T(8,128)S(1)}, u32[]{:S(2)}, u32[]{:S(2)}) collective-permute-start(f32[256,128]{1,0:T(8,128)} %collective-permute-done.5), channel_id=1, source_target_pairs={{2,0},{6,4},{10,8},{14,12},{1,3},{5,7},{9,11},{13,15},{18,16},{22,... | collective-permute-start | bytes 393224 | tf_op jit(solution)/shard_map/ppermute | solution.py:197
  36.8 0.0 copy-start.4
  36.8 1.4 %convolution_add_fusion.2 = f32[256,128]{1,0:T(8,128)S(1)} fusion(f32[256,128]{1,0:T(8,128)} %copy-done.10, f32[256,256]{1,0:T(8,128)} %copy-done.9, f32[256,128]{1,0:T(8,128)} %collective-permute-done.5), kind=kOutput, calls=%fused_computation.2 | convolution fusion | flops 50364416 | bytes 655360 | tf_op jit(solution)/shard_map/dot_general | solution.py:198
  38.2 0.0 copy-start.1
  38.2 0.8 %collective-permute-done.6 = f32[256,128]{1,0:T(8,128)S(1)} collective-permute-done((f32[256,128]{1,0:T(8,128)}, f32[256,128]{1,0:T(8,128)S(1)}, u32[]{:S(2)}, u32[]{:S(2)}) %collective-permute-start.6) | collective-permute-done | bytes 131104 | tf_op jit(solution)/shard_map/ppermute | solution.py:197
  39.0 0.0 copy-done.8
  39.0 0.3 convolution_add_fusion.1
  39.3 0.0 copy-start.2
  39.3 0.0 copy-start.3
  39.3 6.7 %collective-permute-start.7 = (f32[256,128]{1,0:T(8,128)S(1)}, f32[256,128]{1,0:T(8,128)S(1)}, u32[]{:S(2)}, u32[]{:S(2)}) collective-permute-start(f32[256,128]{1,0:T(8,128)S(1)} %convolution_add_fusion.1), channel_id=1, source_target_pairs={{0,1},{2,3},{4,5},{6,7},{8,9},{10,11},{12,13},{14,15},{1,0},{3,2},... | collective-permute-start | bytes 393224 | tf_op jit(solution)/shard_map/ppermute | solution.py:203
  46.1 0.0 copy-done
  46.1 0.0 copy-done.1
  46.1 0.4 fusion.5.diag_ref
  46.5 0.6 %collective-permute-done.7.other_ref = f32[256,128]{1,0:T(8,128)S(1)} collective-permute-done((f32[256,128]{1,0:T(8,128)S(1)}, f32[256,128]{1,0:T(8,128)S(1)}, u32[]{:S(2)}, u32[]{:S(2)}) %collective-permute-start.7) | collective-permute-done | bytes 131104 | tf_op jit(solution)/shard_map/ppermute | solution.py:203
  47.1 0.0 copy-done.6
  47.1 0.0 copy-done.5
  47.1 0.0 copy-done.4
  47.1 0.0 copy-done.2
  47.1 0.0 copy-done.3
  47.1 0.0 copy-start.7
  47.1 1.2 %copy-done.7 = bf16[8,256,256]{2,1,0:T(8,128)(2,1)S(1)} copy-done((bf16[8,256,256]{2,1,0:T(8,128)(2,1)S(1)}, bf16[8,256,256]{2,1,0:T(8,128)(2,1)}, u32[]{:S(2)}) %copy-start.7) | copy-done | bytes 1048600
  48.3 3.1 %apply.1 = bf16[8,256,128]{2,1,0:T(8,128)(2,1)} custom-call(s32[1]{0:T(128)} %bitcast.flag_ref, f32[256,128]{1,0:T(8,128)S(1)} %broadcast_select_fusion.enter_ref, f32[256,128]{1,0:T(8,128)S(1)} %collective-permute-done.7.other_ref, bf16[8,256,256]{2,1,0:T(8,128)(2,1)S(1)} %copy-done.3, bf16[8,256,256]{2,1,0:T(8,128)(2,1)S(1)} %copy-done.5, ...), custom_call_target="tpu_custom_call" | custom-call | tf_op jit(solution)/shard_map/apply/pallas_call | solution.py:248
  (4 shorter events, 0.1 us)
Async XLA Ops:
  0.0 46.1 %copy-start = (bf16[8,256,256]{2,1,0:T(8,128)(2,1)S(1)}, bf16[8,256,256]{2,1,0:T(8,128)(2,1)}, u32[]{:S(2)}) copy-start(bf16[8,256,256]{2,1,0:T(8,128)(2,1)} %param.9) | copy-start | bytes 3145732
  6.1 1.9 %collective-permute-start = (f32[256,384]{1,0:T(8,128)}, f32[256,384]{1,0:T(8,128)S(1)}, u32[]{:S(2)}, u32[]{:S(2)}) collective-permute-start(f32[256,384]{1,0:T(8,128)} %get-tuple-element.9), channel_id=1, source_target_pairs={{0,1},{2,3},{4,5},{6,7},{8,9},{10,11},{12,13},{14,15},{1,0},{3,2},... | collective-permute-start | bytes 1179656 | tf_op jit(solution)/shard_map/ppermute | solution.py:164
  9.4 6.0 %collective-permute-start.2 = (f32[256,128]{1,0:T(8,128)S(1)}, f32[256,128]{1,0:T(8,128)S(1)}, u32[]{:S(2)}, u32[]{:S(2)}) collective-permute-start(f32[256,128]{1,0:T(8,128)S(1)} %slice.30), channel_id=1, source_target_pairs={{0,2},{4,6},{8,10},{12,14},{3,1},{7,5},{11,9},{15,13},{16,18},{20,... | collective-permute-start | bytes 393224 | tf_op jit(solution)/shard_map/ppermute | solution.py:170
  10.7 7.5 %collective-permute-start.1 = (f32[256,256]{1,0:T(8,128)S(1)}, f32[256,256]{1,0:T(8,128)S(1)}, u32[]{:S(2)}, u32[]{:S(2)}) collective-permute-start(f32[256,256]{1,0:T(8,128)S(1)} %slice.29), channel_id=1, source_target_pairs={{0,2},{4,6},{8,10},{12,14},{3,1},{7,5},{11,9},{15,13},{16,18},{20,... | collective-permute-start | bytes 786440 | tf_op jit(solution)/shard_map/ppermute | solution.py:171
  15.4 0.6 %copy-start.10 = (f32[256,128]{1,0:T(8,128)}, f32[256,128]{1,0:T(8,128)S(1)}, u32[]{:S(2)}) copy-start(f32[256,128]{1,0:T(8,128)S(1)} %collective-permute-done.2) | copy-start | bytes 393220
  15.4 23.6 %copy-start.8 = (f32[256,384]{1,0:T(8,128)S(1)}, f32[256,384]{1,0:T(8,128)}, u32[]{:S(2)}) copy-start(f32[256,384]{1,0:T(8,128)} %get-tuple-element.10) | copy-start | bytes 1179652
  16.0 6.4 %collective-permute-start.3 = (f32[256,128]{1,0:T(8,128)S(1)}, f32[256,128]{1,0:T(8,128)S(1)}, u32[]{:S(2)}, u32[]{:S(2)}) collective-permute-start(f32[256,128]{1,0:T(8,128)S(1)} %convolution_add_fusion.5), channel_id=1, source_target_pairs={{2,6},{6,10},{10,14},{5,1},{9,5},{13,9},{18,22},{22,26},{26,30},{2... | collective-permute-start | bytes 393224 | tf_op jit(solution)/shard_map/ppermute | solution.py:153
  18.2 0.7 %copy-start.9 = (f32[256,256]{1,0:T(8,128)}, f32[256,256]{1,0:T(8,128)S(1)}, u32[]{:S(2)}) copy-start(f32[256,256]{1,0:T(8,128)S(1)} %collective-permute-done.1) | copy-start | bytes 786436
  18.2 28.9 %copy-start.6 = (bf16[8,256,256]{2,1,0:T(8,128)(2,1)S(1)}, bf16[8,256,256]{2,1,0:T(8,128)(2,1)}, u32[]{:S(2)}) copy-start(bf16[8,256,256]{2,1,0:T(8,128)(2,1)} %lrows_ref.1) | copy-start | bytes 3145732
  22.4 24.7 %copy-start.5 = (bf16[8,256,256]{2,1,0:T(8,128)(2,1)S(1)}, bf16[8,256,256]{2,1,0:T(8,128)(2,1)}, u32[]{:S(2)}) copy-start(bf16[8,256,256]{2,1,0:T(8,128)(2,1)} %utrans_ref.3) | copy-start | bytes 3145732
  22.7 5.8 %collective-permute-start.4 = (f32[256,128]{1,0:T(8,128)S(1)}, f32[256,128]{1,0:T(8,128)S(1)}, u32[]{:S(2)}, u32[]{:S(2)}) collective-permute-start(f32[256,128]{1,0:T(8,128)S(1)} %convolution_add_fusion.4), channel_id=1, source_target_pairs={{2,6},{6,10},{10,14},{5,1},{9,5},{13,9},{18,22},{22,26},{26,30},{2... | collective-permute-start | bytes 393224 | tf_op jit(solution)/shard_map/ppermute | solution.py:153
  29.5 6.0 %collective-permute-start.5 = (f32[256,128]{1,0:T(8,128)}, f32[256,128]{1,0:T(8,128)}, u32[]{:S(2)}, u32[]{:S(2)}) collective-permute-start(f32[256,128]{1,0:T(8,128)} %convolution_add_fusion.3), channel_id=1, source_target_pairs={{2,6},{6,10},{10,14},{5,1},{9,5},{13,9},{18,22},{22,26},{26,30},{2... | collective-permute-start | bytes 393224 | tf_op jit(solution)/shard_map/ppermute | solution.py:153
  35.5 3.5 %collective-permute-start.6 = (f32[256,128]{1,0:T(8,128)}, f32[256,128]{1,0:T(8,128)S(1)}, u32[]{:S(2)}, u32[]{:S(2)}) collective-permute-start(f32[256,128]{1,0:T(8,128)} %collective-permute-done.5), channel_id=1, source_target_pairs={{2,0},{6,4},{10,8},{14,12},{1,3},{5,7},{9,11},{13,15},{18,16},{22,... | collective-permute-start | bytes 393224 | tf_op jit(solution)/shard_map/ppermute | solution.py:197
  36.8 10.3 %copy-start.4 = (bf16[8,256,256]{2,1,0:T(8,128)(2,1)S(1)}, bf16[8,256,256]{2,1,0:T(8,128)(2,1)}, u32[]{:S(2)}) copy-start(bf16[8,256,256]{2,1,0:T(8,128)(2,1)} %ucols_ref.3) | copy-start | bytes 3145732
  38.2 7.9 %copy-start.1 = (bf16[8,256,128]{2,1,0:T(8,128)(2,1)S(1)}, bf16[8,256,128]{2,1,0:T(8,128)(2,1)}, u32[]{:S(2)}) copy-start(bf16[8,256,128]{2,1,0:T(8,128)(2,1)} %rhs_ref.3) | copy-start | bytes 1572868
  39.3 7.8 %copy-start.2 = (bf16[8,256,256]{2,1,0:T(8,128)(2,1)S(1)}, bf16[8,256,256]{2,1,0:T(8,128)(2,1)}, u32[]{:S(2)}) copy-start(bf16[8,256,256]{2,1,0:T(8,128)(2,1)} %lcols_ref.3) | copy-start | bytes 3145732
  39.3 7.8 %copy-start.3 = (bf16[8,256,256]{2,1,0:T(8,128)(2,1)S(1)}, bf16[8,256,256]{2,1,0:T(8,128)(2,1)}, u32[]{:S(2)}) copy-start(bf16[8,256,256]{2,1,0:T(8,128)(2,1)} %ltrans_ref.3) | copy-start | bytes 3145732
  39.3 7.7 %collective-permute-start.7 = (f32[256,128]{1,0:T(8,128)S(1)}, f32[256,128]{1,0:T(8,128)S(1)}, u32[]{:S(2)}, u32[]{:S(2)}) collective-permute-start(f32[256,128]{1,0:T(8,128)S(1)} %convolution_add_fusion.1), channel_id=1, source_target_pairs={{0,1},{2,3},{4,5},{6,7},{8,9},{10,11},{12,13},{14,15},{1,0},{3,2},... | collective-permute-start | bytes 393224 | tf_op jit(solution)/shard_map/ppermute | solution.py:203
  47.1 1.2 %copy-start.7 = (bf16[8,256,256]{2,1,0:T(8,128)(2,1)S(1)}, bf16[8,256,256]{2,1,0:T(8,128)(2,1)}, u32[]{:S(2)}) copy-start(bf16[8,256,256]{2,1,0:T(8,128)(2,1)} %urows_ref.1) | copy-start | bytes 3145732
